TPU v7x, 32 devices: a whole 2x2x4 slice. The times are simulated.
32 devices in a mesh: groups: 2 (over y), gx: 4 (over z), gy: 2 (over x), gz: 2 (over core).
Axes of the slice: x: 2, y: 2, z: 4, core: 2. Of those that a mesh axis runs over, the one named last changes fastest.
Arguments:
- stream: float32 [256, 64, 512], P('groups', 'gx', 'gy'), parts along dimension 0, may hold values from -6 to 6
- inductance: bfloat16 [16, 32, 8, 2, 128, 128], P(('groups', 'gx'), ('gy', 'gz')), parts along dimension 0, may hold values from -0.25 to 1.25
- near_lists: int32 [16, 32, 8], P(('groups', 'gx'), ('gy', 'gz')), parts along dimension 0, may hold values from 0 to 8, as said below
- filament_leaf: int32 [16384], P(('groups', 'gx', 'gy', 'gz')), parts along dimension 0, may hold values from 0 to 255, as said below
- filament_current: bfloat16 [16384, 128], P(('groups', 'gx', 'gy', 'gz')), parts along dimension 0, may hold values from -6 to 6
- filament_coupling: bfloat16 [16384, 2, 128], P(('groups', 'gx', 'gy', 'gz')), parts along dimension 0, may hold values from -0.75 to 0.75
Outputs:
- loop_voltage: float32 [256, 64, 512], P('groups', 'gx', ('gy', 'gz')), parts along dimension 0
- filament_voltage: bfloat16 [16384, 128], P(('groups', 'gx', 'gy', 'gz')), parts along dimension 0
There are 2 independent parts, one for each index of `groups`. A program takes and returns all parts, laid end to end along the dimension named above; each array names one. Nothing has to cross between parts.
Inputs may be any that keep to these rules, and one draw needn't show every extreme that they name: `near_lists`: entry 0 of every list is 4, the leaf itself; code k names the leaf k // 3 - 1 rows and k % 3 - 1 columns away, and repeats may occur. `filament_leaf`: leaves are numbered row by row over 8 x 32. Device d along gx+gy+gz holds the 2 x 8 leaves of leaf rows (d // (2 * 2)) * 2 on and leaf columns (d % (2 * 2)) * 8 on. Of the 512 filaments of one device, at most 64 lie over the leaves of any one device, and in every device's block some device gets exactly 64.
All inputs are finite; a program needn't handle non-finite values.
Results may differ from a plain program's by a relative error of at most 0.0049.
Values may be sent and summed in bfloat16 or wider, within the bound.
No kernel may reach another device: no remote copies, remote signals or barrier semaphores. Data moves between devices by JAX's collectives and lax.ppermute only.
A program may use at most 128 MiB of HBM per device.

v0:
```python
import jax
import jax.numpy as jnp
from jax import lax
from jax.sharding import PartitionSpec as P

LEAF_R = 8
LEAF_C = 16


def with_halo(value, sides, width):
    for axis, dim in sides:
        size, length = (lax.axis_size(axis), value.shape[dim])
        up = [(i, (i + 1) % size) for i in range(size - 1)]
        down = [(j, i) for i, j in up]
        last = lax.slice_in_dim(value, length - width, length, axis=dim)
        leading = lax.slice_in_dim(value, 0, width, axis=dim)
        before = lax.ppermute(last, axis, up)
        after = lax.ppermute(leading, axis, down)
        value = jnp.concatenate([before, value, after], axis=dim)
    return value


def plane_curl(padded):
    along_y = padded[:, 1:-1, 2:] - padded[:, 1:-1, :-2]
    along_x = padded[:, :-2, 1:-1] - padded[:, 2:, 1:-1]
    return jnp.stack([along_y, along_x])


def to_leaves(grid_values):
    components, port_count, row_count, col_count = grid_values.shape
    blocks = grid_values.reshape(
        components, port_count, row_count // LEAF_R, LEAF_R, col_count // LEAF_C, LEAF_C
    )
    blocks = blocks.transpose(2, 4, 0, 1, 3, 5)
    return blocks.reshape(
        row_count // LEAF_R, col_count // LEAF_C, components, port_count, LEAF_R * LEAF_C
    )


def from_leaves(leaves):
    leaf_rows, leaf_cols, components, port_count, leaf_cells = leaves.shape
    blocks = leaves.reshape(leaf_rows, leaf_cols, components, port_count, LEAF_R, LEAF_C)
    blocks = blocks.transpose(2, 3, 0, 4, 1, 5)
    return blocks.reshape(components, port_count, leaf_rows * LEAF_R, leaf_cols * LEAF_C)


def body(stream, inductance, near_lists, filament_leaf, filament_current, filament_coupling):
    port_count = stream.shape[0]
    leaf_rows = inductance.shape[0]
    leaf_cols = inductance.shape[1]
    near_count = inductance.shape[2]
    leaf_cells = inductance.shape[4]
    leaf_count = leaf_rows * leaf_cols
    half_cols = leaf_cols * LEAF_C
    core_count = lax.axis_size("gz")
    core_index = lax.axis_index("gz")
    first_col = core_index * half_cols
    padded = with_halo(stream, (("gx", 1), ("gy", 2)), 1)
    window = lax.dynamic_slice_in_dim(padded, first_col, half_cols + 2, 2)
    currents = plane_curl(window).astype(jnp.bfloat16)
    bordered = with_halo(to_leaves(currents), (("gx", 0), (("gy", "gz"), 1)), 1)
    row_stride = leaf_cols + 2
    flattened = bordered.reshape((leaf_rows + 2) * row_stride, 2, port_count, leaf_cells)
    row_shift = near_lists // 3 - 1
    col_shift = near_lists % 3 - 1
    source = (jnp.arange(leaf_rows, dtype=jnp.int32)[:, None, None] + 1 + row_shift) * row_stride
    source = source + jnp.arange(leaf_cols, dtype=jnp.int32)[None, :, None] + 1 + col_shift
    sources = jnp.take(flattened, source.reshape(-1), axis=0).reshape(
        leaf_count, near_count, 2, port_count, leaf_cells
    )
    kernels = inductance.reshape(leaf_count, near_count, 2, leaf_cells, leaf_cells)
    near_field = lax.dot_general(
        sources, kernels, (((1, 4), (1, 4)), ((0, 2), (0, 2))), preferred_element_type=jnp.float32
    )
    own_leaves = bordered[1:-1, 1:-1].reshape(leaf_count, 2, port_count, leaf_cells)
    owners = lax.axis_size("gx") * lax.axis_size("gy") * core_count
    filament_count = filament_leaf.shape[0]
    capacity = max(2, 2 * filament_count // owners)
    slot_count = owners * capacity
    plane_cols = leaf_cols * lax.axis_size("gy") * core_count
    leaf_row = filament_leaf // plane_cols
    leaf_col = filament_leaf % plane_cols
    owner_ids = leaf_row // leaf_rows * (lax.axis_size("gy") * core_count) + leaf_col // leaf_cols
    local_ids = leaf_row % leaf_rows * leaf_cols + leaf_col % leaf_cols
    owner_hits = (owner_ids[:, None] == jnp.arange(owners, dtype=jnp.int32)[None, :]).astype(
        jnp.int32
    )
    position = jnp.sum((jnp.cumsum(owner_hits, axis=0) - 1) * owner_hits, axis=1)
    target_slot = owner_ids * capacity + position
    placement_mask = target_slot[None, :] == jnp.arange(slot_count, dtype=jnp.int32)[:, None]
    placement = placement_mask.astype(jnp.bfloat16)
    coupling_rows = filament_coupling.reshape(filament_count, 2 * leaf_cells)
    sent_coupling = jnp.dot(placement, coupling_rows, preferred_element_type=jnp.float32).astype(
        jnp.bfloat16
    )
    sent_current = jnp.dot(placement, filament_current, preferred_element_type=jnp.float32).astype(
        jnp.bfloat16
    )
    sent_leaf = jnp.max(jnp.where(placement_mask, local_ids[None, :], -1), axis=1)
    send_coupling = sent_coupling.reshape(owners, capacity, 2 * leaf_cells)
    send_current = sent_current.reshape(owners, capacity, port_count)
    send_leaf = sent_leaf.reshape(owners, capacity)
    got_coupling, got_current, got_leaf = (
        lax.all_to_all(send_coupling, ("gx", "gy", "gz"), split_axis=0, concat_axis=0, tiled=True),
        lax.all_to_all(send_current, ("gx", "gy", "gz"), split_axis=0, concat_axis=0, tiled=True),
        lax.all_to_all(send_leaf, ("gx", "gy", "gz"), split_axis=0, concat_axis=0, tiled=True),
    )
    got_coupling = got_coupling.reshape(slot_count, 2 * leaf_cells)
    got_current = got_current.reshape(slot_count, port_count)
    got_leaf = got_leaf.reshape(slot_count)
    leaf_hits = (got_leaf[:, None] == jnp.arange(leaf_count, dtype=jnp.int32)[None, :]).astype(
        jnp.bfloat16
    )
    spread = (leaf_hits[:, :, None] * got_coupling[:, None, :]).reshape(
        slot_count, leaf_count * 2 * leaf_cells
    )
    filament_field = lax.dot_general(
        got_current, spread, (((0,), (0,)), ((), ())), preferred_element_type=jnp.float32
    )
    filament_field = filament_field.reshape(port_count, leaf_count, 2, leaf_cells).transpose(
        1, 2, 0, 3
    )
    plane_rows = own_leaves.transpose(2, 0, 1, 3).reshape(port_count, leaf_count * 2 * leaf_cells)
    induced = lax.dot_general(
        spread, plane_rows, (((1,), (1,)), ((), ())), preferred_element_type=jnp.float32
    ).astype(jnp.bfloat16)
    returned = lax.all_to_all(
        induced.reshape(owners, capacity, port_count),
        ("gx", "gy", "gz"),
        split_axis=0,
        concat_axis=0,
        tiled=True,
    )
    returned = returned.reshape(slot_count, port_count)
    filament_voltage = lax.dot_general(
        placement, returned, (((0,), (0,)), ((), ())), preferred_element_type=jnp.float32
    ).astype(jnp.bfloat16)
    total_field = (near_field + filament_field).astype(jnp.bfloat16)
    grid_field = from_leaves(total_field.reshape(leaf_rows, leaf_cols, 2, port_count, leaf_cells))
    bordered_field = with_halo(grid_field, (("gx", 2), (("gy", "gz"), 3)), 1)
    x_field = bordered_field[0].astype(jnp.float32)
    y_field = bordered_field[1].astype(jnp.float32)
    loop_voltage = (
        x_field[:, 1:-1, :-2]
        - x_field[:, 1:-1, 2:]
        + (y_field[:, 2:, 1:-1] - y_field[:, :-2, 1:-1])
    )
    return (loop_voltage, filament_voltage)


def solution(mesh):
    return jax.shard_map(
        body,
        mesh=mesh,
        in_specs=(
            P("groups", "gx", "gy"),
            P(("groups", "gx"), ("gy", "gz"), None, None, None, None),
            P(("groups", "gx"), ("gy", "gz"), None),
            P(("groups", "gx", "gy", "gz")),
            P(("groups", "gx", "gy", "gz"), None),
            P(("groups", "gx", "gy", "gz"), None, None),
        ),
        out_specs=(P("groups", "gx", ("gy", "gz")), P(("groups", "gx", "gy", "gz"), None)),
        check_vma=False,
    )
```

profile of v0, /device:TPU:0, one launch (start us, length us, event | category | flops | bytes accessed | tf_op | source)
XLA Modules:
  0.0 139.7 jit_solution(7152915620468083119)
XLA Ops:
  0.6 0.7 fusion.43
  1.4 1.2 reduce-window.6
  2.6 0.2 slice_reduce_fusion
  2.8 0.1 fusion.30
  2.9 0.4 select_reduce_fusion
  3.3 0.7 all_to_all.16
  4.0 7.4 %all-to-all-start.1 = ((s32[16,1,64]{2,1,0:T(1,128)}), s32[16,1,64]{2,1,0:T(1,128)S(1)}, u32[]{:S(2)}, u32[]{:S(2)}) async-start(s32[16,1,64]{2,1,0:T(1,128)} %all_to_all.16), calls=%async_computation.1 | async-start | bytes 16384 | tf_op jit(solution)/shard_map/all_to_all | solution.py:106
  11.3 2.0 %copy.46 = f32[128,16,256]{0,2,1:T(8,128)S(1)} copy(f32[128,16,256]{2,1,0:T(8,128)} %param.6) | data formatting | bytes 4194304 | tf_op args[0]
  13.3 3.8 %collective-permute-start = (f32[128,1,256]{0,2,1:T(8,128)S(1)}, f32[128,1,256]{0,2,1:T(8,128)S(1)}, u32[]{:S(2)}, u32[]{:S(2)}) collective-permute-start(f32[128,1,256]{0,2,1:T(8,128)S(1)} %get-tuple-element.12), channel_id=1, source_target_pairs={{0,4},{4,8},{8,12},{1,5},{5,9},{9,13},{2,6},{6,10},{10,14},{3,7},{... | collective-permute-start | bytes 393224 | tf_op jit(solution)/shard_map/ppermute | solution.py:17
  17.2 1.3 collective-permute-start.1
  18.5 1.4 fusion.11
  19.9 1.2 fusion.16
  21.0 3.3 %collective-permute-done.1 = f32[128,1,256]{0,2,1:T(8,128)S(1)} collective-permute-done((f32[128,1,256]{0,2,1:T(8,128)S(1)}, f32[128,1,256]{0,2,1:T(8,128)S(1)}, u32[]{:S(2)}, u32[]{:S(2)}) %collective-permute-start.1) | collective-permute-done | bytes 131104 | tf_op jit(solution)/shard_map/ppermute | solution.py:18
  24.4 1.3 collective-permute-start.3
  25.7 4.5 %collective-permute-start.2 = (f32[128,18,1]{0,2,1:T(1,128)S(1)}, f32[128,18,1]{0,2,1:T(1,128)S(1)}, u32[]{:S(2)}, u32[]{:S(2)}) collective-permute-start(f32[128,18,1]{0,2,1:T(1,128)S(1)} %get-tuple-element.9), channel_id=1, source_target_pairs={{0,2},{1,3},{4,6},{5,7},{8,10},{9,11},{12,14},{13,15},{16,18},{17,... | collective-permute-start | bytes 27656 | tf_op jit(solution)/shard_map/ppermute | solution.py:17
  30.2 0.1 fusion.58
  30.3 1.3 collective-permute-done.2
  31.6 0.4 fusion.13
  32.0 0.3 fusion.20
  32.3 0.1 maximum_bitcast_fusion
  32.4 0.3 fusion.50
  32.7 0.8 copy.49
  33.5 0.8 copy.51
  34.4 1.3 collective-permute-start.5
  35.7 4.6 %collective-permute-start.4 = (bf16[1,8,2,128,128]{3,4,2,1,0:T(8,128)(2,1)}, bf16[1,8,2,128,128]{3,4,2,1,0:T(8,128)(2,1)S(1)}, u32[]{:S(2)}, u32[]{:S(2)}) collective-permute-start(bf16[1,8,2,128,128]{3,4,2,1,0:T(8,128)(2,1)} %bitcast.4), channel_id=1, source_target_pairs={{0,4},{4,8},{8,12},{1,5},{5,9},{9,13},{2,6},{6,10},{10,14},{3,7},{... | collective-permute-start | bytes 1572872 | tf_op jit(solution)/shard_map/ppermute | solution.py:17
  40.2 0.1 fusion.37
  40.3 0.1 copy.62
  40.4 0.1 reshape.168
  40.5 5.5 %all-to-all-start.2 = ((bf16[16,64,256]{2,1,0:T(8,128)(2,1)}), bf16[16,64,256]{2,1,0:T(8,128)(2,1)}, u32[]{:S(2)}, u32[]{:S(2)}) async-start(bf16[16,64,256]{2,1,0:T(8,128)(2,1)} %bitcast.19), calls=%async_computation.2 | async-start | bytes 1048576 | tf_op jit(solution)/shard_map/all_to_all | solution.py:104
  46.0 0.3 copy.50
  46.3 1.8 %collective-permute-done.5 = bf16[1,8,2,128,128]{3,4,2,1,0:T(8,128)(2,1)S(1)} collective-permute-done((bf16[1,8,2,128,128]{3,4,2,1,0:T(8,128)(2,1)}, bf16[1,8,2,128,128]{3,4,2,1,0:T(8,128)(2,1)S(1)}, u32[]{:S(2)}, u32[]{:S(2)}) %collective-permute-start.5) | collective-permute-done | bytes 524320 | tf_op jit(solution)/shard_map/ppermute | solution.py:18
  48.2 3.6 %collective-permute-done.4 = bf16[1,8,2,128,128]{3,4,2,1,0:T(8,128)(2,1)S(1)} collective-permute-done((bf16[1,8,2,128,128]{3,4,2,1,0:T(8,128)(2,1)}, bf16[1,8,2,128,128]{3,4,2,1,0:T(8,128)(2,1)S(1)}, u32[]{:S(2)}, u32[]{:S(2)}) %collective-permute-start.4) | collective-permute-done | bytes 524320 | tf_op jit(solution)/shard_map/ppermute | solution.py:17
  51.7 0.1 pad_maximum_fusion.4
  51.8 1.3 collective-permute-start.6
  53.1 1.3 collective-permute-start.7
  54.4 0.1 copy.45
  54.5 0.5 broadcast.190
  55.0 0.7 reduce.5
  55.7 0.1 eq.71
  55.8 3.3 %collective-permute-done.7 = bf16[4,1,2,128,128]{3,4,2,1,0:T(8,128)(2,1)S(1)} collective-permute-done((bf16[4,1,2,128,128]{3,4,2,1,0:T(8,128)(2,1)S(1)}, bf16[4,1,2,128,128]{3,4,2,1,0:T(8,128)(2,1)S(1)}, u32[]{:S(2)}, u32[]{:S(2)}) %collective-permute-start.7) | collective-permute-done | bytes 262176 | tf_op jit(solution)/shard_map/ppermute | solution.py:18
  59.1 1.8 %pad_maximum_fusion = bf16[4,10,2,128,128]{3,4,2,1,0:T(8,128)(2,1)} fusion(bf16[4,1,2,128,128]{3,4,2,1,0:T(8,128)(2,1)S(1)} %collective-permute-done.7, bf16[1,8,2,128,128]{3,4,2,1,0:T(8,128)(2,1)S(1)} %collective-permute-done.5, bf16[2,8,2,128,128]{3,4,2,1,0:T(8,128)(2,1)S(1)} %bitcast.90, bf16[1,8,2,128,128]{3,4,2,1,0:T(8,128)(2,1)S(1)} %collective-permute-done.4, ...), kind=kLoop, calls=%fused_computation.6 | loop fusion | flops 5242880 | bytes 5242880 | tf_op jit(solution)/shard_map/concatenate | solution.py:19
  60.8 3.2 %copy.52 = bf16[4,10,2,128,128]{4,3,2,1,0:T(8,128)(2,1)S(1)} copy(bf16[4,10,2,128,128]{3,4,2,1,0:T(8,128)(2,1)} %pad_maximum_fusion) | data formatting | bytes 5242880 | tf_op jit(solution)/shard_map/concatenate | solution.py:19
  64.1 6.6 %gather_fusion = bf16[128,2,128,128]{3,2,1,0:T(8,128)(2,1)} fusion(bf16[40,2,128,128]{3,2,1,0:T(8,128)(2,1)S(1)} %bitcast.81, s32[1024]{0:T(1024)S(1)} %pad_clamp_fusion), kind=kCustom, calls=%fused_computation | custom fusion | bytes 16777728 | tf_op jit(solution)/shard_map/jit(_take)/gather | solution.py:68
  70.6 13.2 %all-to-all-start = ((bf16[16,64,128]{2,1,0:T(8,128)(2,1)}), bf16[16,64,128]{2,1,0:T(8,128)(2,1)S(1)}, u32[]{:S(2)}, u32[]{:S(2)}) async-start(bf16[16,64,128]{2,1,0:T(8,128)(2,1)} %bitcast.15), calls=%async_computation | async-start | bytes 524288 | tf_op jit(solution)/shard_map/all_to_all | solution.py:105
  83.9 1.2 copy.56
  85.1 3.9 %broadcast_multiply_fusion = bf16[1024,16,256]{0,2,1:T(8,128)(2,1)} fusion(bf16[1024,256]{0,1:T(8,128)(2,1)S(1)} %copy.56, bf16[1024,16]{0,1:T(8,128)(2,1)S(1)} %fusion.28), kind=kLoop, calls=%fused_computation.5 | loop fusion | flops 4194304 | bytes 8945664 | tf_op jit(solution)/shard_map/mul | solution.py:114
  89.1 4.9 %all-to-all-done = bf16[16,64,128]{2,1,0:T(8,128)(2,1)S(1)} async-done(((bf16[16,64,128]{2,1,0:T(8,128)(2,1)}), bf16[16,64,128]{2,1,0:T(8,128)(2,1)S(1)}, u32[]{:S(2)}, u32[]{:S(2)}) %all-to-all-start) | async-done | bytes 262176 | tf_op jit(solution)/shard_map/all_to_all | solution.py:105
  93.9 5.9 %fusion.51 = f32[128,16,2,128]{0,3,2,1:T(8,128)S(1)} fusion(bf16[1024,128,1,1]{1,0,3,2:T(8,128)(2,1)S(1)} %bitcast.96, bf16[16,2,128,1024]{3,2,1,0:T(8,128)(2,1)} %bitcast.82), kind=kOutput, calls=%fused_computation.114 | convolution fusion | flops 1073741824 | bytes 10747904 | tf_op jit(solution)/shard_map/dot_general | solution.py:117
  99.8 7.7 %fusion.3 = bf16[16,2,128,128]{2,3,1,0:T(8,128)(2,1)S(1)} fusion(f32[128,16,2,128]{0,3,2,1:T(8,128)S(1)} %fusion.51, bf16[16,8,2,128,128]{4,3,2,1,0:T(8,128)(2,1)} %bitcast.99, bf16[16,8,2,128,128]{4,3,2,1,0:T(8,128)(2,1)} %bitcast.92, pred[16,8]{1,0:T(8,128)(4,1)S(1)} %copy.45), kind=kOutput, calls=%fused_computation.13 | convolution fusion | flops 1078984704 | bytes 19923072 | tf_op jit(solution)/shard_map/dot_general | solution.py:72
  107.5 0.3 copy.57
  107.8 2.0 %collective-permute-start.8 = (bf16[2,128,1,128]{1,3,2,0:T(8,128)(2,1)S(1)}, bf16[2,128,1,128]{1,3,2,0:T(8,128)(2,1)S(1)}, u32[]{:S(2)}, u32[]{:S(2)}) collective-permute-start(bf16[2,128,1,128]{1,3,2,0:T(8,128)(2,1)S(1)} %get-tuple-element.20), channel_id=1, source_target_pairs={{0,4},{4,8},{8,12},{1,5},{5,9},{9,13},{2,6},{6,10},{10,14},{3,7},{... | collective-permute-start | bytes 196616 | tf_op jit(solution)/shard_map/ppermute | solution.py:17
  109.8 1.3 collective-permute-start.9
  111.1 0.9 collective-permute-done.8
  111.9 4.1 %collective-permute-done.9 = bf16[2,128,1,128]{1,3,2,0:T(8,128)(2,1)S(1)} collective-permute-done((bf16[2,128,1,128]{1,3,2,0:T(8,128)(2,1)S(1)}, bf16[2,128,1,128]{1,3,2,0:T(8,128)(2,1)S(1)}, u32[]{:S(2)}, u32[]{:S(2)}) %collective-permute-start.9) | collective-permute-done | bytes 65568 | tf_op jit(solution)/shard_map/ppermute | solution.py:18
  116.1 1.5 %collective-permute-start.10 = (bf16[2,128,18,1]{1,3,2,0:T(2,128)(2,1)S(1)}, bf16[2,128,18,1]{1,3,2,0:T(2,128)(2,1)S(1)}, u32[]{:S(2)}, u32[]{:S(2)}) collective-permute-start(bf16[2,128,18,1]{1,3,2,0:T(2,128)(2,1)S(1)} %get-tuple-element.18), channel_id=1, source_target_pairs={{0,1},{1,2},{2,3},{4,5},{5,6},{6,7},{8,9},{9,10},{10,11},{12,13},{... | collective-permute-start | bytes 27656 | tf_op jit(solution)/shard_map/ppermute | solution.py:17
  117.6 1.3 collective-permute-start.11
  118.9 3.1 %convolution_convert_fusion = bf16[1024,128]{1,0:T(8,128)(2,1)} fusion(bf16[1024,4096]{0,1:T(8,128)(2,1)S(1)} %bitcast.85, bf16[128,4096]{0,1:T(8,128)(2,1)S(1)} %bitcast.91), kind=kOutput, calls=%fused_computation.26 | convolution fusion | flops 1073872896 | bytes 9699328 | tf_op jit(solution)/shard_map/dot_general | solution.py:124
  122.0 6.2 %all-to-all-start.3 = ((bf16[16,64,128]{2,1,0:T(8,128)(2,1)}), bf16[16,64,128]{2,1,0:T(8,128)(2,1)S(1)}, u32[]{:S(2)}, u32[]{:S(2)}) async-start(bf16[16,64,128]{2,1,0:T(8,128)(2,1)} %bitcast.36), calls=%async_computation.3 | async-start | bytes 524288 | tf_op jit(solution)/shard_map/all_to_all | solution.py:127
  128.2 0.6 pad_maximum_fusion.1
  128.8 0.2 fusion.25
  129.0 0.3 fusion.18
  129.2 1.4 copy.59
  130.6 7.6 %all-to-all-done.3 = bf16[16,64,128]{2,1,0:T(8,128)(2,1)S(1)} async-done(((bf16[16,64,128]{2,1,0:T(8,128)(2,1)}), bf16[16,64,128]{2,1,0:T(8,128)(2,1)S(1)}, u32[]{:S(2)}, u32[]{:S(2)}) %all-to-all-start.3) | async-done | bytes 262176 | tf_op jit(solution)/shard_map/all_to_all | solution.py:127
  138.2 1.4 %fusion.17 = bf16[512,128]{1,0:T(8,128)(2,1)} fusion(bf16[1024,128]{1,0:T(8,128)(2,1)S(1)} %bitcast.97, s32[512]{0:T(512)S(1)} %multiply_add_fusion), kind=kOutput, calls=%fused_computation.27 | convolution fusion | flops 134807552 | bytes 395264 | tf_op jit(solution)/shard_map/dot_general | solution.py:135
  (35 shorter events, 0.2 us)
Async XLA Ops:
  0.6 19.2 %copy-start = (bf16[512,128]{1,0:T(8,128)(2,1)S(1)}, bf16[512,128]{1,0:T(8,128)(2,1)}, u32[]{:S(2)}) copy-start(bf16[512,128]{1,0:T(8,128)(2,1)} %param.10) | copy-start | bytes 393220
  2.6 15.9 %copy-start.4 = (bf16[512,2,128]{2,1,0:T(2,128)(2,1)S(1)}, bf16[512,2,128]{2,1,0:T(2,128)(2,1)}, u32[]{:S(2)}) copy-start(bf16[512,2,128]{2,1,0:T(2,128)(2,1)} %param.11) | copy-start | bytes 786436
  4.0 36.5 %all-to-all-start.1 = ((s32[16,1,64]{2,1,0:T(1,128)}), s32[16,1,64]{2,1,0:T(1,128)S(1)}, u32[]{:S(2)}, u32[]{:S(2)}) async-start(s32[16,1,64]{2,1,0:T(1,128)} %all_to_all.16), calls=%async_computation.1 | async-start | bytes 16384 | tf_op jit(solution)/shard_map/all_to_all | solution.py:106
  13.3 7.7 %collective-permute-start = (f32[128,1,256]{0,2,1:T(8,128)S(1)}, f32[128,1,256]{0,2,1:T(8,128)S(1)}, u32[]{:S(2)}, u32[]{:S(2)}) collective-permute-start(f32[128,1,256]{0,2,1:T(8,128)S(1)} %get-tuple-element.12), channel_id=1, source_target_pairs={{0,4},{4,8},{8,12},{1,5},{5,9},{9,13},{2,6},{6,10},{10,14},{3,7},{... | collective-permute-start | bytes 393224 | tf_op jit(solution)/shard_map/ppermute | solution.py:17
  17.2 7.2 %collective-permute-start.1 = (f32[128,1,256]{0,2,1:T(8,128)S(1)}, f32[128,1,256]{0,2,1:T(8,128)S(1)}, u32[]{:S(2)}, u32[]{:S(2)}) collective-permute-start(f32[128,1,256]{0,2,1:T(8,128)S(1)} %get-tuple-element.13), channel_id=1, source_target_pairs={{4,0},{8,4},{12,8},{5,1},{9,5},{13,9},{6,2},{10,6},{14,10},{7,3},{... | collective-permute-start | bytes 393224 | tf_op jit(solution)/shard_map/ppermute | solution.py:18
  18.5 11.7 %copy-start.3 = (s32[2,8,8]{2,1,0:T(8,128)S(1)}, s32[2,8,8]{2,1,0:T(8,128)}, u32[]{:S(2)}) copy-start(s32[2,8,8]{2,1,0:T(8,128)} %param.8) | copy-start | bytes 1540
  24.4 5.9 %collective-permute-start.3 = (f32[128,18,1]{0,2,1:T(1,128)S(1)}, f32[128,18,1]{0,2,1:T(1,128)S(1)}, u32[]{:S(2)}, u32[]{:S(2)}) collective-permute-start(f32[128,18,1]{0,2,1:T(1,128)S(1)} %get-tuple-element.8), channel_id=1, source_target_pairs={{2,0},{3,1},{6,4},{7,5},{10,8},{11,9},{14,12},{15,13},{18,16},{19,... | collective-permute-start | bytes 27656 | tf_op jit(solution)/shard_map/ppermute | solution.py:18
  25.7 5.9 %collective-permute-start.2 = (f32[128,18,1]{0,2,1:T(1,128)S(1)}, f32[128,18,1]{0,2,1:T(1,128)S(1)}, u32[]{:S(2)}, u32[]{:S(2)}) collective-permute-start(f32[128,18,1]{0,2,1:T(1,128)S(1)} %get-tuple-element.9), channel_id=1, source_target_pairs={{0,2},{1,3},{4,6},{5,7},{8,10},{9,11},{12,14},{13,15},{16,18},{17,... | collective-permute-start | bytes 27656 | tf_op jit(solution)/shard_map/ppermute | solution.py:17
  34.4 13.8 %collective-permute-start.5 = (bf16[1,8,2,128,128]{3,4,2,1,0:T(8,128)(2,1)}, bf16[1,8,2,128,128]{3,4,2,1,0:T(8,128)(2,1)S(1)}, u32[]{:S(2)}, u32[]{:S(2)}) collective-permute-start(bf16[1,8,2,128,128]{3,4,2,1,0:T(8,128)(2,1)} %bitcast.6), channel_id=1, source_target_pairs={{4,0},{8,4},{12,8},{5,1},{9,5},{13,9},{6,2},{10,6},{14,10},{7,3},{... | collective-permute-start | bytes 1572872 | tf_op jit(solution)/shard_map/ppermute | solution.py:18
  35.7 16.1 %collective-permute-start.4 = (bf16[1,8,2,128,128]{3,4,2,1,0:T(8,128)(2,1)}, bf16[1,8,2,128,128]{3,4,2,1,0:T(8,128)(2,1)S(1)}, u32[]{:S(2)}, u32[]{:S(2)}) collective-permute-start(bf16[1,8,2,128,128]{3,4,2,1,0:T(8,128)(2,1)} %bitcast.4), channel_id=1, source_target_pairs={{0,4},{4,8},{8,12},{1,5},{5,9},{9,13},{2,6},{6,10},{10,14},{3,7},{... | collective-permute-start | bytes 1572872 | tf_op jit(solution)/shard_map/ppermute | solution.py:17
  40.5 30.1 %all-to-all-start.2 = ((bf16[16,64,256]{2,1,0:T(8,128)(2,1)}), bf16[16,64,256]{2,1,0:T(8,128)(2,1)}, u32[]{:S(2)}, u32[]{:S(2)}) async-start(bf16[16,64,256]{2,1,0:T(8,128)(2,1)} %bitcast.19), calls=%async_computation.2 | async-start | bytes 1048576 | tf_op jit(solution)/shard_map/all_to_all | solution.py:104
  46.3 12.7 %copy-start.1 = (bf16[2,8,2,128,8,16]{3,5,4,2,1,0:T(8,128)(2,1)}, bf16[2,8,2,128,8,16]{3,5,4,2,1,0:T(8,128)(2,1)S(1)}, u32[]{:S(2)}) copy-start(bf16[2,8,2,128,8,16]{3,5,4,2,1,0:T(8,128)(2,1)S(1)} %copy.50) | copy-start | bytes 3145732
  51.8 4.0 %collective-permute-start.6 = (bf16[4,1,2,128,128]{3,4,2,1,0:T(8,128)(2,1)S(1)}, bf16[4,1,2,128,128]{3,4,2,1,0:T(8,128)(2,1)S(1)}, u32[]{:S(2)}, u32[]{:S(2)}) collective-permute-start(bf16[4,1,2,128,128]{3,4,2,1,0:T(8,128)(2,1)S(1)} %get-tuple-element.10), channel_id=1, source_target_pairs={{0,1},{1,2},{2,3},{4,5},{5,6},{6,7},{8,9},{9,10},{10,11},{12,13},{... | collective-permute-start | bytes 786440 | tf_op jit(solution)/shard_map/ppermute | solution.py:17
  53.1 6.0 %collective-permute-start.7 = (bf16[4,1,2,128,128]{3,4,2,1,0:T(8,128)(2,1)S(1)}, bf16[4,1,2,128,128]{3,4,2,1,0:T(8,128)(2,1)S(1)}, u32[]{:S(2)}, u32[]{:S(2)}) collective-permute-start(bf16[4,1,2,128,128]{3,4,2,1,0:T(8,128)(2,1)S(1)} %get-tuple-element.11), channel_id=1, source_target_pairs={{1,0},{2,1},{3,2},{5,4},{6,5},{7,6},{9,8},{10,9},{11,10},{13,12},{... | collective-permute-start | bytes 786440 | tf_op jit(solution)/shard_map/ppermute | solution.py:18
  70.6 23.3 %all-to-all-start = ((bf16[16,64,128]{2,1,0:T(8,128)(2,1)}), bf16[16,64,128]{2,1,0:T(8,128)(2,1)S(1)}, u32[]{:S(2)}, u32[]{:S(2)}) async-start(bf16[16,64,128]{2,1,0:T(8,128)(2,1)} %bitcast.15), calls=%async_computation | async-start | bytes 524288 | tf_op jit(solution)/shard_map/all_to_all | solution.py:105
  93.9 24.9 %slice-start = ((s8[8388608]{0:T(1024)(128)(4,1)}), s8[4194304]{0:T(1024)(128)(4,1)S(1)}, s32[]{:S(2)}) async-start(s8[8388608]{0:T(1024)(128)(4,1)} %bitcast.83), calls=%async_computation.4 | async-start | bytes 8388608
  99.8 19.1 %slice-start.1 = ((s8[8388608]{0:T(1024)(128)(4,1)}), s8[4194304]{0:T(1024)(128)(4,1)S(1)}, s32[]{:S(2)}) async-start(s8[8388608]{0:T(1024)(128)(4,1)} %bitcast.83), calls=%async_computation.5 | async-start | bytes 8388608
  107.5 11.4 %copy-start.2 = (bf16[2,8,2,128,8,16]{3,5,4,2,1,0:T(8,128)(2,1)S(1)}, bf16[2,8,2,128,8,16]{3,5,4,2,1,0:T(8,128)(2,1)}, u32[]{:S(2)}) copy-start(bf16[2,8,2,128,8,16]{3,5,4,2,1,0:T(8,128)(2,1)} %copy-done.1) | copy-start | bytes 3145732
  107.8 4.1 %collective-permute-start.8 = (bf16[2,128,1,128]{1,3,2,0:T(8,128)(2,1)S(1)}, bf16[2,128,1,128]{1,3,2,0:T(8,128)(2,1)S(1)}, u32[]{:S(2)}, u32[]{:S(2)}) collective-permute-start(bf16[2,128,1,128]{1,3,2,0:T(8,128)(2,1)S(1)} %get-tuple-element.20), channel_id=1, source_target_pairs={{0,4},{4,8},{8,12},{1,5},{5,9},{9,13},{2,6},{6,10},{10,14},{3,7},{... | collective-permute-start | bytes 196616 | tf_op jit(solution)/shard_map/ppermute | solution.py:17
  109.8 6.3 %collective-permute-start.9 = (bf16[2,128,1,128]{1,3,2,0:T(8,128)(2,1)S(1)}, bf16[2,128,1,128]{1,3,2,0:T(8,128)(2,1)S(1)}, u32[]{:S(2)}, u32[]{:S(2)}) collective-permute-start(bf16[2,128,1,128]{1,3,2,0:T(8,128)(2,1)S(1)} %get-tuple-element.21), channel_id=1, source_target_pairs={{4,0},{8,4},{12,8},{5,1},{9,5},{13,9},{6,2},{10,6},{14,10},{7,3},{... | collective-permute-start | bytes 196616 | tf_op jit(solution)/shard_map/ppermute | solution.py:18
  116.1 12.1 %collective-permute-start.10 = (bf16[2,128,18,1]{1,3,2,0:T(2,128)(2,1)S(1)}, bf16[2,128,18,1]{1,3,2,0:T(2,128)(2,1)S(1)}, u32[]{:S(2)}, u32[]{:S(2)}) collective-permute-start(bf16[2,128,18,1]{1,3,2,0:T(2,128)(2,1)S(1)} %get-tuple-element.18), channel_id=1, source_target_pairs={{0,1},{1,2},{2,3},{4,5},{5,6},{6,7},{8,9},{9,10},{10,11},{12,13},{... | collective-permute-start | bytes 27656 | tf_op jit(solution)/shard_map/ppermute | solution.py:17
  117.6 10.6 %collective-permute-start.11 = (bf16[2,128,18,1]{1,3,2,0:T(2,128)(2,1)S(1)}, bf16[2,128,18,1]{1,3,2,0:T(2,128)(2,1)S(1)}, u32[]{:S(2)}, u32[]{:S(2)}) collective-permute-start(bf16[2,128,18,1]{1,3,2,0:T(2,128)(2,1)S(1)} %get-tuple-element.19), channel_id=1, source_target_pairs={{1,0},{2,1},{3,2},{5,4},{6,5},{7,6},{9,8},{10,9},{11,10},{13,12},{... | collective-permute-start | bytes 27656 | tf_op jit(solution)/shard_map/ppermute | solution.py:18
  122.0 16.3 %all-to-all-start.3 = ((bf16[16,64,128]{2,1,0:T(8,128)(2,1)}), bf16[16,64,128]{2,1,0:T(8,128)(2,1)S(1)}, u32[]{:S(2)}, u32[]{:S(2)}) async-start(bf16[16,64,128]{2,1,0:T(8,128)(2,1)} %bitcast.36), calls=%async_computation.3 | async-start | bytes 524288 | tf_op jit(solution)/shard_map/all_to_all | solution.py:127
where the time goes:
time: 141 us; the launch traced here: 140 us
  starting transfers between devices  57.8 us (41%)
  waiting for transfers between devices  30.7 us (22%)
  matrix products  20.6 us (15%)
  local copies, waits for them, and re-layouts  18.7 us (13%)
  other arithmetic  10.8 us (8%)
    ppermute x6, starting transfers between devices, with_halo(): before = lax.ppermute(last, axis, up)  17.7 us
    all_to_all x1, starting transfers between devices, body(): lax.all_to_all(send_current, ('gx', 'gy', 'gz'), split_axis=0, concat_axi...  13.2 us
    ppermute x6, waiting for transfers between devices, with_halo(): after = lax.ppermute(leading, axis, down)  12.5 us
    ppermute x6, starting transfers between devices, with_halo(): after = lax.ppermute(leading, axis, down)  7.74 us
    dot_general x1, matrix products, body(): lax.dot_general(sources, kernels, (((1, 4), (1, 4)), ((0, 2), (0, 2))), p...  7.68 us
    all_to_all x1, waiting for transfers between devices, body(): lax.all_to_all(induced.reshape(owners, capacity, port_count), ('gx', 'gy'...  7.61 us
    all_to_all x1, starting transfers between devices, body(): lax.all_to_all(send_leaf, ('gx', 'gy', 'gz'), split_axis=0, concat_axis=0...  7.36 us
    gather x1, local copies, waits for them, and re-layouts, body(): jnp.take(flattened, source.reshape(-1), axis=0)  6.57 us
  transfers between devices with their start and end apart: 16, of which 9 were waited for; matrix products, arithmetic and copies ran while one was open for 23% of the time, Pallas kernels for 0%

commit v1 on v0

v1 whole, which is shorter than its diff:
```python
import jax
import jax.numpy as jnp
from jax import lax
from jax.sharding import PartitionSpec as P

LEAF_R = 8
LEAF_C = 16
AXES = ("gx", "gy", "gz")


def plane_curl(padded):
    along_y = padded[:, 1:-1, 2:] - padded[:, 1:-1, :-2]
    along_x = padded[:, :-2, 1:-1] - padded[:, 2:, 1:-1]
    return jnp.stack([along_y, along_x])


def to_leaves(grid_values):
    components, port_count, row_count, col_count = grid_values.shape
    blocks = grid_values.reshape(
        components, port_count, row_count // LEAF_R, LEAF_R, col_count // LEAF_C, LEAF_C
    )
    blocks = blocks.transpose(2, 4, 0, 1, 3, 5)
    return blocks.reshape(
        row_count // LEAF_R, col_count // LEAF_C, components, port_count, LEAF_R * LEAF_C
    )


def from_leaves(leaves):
    leaf_rows, leaf_cols, components, port_count, leaf_cells = leaves.shape
    blocks = leaves.reshape(leaf_rows, leaf_cols, components, port_count, LEAF_R, LEAF_C)
    blocks = blocks.transpose(2, 3, 0, 4, 1, 5)
    return blocks.reshape(components, port_count, leaf_rows * LEAF_R, leaf_cols * LEAF_C)


def device_grid():
    nx, ny, nz = (lax.axis_size(a) for a in AXES)
    return nx, ny, nz


def pairs_by(fn):
    nx, ny, nz = device_grid()
    out = []
    for x in range(nx):
        for y in range(ny):
            for z in range(nz):
                target = fn(x, y, z)
                if target is None:
                    continue
                tx, ty, tz = target
                if 0 <= tx < nx and 0 <= ty < ny and 0 <= tz < nz:
                    out.append(((x * ny + y) * nz + z, (tx * ny + ty) * nz + tz))
    return out


def send(value, fn):
    return lax.ppermute(value, AXES, pairs_by(fn))


def sideways(x, y, z, dx):
    nz = lax.axis_size("gz")
    if z == nz - 1:
        return (x + dx, y + 1, 0)
    if z == 0:
        return (x + dx, y - 1, nz - 1)
    return None


def stream_window(stream, half):
    nx, ny, nz = device_grid()
    gz = lax.axis_index("gz")
    rows, width = stream.shape[1], stream.shape[2]
    hr, hc = LEAF_R + 1, LEAF_C + 1
    mid_w = half + hc
    mid = lax.dynamic_slice_in_dim(stream, gz * (width - mid_w), mid_w, 2)
    side = lax.dynamic_slice_in_dim(stream, gz * (width - hc), hc, 2)
    h_got = send(side, lambda x, y, z: sideways(x, y, z, 0))
    v_top = send(mid[:, rows - hr :], lambda x, y, z: (x + 1, y, z))
    v_bot = send(mid[:, :hr], lambda x, y, z: (x - 1, y, z))
    d_top = send(side[:, rows - hr :], lambda x, y, z: sideways(x, y, z, 1))
    d_bot = send(side[:, :hr], lambda x, y, z: sideways(x, y, z, -1))
    left = gz == 0

    def join(core, edge):
        return jnp.where(left, jnp.concatenate([edge, core], 2), jnp.concatenate([core, edge], 2))

    return jnp.concatenate([join(v_top, d_top), join(mid, h_got), join(v_bot, d_bot)], 1)


def field_halo(grid_field):
    x_field = grid_field[0]
    y_field = grid_field[1]
    rows = y_field.shape[1]
    cols = x_field.shape[2]

    def step(x, y, z, dc):
        nz = lax.axis_size("gz")
        c = y * nz + z + dc
        return (x, c // nz, c % nz) if c >= 0 else None

    x_left = send(x_field[:, :, cols - 1 :], lambda x, y, z: step(x, y, z, 1))
    x_right = send(x_field[:, :, :1], lambda x, y, z: step(x, y, z, -1))
    y_top = send(y_field[:, rows - 1 :], lambda x, y, z: (x + 1, y, z))
    y_bot = send(y_field[:, :1], lambda x, y, z: (x - 1, y, z))
    x_pad = jnp.concatenate([x_left, x_field, x_right], 2).astype(jnp.float32)
    y_pad = jnp.concatenate([y_top, y_field, y_bot], 1).astype(jnp.float32)
    return x_pad[:, :, :-2] - x_pad[:, :, 2:] + (y_pad[:, 2:] - y_pad[:, :-2])


def body(stream, inductance, near_lists, filament_leaf, filament_current, filament_coupling):
    port_count = stream.shape[0]
    leaf_rows = inductance.shape[0]
    leaf_cols = inductance.shape[1]
    near_count = inductance.shape[2]
    leaf_cells = inductance.shape[4]
    leaf_count = leaf_rows * leaf_cols
    half_cols = leaf_cols * LEAF_C
    nx, ny, nz = device_grid()
    gx = lax.axis_index("gx")
    col_index = lax.axis_index("gy") * nz + lax.axis_index("gz")
    me = gx * (ny * nz) + col_index
    owners = nx * ny * nz

    filament_count = filament_leaf.shape[0]
    capacity = max(2, 2 * filament_count // owners)
    slot_count = owners * capacity
    plane_cols = leaf_cols * ny * nz

    def owner_and_local(leaf):
        leaf_row = leaf // plane_cols
        leaf_col = leaf % plane_cols
        owner = leaf_row // leaf_rows * (ny * nz) + leaf_col // leaf_cols
        local = leaf_row % leaf_rows * leaf_cols + leaf_col % leaf_cols
        return owner, local

    owner_ids, _ = owner_and_local(filament_leaf)
    owner_hits = (owner_ids[:, None] == jnp.arange(owners, dtype=jnp.int32)[None, :]).astype(
        jnp.int32
    )
    position = jnp.sum((jnp.cumsum(owner_hits, axis=0) - 1) * owner_hits, axis=1)
    target_slot = owner_ids * capacity + position
    placement_mask = target_slot[None, :] == jnp.arange(slot_count, dtype=jnp.int32)[:, None]
    placement = placement_mask.astype(jnp.bfloat16)
    rows_out = jnp.concatenate(
        [filament_coupling.reshape(filament_count, 2 * leaf_cells), filament_current], 1
    )
    sent = jnp.dot(placement, rows_out, preferred_element_type=jnp.float32).astype(jnp.bfloat16)
    got = lax.all_to_all(
        sent.reshape(owners, capacity, -1), AXES, split_axis=0, concat_axis=0, tiled=True
    ).reshape(slot_count, -1)
    got_coupling = got[:, : 2 * leaf_cells]
    got_current = got[:, 2 * leaf_cells :]

    all_leaf = lax.all_gather(filament_leaf, AXES, tiled=True).reshape(owners, filament_count)
    src_owner, src_local = owner_and_local(all_leaf)
    mine = (src_owner == me).astype(jnp.int32)
    src_pos = jnp.cumsum(mine, axis=1) - 1
    slot_hit = (mine[:, :, None] > 0) & (
        src_pos[:, :, None] == jnp.arange(capacity, dtype=jnp.int32)[None, None, :]
    )
    got_leaf = jnp.max(jnp.where(slot_hit, src_local[:, :, None], -1), axis=1).reshape(slot_count)

    window = stream_window(stream, half_cols)
    currents = plane_curl(window).astype(jnp.bfloat16)
    bordered = to_leaves(currents)
    ring_rows = jnp.arange(leaf_rows + 2, dtype=jnp.int32)
    ring_cols = jnp.arange(leaf_cols + 2, dtype=jnp.int32)
    row_ok = ((ring_rows > 0) | (gx > 0)) & ((ring_rows < leaf_rows + 1) | (gx < nx - 1))
    col_ok = ((ring_cols > 0) | (col_index > 0)) & (
        (ring_cols < leaf_cols + 1) | (col_index < ny * nz - 1)
    )
    inside = (row_ok[:, None] & col_ok[None, :]).astype(jnp.bfloat16)
    bordered = bordered * inside[:, :, None, None, None]

    row_stride = leaf_cols + 2
    flattened = bordered.reshape((leaf_rows + 2) * row_stride, 2, port_count, leaf_cells)
    row_shift = near_lists // 3 - 1
    col_shift = near_lists % 3 - 1
    source = (jnp.arange(leaf_rows, dtype=jnp.int32)[:, None, None] + 1 + row_shift) * row_stride
    source = source + jnp.arange(leaf_cols, dtype=jnp.int32)[None, :, None] + 1 + col_shift
    sources = jnp.take(flattened, source.reshape(-1), axis=0).reshape(
        leaf_count, near_count, 2, port_count, leaf_cells
    )
    kernels = inductance.reshape(leaf_count, near_count, 2, leaf_cells, leaf_cells)
    near_field = lax.dot_general(
        sources, kernels, (((1, 4), (1, 4)), ((0, 2), (0, 2))), preferred_element_type=jnp.float32
    )
    own_leaves = bordered[1:-1, 1:-1].reshape(leaf_count, 2, port_count, leaf_cells)

    leaf_hits = (got_leaf[:, None] == jnp.arange(leaf_count, dtype=jnp.int32)[None, :]).astype(
        jnp.bfloat16
    )
    spread = (leaf_hits[:, :, None] * got_coupling[:, None, :]).reshape(
        slot_count, leaf_count * 2 * leaf_cells
    )
    filament_field = lax.dot_general(
        got_current, spread, (((0,), (0,)), ((), ())), preferred_element_type=jnp.float32
    )
    filament_field = filament_field.reshape(port_count, leaf_count, 2, leaf_cells).transpose(
        1, 2, 0, 3
    )
    plane_rows = own_leaves.transpose(2, 0, 1, 3).reshape(port_count, leaf_count * 2 * leaf_cells)
    induced = lax.dot_general(
        spread, plane_rows, (((1,), (1,)), ((), ())), preferred_element_type=jnp.float32
    ).astype(jnp.bfloat16)
    returned = lax.all_to_all(
        induced.reshape(owners, capacity, port_count), AXES, split_axis=0, concat_axis=0, tiled=True
    ).reshape(slot_count, port_count)
    filament_voltage = lax.dot_general(
        placement, returned, (((0,), (0,)), ((), ())), preferred_element_type=jnp.float32
    ).astype(jnp.bfloat16)

    total_field = (near_field + filament_field).astype(jnp.bfloat16)
    grid_field = from_leaves(total_field.reshape(leaf_rows, leaf_cols, 2, port_count, leaf_cells))
    loop_voltage = field_halo(grid_field)
    return (loop_voltage, filament_voltage)


def solution(mesh):
    return jax.shard_map(
        body,
        mesh=mesh,
        in_specs=(
            P("groups", "gx", "gy"),
            P(("groups", "gx"), ("gy", "gz"), None, None, None, None),
            P(("groups", "gx"), ("gy", "gz"), None),
            P(("groups", "gx", "gy", "gz")),
            P(("groups", "gx", "gy", "gz"), None),
            P(("groups", "gx", "gy", "gz"), None, None),
        ),
        out_specs=(P("groups", "gx", ("gy", "gz")), P(("groups", "gx", "gy", "gz"), None)),
        check_vma=False,
    )
```

time: 141 us -> 135 us (0.957)
  blocking collectives: 0 us -> 30.4 us
  starting transfers between devices: 57.8 us -> 29.2 us
  waiting for transfers between devices: 30.7 us -> 4.37 us
  local copies, waits for them, and re-layouts: 18.7 us -> 34.8 us
  other arithmetic: 10.8 us -> 12.9 us
    all_gather x0 -> x1, blocking collectives: none -> 30.4 us  [body(): lax.all_gather(filament_leaf, AXES, tiled=True)]
    all_to_all x4 -> x2, starting transfers between devices: 32.3 us -> 12.8 us  [the longest x1 7.41 us: body(): lax.all_to_all(sent.reshape(owners, capacity, -1), AXES, split_axis=0, co...]
    ppermute x12 -> x9, waiting for transfers between devices: 18.2 us -> 4.36 us  [send(): return lax.ppermute(value, AXES, pairs_by(fn))]
    all_to_all x4 -> x2, waiting for transfers between devices: 12.5 us -> 0.01 us  [the longest x1 0.01 us: body(): lax.all_to_all(sent.reshape(owners, capacity, -1), AXES, split_axis=0, co...]
    gather x1 -> x2, local copies, waits for them, and re-layouts: 6.57 us -> 18.5 us  [body(): jnp.take(flattened, source.reshape(-1), axis=0)]
    ppermute x12 -> x9, starting transfers between devices: 25.4 us -> 16.4 us  [send(): return lax.ppermute(value, AXES, pairs_by(fn))]
    unnamed x16, local copies, waits for them, and re-layouts: 3.41 us -> 9.53 us
    concatenate x1 -> x0, local copies, waits for them, and re-layouts: 3.23 us -> none  [with_halo(): value = jnp.concatenate([before, value, after], axis=dim)]
  transfers between devices with their start and end apart: 16 -> 11, of which waited for: 9 -> 2; matrix products, arithmetic and copies ran while one was open for 23% -> 37% of each run, Pallas kernels for 0% -> 0%
where the time goes in v1:
time: 135 us; the launch traced here: 133 us
  local copies, waits for them, and re-layouts  34.8 us (26%)
  blocking collectives  30.4 us (23%)
  starting transfers between devices  29.2 us (22%)
  matrix products  20.4 us (15%)
  other arithmetic  12.9 us (10%)
  waiting for transfers between devices  4.37 us (3%)
    all_gather x1, blocking collectives, body(): lax.all_gather(filament_leaf, AXES, tiled=True)  30.4 us
    gather x2, local copies, waits for them, and re-layouts, body(): jnp.take(flattened, source.reshape(-1), axis=0)  18.5 us
    ppermute x9, starting transfers between devices, send(): return lax.ppermute(value, AXES, pairs_by(fn))  16.4 us
    unnamed x16, local copies, waits for them, and re-layouts  9.53 us
    dot_general x1, matrix products, body(): lax.dot_general(sources, kernels, (((1, 4), (1, 4)), ((0, 2), (0, 2))), p...  7.56 us
    all_to_all x1, starting transfers between devices, body(): lax.all_to_all(sent.reshape(owners, capacity, -1), AXES, split_axis=0, co...  7.41 us
    dot_general x1, matrix products, body(): lax.dot_general(got_current, spread, (((0,), (0,)), ((), ())), preferred_...  5.82 us
    all_to_all x1, starting transfers between devices, body(): lax.all_to_all(induced.reshape(owners, capacity, port_count), AXES, split...  5.38 us
  transfers between devices with their start and end apart: 11, of which 2 were waited for; matrix products, arithmetic and copies ran while one was open for 37% of the time, Pallas kernels for 0%

profile of v1, /device:TPU:0, one launch (start us, length us, event | category | flops | bytes accessed | tf_op | source)
XLA Modules:
  0.0 133.2 jit_solution(13138170125453125483)
XLA Ops:
  0.6 0.8 fusion.74
  1.5 0.7 fusion.57
  2.2 1.2 reduce-window.14
  3.4 0.2 slice_reduce_fusion.1
  3.6 0.1 fusion.34
  3.7 0.7 multiply_add_fusion
  4.4 1.0 copy.112
  5.4 2.5 %fusion.13 = bf16[1024,384]{1,0:T(8,128)(2,1)} fusion(s32[512]{0:T(512)S(1)} %multiply_add_fusion, bf16[512,128]{1,0:T(8,128)(2,1)} %param.10, bf16[512,256]{1,0:T(8,128)(2,1)S(1)} %bitcast.121), kind=kOutput, calls=%fused_computation.20 | convolution fusion | flops 404357120 | bytes 1181696 | tf_op jit(solution)/shard_map/dot_general | solution.py:146
  7.9 7.4 %all-to-all-start = ((bf16[16,64,384]{2,1,0:T(8,128)(2,1)}), bf16[16,64,384]{2,1,0:T(8,128)(2,1)}, u32[]{:S(2)}, u32[]{:S(2)}) async-start(bf16[16,64,384]{2,1,0:T(8,128)(2,1)} %bitcast.12), calls=%async_computation | async-start | bytes 1572864 | tf_op jit(solution)/shard_map/all_to_all | solution.py:147
  15.4 0.3 constant_dynamic-slice_fusion.1
  15.7 0.4 copy.72
  16.1 0.7 collective-permute-start.2
  16.8 0.7 fusion.68
  17.5 0.7 collective-permute-start
  18.2 0.7 collective-permute-start.3
  18.9 2.0 %constant_dynamic-slice_fusion = f32[128,16,145]{2,1,0:T(8,128)} fusion(f32[128,16,256]{2,1,0:T(8,128)S(1)} %copy-done, s32[]{:T(128)S(6)} %select_n.153), kind=kLoop, calls=%fused_computation.157 | loop fusion | bytes 2375684 | tf_op jit(solution)/shard_map/dynamic_slice | solution.py:74
  20.8 2.0 %copy.73 = f32[128,16,145]{0,2,1:T(8,128)S(1)} copy(f32[128,16,145]{2,1,0:T(8,128)} %constant_dynamic-slice_fusion) | data formatting | bytes 2375680
  22.8 0.1 fusion.64
  22.9 4.6 %collective-permute-start.1 = (f32[128,9,145]{0,2,1:T(8,128)S(1)}, f32[128,9,145]{0,2,1:T(8,128)}, u32[]{:S(2)}, u32[]{:S(2)}) collective-permute-start(f32[128,9,145]{0,2,1:T(8,128)S(1)} %get-tuple-element.10), channel_id=1, source_target_pairs={{0,4},{1,5},{2,6},{3,7},{4,8},{5,9},{6,10},{7,11},{8,12},{9,13},{1... | collective-permute-start | bytes 2004488 | tf_op jit(solution)/shard_map/ppermute | solution.py:56
  27.5 1.3 collective-permute-start.4
  28.9 0.1 fusion.73
  29.0 0.1 and.191
  29.3 0.1 and.188
  29.5 30.4 %all-gather = s32[16,1,512]{2,1,0:T(1,128)S(1)} all-gather(s32[1,1,512]{2,1,0:T(1,128)S(1)} %bitcast.122), channel_id=1, replica_groups=mesh['groups'=2,'gx'=4,'gy'=2,'gz'=2] {'gx','gy','gz'}, dimensions={0}, use_global_device_ids=true | all-gather | bytes 34816 | tf_op jit(solution)/shard_map/all_gather | solution.py:153
  60.0 0.1 convert_compare_fusion
  60.1 1.2 reduce-window.16
  61.3 0.2 slice_reduce_fusion
  61.5 0.1 copy_bitcast_fusion.2
  61.6 0.7 select_reduce_fusion
  62.4 0.1 reshape.384
  62.6 0.1 copy.51
  62.7 0.2 maximum_select_fusion
  62.8 1.5 %maximum_select_fusion.1 = f32[128,9,162]{0,2,1:T(8,128)S(1)} fusion(f32[128,9,145]{0,2,1:T(8,128)} %collective-permute-done.1, f32[128,9,17]{0,2,1:T(8,128)S(1)} %collective-permute-done, pred[]{:T(512)S(6)} %eq.94), kind=kLoop, calls=%fused_computation.32 | loop fusion | flops 559872 | bytes 1492993 | tf_op jit(solution)/shard_map/jit(_where)/select_n | solution.py:84
  64.3 1.4 %maximum_select_fusion.2 = f32[128,9,162]{0,2,1:T(8,128)S(1)} fusion(f32[128,9,145]{0,2,1:T(8,128)} %collective-permute-done.4, f32[128,9,17]{0,2,1:T(8,128)S(1)} %collective-permute-done.3, pred[]{:T(512)S(6)} %eq.94), kind=kLoop, calls=%fused_computation.33 | loop fusion | flops 559872 | bytes 1492993 | tf_op jit(solution)/shard_map/jit(_where)/select_n | solution.py:84
  65.8 0.2 pad_maximum_fusion
  66.0 0.7 fusion.4
  66.7 0.2 maximum_bitcast_fusion
  66.9 0.8 copy.54
  67.7 1.5 %copy-done.3 = bf16[4,10,2,128,8,16]{3,5,4,2,1,0:T(8,128)(2,1)} copy-done((bf16[4,10,2,128,8,16]{3,5,4,2,1,0:T(8,128)(2,1)}, bf16[4,10,2,128,8,16]{3,5,4,2,1,0:T(8,128)(2,1)S(1)}, u32[]{:S(2)}) %copy-start.3) | copy-done | bytes 2621464
  69.2 0.2 broadcast_multiply_fusion.1
  69.5 6.5 %gather_fusion = bf16[128,2,128,128]{2,3,1,0:T(8,128)(2,1)} fusion(bf16[40,2,128,128]{2,3,1,0:T(8,128)(2,1)S(1)} %broadcast_multiply_fusion.1, s32[1024]{0:T(1024)S(1)} %pad_clamp_fusion), kind=kCustom, calls=%fused_computation | custom fusion | bytes 16777728 | tf_op jit(solution)/shard_map/jit(_take)/gather | solution.py:180
  76.0 11.9 %copy.55 = bf16[128,2,128,128]{3,2,1,0:T(8,128)(2,1)} copy(bf16[128,2,128,128]{2,3,1,0:T(8,128)(2,1)} %gather_fusion) | data formatting | bytes 16777216 | tf_op jit(solution)/shard_map/jit(_take)/gather | solution.py:180
  87.9 1.4 %slice_multiply_fusion = bf16[2,8,2,128,128]{3,4,2,1,0:T(8,128)(2,1)S(1)} fusion(bf16[4,10,2,128,128]{3,4,2,1,0:T(8,128)(2,1)} %bitcast.107, bf16[2,8]{1,0:T(2,128)(2,1)S(1)} %slice.127), kind=kLoop, calls=%fused_computation.25 | loop fusion | flops 524288 | bytes 2097184 | tf_op jit(solution)/shard_map/mul | solution.py:172
  89.3 1.1 slice.115
  90.4 0.2 copy.64
  90.6 0.7 broadcast_multiply_fusion
  91.3 3.2 %copy-done.2 = bf16[1024,16,256]{0,2,1:T(8,128)(2,1)} copy-done((bf16[1024,16,256]{0,2,1:T(8,128)(2,1)}, bf16[1024,16,256]{0,2,1:T(8,128)(2,1)S(1)}, u32[]{:S(2)}) %copy-start.2) | copy-done | bytes 8388632
  94.5 3.1 %convolution_convert_fusion = bf16[1024,128]{1,0:T(8,128)(2,1)} fusion(bf16[1024,4096]{0,1:T(8,128)(2,1)S(1)} %bitcast.104, bf16[128,4096]{0,1:T(8,128)(2,1)S(1)} %bitcast.116), kind=kOutput, calls=%fused_computation.23 | convolution fusion | flops 1073872896 | bytes 9699328 | tf_op jit(solution)/shard_map/dot_general | solution.py:202
  97.6 5.4 %all-to-all-start.1 = ((bf16[16,64,128]{2,1,0:T(8,128)(2,1)}), bf16[16,64,128]{2,1,0:T(8,128)(2,1)S(1)}, u32[]{:S(2)}, u32[]{:S(2)}) async-start(bf16[16,64,128]{2,1,0:T(8,128)(2,1)} %bitcast.30), calls=%async_computation.1 | async-start | bytes 524288 | tf_op jit(solution)/shard_map/all_to_all | solution.py:205
  103.0 5.8 %fusion.21 = f32[128,16,2,128]{0,3,2,1:T(8,128)S(1)} fusion(bf16[16,2,128,1024]{3,2,1,0:T(8,128)(2,1)} %bitcast.105, bf16[1024,384]{1,0:T(8,128)(2,1)} %bitcast.13), kind=kOutput, calls=%fused_computation.41 | convolution fusion | flops 1073741824 | bytes 10747904 | tf_op jit(solution)/shard_map/dot_general | solution.py:195
  108.8 7.6 %fusion.5 = bf16[16,2,128,128]{2,3,1,0:T(8,128)(2,1)S(1)} fusion(f32[128,16,2,128]{0,3,2,1:T(8,128)S(1)} %fusion.21, bf16[16,8,2,128,128]{4,3,2,1,0:T(8,128)(2,1)} %bitcast.123, bf16[16,8,2,128,128]{4,3,2,1,0:T(8,128)(2,1)} %bitcast.108, pred[16,8]{1,0:T(8,128)(4,1)S(1)} %copy.51), kind=kOutput, calls=%fused_computation.13 | convolution fusion | flops 1078984704 | bytes 19923072 | tf_op jit(solution)/shard_map/dot_general | solution.py:184
  116.4 0.3 copy.111
  116.7 0.3 fusion.65
  117.0 2.3 %collective-permute-start.5 = (bf16[128,16,1]{0,2,1:T(2,128)(2,1)S(1)}, bf16[128,16,1]{0,2,1:T(2,128)(2,1)S(1)}, u32[]{:S(2)}, u32[]{:S(2)}) collective-permute-start(bf16[128,16,1]{0,2,1:T(2,128)(2,1)S(1)} %get-tuple-element.14), channel_id=1, source_target_pairs={{0,1},{1,2},{2,3},{4,5},{5,6},{6,7},{8,9},{9,10},{10,11},{12,13},{... | collective-permute-start | bytes 12296 | tf_op jit(solution)/shard_map/ppermute | solution.py:56
  119.3 1.3 collective-permute-start.6
  120.7 3.6 %collective-permute-start.7 = (bf16[128,1,128]{0,2,1:T(8,128)(2,1)S(1)}, bf16[128,1,128]{0,2,1:T(8,128)(2,1)S(1)}, u32[]{:S(2)}, u32[]{:S(2)}) collective-permute-start(bf16[128,1,128]{0,2,1:T(8,128)(2,1)S(1)} %get-tuple-element.16), channel_id=1, source_target_pairs={{0,4},{1,5},{2,6},{3,7},{4,8},{5,9},{6,10},{7,11},{8,12},{9,13},{1... | collective-permute-start | bytes 98312 | tf_op jit(solution)/shard_map/ppermute | solution.py:56
  124.2 1.3 collective-permute-start.8
  125.6 0.1 maximum_convert_fusion.1
  125.7 0.1 collective-permute-done.7
  125.8 4.2 %collective-permute-done.8 = bf16[128,1,128]{0,2,1:T(8,128)(2,1)S(1)} collective-permute-done((bf16[128,1,128]{0,2,1:T(8,128)(2,1)S(1)}, bf16[128,1,128]{0,2,1:T(8,128)(2,1)S(1)}, u32[]{:S(2)}, u32[]{:S(2)}) %collective-permute-start.8) | collective-permute-done | bytes 32800 | tf_op jit(solution)/shard_map/ppermute | solution.py:56
  130.0 0.1 maximum_convert_fusion
  130.2 0.2 fusion.15
  130.3 1.4 %copy.67 = f32[128,16,128]{2,1,0:T(8,128)} copy(f32[128,16,128]{0,2,1:T(8,128)S(1)} %fusion.15) | data formatting | bytes 2097152
  131.7 1.4 %fusion.14 = bf16[512,128]{1,0:T(8,128)(2,1)} fusion(bf16[1024,128]{1,0:T(8,128)(2,1)S(1)} %bitcast.120, s32[512]{0:T(512)S(1)} %multiply_add_fusion), kind=kOutput, calls=%fused_computation.24 | convolution fusion | flops 134807552 | bytes 395264 | tf_op jit(solution)/shard_map/dot_general | solution.py:208
  (43 shorter events, 0.8 us)
Async XLA Ops:
  0.6 14.7 %copy-start = (f32[128,16,256]{2,1,0:T(8,128)S(1)}, f32[128,16,256]{2,1,0:T(8,128)}, u32[]{:S(2)}) copy-start(f32[128,16,256]{2,1,0:T(8,128)} %param.6) | copy-start | bytes 6291460
  7.9 81.4 %all-to-all-start = ((bf16[16,64,384]{2,1,0:T(8,128)(2,1)}), bf16[16,64,384]{2,1,0:T(8,128)(2,1)}, u32[]{:S(2)}, u32[]{:S(2)}) async-start(bf16[16,64,384]{2,1,0:T(8,128)(2,1)} %bitcast.12), calls=%async_computation | async-start | bytes 1572864 | tf_op jit(solution)/shard_map/all_to_all | solution.py:147
  16.1 46.5 %collective-permute-start.2 = (f32[128,16,17]{0,2,1:T(8,128)S(1)}, f32[128,16,17]{0,2,1:T(8,128)S(1)}, u32[]{:S(2)}, u32[]{:S(2)}) collective-permute-start(f32[128,16,17]{0,2,1:T(8,128)S(1)} %copy.72), channel_id=1, source_target_pairs={{1,2},{2,1},{5,6},{6,5},{9,10},{10,9},{13,14},{14,13},{17,18},{18,... | collective-permute-start | bytes 417800 | tf_op jit(solution)/shard_map/ppermute | solution.py:56
  17.5 45.3 %collective-permute-start = (f32[128,9,17]{0,2,1:T(8,128)}, f32[128,9,17]{0,2,1:T(8,128)S(1)}, u32[]{:S(2)}, u32[]{:S(2)}) collective-permute-start(f32[128,9,17]{0,2,1:T(8,128)} %get-tuple-element.18), channel_id=1, source_target_pairs={{1,6},{2,5},{5,10},{6,9},{9,14},{10,13},{17,22},{18,21},{21,26},{2... | collective-permute-start | bytes 235016 | tf_op jit(solution)/shard_map/ppermute | solution.py:56
  18.2 46.1 %collective-permute-start.3 = (f32[128,9,17]{0,2,1:T(8,128)}, f32[128,9,17]{0,2,1:T(8,128)S(1)}, u32[]{:S(2)}, u32[]{:S(2)}) collective-permute-start(f32[128,9,17]{0,2,1:T(8,128)} %get-tuple-element.19), channel_id=1, source_target_pairs={{5,2},{6,1},{9,6},{10,5},{13,10},{14,9},{21,18},{22,17},{25,22},{2... | collective-permute-start | bytes 235016 | tf_op jit(solution)/shard_map/ppermute | solution.py:56
  20.8 8.1 %copy-start.5 = (s32[2,8,8]{2,1,0:T(8,128)S(1)}, s32[2,8,8]{2,1,0:T(8,128)}, u32[]{:S(2)}) copy-start(s32[2,8,8]{2,1,0:T(8,128)} %param.8) | copy-start | bytes 1540
  20.8 8.6 %copy-start.4 = (s32[512]{0:T(512)S(1)}, s32[512]{0:T(512)}, u32[]{:S(2)}) copy-start(s32[512]{0:T(512)} %param.9) | copy-start | bytes 6148
  22.9 39.9 %collective-permute-start.1 = (f32[128,9,145]{0,2,1:T(8,128)S(1)}, f32[128,9,145]{0,2,1:T(8,128)}, u32[]{:S(2)}, u32[]{:S(2)}) collective-permute-start(f32[128,9,145]{0,2,1:T(8,128)S(1)} %get-tuple-element.10), channel_id=1, source_target_pairs={{0,4},{1,5},{2,6},{3,7},{4,8},{5,9},{6,10},{7,11},{8,12},{9,13},{1... | collective-permute-start | bytes 2004488 | tf_op jit(solution)/shard_map/ppermute | solution.py:56
  27.5 36.8 %collective-permute-start.4 = (f32[128,9,145]{0,2,1:T(8,128)S(1)}, f32[128,9,145]{0,2,1:T(8,128)}, u32[]{:S(2)}, u32[]{:S(2)}) collective-permute-start(f32[128,9,145]{0,2,1:T(8,128)S(1)} %get-tuple-element.11), channel_id=1, source_target_pairs={{4,0},{5,1},{6,2},{7,3},{8,4},{9,5},{10,6},{11,7},{12,8},{13,9},{1... | collective-permute-start | bytes 2004488 | tf_op jit(solution)/shard_map/ppermute | solution.py:56
  67.7 1.5 %copy-start.3 = (bf16[4,10,2,128,8,16]{3,5,4,2,1,0:T(8,128)(2,1)}, bf16[4,10,2,128,8,16]{3,5,4,2,1,0:T(8,128)(2,1)S(1)}, u32[]{:S(2)}) copy-start(bf16[4,10,2,128,8,16]{3,5,4,2,1,0:T(8,128)(2,1)S(1)} %copy.54) | copy-start | bytes 7864324
  91.3 3.2 %copy-start.2 = (bf16[1024,16,256]{0,2,1:T(8,128)(2,1)}, bf16[1024,16,256]{0,2,1:T(8,128)(2,1)S(1)}, u32[]{:S(2)}) copy-start(bf16[1024,16,256]{0,2,1:T(8,128)(2,1)S(1)} %broadcast_multiply_fusion) | copy-start | bytes 25165828
  97.6 34.1 %all-to-all-start.1 = ((bf16[16,64,128]{2,1,0:T(8,128)(2,1)}), bf16[16,64,128]{2,1,0:T(8,128)(2,1)S(1)}, u32[]{:S(2)}, u32[]{:S(2)}) async-start(bf16[16,64,128]{2,1,0:T(8,128)(2,1)} %bitcast.30), calls=%async_computation.1 | async-start | bytes 524288 | tf_op jit(solution)/shard_map/all_to_all | solution.py:205
  117.0 8.5 %collective-permute-start.5 = (bf16[128,16,1]{0,2,1:T(2,128)(2,1)S(1)}, bf16[128,16,1]{0,2,1:T(2,128)(2,1)S(1)}, u32[]{:S(2)}, u32[]{:S(2)}) collective-permute-start(bf16[128,16,1]{0,2,1:T(2,128)(2,1)S(1)} %get-tuple-element.14), channel_id=1, source_target_pairs={{0,1},{1,2},{2,3},{4,5},{5,6},{6,7},{8,9},{9,10},{10,11},{12,13},{... | collective-permute-start | bytes 12296 | tf_op jit(solution)/shard_map/ppermute | solution.py:56
  119.3 6.2 %collective-permute-start.6 = (bf16[128,16,1]{0,2,1:T(2,128)(2,1)S(1)}, bf16[128,16,1]{0,2,1:T(2,128)(2,1)S(1)}, u32[]{:S(2)}, u32[]{:S(2)}) collective-permute-start(bf16[128,16,1]{0,2,1:T(2,128)(2,1)S(1)} %get-tuple-element.15), channel_id=1, source_target_pairs={{1,0},{2,1},{3,2},{5,4},{6,5},{7,6},{9,8},{10,9},{11,10},{13,12},{... | collective-permute-start | bytes 12296 | tf_op jit(solution)/shard_map/ppermute | solution.py:56
  120.7 5.1 %collective-permute-start.7 = (bf16[128,1,128]{0,2,1:T(8,128)(2,1)S(1)}, bf16[128,1,128]{0,2,1:T(8,128)(2,1)S(1)}, u32[]{:S(2)}, u32[]{:S(2)}) collective-permute-start(bf16[128,1,128]{0,2,1:T(8,128)(2,1)S(1)} %get-tuple-element.16), channel_id=1, source_target_pairs={{0,4},{1,5},{2,6},{3,7},{4,8},{5,9},{6,10},{7,11},{8,12},{9,13},{1... | collective-permute-start | bytes 98312 | tf_op jit(solution)/shard_map/ppermute | solution.py:56
  124.2 5.8 %collective-permute-start.8 = (bf16[128,1,128]{0,2,1:T(8,128)(2,1)S(1)}, bf16[128,1,128]{0,2,1:T(8,128)(2,1)S(1)}, u32[]{:S(2)}, u32[]{:S(2)}) collective-permute-start(bf16[128,1,128]{0,2,1:T(8,128)(2,1)S(1)} %get-tuple-element.17), channel_id=1, source_target_pairs={{4,0},{5,1},{6,2},{7,3},{8,4},{9,5},{10,6},{11,7},{12,8},{13,9},{1... | collective-permute-start | bytes 98312 | tf_op jit(solution)/shard_map/ppermute | solution.py:56
  130.1 3.0 %copy-start.1 = (f32[128,16,256]{2,1,0:T(8,128)S(1)}, f32[128,16,256]{2,1,0:T(8,128)}, u32[]{:S(2)}) copy-start(f32[128,16,256]{2,1,0:T(8,128)} %param.6) | copy-start | bytes 6291460

commit v2 on v1

--- a/solution.py
+++ b/solution.py
@@ -1,6 +1,8 @@
 import jax
 import jax.numpy as jnp
 from jax import lax
+from jax.experimental import pallas as pl
+from jax.experimental.pallas import tpu as pltpu
 from jax.sharding import PartitionSpec as P
 
 LEAF_R = 8
@@ -106,6 +108,83 @@
     return x_pad[:, :, :-2] - x_pad[:, :, 2:] + (y_pad[:, 2:] - y_pad[:, :-2])
 
 
+def leaf_kernel(codes_ref, bord_ref, ind_ref, leaf_ref, cpl_ref, cur_ref, field_ref, volt_ref, acc_ref):
+    leaf = pl.program_id(0)
+    leaf_cols = bord_ref.shape[1] - 2
+    near_count = ind_ref.shape[1]
+    components = ind_ref.shape[2]
+    cells = ind_ref.shape[3]
+    row = leaf // leaf_cols
+    col = leaf % leaf_cols
+
+    @pl.when(leaf == 0)
+    def _():
+        acc_ref[...] = jnp.zeros_like(acc_ref)
+
+    mask = leaf_ref[...] == leaf
+    coupling = jnp.where(mask, cpl_ref[...], jnp.zeros_like(cpl_ref[...]))
+    current = cur_ref[...]
+    volt = acc_ref[...]
+    for c in range(components):
+        total = jnp.zeros((current.shape[0], cells), jnp.float32)
+        for n in range(near_count):
+            code = codes_ref[leaf * near_count + n]
+            src_row = jnp.minimum(jnp.maximum(row + code // 3, 0), bord_ref.shape[0] - 1)
+            src_col = jnp.minimum(jnp.maximum(col + code % 3, 0), bord_ref.shape[1] - 1)
+            total += lax.dot_general(
+                bord_ref[src_row, src_col, c],
+                ind_ref[0, n, c],
+                (((1,), (1,)), ((), ())),
+                preferred_element_type=jnp.float32,
+            )
+        part = coupling[:, c * cells : (c + 1) * cells]
+        total += jnp.dot(current, part, preferred_element_type=jnp.float32)
+        field_ref[0, c] = total.astype(field_ref.dtype)
+        volt += lax.dot_general(
+            part, bord_ref[row + 1, col + 1, c], (((1,), (1,)), ((), ())),
+            preferred_element_type=jnp.float32,
+        )
+    acc_ref[...] = volt
+
+    @pl.when(leaf == pl.num_programs(0) - 1)
+    def _():
+        volt_ref[...] = volt.astype(volt_ref.dtype)
+
+
+def leaf_fields(codes, bordered, kernels, slot_leaf, coupling, current_t):
+    leaf_count, near_count, components, cells, _ = kernels.shape
+    port_count, slot_count = current_t.shape
+
+    def whole(shape):
+        return pl.BlockSpec(shape, lambda l, codes: (0,) * len(shape))
+
+    grid_spec = pltpu.PrefetchScalarGridSpec(
+        num_scalar_prefetch=1,
+        grid=(leaf_count,),
+        in_specs=[
+            whole(bordered.shape),
+            pl.BlockSpec((1, near_count, components, cells, cells), lambda l, codes: (l, 0, 0, 0, 0)),
+            whole(slot_leaf.shape),
+            whole(coupling.shape),
+            whole(current_t.shape),
+        ],
+        out_specs=[
+            pl.BlockSpec((1, components, port_count, cells), lambda l, codes: (l, 0, 0, 0)),
+            whole((slot_count, port_count)),
+        ],
+        scratch_shapes=[pltpu.VMEM((slot_count, port_count), jnp.float32)],
+    )
+    return pl.pallas_call(
+        leaf_kernel,
+        grid_spec=grid_spec,
+        out_shape=[
+            jax.ShapeDtypeStruct((leaf_count, components, port_count, cells), jnp.bfloat16),
+            jax.ShapeDtypeStruct((slot_count, port_count), jnp.bfloat16),
+        ],
+        compiler_params=pltpu.CompilerParams(dimension_semantics=("arbitrary",)),
+    )(codes, bordered, kernels, slot_leaf, coupling, current_t)
+
+
 def body(stream, inductance, near_lists, filament_leaf, filament_current, filament_coupling):
     port_count = stream.shape[0]
     leaf_rows = inductance.shape[0]
@@ -117,22 +196,16 @@
     nx, ny, nz = device_grid()
     gx = lax.axis_index("gx")
     col_index = lax.axis_index("gy") * nz + lax.axis_index("gz")
-    me = gx * (ny * nz) + col_index
     owners = nx * ny * nz
 
     filament_count = filament_leaf.shape[0]
     capacity = max(2, 2 * filament_count // owners)
     slot_count = owners * capacity
     plane_cols = leaf_cols * ny * nz
-
-    def owner_and_local(leaf):
-        leaf_row = leaf // plane_cols
-        leaf_col = leaf % plane_cols
-        owner = leaf_row // leaf_rows * (ny * nz) + leaf_col // leaf_cols
-        local = leaf_row % leaf_rows * leaf_cols + leaf_col % leaf_cols
-        return owner, local
-
-    owner_ids, _ = owner_and_local(filament_leaf)
+    leaf_row = filament_leaf // plane_cols
+    leaf_col = filament_leaf % plane_cols
+    owner_ids = leaf_row // leaf_rows * (ny * nz) + leaf_col // leaf_cols
+    local_ids = leaf_row % leaf_rows * leaf_cols + leaf_col % leaf_cols
     owner_hits = (owner_ids[:, None] == jnp.arange(owners, dtype=jnp.int32)[None, :]).astype(
         jnp.int32
     )
@@ -140,24 +213,24 @@
     target_slot = owner_ids * capacity + position
     placement_mask = target_slot[None, :] == jnp.arange(slot_count, dtype=jnp.int32)[:, None]
     placement = placement_mask.astype(jnp.bfloat16)
+    row_width = 2 * leaf_cells + port_count
     rows_out = jnp.concatenate(
         [filament_coupling.reshape(filament_count, 2 * leaf_cells), filament_current], 1
     )
     sent = jnp.dot(placement, rows_out, preferred_element_type=jnp.float32).astype(jnp.bfloat16)
-    got = lax.all_to_all(
-        sent.reshape(owners, capacity, -1), AXES, split_axis=0, concat_axis=0, tiled=True
-    ).reshape(slot_count, -1)
-    got_coupling = got[:, : 2 * leaf_cells]
-    got_current = got[:, 2 * leaf_cells :]
-
-    all_leaf = lax.all_gather(filament_leaf, AXES, tiled=True).reshape(owners, filament_count)
-    src_owner, src_local = owner_and_local(all_leaf)
-    mine = (src_owner == me).astype(jnp.int32)
-    src_pos = jnp.cumsum(mine, axis=1) - 1
-    slot_hit = (mine[:, :, None] > 0) & (
-        src_pos[:, :, None] == jnp.arange(capacity, dtype=jnp.int32)[None, None, :]
-    )
-    got_leaf = jnp.max(jnp.where(slot_hit, src_local[:, :, None], -1), axis=1).reshape(slot_count)
+    sent_leaf = jnp.max(jnp.where(placement_mask, local_ids[None, :], -1), axis=1)
+    payload = jnp.concatenate(
+        [
+            sent.reshape(owners, capacity * row_width),
+            sent_leaf.astype(jnp.bfloat16).reshape(owners, capacity),
+        ],
+        1,
+    )
+    got = lax.all_to_all(payload, AXES, split_axis=0, concat_axis=0, tiled=True)
+    got_rows = got[:, : capacity * row_width].reshape(slot_count, row_width)
+    got_leaf = got[:, capacity * row_width :].reshape(slot_count, 1).astype(jnp.int32)
+    got_coupling = got_rows[:, : 2 * leaf_cells]
+    got_current_t = got_rows[:, 2 * leaf_cells :].T
 
     window = stream_window(stream, half_cols)
     currents = plane_curl(window).astype(jnp.bfloat16)
@@ -171,37 +244,10 @@
     inside = (row_ok[:, None] & col_ok[None, :]).astype(jnp.bfloat16)
     bordered = bordered * inside[:, :, None, None, None]
 
-    row_stride = leaf_cols + 2
-    flattened = bordered.reshape((leaf_rows + 2) * row_stride, 2, port_count, leaf_cells)
-    row_shift = near_lists // 3 - 1
-    col_shift = near_lists % 3 - 1
-    source = (jnp.arange(leaf_rows, dtype=jnp.int32)[:, None, None] + 1 + row_shift) * row_stride
-    source = source + jnp.arange(leaf_cols, dtype=jnp.int32)[None, :, None] + 1 + col_shift
-    sources = jnp.take(flattened, source.reshape(-1), axis=0).reshape(
-        leaf_count, near_count, 2, port_count, leaf_cells
-    )
     kernels = inductance.reshape(leaf_count, near_count, 2, leaf_cells, leaf_cells)
-    near_field = lax.dot_general(
-        sources, kernels, (((1, 4), (1, 4)), ((0, 2), (0, 2))), preferred_element_type=jnp.float32
-    )
-    own_leaves = bordered[1:-1, 1:-1].reshape(leaf_count, 2, port_count, leaf_cells)
-
-    leaf_hits = (got_leaf[:, None] == jnp.arange(leaf_count, dtype=jnp.int32)[None, :]).astype(
-        jnp.bfloat16
-    )
-    spread = (leaf_hits[:, :, None] * got_coupling[:, None, :]).reshape(
-        slot_count, leaf_count * 2 * leaf_cells
-    )
-    filament_field = lax.dot_general(
-        got_current, spread, (((0,), (0,)), ((), ())), preferred_element_type=jnp.float32
-    )
-    filament_field = filament_field.reshape(port_count, leaf_count, 2, leaf_cells).transpose(
-        1, 2, 0, 3
-    )
-    plane_rows = own_leaves.transpose(2, 0, 1, 3).reshape(port_count, leaf_count * 2 * leaf_cells)
-    induced = lax.dot_general(
-        spread, plane_rows, (((1,), (1,)), ((), ())), preferred_element_type=jnp.float32
-    ).astype(jnp.bfloat16)
+    total_field, induced = leaf_fields(
+        near_lists.reshape(-1), bordered, kernels, got_leaf, got_coupling, got_current_t
+    )
     returned = lax.all_to_all(
         induced.reshape(owners, capacity, port_count), AXES, split_axis=0, concat_axis=0, tiled=True
     ).reshape(slot_count, port_count)
@@ -209,7 +255,6 @@
         placement, returned, (((0,), (0,)), ((), ())), preferred_element_type=jnp.float32
     ).astype(jnp.bfloat16)
 
-    total_field = (near_field + filament_field).astype(jnp.bfloat16)
     grid_field = from_leaves(total_field.reshape(leaf_rows, leaf_cols, 2, port_count, leaf_cells))
     loop_voltage = field_halo(grid_field)
     return (loop_voltage, filament_voltage)

time: 135 us -> 140 us (1.037)
  blocking collectives: 30.4 us -> 0 us
  Pallas kernels: 0 us -> 19.1 us
  matrix products: 20.4 us -> 3.93 us
  starting transfers between devices: 29.2 us -> 39.6 us
  local copies, waits for them, and re-layouts: 34.8 us -> 44.5 us
  waiting for transfers between devices: 4.37 us -> 10.9 us
  other arithmetic: 12.9 us -> 19.3 us
    all_gather x1 -> x0, blocking collectives: 30.4 us -> none  [body(): lax.all_gather(filament_leaf, AXES, tiled=True)]
    pallas_call x0 -> x1, Pallas kernels: none -> 19.1 us  [leaf_fields(): pl.pallas_call(leaf_kernel, grid_spec=grid_spec, out_shape=[jax.ShapeDtyp...]
    gather x2 -> x0, local copies, waits for them, and re-layouts: 18.5 us -> none  [body(): jnp.take(flattened, source.reshape(-1), axis=0)]
    dot_general x3 -> x0, matrix products: 16.5 us -> none  [the longest x1 7.56 us: body(): lax.dot_general(sources, kernels, (((1, 4), (1, 4)), ((0, 2), (0, 2))), p...]
    reshape x2 -> x4, local copies, waits for them, and re-layouts: 0.15 us -> 9.8 us  [the longest x1 4.38 us: to_leaves(): blocks.reshape(row_count // LEAF_R, col_count // LEAF_C, components, port...]
    unnamed x16 -> x18, local copies, waits for them, and re-layouts: 9.53 us -> 18 us
    all_to_all x1, waiting for transfers between devices: 0.01 us -> 8.18 us  [body(): lax.all_to_all(induced.reshape(owners, capacity, port_count), AXES, split...]
    all_to_all x0 -> x2, other arithmetic: none -> 5.06 us  [body(): got = lax.all_to_all(payload, AXES, split_axis=0, concat_axis=0, tiled=True)]
  transfers between devices with their start and end apart: 11 -> 11, of which waited for: 2 -> 2; matrix products, arithmetic and copies ran while one was open for 37% -> 30% of each run, Pallas kernels for 0% -> 0%
where the time goes in v2:
time: 140 us; the launch traced here: 138 us
  local copies, waits for them, and re-layouts  44.5 us (32%)
  starting transfers between devices  39.6 us (28%)
  other arithmetic  19.3 us (14%)
  Pallas kernels  19.1 us (14%)
  waiting for transfers between devices  10.9 us (8%)
  matrix products  3.93 us (3%)
    ppermute x9, starting transfers between devices, send(): return lax.ppermute(value, AXES, pairs_by(fn))  20.5 us
    pallas_call x1, Pallas kernels, leaf_fields(): pl.pallas_call(leaf_kernel, grid_spec=grid_spec, out_shape=[jax.ShapeDtyp...  19.1 us
    unnamed x18, local copies, waits for them, and re-layouts  18 us
    all_to_all x1, starting transfers between devices, body(): got = lax.all_to_all(payload, AXES, split_axis=0, concat_axis=0, tiled=True)  11.6 us
    all_to_all x1, waiting for transfers between devices, body(): lax.all_to_all(induced.reshape(owners, capacity, port_count), AXES, split...  8.18 us
    all_to_all x1, starting transfers between devices, body(): lax.all_to_all(induced.reshape(owners, capacity, port_count), AXES, split...  7.56 us
    all_to_all x2, other arithmetic, body(): got = lax.all_to_all(payload, AXES, split_axis=0, concat_axis=0, tiled=True)  5.06 us
    reshape x1, local copies, waits for them, and re-layouts, to_leaves(): blocks.reshape(row_count // LEAF_R, col_count // LEAF_C, components, port...  4.38 us
  transfers between devices with their start and end apart: 11, of which 2 were waited for; matrix products, arithmetic and copies ran while one was open for 30% of the time, Pallas kernels for 0%

profile of v2, /device:TPU:0, one launch (start us, length us, event | category | flops | bytes accessed | tf_op | source)
XLA Modules:
  0.0 138.2 jit_solution(4357638816059402019)
XLA Ops:
  0.6 0.0 copy-start
  0.6 1.6 %copy-done = f32[128,16,256]{2,1,0:T(8,128)S(1)} copy-done((f32[128,16,256]{2,1,0:T(8,128)S(1)}, f32[128,16,256]{2,1,0:T(8,128)}, u32[]{:S(2)}) %copy-start) | copy-done | bytes 2097176
  2.2 2.0 %constant_dynamic-slice_fusion = f32[128,16,145]{2,1,0:T(8,128)} fusion(f32[128,16,256]{2,1,0:T(8,128)S(1)} %copy-done, s32[]{:T(128)S(6)} %select_n.58), kind=kLoop, calls=%fused_computation.70 | loop fusion | bytes 2375684 | tf_op jit(solution)/shard_map/dynamic_slice | solution.py:76
  4.2 2.0 %copy.61 = f32[128,16,145]{0,2,1:T(8,128)S(1)} copy(f32[128,16,145]{2,1,0:T(8,128)} %constant_dynamic-slice_fusion) | data formatting | bytes 2375680
  6.1 1.2 fusion.23
  7.3 5.9 %collective-permute-start.1 = (f32[128,9,145]{0,2,1:T(8,128)}, f32[128,9,145]{0,2,1:T(8,128)}, u32[]{:S(2)}, u32[]{:S(2)}) collective-permute-start(f32[128,9,145]{0,2,1:T(8,128)} %get-tuple-element.16), channel_id=1, source_target_pairs={{0,4},{1,5},{2,6},{3,7},{4,8},{5,9},{6,10},{7,11},{8,12},{9,13},{1... | collective-permute-start | bytes 2004488 | tf_op jit(solution)/shard_map/ppermute | solution.py:58
  13.3 1.3 constant_dynamic-slice_fusion.1
  14.6 1.6 %copy.60 = f32[128,16,17]{0,2,1:T(8,128)S(1)} copy(f32[128,16,17]{2,1,0:T(8,128)} %constant_dynamic-slice_fusion.1) | data formatting | bytes 278528
  16.2 1.3 collective-permute-start.2
  17.5 0.7 fusion.27
  18.2 1.3 collective-permute-start
  19.5 1.3 collective-permute-start.4
  20.8 1.3 collective-permute-start.3
  22.2 0.6 fusion.14
  22.8 3.1 %reduce-window.6 = s32[16,4,128]{2,0,1:T(8,128)} reduce-window(s32[16,4,128]{2,0,1:T(8,128)} %fusion.14, s32[]{:T(128)} %constant.85.clone.1), window={size=1x1x128 pad=0_0x0_0x127_0}, to_apply=%region_0.1 | reduce-window | flops 1040384 | bytes 65540 | tf_op jit(solution)/shard_map/reduce-window
  25.9 1.0 slice_reduce_fusion
  26.9 0.9 fusion.13
  27.8 0.4 select_reduce_fusion
  28.2 0.1 convert_element_type.43
  28.3 1.0 copy.69
  29.2 2.5 %fusion.4 = bf16[1024,384]{1,0:T(8,128)(2,1)} fusion(s32[512]{0:T(512)S(1)} %multiply_add_fusion, bf16[512,128]{1,0:T(8,128)(2,1)} %param.10, bf16[512,256]{1,0:T(8,128)(2,1)S(1)} %bitcast.54), kind=kOutput, calls=%fused_computation.10 | convolution fusion | flops 404357120 | bytes 1181696 | tf_op jit(solution)/shard_map/dot_general | solution.py:220
  31.7 2.4 %reshape.131 = bf16[16,24576]{1,0:T(8,128)(2,1)} reshape(bf16[1024,384]{1,0:T(8,128)(2,1)} %fusion.4) | data formatting | bytes 1572864 | tf_op jit(solution)/shard_map/reshape | solution.py:224
  34.1 2.1 %maximum_bitcast_fusion.1 = bf16[16,1,24640]{2,0,1:T(8,128)(2,1)} fusion(bf16[16,64]{1,0:T(8,128)(2,1)S(1)} %convert_element_type.43, bf16[16,24576]{1,0:T(8,128)(2,1)} %reshape.131), kind=kLoop, calls=%fused_computation.19 | loop fusion | flops 1576960 | bytes 1576960 | tf_op jit(solution)/shard_map/all_to_all | solution.py:229
  36.2 0.5 broadcast.184
  36.7 3.0 %reduce.2 = bf16[16,24640]{1,0:T(8,128)(2,1)} reduce(bf16[16,1,24640]{2,0,1:T(8,128)(2,1)} %maximum_bitcast_fusion.1, bf16[]{:T(256)} %broadcast.184), dimensions={1}, to_apply=%copy.52.reduce_sub_computation | reduce | bytes 1576962 | tf_op jit(solution)/shard_map/all_to_all | solution.py:229
  39.7 2.5 %reshape.138 = bf16[16,2,12320]{2,1,0:T(2,128)(2,1)} reshape(bf16[16,24640]{1,0:T(8,128)(2,1)} %reduce.2) | data formatting | bytes 1576960
  42.2 11.6 %all-to-all-start = ((bf16[16,2,12320]{2,1,0:T(2,128)(2,1)}), bf16[16,2,12320]{2,1,0:T(2,128)(2,1)}, u32[]{:S(2)}, u32[]{:S(2)}) async-start(bf16[16,2,12320]{2,1,0:T(2,128)(2,1)} %reshape.138), calls=%async_computation | async-start | bytes 1589248 | tf_op jit(solution)/shard_map/all_to_all | solution.py:229
  53.9 0.7 reshape.126.codes_ref
  54.5 0.1 and_convert_fusion
  54.6 0.0 collective-permute-done.2
  54.6 1.2 maximum_select_fusion
  55.8 0.0 collective-permute-done
  55.8 1.5 %maximum_select_fusion.1 = f32[128,9,162]{0,2,1:T(8,128)S(1)} fusion(f32[128,9,145]{0,2,1:T(8,128)} %collective-permute-done.1, f32[128,9,17]{0,2,1:T(8,128)} %collective-permute-done, pred[]{:T(512)S(6)} %eq.43), kind=kLoop, calls=%fused_computation.21 | loop fusion | flops 559872 | bytes 1492993 | tf_op jit(solution)/shard_map/jit(_where)/select_n | solution.py:86
  57.3 1.5 %maximum_select_fusion.2 = f32[128,9,162]{0,2,1:T(8,128)S(1)} fusion(f32[128,9,145]{0,2,1:T(8,128)} %collective-permute-done.4, f32[128,9,17]{0,2,1:T(8,128)} %collective-permute-done.3, pred[]{:T(512)S(6)} %eq.43), kind=kLoop, calls=%fused_computation.22 | loop fusion | flops 559872 | bytes 1492993 | tf_op jit(solution)/shard_map/jit(_where)/select_n | solution.py:86
  58.8 0.2 pad_maximum_fusion
  59.0 0.7 fusion.1
  59.7 0.2 maximum_bitcast_fusion
  59.9 2.3 %copy.49 = bf16[4,10,2,128,8,16]{3,5,4,2,1,0:T(8,128)(2,1)} copy(bf16[4,10,2,128,8,16]{3,5,1,4,0,2:T(8,128)(2,1)S(1)} %maximum_bitcast_fusion) | data formatting | bytes 5242880 | tf_op jit(solution)/shard_map/transpose | solution.py:24
  62.2 4.4 %copy.50 = bf16[4,10,2,128,128]{4,3,2,1,0:T(8,128)(2,1)} copy(bf16[4,10,2,128,128]{3,4,2,1,0:T(8,128)(2,1)} %bitcast.40) | data formatting | bytes 5242880 | tf_op jit(solution)/shard_map/reshape | solution.py:25
  66.6 3.5 %broadcast_multiply_fusion.bord_ref = bf16[4,10,2,128,128]{4,3,2,1,0:T(8,128)(2,1)} fusion(bf16[4,10,2,128,128]{4,3,2,1,0:T(8,128)(2,1)} %copy.50, bf16[4,10]{1,0:T(4,128)(2,1)S(1)} %and_convert_fusion), kind=kLoop, calls=%fused_computation.12 | loop fusion | flops 1310720 | bytes 5242960 | tf_op jit(solution)/shard_map/mul | solution.py:245
  70.0 2.7 %all-to-all-done = bf16[16,2,12320]{2,1,0:T(2,128)(2,1)} async-done(((bf16[16,2,12320]{2,1,0:T(2,128)(2,1)}), bf16[16,2,12320]{2,1,0:T(2,128)(2,1)}, u32[]{:S(2)}, u32[]{:S(2)}) %all-to-all-start) | async-done | bytes 788512 | tf_op jit(solution)/shard_map/all_to_all | solution.py:229
  72.7 5.6 %reshape.139 = bf16[16,1,24640]{2,1,0:T(2,128)(2,1)} reshape(bf16[16,2,12320]{2,1,0:T(2,128)(2,1)} %all-to-all-done) | data formatting | bytes 1576960
  78.3 1.5 %copy.68 = bf16[16,1,24640]{2,0,1:T(8,128)(2,1)S(1)} copy(bf16[16,1,24640]{2,1,0:T(2,128)(2,1)} %reshape.139) | data formatting | bytes 1576960
  79.8 0.9 slice.108
  80.7 2.4 %reshape.132 = bf16[1024,384]{1,0:T(8,128)(2,1)} reshape(bf16[16,24576]{1,0:T(8,128)(2,1)} %slice.108) | data formatting | bytes 1572864 | tf_op jit(solution)/shard_map/reshape | solution.py:230
  83.1 1.0 slice.110
  84.1 1.9 %slice.109.cpl_ref = bf16[1024,256]{1,0:T(8,128)(2,1)} slice(bf16[1024,384]{1,0:T(8,128)(2,1)} %reshape.132), slice={[0:1024], [0:256]} | slice | bytes 1048576 | tf_op jit(solution)/shard_map/slice | solution.py:232
  86.0 0.9 copy.62
  86.8 1.3 reshape.136.leaf_ref
  88.1 19.1 %shard_map.77 = (bf16[16,2,128,128]{3,2,1,0:T(8,128)(2,1)}, bf16[1024,128]{1,0:T(8,128)(2,1)}) custom-call(s32[128]{0:T(128)} %reshape.126.codes_ref, bf16[4,10,2,128,128]{4,3,2,1,0:T(8,128)(2,1)} %broadcast_multiply_fusion.bord_ref, bf16[16,8,2,128,128]{4,3,2,1,0:T(8,128)(2,1)} %bitcast.41, s32[1024,1]{1,0:T(8,128)} %reshape.136.leaf_ref, ...), custom_call_target="tpu_custom_call" | custom-call | tf_op jit(solution)/shard_map/pallas_call | solution.py:177
  107.2 1.6 %copy.55 = bf16[16,2,128,128]{2,3,1,0:T(8,128)(2,1)S(1)} copy(bf16[16,2,128,128]{3,2,1,0:T(8,128)(2,1)} %get-tuple-element.4) | data formatting | bytes 2097152 | tf_op jit(solution)/shard_map/pallas_call | solution.py:177
  108.8 0.3 fusion.24
  109.1 0.6 fusion.25
  109.8 2.2 %collective-permute-start.5 = (bf16[128,16,1]{0,2,1:T(2,128)(2,1)}, bf16[128,16,1]{0,2,1:T(2,128)(2,1)S(1)}, u32[]{:S(2)}, u32[]{:S(2)}) collective-permute-start(bf16[128,16,1]{0,2,1:T(2,128)(2,1)} %get-tuple-element.20), channel_id=1, source_target_pairs={{0,1},{1,2},{2,3},{4,5},{5,6},{6,7},{8,9},{9,10},{10,11},{12,13},{... | collective-permute-start | bytes 12296 | tf_op jit(solution)/shard_map/ppermute | solution.py:58
  111.9 1.3 collective-permute-start.6
  113.3 4.6 %collective-permute-start.7 = (bf16[128,1,128]{0,2,1:T(8,128)(2,1)S(1)}, bf16[128,1,128]{0,2,1:T(8,128)(2,1)S(1)}, u32[]{:S(2)}, u32[]{:S(2)}) collective-permute-start(bf16[128,1,128]{0,2,1:T(8,128)(2,1)S(1)} %get-tuple-element.22), channel_id=1, source_target_pairs={{0,4},{1,5},{2,6},{3,7},{4,8},{5,9},{6,10},{7,11},{8,12},{9,13},{1... | collective-permute-start | bytes 98312 | tf_op jit(solution)/shard_map/ppermute | solution.py:58
  117.9 1.3 collective-permute-start.8
  119.2 7.6 %all-to-all-start.1 = ((bf16[16,64,128]{2,1,0:T(8,128)(2,1)}), bf16[16,64,128]{2,1,0:T(8,128)(2,1)S(1)}, u32[]{:S(2)}, u32[]{:S(2)}) async-start(bf16[16,64,128]{2,1,0:T(8,128)(2,1)} %bitcast.14), calls=%async_computation.1 | async-start | bytes 524288 | tf_op jit(solution)/shard_map/all_to_all | solution.py:251
  126.8 0.1 maximum_convert_fusion.1
  126.9 0.1 maximum_convert_fusion
  127.1 0.2 fusion.6
  127.2 1.4 copy.58
  128.6 8.2 %all-to-all-done.1 = bf16[16,64,128]{2,1,0:T(8,128)(2,1)S(1)} async-done(((bf16[16,64,128]{2,1,0:T(8,128)(2,1)}), bf16[16,64,128]{2,1,0:T(8,128)(2,1)S(1)}, u32[]{:S(2)}, u32[]{:S(2)}) %all-to-all-start.1) | async-done | bytes 262176 | tf_op jit(solution)/shard_map/all_to_all | solution.py:251
  136.8 1.4 %fusion.5 = bf16[512,128]{1,0:T(8,128)(2,1)} fusion(bf16[1024,128]{1,0:T(8,128)(2,1)S(1)} %bitcast.53, s32[512]{0:T(512)S(1)} %copy-done.3), kind=kOutput, calls=%fused_computation.13 | convolution fusion | flops 134807552 | bytes 395264 | tf_op jit(solution)/shard_map/dot_general | solution.py:254
  (26 shorter events, 0.2 us)
Async XLA Ops:
  0.6 1.6 %copy-start = (f32[128,16,256]{2,1,0:T(8,128)S(1)}, f32[128,16,256]{2,1,0:T(8,128)}, u32[]{:S(2)}) copy-start(f32[128,16,256]{2,1,0:T(8,128)} %param.6) | copy-start | bytes 6291460
  7.3 14.8 %copy-start.4 = (s32[512]{0:T(512)S(1)}, s32[512]{0:T(512)}, u32[]{:S(2)}) copy-start(s32[512]{0:T(512)} %param.9) | copy-start | bytes 6148
  7.3 48.5 %collective-permute-start.1 = (f32[128,9,145]{0,2,1:T(8,128)}, f32[128,9,145]{0,2,1:T(8,128)}, u32[]{:S(2)}, u32[]{:S(2)}) collective-permute-start(f32[128,9,145]{0,2,1:T(8,128)} %get-tuple-element.16), channel_id=1, source_target_pairs={{0,4},{1,5},{2,6},{3,7},{4,8},{5,9},{6,10},{7,11},{8,12},{9,13},{1... | collective-permute-start | bytes 2004488 | tf_op jit(solution)/shard_map/ppermute | solution.py:58
  16.2 38.4 %collective-permute-start.2 = (f32[128,16,17]{0,2,1:T(8,128)S(1)}, f32[128,16,17]{0,2,1:T(8,128)}, u32[]{:S(2)}, u32[]{:S(2)}) collective-permute-start(f32[128,16,17]{0,2,1:T(8,128)S(1)} %copy.60), channel_id=1, source_target_pairs={{1,2},{2,1},{5,6},{6,5},{9,10},{10,9},{13,14},{14,13},{17,18},{18,... | collective-permute-start | bytes 417800 | tf_op jit(solution)/shard_map/ppermute | solution.py:58
  18.2 37.6 %collective-permute-start = (f32[128,9,17]{0,2,1:T(8,128)}, f32[128,9,17]{0,2,1:T(8,128)}, u32[]{:S(2)}, u32[]{:S(2)}) collective-permute-start(f32[128,9,17]{0,2,1:T(8,128)} %get-tuple-element.24), channel_id=1, source_target_pairs={{1,6},{2,5},{5,10},{6,9},{9,14},{10,13},{17,22},{18,21},{21,26},{2... | collective-permute-start | bytes 235016 | tf_op jit(solution)/shard_map/ppermute | solution.py:58
  19.5 37.8 %collective-permute-start.4 = (f32[128,9,145]{0,2,1:T(8,128)}, f32[128,9,145]{0,2,1:T(8,128)}, u32[]{:S(2)}, u32[]{:S(2)}) collective-permute-start(f32[128,9,145]{0,2,1:T(8,128)} %get-tuple-element.17), channel_id=1, source_target_pairs={{4,0},{5,1},{6,2},{7,3},{8,4},{9,5},{10,6},{11,7},{12,8},{13,9},{1... | collective-permute-start | bytes 2004488 | tf_op jit(solution)/shard_map/ppermute | solution.py:58
  20.8 36.5 %collective-permute-start.3 = (f32[128,9,17]{0,2,1:T(8,128)}, f32[128,9,17]{0,2,1:T(8,128)}, u32[]{:S(2)}, u32[]{:S(2)}) collective-permute-start(f32[128,9,17]{0,2,1:T(8,128)} %get-tuple-element.25), channel_id=1, source_target_pairs={{5,2},{6,1},{9,6},{10,5},{13,10},{14,9},{21,18},{22,17},{25,22},{2... | collective-permute-start | bytes 235016 | tf_op jit(solution)/shard_map/ppermute | solution.py:58
  27.8 6.3 %copy-start.2 = (s32[512]{0:T(512)}, s32[512]{0:T(512)S(1)}, u32[]{:S(2)}) copy-start(s32[512]{0:T(512)S(1)} %multiply_add_fusion) | copy-start | bytes 6148
  36.7 17.1 %copy-start.1 = (s32[2,8,8]{2,1,0:T(8,128)S(1)}, s32[2,8,8]{2,1,0:T(8,128)}, u32[]{:S(2)}) copy-start(s32[2,8,8]{2,1,0:T(8,128)} %param.8) | copy-start | bytes 1540
  42.2 30.5 %all-to-all-start = ((bf16[16,2,12320]{2,1,0:T(2,128)(2,1)}), bf16[16,2,12320]{2,1,0:T(2,128)(2,1)}, u32[]{:S(2)}, u32[]{:S(2)}) async-start(bf16[16,2,12320]{2,1,0:T(2,128)(2,1)} %reshape.138), calls=%async_computation | async-start | bytes 1589248 | tf_op jit(solution)/shard_map/all_to_all | solution.py:229
  109.8 17.0 %collective-permute-start.5 = (bf16[128,16,1]{0,2,1:T(2,128)(2,1)}, bf16[128,16,1]{0,2,1:T(2,128)(2,1)S(1)}, u32[]{:S(2)}, u32[]{:S(2)}) collective-permute-start(bf16[128,16,1]{0,2,1:T(2,128)(2,1)} %get-tuple-element.20), channel_id=1, source_target_pairs={{0,1},{1,2},{2,3},{4,5},{5,6},{6,7},{8,9},{9,10},{10,11},{12,13},{... | collective-permute-start | bytes 12296 | tf_op jit(solution)/shard_map/ppermute | solution.py:58
  111.9 14.9 %collective-permute-start.6 = (bf16[128,16,1]{0,2,1:T(2,128)(2,1)}, bf16[128,16,1]{0,2,1:T(2,128)(2,1)S(1)}, u32[]{:S(2)}, u32[]{:S(2)}) collective-permute-start(bf16[128,16,1]{0,2,1:T(2,128)(2,1)} %get-tuple-element.21), channel_id=1, source_target_pairs={{1,0},{2,1},{3,2},{5,4},{6,5},{7,6},{9,8},{10,9},{11,10},{13,12},{... | collective-permute-start | bytes 12296 | tf_op jit(solution)/shard_map/ppermute | solution.py:58
  113.3 13.6 %collective-permute-start.7 = (bf16[128,1,128]{0,2,1:T(8,128)(2,1)S(1)}, bf16[128,1,128]{0,2,1:T(8,128)(2,1)S(1)}, u32[]{:S(2)}, u32[]{:S(2)}) collective-permute-start(bf16[128,1,128]{0,2,1:T(8,128)(2,1)S(1)} %get-tuple-element.22), channel_id=1, source_target_pairs={{0,4},{1,5},{2,6},{3,7},{4,8},{5,9},{6,10},{7,11},{8,12},{9,13},{1... | collective-permute-start | bytes 98312 | tf_op jit(solution)/shard_map/ppermute | solution.py:58
  117.9 9.0 %collective-permute-start.8 = (bf16[128,1,128]{0,2,1:T(8,128)(2,1)S(1)}, bf16[128,1,128]{0,2,1:T(8,128)(2,1)S(1)}, u32[]{:S(2)}, u32[]{:S(2)}) collective-permute-start(bf16[128,1,128]{0,2,1:T(8,128)(2,1)S(1)} %get-tuple-element.23), channel_id=1, source_target_pairs={{4,0},{5,1},{6,2},{7,3},{8,4},{9,5},{10,6},{11,7},{12,8},{13,9},{1... | collective-permute-start | bytes 98312 | tf_op jit(solution)/shard_map/ppermute | solution.py:58
  119.2 17.6 %all-to-all-start.1 = ((bf16[16,64,128]{2,1,0:T(8,128)(2,1)}), bf16[16,64,128]{2,1,0:T(8,128)(2,1)S(1)}, u32[]{:S(2)}, u32[]{:S(2)}) async-start(bf16[16,64,128]{2,1,0:T(8,128)(2,1)} %bitcast.14), calls=%async_computation.1 | async-start | bytes 524288 | tf_op jit(solution)/shard_map/all_to_all | solution.py:251
  127.2 9.6 %copy-start.3 = (s32[512]{0:T(512)S(1)}, s32[512]{0:T(512)}, u32[]{:S(2)}) copy-start(s32[512]{0:T(512)} %copy-done.2) | copy-start | bytes 6148

commit v3 on v2

v3 whole, which is shorter than its diff:
```python
import jax
import jax.numpy as jnp
from jax import lax
from jax.experimental import pallas as pl
from jax.experimental.pallas import tpu as pltpu
from jax.sharding import PartitionSpec as P

LEAF_R = 8
LEAF_C = 16
AXES = ("gx", "gy", "gz")


def plane_curl(padded):
    along_y = padded[1:-1, 2:] - padded[1:-1, :-2]
    along_x = padded[:-2, 1:-1] - padded[2:, 1:-1]
    return jnp.stack([along_y, along_x])


def to_leaves(grid_values):
    components, row_count, col_count, port_count = grid_values.shape
    blocks = grid_values.reshape(
        components, row_count // LEAF_R, LEAF_R, col_count // LEAF_C, LEAF_C, port_count
    )
    blocks = blocks.transpose(1, 3, 0, 2, 4, 5)
    return blocks.reshape(
        row_count // LEAF_R, col_count // LEAF_C, components, LEAF_R * LEAF_C, port_count
    )


def from_leaves(leaves):
    leaf_rows, leaf_cols, components, leaf_cells, port_count = leaves.shape
    blocks = leaves.reshape(leaf_rows, leaf_cols, components, LEAF_R, LEAF_C, port_count)
    blocks = blocks.transpose(2, 0, 3, 1, 4, 5)
    return blocks.reshape(components, leaf_rows * LEAF_R, leaf_cols * LEAF_C, port_count)


def device_grid():
    nx, ny, nz = (lax.axis_size(a) for a in AXES)
    return nx, ny, nz


def pairs_by(fn):
    nx, ny, nz = device_grid()
    out = []
    for x in range(nx):
        for y in range(ny):
            for z in range(nz):
                target = fn(x, y, z)
                if target is None:
                    continue
                tx, ty, tz = target
                if 0 <= tx < nx and 0 <= ty < ny and 0 <= tz < nz:
                    out.append(((x * ny + y) * nz + z, (tx * ny + ty) * nz + tz))
    return out


def send(value, fn):
    return lax.ppermute(value, AXES, pairs_by(fn))


def sideways(x, y, z, dx):
    nz = lax.axis_size("gz")
    if z == nz - 1:
        return (x + dx, y + 1, 0)
    if z == 0:
        return (x + dx, y - 1, nz - 1)
    return None


def stream_window(stream, half):
    gz = lax.axis_index("gz")
    rows, width = stream.shape[0], stream.shape[1]
    hr, hc = LEAF_R + 1, LEAF_C + 1
    mid_w = half + hc
    mid = lax.dynamic_slice_in_dim(stream, gz * (width - mid_w), mid_w, 1)
    side = lax.dynamic_slice_in_dim(stream, gz * (width - hc), hc, 1)
    h_got = send(side, lambda x, y, z: sideways(x, y, z, 0))
    v_top = send(mid[rows - hr :], lambda x, y, z: (x + 1, y, z))
    v_bot = send(mid[:hr], lambda x, y, z: (x - 1, y, z))
    d_top = send(side[rows - hr :], lambda x, y, z: sideways(x, y, z, 1))
    d_bot = send(side[:hr], lambda x, y, z: sideways(x, y, z, -1))
    left = gz == 0

    def join(core, edge):
        return jnp.where(left, jnp.concatenate([edge, core], 1), jnp.concatenate([core, edge], 1))

    return jnp.concatenate([join(v_top, d_top), join(mid, h_got), join(v_bot, d_bot)], 0)


def field_halo(grid_field):
    x_field = grid_field[0]
    y_field = grid_field[1]
    rows = y_field.shape[0]
    cols = x_field.shape[1]

    def step(x, y, z, dc):
        nz = lax.axis_size("gz")
        c = y * nz + z + dc
        return (x, c // nz, c % nz) if c >= 0 else None

    x_left = send(x_field[:, cols - 1 :], lambda x, y, z: step(x, y, z, 1))
    x_right = send(x_field[:, :1], lambda x, y, z: step(x, y, z, -1))
    y_top = send(y_field[rows - 1 :], lambda x, y, z: (x + 1, y, z))
    y_bot = send(y_field[:1], lambda x, y, z: (x - 1, y, z))
    x_pad = jnp.concatenate([x_left, x_field, x_right], 1).astype(jnp.float32)
    y_pad = jnp.concatenate([y_top, y_field, y_bot], 0).astype(jnp.float32)
    return x_pad[:, :-2] - x_pad[:, 2:] + (y_pad[2:] - y_pad[:-2])


def leaf_kernel(
    codes_ref, scale_ref, bord_ref, ind_ref, row_leaf_ref, col_leaf_ref, cpl_ref, cpl_t_ref,
    cur_ref, field_ref, volt_ref, acc_ref,
):
    leaf = pl.program_id(0)
    leaf_cols = bord_ref.shape[1] - 2
    near_count = ind_ref.shape[1]
    components = ind_ref.shape[2]
    cells = ind_ref.shape[3]
    row = leaf // leaf_cols
    col = leaf % leaf_cols

    @pl.when(leaf == 0)
    def _():
        acc_ref[...] = jnp.zeros_like(acc_ref)

    coupling_t = cpl_t_ref[...]
    coupling_t = jnp.where(row_leaf_ref[...] == leaf, coupling_t, jnp.zeros_like(coupling_t))
    coupling = cpl_ref[...]
    coupling = jnp.where(col_leaf_ref[...] == leaf, coupling, jnp.zeros_like(coupling))
    current = cur_ref[...]
    volt = acc_ref[...]
    for c in range(components):
        total = jnp.dot(
            coupling_t[c * cells : (c + 1) * cells], current, preferred_element_type=jnp.float32
        )
        for n in range(near_count):
            code = codes_ref[leaf * near_count + n]
            src_row = jnp.minimum(jnp.maximum(row + code // 3, 0), bord_ref.shape[0] - 1)
            src_col = jnp.minimum(jnp.maximum(col + code % 3, 0), bord_ref.shape[1] - 1)
            part = jnp.dot(
                ind_ref[0, n, c], bord_ref[src_row, src_col, c], preferred_element_type=jnp.float32
            )
            total += part * scale_ref[leaf * near_count + n]
        field_ref[0, c] = total.astype(field_ref.dtype)
        volt += jnp.dot(
            coupling[:, c * cells : (c + 1) * cells],
            bord_ref[row + 1, col + 1, c],
            preferred_element_type=jnp.float32,
        )
    acc_ref[...] = volt

    @pl.when(leaf == pl.num_programs(0) - 1)
    def _():
        volt_ref[...] = volt.astype(volt_ref.dtype)


def leaf_fields(codes, scales, bordered, kernels, slot_leaf, coupling, current):
    leaf_count, near_count, components, cells, _ = kernels.shape
    slot_count, port_count = current.shape
    coupling_t = coupling.T
    row_leaf = slot_leaf.reshape(1, slot_count)
    col_leaf = slot_leaf.reshape(slot_count, 1)
    operands = (bordered, kernels, row_leaf, col_leaf, coupling, coupling_t, current)

    def whole(shape):
        return pl.BlockSpec(shape, lambda l, codes, scales: (0,) * len(shape))

    in_specs = [whole(x.shape) for x in operands]
    in_specs[1] = pl.BlockSpec(
        (1, near_count, components, cells, cells), lambda l, codes, scales: (l, 0, 0, 0, 0)
    )
    grid_spec = pltpu.PrefetchScalarGridSpec(
        num_scalar_prefetch=2,
        grid=(leaf_count,),
        in_specs=in_specs,
        out_specs=[
            pl.BlockSpec((1, components, cells, port_count), lambda l, codes, scales: (l, 0, 0, 0)),
            whole((slot_count, port_count)),
        ],
        scratch_shapes=[pltpu.VMEM((slot_count, port_count), jnp.float32)],
    )
    return pl.pallas_call(
        leaf_kernel,
        grid_spec=grid_spec,
        out_shape=[
            jax.ShapeDtypeStruct((leaf_count, components, cells, port_count), jnp.bfloat16),
            jax.ShapeDtypeStruct((slot_count, port_count), jnp.bfloat16),
        ],
        compiler_params=pltpu.CompilerParams(dimension_semantics=("arbitrary",)),
    )(codes, scales, *operands)


def body(stream, inductance, near_lists, filament_leaf, filament_current, filament_coupling):
    port_count = stream.shape[0]
    leaf_rows = inductance.shape[0]
    leaf_cols = inductance.shape[1]
    near_count = inductance.shape[2]
    leaf_cells = inductance.shape[4]
    leaf_count = leaf_rows * leaf_cols
    half_cols = leaf_cols * LEAF_C
    nx, ny, nz = device_grid()
    gx = lax.axis_index("gx")
    col_index = lax.axis_index("gy") * nz + lax.axis_index("gz")
    owners = nx * ny * nz

    filament_count = filament_leaf.shape[0]
    capacity = max(2, 2 * filament_count // owners)
    slot_count = owners * capacity
    plane_cols = leaf_cols * ny * nz
    leaf_row = filament_leaf // plane_cols
    leaf_col = filament_leaf % plane_cols
    owner_ids = leaf_row // leaf_rows * (ny * nz) + leaf_col // leaf_cols
    local_ids = leaf_row % leaf_rows * leaf_cols + leaf_col % leaf_cols
    owner_hits = (owner_ids[:, None] == jnp.arange(owners, dtype=jnp.int32)[None, :]).astype(
        jnp.int32
    )
    position = jnp.sum((jnp.cumsum(owner_hits, axis=0) - 1) * owner_hits, axis=1)
    target_slot = owner_ids * capacity + position
    placement_mask = target_slot[None, :] == jnp.arange(slot_count, dtype=jnp.int32)[:, None]
    placement = placement_mask.astype(jnp.bfloat16)
    row_width = 2 * leaf_cells + port_count
    rows_out = jnp.concatenate(
        [filament_coupling.reshape(filament_count, 2 * leaf_cells), filament_current], 1
    )
    sent = jnp.dot(placement, rows_out, preferred_element_type=jnp.float32).astype(jnp.bfloat16)
    sent_leaf = jnp.max(jnp.where(placement_mask, local_ids[None, :], -1), axis=1)
    leaf_row_block = jnp.pad(
        sent_leaf.astype(jnp.bfloat16).reshape(owners, 1, capacity),
        ((0, 0), (0, 0), (0, row_width - capacity)),
    )
    payload = jnp.concatenate([sent.reshape(owners, capacity, row_width), leaf_row_block], 1)
    got = lax.all_to_all(payload, AXES, split_axis=0, concat_axis=0, tiled=True)
    got_rows = got[:, :capacity].reshape(slot_count, row_width)
    got_leaf = got[:, capacity, :capacity].reshape(slot_count).astype(jnp.int32)
    got_coupling = got_rows[:, : 2 * leaf_cells]
    got_current = got_rows[:, 2 * leaf_cells :]

    window = stream_window(stream.transpose(1, 2, 0), half_cols)
    currents = plane_curl(window).astype(jnp.bfloat16)
    bordered = to_leaves(currents)
    ring_rows = jnp.arange(leaf_rows + 2, dtype=jnp.int32)
    ring_cols = jnp.arange(leaf_cols + 2, dtype=jnp.int32)
    row_ok = ((ring_rows > 0) | (gx > 0)) & ((ring_rows < leaf_rows + 1) | (gx < nx - 1))
    col_ok = ((ring_cols > 0) | (col_index > 0)) & (
        (ring_cols < leaf_cols + 1) | (col_index < ny * nz - 1)
    )
    src_row = jnp.arange(leaf_rows, dtype=jnp.int32)[:, None, None] + near_lists // 3
    src_col = jnp.arange(leaf_cols, dtype=jnp.int32)[None, :, None] + near_lists % 3
    scales = (row_ok[src_row] & col_ok[src_col]).astype(jnp.float32).reshape(-1)

    kernels = inductance.reshape(leaf_count, near_count, 2, leaf_cells, leaf_cells)
    total_field, induced = leaf_fields(
        near_lists.reshape(-1), scales, bordered, kernels, got_leaf, got_coupling, got_current
    )
    returned = lax.all_to_all(
        induced.reshape(owners, capacity, port_count), AXES, split_axis=0, concat_axis=0, tiled=True
    ).reshape(slot_count, port_count)
    filament_voltage = lax.dot_general(
        placement, returned, (((0,), (0,)), ((), ())), preferred_element_type=jnp.float32
    ).astype(jnp.bfloat16)

    grid_field = from_leaves(total_field.reshape(leaf_rows, leaf_cols, 2, leaf_cells, port_count))
    loop_voltage = field_halo(grid_field).transpose(2, 0, 1)
    return (loop_voltage, filament_voltage)


def solution(mesh):
    return jax.shard_map(
        body,
        mesh=mesh,
        in_specs=(
            P("groups", "gx", "gy"),
            P(("groups", "gx"), ("gy", "gz"), None, None, None, None),
            P(("groups", "gx"), ("gy", "gz"), None),
            P(("groups", "gx", "gy", "gz")),
            P(("groups", "gx", "gy", "gz"), None),
            P(("groups", "gx", "gy", "gz"), None, None),
        ),
        out_specs=(P("groups", "gx", ("gy", "gz")), P(("groups", "gx", "gy", "gz"), None)),
        check_vma=False,
    )
```

time: 140 us -> 119 us (0.85)
  local copies, waits for them, and re-layouts: 44.5 us -> 29.5 us
  starting transfers between devices: 39.6 us -> 36.5 us
  other arithmetic: 19.3 us -> 16.4 us
  waiting for transfers between devices: 10.9 us -> 13.7 us
  Pallas kernels: 19.1 us -> 17.1 us
    unnamed x18 -> x14, local copies, waits for them, and re-layouts: 18 us -> 7.55 us
    reshape x3 -> x0, local copies, waits for them, and re-layouts: 9.14 us -> none  [the longest x1 4.38 us: to_leaves(): blocks.reshape(row_count // LEAF_R, col_count // LEAF_C, components, port...]
    all_to_all x2 -> x0, other arithmetic: 5.06 us -> none  [body(): got = lax.all_to_all(payload, AXES, split_axis=0, concat_axis=0, tiled=True)]
    another operation x1 -> x4, local copies, waits for them, and re-layouts: 0.01 us -> 4.75 us
    mul x1 -> x0, other arithmetic: 3.48 us -> none  [body(): bordered = bordered * inside[:, :, None, None, None]]
    dynamic_slice x2 -> x0, local copies, waits for them, and re-layouts: 3.26 us -> none  [the longest x1 1.95 us: stream_window(): mid = lax.dynamic_slice_in_dim(stream, gz * (width - mid_w), mid_w, 2)]
    all_to_all x1, waiting for transfers between devices: 2.67 us -> 5.53 us  [body(): got = lax.all_to_all(payload, AXES, split_axis=0, concat_axis=0, tiled=True)]
    all_to_all x1, starting transfers between devices: 11.6 us -> 8.9 us  [body(): got = lax.all_to_all(payload, AXES, split_axis=0, concat_axis=0, tiled=True)]
  transfers between devices with their start and end apart: 11 -> 11, of which waited for: 2 -> 2; matrix products, arithmetic and copies ran while one was open for 30% -> 27% of each run, Pallas kernels for 0% -> 0%
where the time goes in v3:
time: 119 us; the launch traced here: 117 us
  starting transfers between devices  36.5 us (31%)
  local copies, waits for them, and re-layouts  29.5 us (25%)
  Pallas kernels  17.1 us (14%)
  other arithmetic  16.4 us (14%)
  waiting for transfers between devices  13.7 us (12%)
  matrix products  3.06 us (3%)
    ppermute x9, starting transfers between devices, send(): return lax.ppermute(value, AXES, pairs_by(fn))  22.5 us
    pallas_call x1, Pallas kernels, leaf_fields(): pl.pallas_call(leaf_kernel, grid_spec=grid_spec, out_shape=[jax.ShapeDtyp...  17.1 us
    all_to_all x1, starting transfers between devices, body(): got = lax.all_to_all(payload, AXES, split_axis=0, concat_axis=0, tiled=True)  8.9 us
    all_to_all x1, waiting for transfers between devices, body(): lax.all_to_all(induced.reshape(owners, capacity, port_count), AXES, split...  8.18 us
    unnamed x14, local copies, waits for them, and re-layouts  7.55 us
    all_to_all x1, waiting for transfers between devices, body(): got = lax.all_to_all(payload, AXES, split_axis=0, concat_axis=0, tiled=True)  5.53 us
    all_to_all x1, starting transfers between devices, body(): lax.all_to_all(induced.reshape(owners, capacity, port_count), AXES, split...  5.04 us
    select_n x3, other arithmetic, join(): jnp.where(left, jnp.concatenate([edge, core], 1), jnp.concatenate([core,...  4.15 us
  transfers between devices with their start and end apart: 11, of which 2 were waited for; matrix products, arithmetic and copies ran while one was open for 27% of the time, Pallas kernels for 0%

profile of v3, /device:TPU:0, one launch (start us, length us, event | category | flops | bytes accessed | tf_op | source)
XLA Modules:
  0.0 117.2 jit_solution(14938704979690313648)
XLA Ops:
  0.6 0.0 copy-start
  0.6 1.6 %copy-done = f32[128,16,256]{2,1,0:T(8,128)S(1)} copy-done((f32[128,16,256]{2,1,0:T(8,128)S(1)}, f32[128,16,256]{2,1,0:T(8,128)}, u32[]{:S(2)}) %copy-start) | copy-done | bytes 2097176
  2.2 1.9 %constant_dynamic-slice_fusion = f32[128,16,145]{2,1,0:T(8,128)} fusion(f32[128,16,256]{2,1,0:T(8,128)S(1)} %copy-done, s32[]{:T(128)S(6)} %select_n.79), kind=kLoop, calls=%fused_computation.85 | loop fusion | bytes 2375684 | tf_op jit(solution)/shard_map/dynamic-slice.1
  4.2 2.0 %copy.42 = f32[128,16,145]{0,2,1:T(8,128)S(1)} copy(f32[128,16,145]{2,1,0:T(8,128)} %constant_dynamic-slice_fusion) | data formatting | bytes 2375680
  6.1 1.2 %fusion.30 = (f32[9,145,128]{2,1,0:T(8,128)}, f32[9,145,128]{2,1,0:T(8,128)}) fusion(f32[16,145,128]{2,1,0:T(8,128)S(1)} %bitcast.44), kind=kLoop, calls=%fused_computation.90 | loop fusion | bytes 2672640 | tf_op jit(solution)/shard_map/slice | solution.py:78
  7.3 1.3 %collective-permute-start.4 = (f32[9,145,128]{2,1,0:T(8,128)}, f32[9,145,128]{2,1,0:T(8,128)}, u32[]{:S(2)}, u32[]{:S(2)}) collective-permute-start(f32[9,145,128]{2,1,0:T(8,128)} %get-tuple-element.15), channel_id=1, source_target_pairs={{4,0},{5,1},{6,2},{7,3},{8,4},{9,5},{10,6},{11,7},{12,8},{13,9},{1... | collective-permute-start | bytes 2004488 | tf_op jit(solution)/shard_map/ppermute | solution.py:58
  8.6 0.0 copy-start.4
  8.6 1.3 %constant_dynamic-slice_fusion.1 = f32[128,16,17]{2,1,0:T(8,128)} fusion(f32[128,16,256]{2,1,0:T(8,128)S(1)} %copy-done, s32[]{:T(128)S(6)} %select_n.78), kind=kLoop, calls=%fused_computation.86 | loop fusion | bytes 278532 | tf_op jit(solution)/shard_map/dynamic-slice
  9.9 1.6 %copy.41 = f32[128,16,17]{0,2,1:T(8,128)S(1)} copy(f32[128,16,17]{2,1,0:T(8,128)} %constant_dynamic-slice_fusion.1) | data formatting | bytes 278528
  11.6 1.3 %collective-permute-start.2 = (f32[16,17,128]{2,1,0:T(8,128)S(1)}, f32[16,17,128]{2,1,0:T(8,128)}, u32[]{:S(2)}, u32[]{:S(2)}) collective-permute-start(f32[16,17,128]{2,1,0:T(8,128)S(1)} %bitcast.58), channel_id=1, source_target_pairs={{1,2},{2,1},{5,6},{6,5},{9,10},{10,9},{13,14},{14,13},{17,18},{18,... | collective-permute-start | bytes 417800 | tf_op jit(solution)/shard_map/ppermute | solution.py:58
  12.9 0.7 fusion.34
  13.6 1.3 %collective-permute-start.3 = (f32[9,17,128]{2,1,0:T(8,128)}, f32[9,17,128]{2,1,0:T(8,128)}, u32[]{:S(2)}, u32[]{:S(2)}) collective-permute-start(f32[9,17,128]{2,1,0:T(8,128)} %get-tuple-element.25), channel_id=1, source_target_pairs={{5,2},{6,1},{9,6},{10,5},{13,10},{14,9},{21,18},{22,17},{25,22},{2... | collective-permute-start | bytes 235016 | tf_op jit(solution)/shard_map/ppermute | solution.py:58
  14.9 6.4 %collective-permute-start.1 = (f32[9,145,128]{2,1,0:T(8,128)}, f32[9,145,128]{2,1,0:T(8,128)}, u32[]{:S(2)}, u32[]{:S(2)}) collective-permute-start(f32[9,145,128]{2,1,0:T(8,128)} %get-tuple-element.14), channel_id=1, source_target_pairs={{0,4},{1,5},{2,6},{3,7},{4,8},{5,9},{6,10},{7,11},{8,12},{9,13},{1... | collective-permute-start | bytes 2004488 | tf_op jit(solution)/shard_map/ppermute | solution.py:58
  21.3 1.3 %collective-permute-start = (f32[9,17,128]{2,1,0:T(8,128)}, f32[9,17,128]{2,1,0:T(8,128)}, u32[]{:S(2)}, u32[]{:S(2)}) collective-permute-start(f32[9,17,128]{2,1,0:T(8,128)} %get-tuple-element.24), channel_id=1, source_target_pairs={{1,6},{2,5},{5,10},{6,9},{9,14},{10,13},{17,22},{18,21},{21,26},{2... | collective-permute-start | bytes 235016 | tf_op jit(solution)/shard_map/ppermute | solution.py:58
  22.6 0.6 fusion.22
  23.2 0.6 fusion.17
  23.8 3.1 %reduce-window.6 = s32[16,4,128]{2,0,1:T(8,128)} reduce-window(s32[16,4,128]{2,0,1:T(8,128)} %fusion.17, s32[]{:T(128)} %constant.103.clone.1), window={size=1x1x128 pad=0_0x0_0x127_0}, to_apply=%region_0.1 | reduce-window | flops 1040384 | bytes 65540 | tf_op jit(solution)/shard_map/reduce-window
  27.0 1.0 slice_reduce_fusion
  28.0 0.9 fusion.16
  28.9 1.0 select_reduce_fusion
  29.9 0.1 convert_element_type.84
  30.0 1.0 copy.50
  31.0 1.6 %fusion.5 = bf16[1024,384]{1,0:T(8,128)(2,1)S(1)} fusion(s32[512]{0:T(512)S(1)} %multiply_add_fusion, bf16[512,128]{1,0:T(8,128)(2,1)} %param.10, bf16[512,256]{1,0:T(8,128)(2,1)S(1)} %bitcast.63), kind=kOutput, calls=%fused_computation.14 | convolution fusion | flops 404357120 | bytes 1181696 | tf_op jit(solution)/shard_map/dot_general | solution.py:225
  32.6 1.0 fusion.11
  33.6 8.9 %all-to-all-start = ((bf16[16,65,384]{2,1,0:T(8,128)(2,1)}), bf16[16,65,384]{2,1,0:T(8,128)(2,1)}, u32[]{:S(2)}, u32[]{:S(2)}) async-start(bf16[16,65,384]{2,1,0:T(8,128)(2,1)} %fusion.11), calls=%async_computation | async-start | bytes 1769472 | tf_op jit(solution)/shard_map/all_to_all | solution.py:232
  42.6 0.6 compare_select_fusion
  43.2 0.1 reshape.118
  43.3 1.4 %reshape.104.codes_ref = s32[128]{0:T(128)} reshape(s32[2,8,8]{2,1,0:T(8,128)} %param.8) | data formatting | bytes 1024 | tf_op jit(solution)/shard_map/reshape | solution.py:253
  44.7 1.4 %reshape.126 = s32[128]{0:T(128)} reshape(s32[2,8,8]{2,1,0:T(8,128)} %get-tuple-element.26) | data formatting | bytes 1024 | tf_op jit(solution)/shard_map/broadcast_in_dim | solution.py:249
  46.0 1.2 %gather_fusion = pred[128]{0:T(512)(128)(4,1)S(1)} fusion(pred[4]{0:T(512)(128)(4,1)S(1)} %or_and_fusion.1, s32[1024]{0:T(1024)S(1)} %pad_clamp_fusion.1), kind=kCustom, calls=%fused_computation | custom fusion | bytes 768 | tf_op jit(solution)/shard_map/gather | solution.py:249
  47.3 0.7 pad_clamp_fusion
  48.0 1.2 %gather_fusion.1 = pred[128]{0:T(512)(128)(4,1)S(1)} fusion(pred[10]{0:T(512)(128)(4,1)S(1)} %or_and_fusion, s32[1024]{0:T(1024)S(1)} %pad_clamp_fusion), kind=kCustom, calls=%fused_computation.1 | custom fusion | bytes 768 | tf_op jit(solution)/shard_map/gather | solution.py:249
  49.2 0.5 and_convert_fusion.scale_ref
  49.7 1.2 %maximum_select_fusion = f32[16,162,128]{2,1,0:T(8,128)S(1)} fusion(f32[16,145,128]{2,1,0:T(8,128)S(1)} %bitcast.45, f32[16,17,128]{2,1,0:T(8,128)} %collective-permute-done.2, pred[]{:T(512)S(6)} %eq.45), kind=kLoop, calls=%fused_computation.15 | loop fusion | flops 995328 | bytes 2654209 | tf_op jit(solution)/shard_map/jit(_where)/select_n | solution.py:85
  50.9 1.5 %maximum_select_fusion.2 = f32[9,162,128]{2,1,0:T(8,128)S(1)} fusion(f32[9,145,128]{2,1,0:T(8,128)} %collective-permute-done.4, f32[9,17,128]{2,1,0:T(8,128)} %collective-permute-done.3, pred[]{:T(512)S(6)} %eq.45), kind=kLoop, calls=%fused_computation.26 | loop fusion | flops 559872 | bytes 1492993 | tf_op jit(solution)/shard_map/jit(_where)/select_n | solution.py:85
  52.4 1.5 %maximum_select_fusion.1 = f32[9,162,128]{2,1,0:T(8,128)S(1)} fusion(f32[9,145,128]{2,1,0:T(8,128)} %collective-permute-done.1, f32[9,17,128]{2,1,0:T(8,128)} %collective-permute-done, pred[]{:T(512)S(6)} %eq.45), kind=kLoop, calls=%fused_computation.25 | loop fusion | flops 559872 | bytes 1492993 | tf_op jit(solution)/shard_map/jit(_where)/select_n | solution.py:85
  53.9 0.2 pad_maximum_fusion
  54.1 0.7 fusion.1
  54.8 0.2 maximum_bitcast_fusion
  55.1 2.3 %copy.34 = bf16[4,10,2,8,16,128]{5,4,3,2,1,0:T(8,128)(2,1)} copy(bf16[4,10,2,8,16,128]{5,4,1,3,0,2:T(8,128)(2,1)S(1)} %maximum_bitcast_fusion) | data formatting | bytes 5242880 | tf_op jit(solution)/shard_map/transpose | solution.py:24
  57.3 5.5 %all-to-all-done = bf16[16,65,384]{2,1,0:T(8,128)(2,1)} async-done(((bf16[16,65,384]{2,1,0:T(8,128)(2,1)}), bf16[16,65,384]{2,1,0:T(8,128)(2,1)}, u32[]{:S(2)}, u32[]{:S(2)}) %all-to-all-start) | async-done | bytes 798752 | tf_op jit(solution)/shard_map/all_to_all | solution.py:232
  62.9 1.2 %slice.112 = bf16[16,64,384]{2,1,0:T(8,128)(2,1)S(1)} slice(bf16[16,65,384]{2,1,0:T(8,128)(2,1)} %all-to-all-done), slice={[0:16], [0:64], [0:384]} | slice | bytes 1572864 | tf_op jit(solution)/shard_map/slice | solution.py:233
  64.1 0.9 slice_bitcast_fusion
  65.0 0.7 slice.114.cur_ref
  65.7 0.8 fusion.29
  66.5 0.7 reshape.114.row_leaf_ref
  67.2 0.8 slice_convert_fusion
  67.9 1.3 %reshape.139.col_leaf_ref = s32[1024,1]{1,0:T(8,128)} reshape(s32[16,64]{1,0:T(8,128)S(1)} %bitcast.64) | data formatting | bytes 8192 | tf_op jit(solution)/shard_map/convert_element_type | solution.py:234
  69.2 1.0 copy.38.cpl_t_ref
  70.2 17.1 %shard_map.77 = (bf16[16,2,128,128]{3,2,1,0:T(8,128)(2,1)}, bf16[1024,128]{1,0:T(8,128)(2,1)}) custom-call(s32[128]{0:T(128)} %reshape.104.codes_ref, f32[128]{0:T(128)} %and_convert_fusion.scale_ref, bf16[4,10,2,128,128]{4,3,2,1,0:T(8,128)(2,1)} %bitcast.46, bf16[16,8,2,128,128]{4,3,2,1,0:T(8,128)(2,1)} %bitcast.47, s32[1,1024]{1,0:T(1,128)} %reshape.114.row_leaf_ref, ...), custom_call_target="tpu_custom_call" | custom-call | tf_op jit(solution)/shard_map/pallas_call | solution.py:182
  87.3 1.5 %copy.49 = bf16[2,8,2,8,16,128]{5,4,1,3,0,2:T(8,128)(2,1)S(1)} copy(bf16[2,8,2,8,16,128]{5,4,3,2,1,0:T(8,128)(2,1)} %bitcast.57) | data formatting | bytes 2097152 | tf_op jit(solution)/shard_map/reshape;reshape | solution.py:32
  88.8 0.3 fusion.31
  89.1 0.6 fusion.32
  89.7 1.3 %collective-permute-start.6 = (bf16[16,1,128]{2,1,0:T(2,128)(2,1)}, bf16[16,1,128]{2,1,0:T(2,128)(2,1)S(1)}, u32[]{:S(2)}, u32[]{:S(2)}) collective-permute-start(bf16[16,1,128]{2,1,0:T(2,128)(2,1)} %get-tuple-element.21), channel_id=1, source_target_pairs={{1,0},{2,1},{3,2},{5,4},{6,5},{7,6},{9,8},{10,9},{11,10},{13,12},{... | collective-permute-start | bytes 12296 | tf_op jit(solution)/shard_map/ppermute | solution.py:58
  91.0 3.0 %collective-permute-start.5 = (bf16[16,1,128]{2,1,0:T(2,128)(2,1)}, bf16[16,1,128]{2,1,0:T(2,128)(2,1)S(1)}, u32[]{:S(2)}, u32[]{:S(2)}) collective-permute-start(bf16[16,1,128]{2,1,0:T(2,128)(2,1)} %get-tuple-element.20), channel_id=1, source_target_pairs={{0,1},{1,2},{2,3},{4,5},{5,6},{6,7},{8,9},{9,10},{10,11},{12,13},{... | collective-permute-start | bytes 12296 | tf_op jit(solution)/shard_map/ppermute | solution.py:58
  94.0 1.3 %collective-permute-start.8 = (bf16[1,128,128]{2,1,0:T(8,128)(2,1)S(1)}, bf16[1,128,128]{2,1,0:T(8,128)(2,1)S(1)}, u32[]{:S(2)}, u32[]{:S(2)}) collective-permute-start(bf16[1,128,128]{2,1,0:T(8,128)(2,1)S(1)} %get-tuple-element.23), channel_id=1, source_target_pairs={{4,0},{5,1},{6,2},{7,3},{8,4},{9,5},{10,6},{11,7},{12,8},{13,9},{1... | collective-permute-start | bytes 98312 | tf_op jit(solution)/shard_map/ppermute | solution.py:58
  95.3 5.3 %collective-permute-start.7 = (bf16[1,128,128]{2,1,0:T(8,128)(2,1)S(1)}, bf16[1,128,128]{2,1,0:T(8,128)(2,1)S(1)}, u32[]{:S(2)}, u32[]{:S(2)}) collective-permute-start(bf16[1,128,128]{2,1,0:T(8,128)(2,1)S(1)} %get-tuple-element.22), channel_id=1, source_target_pairs={{0,4},{1,5},{2,6},{3,7},{4,8},{5,9},{6,10},{7,11},{8,12},{9,13},{1... | collective-permute-start | bytes 98312 | tf_op jit(solution)/shard_map/ppermute | solution.py:58
  100.7 5.0 %all-to-all-start.1 = ((bf16[16,64,128]{2,1,0:T(8,128)(2,1)}), bf16[16,64,128]{2,1,0:T(8,128)(2,1)S(1)}, u32[]{:S(2)}, u32[]{:S(2)}) async-start(bf16[16,64,128]{2,1,0:T(8,128)(2,1)} %bitcast.17), calls=%async_computation.1 | async-start | bytes 524288 | tf_op jit(solution)/shard_map/all_to_all | solution.py:255
  105.7 0.1 maximum_convert_fusion.1
  105.9 0.1 maximum_convert_fusion
  106.0 0.2 fusion.8
  106.2 1.4 %copy.40 = f32[128,16,128]{2,1,0:T(8,128)} copy(f32[128,16,128]{0,2,1:T(8,128)S(1)} %fusion.8) | data formatting | bytes 2097152
  107.6 8.2 %all-to-all-done.1 = bf16[16,64,128]{2,1,0:T(8,128)(2,1)S(1)} async-done(((bf16[16,64,128]{2,1,0:T(8,128)(2,1)}), bf16[16,64,128]{2,1,0:T(8,128)(2,1)S(1)}, u32[]{:S(2)}, u32[]{:S(2)}) %all-to-all-start.1) | async-done | bytes 262176 | tf_op jit(solution)/shard_map/all_to_all | solution.py:255
  115.8 1.4 %fusion.6 = bf16[512,128]{1,0:T(8,128)(2,1)} fusion(bf16[1024,128]{1,0:T(8,128)(2,1)S(1)} %bitcast.62, s32[512]{0:T(512)S(1)} %copy-done.3), kind=kOutput, calls=%fused_computation.16 | convolution fusion | flops 134807552 | bytes 395264 | tf_op jit(solution)/shard_map/dot_general | solution.py:258
  (24 shorter events, 0.1 us)
Async XLA Ops:
  0.6 1.6 %copy-start = (f32[128,16,256]{2,1,0:T(8,128)S(1)}, f32[128,16,256]{2,1,0:T(8,128)}, u32[]{:S(2)}) copy-start(f32[128,16,256]{2,1,0:T(8,128)} %param.6) | copy-start | bytes 6291460
  7.3 43.6 %collective-permute-start.4 = (f32[9,145,128]{2,1,0:T(8,128)}, f32[9,145,128]{2,1,0:T(8,128)}, u32[]{:S(2)}, u32[]{:S(2)}) collective-permute-start(f32[9,145,128]{2,1,0:T(8,128)} %get-tuple-element.15), channel_id=1, source_target_pairs={{4,0},{5,1},{6,2},{7,3},{8,4},{9,5},{10,6},{11,7},{12,8},{13,9},{1... | collective-permute-start | bytes 2004488 | tf_op jit(solution)/shard_map/ppermute | solution.py:58
  8.6 14.0 %copy-start.4 = (s32[512]{0:T(512)S(1)}, s32[512]{0:T(512)}, u32[]{:S(2)}) copy-start(s32[512]{0:T(512)} %param.9) | copy-start | bytes 6148
  11.6 38.2 %collective-permute-start.2 = (f32[16,17,128]{2,1,0:T(8,128)S(1)}, f32[16,17,128]{2,1,0:T(8,128)}, u32[]{:S(2)}, u32[]{:S(2)}) collective-permute-start(f32[16,17,128]{2,1,0:T(8,128)S(1)} %bitcast.58), channel_id=1, source_target_pairs={{1,2},{2,1},{5,6},{6,5},{9,10},{10,9},{13,14},{14,13},{17,18},{18,... | collective-permute-start | bytes 417800 | tf_op jit(solution)/shard_map/ppermute | solution.py:58
  13.6 37.3 %collective-permute-start.3 = (f32[9,17,128]{2,1,0:T(8,128)}, f32[9,17,128]{2,1,0:T(8,128)}, u32[]{:S(2)}, u32[]{:S(2)}) collective-permute-start(f32[9,17,128]{2,1,0:T(8,128)} %get-tuple-element.25), channel_id=1, source_target_pairs={{5,2},{6,1},{9,6},{10,5},{13,10},{14,9},{21,18},{22,17},{25,22},{2... | collective-permute-start | bytes 235016 | tf_op jit(solution)/shard_map/ppermute | solution.py:58
  14.9 37.5 %collective-permute-start.1 = (f32[9,145,128]{2,1,0:T(8,128)}, f32[9,145,128]{2,1,0:T(8,128)}, u32[]{:S(2)}, u32[]{:S(2)}) collective-permute-start(f32[9,145,128]{2,1,0:T(8,128)} %get-tuple-element.14), channel_id=1, source_target_pairs={{0,4},{1,5},{2,6},{3,7},{4,8},{5,9},{6,10},{7,11},{8,12},{9,13},{1... | collective-permute-start | bytes 2004488 | tf_op jit(solution)/shard_map/ppermute | solution.py:58
  21.3 31.1 %collective-permute-start = (f32[9,17,128]{2,1,0:T(8,128)}, f32[9,17,128]{2,1,0:T(8,128)}, u32[]{:S(2)}, u32[]{:S(2)}) collective-permute-start(f32[9,17,128]{2,1,0:T(8,128)} %get-tuple-element.24), channel_id=1, source_target_pairs={{1,6},{2,5},{5,10},{6,9},{9,14},{10,13},{17,22},{18,21},{21,26},{2... | collective-permute-start | bytes 235016 | tf_op jit(solution)/shard_map/ppermute | solution.py:58
  28.8 2.1 %copy-start.2 = (s32[512]{0:T(512)}, s32[512]{0:T(512)S(1)}, u32[]{:S(2)}) copy-start(s32[512]{0:T(512)S(1)} %multiply_add_fusion) | copy-start | bytes 6148
  32.6 9.9 %copy-start.1 = (s32[2,8,8]{2,1,0:T(8,128)S(1)}, s32[2,8,8]{2,1,0:T(8,128)}, u32[]{:S(2)}) copy-start(s32[2,8,8]{2,1,0:T(8,128)} %param.8) | copy-start | bytes 1540
  33.6 29.3 %all-to-all-start = ((bf16[16,65,384]{2,1,0:T(8,128)(2,1)}), bf16[16,65,384]{2,1,0:T(8,128)(2,1)}, u32[]{:S(2)}, u32[]{:S(2)}) async-start(bf16[16,65,384]{2,1,0:T(8,128)(2,1)} %fusion.11), calls=%async_computation | async-start | bytes 1769472 | tf_op jit(solution)/shard_map/all_to_all | solution.py:232
  89.7 16.0 %collective-permute-start.6 = (bf16[16,1,128]{2,1,0:T(2,128)(2,1)}, bf16[16,1,128]{2,1,0:T(2,128)(2,1)S(1)}, u32[]{:S(2)}, u32[]{:S(2)}) collective-permute-start(bf16[16,1,128]{2,1,0:T(2,128)(2,1)} %get-tuple-element.21), channel_id=1, source_target_pairs={{1,0},{2,1},{3,2},{5,4},{6,5},{7,6},{9,8},{10,9},{11,10},{13,12},{... | collective-permute-start | bytes 12296 | tf_op jit(solution)/shard_map/ppermute | solution.py:58
  91.0 14.7 %collective-permute-start.5 = (bf16[16,1,128]{2,1,0:T(2,128)(2,1)}, bf16[16,1,128]{2,1,0:T(2,128)(2,1)S(1)}, u32[]{:S(2)}, u32[]{:S(2)}) collective-permute-start(bf16[16,1,128]{2,1,0:T(2,128)(2,1)} %get-tuple-element.20), channel_id=1, source_target_pairs={{0,1},{1,2},{2,3},{4,5},{5,6},{6,7},{8,9},{9,10},{10,11},{12,13},{... | collective-permute-start | bytes 12296 | tf_op jit(solution)/shard_map/ppermute | solution.py:58
  94.0 11.8 %collective-permute-start.8 = (bf16[1,128,128]{2,1,0:T(8,128)(2,1)S(1)}, bf16[1,128,128]{2,1,0:T(8,128)(2,1)S(1)}, u32[]{:S(2)}, u32[]{:S(2)}) collective-permute-start(bf16[1,128,128]{2,1,0:T(8,128)(2,1)S(1)} %get-tuple-element.23), channel_id=1, source_target_pairs={{4,0},{5,1},{6,2},{7,3},{8,4},{9,5},{10,6},{11,7},{12,8},{13,9},{1... | collective-permute-start | bytes 98312 | tf_op jit(solution)/shard_map/ppermute | solution.py:58
  95.3 10.5 %collective-permute-start.7 = (bf16[1,128,128]{2,1,0:T(8,128)(2,1)S(1)}, bf16[1,128,128]{2,1,0:T(8,128)(2,1)S(1)}, u32[]{:S(2)}, u32[]{:S(2)}) collective-permute-start(bf16[1,128,128]{2,1,0:T(8,128)(2,1)S(1)} %get-tuple-element.22), channel_id=1, source_target_pairs={{0,4},{1,5},{2,6},{3,7},{4,8},{5,9},{6,10},{7,11},{8,12},{9,13},{1... | collective-permute-start | bytes 98312 | tf_op jit(solution)/shard_map/ppermute | solution.py:58
  100.7 15.1 %all-to-all-start.1 = ((bf16[16,64,128]{2,1,0:T(8,128)(2,1)}), bf16[16,64,128]{2,1,0:T(8,128)(2,1)S(1)}, u32[]{:S(2)}, u32[]{:S(2)}) async-start(bf16[16,64,128]{2,1,0:T(8,128)(2,1)} %bitcast.17), calls=%async_computation.1 | async-start | bytes 524288 | tf_op jit(solution)/shard_map/all_to_all | solution.py:255
  106.2 9.6 %copy-start.3 = (s32[512]{0:T(512)S(1)}, s32[512]{0:T(512)}, u32[]{:S(2)}) copy-start(s32[512]{0:T(512)} %copy-done.2) | copy-start | bytes 6148

commit v4 on v3

--- a/solution.py
+++ b/solution.py
@@ -211,10 +211,9 @@
     leaf_col = filament_leaf % plane_cols
     owner_ids = leaf_row // leaf_rows * (ny * nz) + leaf_col // leaf_cols
     local_ids = leaf_row % leaf_rows * leaf_cols + leaf_col % leaf_cols
-    owner_hits = (owner_ids[:, None] == jnp.arange(owners, dtype=jnp.int32)[None, :]).astype(
-        jnp.int32
-    )
-    position = jnp.sum((jnp.cumsum(owner_hits, axis=0) - 1) * owner_hits, axis=1)
+    index = jnp.arange(filament_count, dtype=jnp.int32)
+    earlier = (owner_ids[None, :] == owner_ids[:, None]) & (index[None, :] < index[:, None])
+    position = jnp.sum(earlier.astype(jnp.int32), axis=1)
     target_slot = owner_ids * capacity + position
     placement_mask = target_slot[None, :] == jnp.arange(slot_count, dtype=jnp.int32)[:, None]
     placement = placement_mask.astype(jnp.bfloat16)
@@ -223,7 +222,9 @@
         [filament_coupling.reshape(filament_count, 2 * leaf_cells), filament_current], 1
     )
     sent = jnp.dot(placement, rows_out, preferred_element_type=jnp.float32).astype(jnp.bfloat16)
-    sent_leaf = jnp.max(jnp.where(placement_mask, local_ids[None, :], -1), axis=1)
+    sent_leaf = jnp.dot(
+        placement, (local_ids + 1).astype(jnp.bfloat16), preferred_element_type=jnp.float32
+    ) - 1.0
     leaf_row_block = jnp.pad(
         sent_leaf.astype(jnp.bfloat16).reshape(owners, 1, capacity),
         ((0, 0), (0, 0), (0, row_width - capacity)),

time: 119 us -> 112 us (0.941)
  other arithmetic: 16.4 us -> 10.3 us
    another operation x3 -> x1, other arithmetic: 3.86 us -> 0.69 us
    another operation x3 -> x2, local copies, waits for them, and re-layouts: 3.26 us -> 3.25 us
  transfers between devices with their start and end apart: 11 -> 11, of which waited for: 2 -> 2; matrix products, arithmetic and copies ran while one was open for 27% -> 22% of each run, Pallas kernels for 0% -> 0%
where the time goes in v4:
time: 112 us; the launch traced here: 111 us
  starting transfers between devices  36.5 us (33%)
  local copies, waits for them, and re-layouts  28.4 us (25%)
  Pallas kernels  17.1 us (15%)
  waiting for transfers between devices  13.9 us (12%)
  other arithmetic  10.3 us (9%)
  matrix products  3.51 us (3%)
    ppermute x9, starting transfers between devices, send(): return lax.ppermute(value, AXES, pairs_by(fn))  22.5 us
    pallas_call x1, Pallas kernels, leaf_fields(): pl.pallas_call(leaf_kernel, grid_spec=grid_spec, out_shape=[jax.ShapeDtyp...  17.1 us
    all_to_all x1, starting transfers between devices, body(): got = lax.all_to_all(payload, AXES, split_axis=0, concat_axis=0, tiled=True)  8.91 us
    all_to_all x1, waiting for transfers between devices, body(): lax.all_to_all(induced.reshape(owners, capacity, port_count), AXES, split...  8.18 us
    unnamed x14, local copies, waits for them, and re-layouts  7.56 us
    all_to_all x1, waiting for transfers between devices, body(): got = lax.all_to_all(payload, AXES, split_axis=0, concat_axis=0, tiled=True)  5.73 us
    all_to_all x1, starting transfers between devices, body(): lax.all_to_all(induced.reshape(owners, capacity, port_count), AXES, split...  5.04 us
    select_n x3, other arithmetic, join(): jnp.where(left, jnp.concatenate([edge, core], 1), jnp.concatenate([core,...  4.09 us
  transfers between devices with their start and end apart: 11, of which 2 were waited for; matrix products, arithmetic and copies ran while one was open for 22% of the time, Pallas kernels for 0%

profile of v4, /device:TPU:0, one launch (start us, length us, event | category | flops | bytes accessed | tf_op | source)
XLA Modules:
  0.0 110.7 jit_solution(11195006058507786828)
XLA Ops:
  0.6 0.0 copy-start
  0.6 1.6 %copy-done = f32[128,16,256]{2,1,0:T(8,128)S(1)} copy-done((f32[128,16,256]{2,1,0:T(8,128)S(1)}, f32[128,16,256]{2,1,0:T(8,128)}, u32[]{:S(2)}) %copy-start) | copy-done | bytes 2097176
  2.2 1.9 %constant_dynamic-slice_fusion = f32[128,16,145]{2,1,0:T(8,128)} fusion(f32[128,16,256]{2,1,0:T(8,128)S(1)} %copy-done, s32[]{:T(128)S(6)} %select_n.75), kind=kLoop, calls=%fused_computation.84 | loop fusion | bytes 2375684 | tf_op jit(solution)/shard_map/dynamic-slice.1
  4.2 2.0 %copy.39 = f32[128,16,145]{0,2,1:T(8,128)S(1)} copy(f32[128,16,145]{2,1,0:T(8,128)} %constant_dynamic-slice_fusion) | data formatting | bytes 2375680
  6.1 1.2 %fusion.32 = (f32[9,145,128]{2,1,0:T(8,128)}, f32[9,145,128]{2,1,0:T(8,128)}) fusion(f32[16,145,128]{2,1,0:T(8,128)S(1)} %bitcast.30), kind=kLoop, calls=%fused_computation.89 | loop fusion | bytes 2672640 | tf_op jit(solution)/shard_map/slice | solution.py:78
  7.3 1.3 %collective-permute-start.4 = (f32[9,145,128]{2,1,0:T(8,128)}, f32[9,145,128]{2,1,0:T(8,128)}, u32[]{:S(2)}, u32[]{:S(2)}) collective-permute-start(f32[9,145,128]{2,1,0:T(8,128)} %get-tuple-element.15), channel_id=1, source_target_pairs={{4,0},{5,1},{6,2},{7,3},{8,4},{9,5},{10,6},{11,7},{12,8},{13,9},{1... | collective-permute-start | bytes 2004488 | tf_op jit(solution)/shard_map/ppermute | solution.py:58
  8.6 0.0 copy-start.4
  8.6 1.3 %constant_dynamic-slice_fusion.1 = f32[128,16,17]{2,1,0:T(8,128)} fusion(f32[128,16,256]{2,1,0:T(8,128)S(1)} %copy-done, s32[]{:T(128)S(6)} %select_n.74), kind=kLoop, calls=%fused_computation.85 | loop fusion | bytes 278532 | tf_op jit(solution)/shard_map/dynamic-slice
  9.9 1.6 %copy.38 = f32[128,16,17]{0,2,1:T(8,128)S(1)} copy(f32[128,16,17]{2,1,0:T(8,128)} %constant_dynamic-slice_fusion.1) | data formatting | bytes 278528
  11.6 1.3 %collective-permute-start.2 = (f32[16,17,128]{2,1,0:T(8,128)S(1)}, f32[16,17,128]{2,1,0:T(8,128)}, u32[]{:S(2)}, u32[]{:S(2)}) collective-permute-start(f32[16,17,128]{2,1,0:T(8,128)S(1)} %bitcast.44), channel_id=1, source_target_pairs={{1,2},{2,1},{5,6},{6,5},{9,10},{10,9},{13,14},{14,13},{17,18},{18,... | collective-permute-start | bytes 417800 | tf_op jit(solution)/shard_map/ppermute | solution.py:58
  12.9 0.7 fusion.36
  13.6 1.3 %collective-permute-start.3 = (f32[9,17,128]{2,1,0:T(8,128)}, f32[9,17,128]{2,1,0:T(8,128)}, u32[]{:S(2)}, u32[]{:S(2)}) collective-permute-start(f32[9,17,128]{2,1,0:T(8,128)} %get-tuple-element.25), channel_id=1, source_target_pairs={{5,2},{6,1},{9,6},{10,5},{13,10},{14,9},{21,18},{22,17},{25,22},{2... | collective-permute-start | bytes 235016 | tf_op jit(solution)/shard_map/ppermute | solution.py:58
  14.9 6.4 %collective-permute-start.1 = (f32[9,145,128]{2,1,0:T(8,128)}, f32[9,145,128]{2,1,0:T(8,128)}, u32[]{:S(2)}, u32[]{:S(2)}) collective-permute-start(f32[9,145,128]{2,1,0:T(8,128)} %get-tuple-element.14), channel_id=1, source_target_pairs={{0,4},{1,5},{2,6},{3,7},{4,8},{5,9},{6,10},{7,11},{8,12},{9,13},{1... | collective-permute-start | bytes 2004488 | tf_op jit(solution)/shard_map/ppermute | solution.py:58
  21.3 1.3 %collective-permute-start = (f32[9,17,128]{2,1,0:T(8,128)}, f32[9,17,128]{2,1,0:T(8,128)}, u32[]{:S(2)}, u32[]{:S(2)}) collective-permute-start(f32[9,17,128]{2,1,0:T(8,128)} %get-tuple-element.24), channel_id=1, source_target_pairs={{1,6},{2,5},{5,10},{6,9},{9,14},{10,13},{17,22},{18,21},{21,26},{2... | collective-permute-start | bytes 235016 | tf_op jit(solution)/shard_map/ppermute | solution.py:58
  22.6 0.2 convert_reduce_fusion
  22.9 0.5 fusion.3
  23.4 0.1 reshape.116
  23.5 1.0 copy.45
  24.5 1.6 %fusion.6 = bf16[1024,384]{1,0:T(8,128)(2,1)S(1)} fusion(s32[512]{0:T(512)S(1)} %multiply_add_fusion, bf16[512,128]{1,0:T(8,128)(2,1)} %param.10, bf16[512,256]{1,0:T(8,128)(2,1)S(1)} %bitcast.49), kind=kOutput, calls=%fused_computation.14 | convolution fusion | flops 404357120 | bytes 1181696 | tf_op jit(solution)/shard_map/dot_general | solution.py:224
  26.1 0.0 copy-start.1
  26.1 1.0 fusion.14
  27.1 8.9 %all-to-all-start = ((bf16[16,65,384]{2,1,0:T(8,128)(2,1)}), bf16[16,65,384]{2,1,0:T(8,128)(2,1)}, u32[]{:S(2)}, u32[]{:S(2)}) async-start(bf16[16,65,384]{2,1,0:T(8,128)(2,1)} %fusion.14), calls=%async_computation | async-start | bytes 1769472 | tf_op jit(solution)/shard_map/all_to_all | solution.py:233
  36.0 0.6 compare_select_fusion
  36.7 0.1 reshape.92
  36.8 1.4 %reshape.78.codes_ref = s32[128]{0:T(128)} reshape(s32[2,8,8]{2,1,0:T(8,128)} %param.8) | data formatting | bytes 1024 | tf_op jit(solution)/shard_map/reshape | solution.py:254
  38.1 1.3 %reshape.100 = s32[128]{0:T(128)} reshape(s32[2,8,8]{2,1,0:T(8,128)} %get-tuple-element.26) | data formatting | bytes 1024 | tf_op jit(solution)/shard_map/broadcast_in_dim | solution.py:250
  39.5 1.2 %gather_fusion = pred[128]{0:T(512)(128)(4,1)S(1)} fusion(pred[4]{0:T(512)(128)(4,1)S(1)} %or_and_fusion.1, s32[1024]{0:T(1024)S(1)} %pad_clamp_fusion.1), kind=kCustom, calls=%fused_computation | custom fusion | bytes 768 | tf_op jit(solution)/shard_map/gather | solution.py:250
  40.7 0.6 pad_clamp_fusion
  41.3 1.2 %gather_fusion.1 = pred[128]{0:T(512)(128)(4,1)S(1)} fusion(pred[10]{0:T(512)(128)(4,1)S(1)} %or_and_fusion, s32[1024]{0:T(1024)S(1)} %pad_clamp_fusion), kind=kCustom, calls=%fused_computation.1 | custom fusion | bytes 768 | tf_op jit(solution)/shard_map/gather | solution.py:250
  42.6 0.5 and_convert_fusion.scale_ref
  43.1 0.0 collective-permute-done.2
  43.1 1.2 %maximum_select_fusion = f32[16,162,128]{2,1,0:T(8,128)S(1)} fusion(f32[16,145,128]{2,1,0:T(8,128)S(1)} %bitcast.31, f32[16,17,128]{2,1,0:T(8,128)} %collective-permute-done.2, pred[]{:T(512)S(6)} %eq.35), kind=kLoop, calls=%fused_computation.15 | loop fusion | flops 995328 | bytes 2654209 | tf_op jit(solution)/shard_map/jit(_where)/select_n | solution.py:85
  44.3 0.0 collective-permute-done.3
  44.3 1.5 %maximum_select_fusion.2 = f32[9,162,128]{2,1,0:T(8,128)S(1)} fusion(f32[9,145,128]{2,1,0:T(8,128)} %collective-permute-done.4, f32[9,17,128]{2,1,0:T(8,128)} %collective-permute-done.3, pred[]{:T(512)S(6)} %eq.35), kind=kLoop, calls=%fused_computation.30 | loop fusion | flops 559872 | bytes 1492993 | tf_op jit(solution)/shard_map/jit(_where)/select_n | solution.py:85
  45.8 0.0 collective-permute-done
  45.8 1.5 %maximum_select_fusion.1 = f32[9,162,128]{2,1,0:T(8,128)S(1)} fusion(f32[9,145,128]{2,1,0:T(8,128)} %collective-permute-done.1, f32[9,17,128]{2,1,0:T(8,128)} %collective-permute-done, pred[]{:T(512)S(6)} %eq.35), kind=kLoop, calls=%fused_computation.29 | loop fusion | flops 559872 | bytes 1492993 | tf_op jit(solution)/shard_map/jit(_where)/select_n | solution.py:85
  47.2 0.2 pad_maximum_fusion
  47.4 0.7 fusion.1
  48.1 0.2 maximum_bitcast_fusion
  48.4 2.2 %copy.32 = bf16[4,10,2,8,16,128]{5,4,3,2,1,0:T(8,128)(2,1)} copy(bf16[4,10,2,8,16,128]{5,4,1,3,0,2:T(8,128)(2,1)S(1)} %maximum_bitcast_fusion) | data formatting | bytes 5242880 | tf_op jit(solution)/shard_map/transpose | solution.py:24
  50.6 5.7 %all-to-all-done = bf16[16,65,384]{2,1,0:T(8,128)(2,1)} async-done(((bf16[16,65,384]{2,1,0:T(8,128)(2,1)}), bf16[16,65,384]{2,1,0:T(8,128)(2,1)}, u32[]{:S(2)}, u32[]{:S(2)}) %all-to-all-start) | async-done | bytes 798752 | tf_op jit(solution)/shard_map/all_to_all | solution.py:233
  56.4 1.2 %slice.103 = bf16[16,64,384]{2,1,0:T(8,128)(2,1)S(1)} slice(bf16[16,65,384]{2,1,0:T(8,128)(2,1)} %all-to-all-done), slice={[0:16], [0:64], [0:384]} | slice | bytes 1572864 | tf_op jit(solution)/shard_map/slice | solution.py:234
  57.6 0.9 slice_bitcast_fusion
  58.4 0.7 slice.105.cur_ref
  59.2 0.8 fusion.31
  60.0 0.7 reshape.88.row_leaf_ref
  60.6 0.8 slice_convert_fusion
  61.4 1.3 %reshape.115.col_leaf_ref = s32[1024,1]{1,0:T(8,128)} reshape(s32[16,64]{1,0:T(8,128)S(1)} %bitcast.50) | data formatting | bytes 8192 | tf_op jit(solution)/shard_map/convert_element_type | solution.py:235
  62.7 1.0 copy.35.cpl_t_ref
  63.7 17.1 %shard_map.77 = (bf16[16,2,128,128]{3,2,1,0:T(8,128)(2,1)}, bf16[1024,128]{1,0:T(8,128)(2,1)}) custom-call(s32[128]{0:T(128)} %reshape.78.codes_ref, f32[128]{0:T(128)} %and_convert_fusion.scale_ref, bf16[4,10,2,128,128]{4,3,2,1,0:T(8,128)(2,1)} %bitcast.32, bf16[16,8,2,128,128]{4,3,2,1,0:T(8,128)(2,1)} %bitcast.33, s32[1,1024]{1,0:T(1,128)} %reshape.88.row_leaf_ref, ...), custom_call_target="tpu_custom_call" | custom-call | tf_op jit(solution)/shard_map/pallas_call | solution.py:182
  80.8 1.5 %copy.44 = bf16[2,8,2,8,16,128]{5,4,1,3,0,2:T(8,128)(2,1)S(1)} copy(bf16[2,8,2,8,16,128]{5,4,3,2,1,0:T(8,128)(2,1)} %bitcast.43) | data formatting | bytes 2097152 | tf_op jit(solution)/shard_map/reshape;reshape | solution.py:32
  82.3 0.3 fusion.33
  82.6 0.6 fusion.34
  83.2 1.3 %collective-permute-start.6 = (bf16[16,1,128]{2,1,0:T(2,128)(2,1)}, bf16[16,1,128]{2,1,0:T(2,128)(2,1)S(1)}, u32[]{:S(2)}, u32[]{:S(2)}) collective-permute-start(bf16[16,1,128]{2,1,0:T(2,128)(2,1)} %get-tuple-element.21), channel_id=1, source_target_pairs={{1,0},{2,1},{3,2},{5,4},{6,5},{7,6},{9,8},{10,9},{11,10},{13,12},{... | collective-permute-start | bytes 12296 | tf_op jit(solution)/shard_map/ppermute | solution.py:58
  84.5 3.0 %collective-permute-start.5 = (bf16[16,1,128]{2,1,0:T(2,128)(2,1)}, bf16[16,1,128]{2,1,0:T(2,128)(2,1)S(1)}, u32[]{:S(2)}, u32[]{:S(2)}) collective-permute-start(bf16[16,1,128]{2,1,0:T(2,128)(2,1)} %get-tuple-element.20), channel_id=1, source_target_pairs={{0,1},{1,2},{2,3},{4,5},{5,6},{6,7},{8,9},{9,10},{10,11},{12,13},{... | collective-permute-start | bytes 12296 | tf_op jit(solution)/shard_map/ppermute | solution.py:58
  87.5 1.3 %collective-permute-start.8 = (bf16[1,128,128]{2,1,0:T(8,128)(2,1)S(1)}, bf16[1,128,128]{2,1,0:T(8,128)(2,1)S(1)}, u32[]{:S(2)}, u32[]{:S(2)}) collective-permute-start(bf16[1,128,128]{2,1,0:T(8,128)(2,1)S(1)} %get-tuple-element.23), channel_id=1, source_target_pairs={{4,0},{5,1},{6,2},{7,3},{8,4},{9,5},{10,6},{11,7},{12,8},{13,9},{1... | collective-permute-start | bytes 98312 | tf_op jit(solution)/shard_map/ppermute | solution.py:58
  88.8 5.3 %collective-permute-start.7 = (bf16[1,128,128]{2,1,0:T(8,128)(2,1)S(1)}, bf16[1,128,128]{2,1,0:T(8,128)(2,1)S(1)}, u32[]{:S(2)}, u32[]{:S(2)}) collective-permute-start(bf16[1,128,128]{2,1,0:T(8,128)(2,1)S(1)} %get-tuple-element.22), channel_id=1, source_target_pairs={{0,4},{1,5},{2,6},{3,7},{4,8},{5,9},{6,10},{7,11},{8,12},{9,13},{1... | collective-permute-start | bytes 98312 | tf_op jit(solution)/shard_map/ppermute | solution.py:58
  94.2 5.0 %all-to-all-start.1 = ((bf16[16,64,128]{2,1,0:T(8,128)(2,1)}), bf16[16,64,128]{2,1,0:T(8,128)(2,1)S(1)}, u32[]{:S(2)}, u32[]{:S(2)}) async-start(bf16[16,64,128]{2,1,0:T(8,128)(2,1)} %bitcast.16), calls=%async_computation.1 | async-start | bytes 524288 | tf_op jit(solution)/shard_map/all_to_all | solution.py:256
  99.2 0.1 maximum_convert_fusion.1
  99.4 0.1 maximum_convert_fusion
  99.5 0.2 fusion.9
  99.7 1.4 %copy.37 = f32[128,16,128]{2,1,0:T(8,128)} copy(f32[128,16,128]{0,2,1:T(8,128)S(1)} %fusion.9) | data formatting | bytes 2097152
  101.1 8.2 %all-to-all-done.1 = bf16[16,64,128]{2,1,0:T(8,128)(2,1)S(1)} async-done(((bf16[16,64,128]{2,1,0:T(8,128)(2,1)}), bf16[16,64,128]{2,1,0:T(8,128)(2,1)S(1)}, u32[]{:S(2)}, u32[]{:S(2)}) %all-to-all-start.1) | async-done | bytes 262176 | tf_op jit(solution)/shard_map/all_to_all | solution.py:256
  109.3 1.4 %fusion.7 = bf16[512,128]{1,0:T(8,128)(2,1)} fusion(bf16[1024,128]{1,0:T(8,128)(2,1)S(1)} %bitcast.48, s32[512]{0:T(512)S(1)} %copy-done.3), kind=kOutput, calls=%fused_computation.16 | convolution fusion | flops 134807552 | bytes 395264 | tf_op jit(solution)/shard_map/dot_general | solution.py:259
  (20 shorter events, 0.1 us)
Async XLA Ops:
  0.6 1.6 %copy-start = (f32[128,16,256]{2,1,0:T(8,128)S(1)}, f32[128,16,256]{2,1,0:T(8,128)}, u32[]{:S(2)}) copy-start(f32[128,16,256]{2,1,0:T(8,128)} %param.6) | copy-start | bytes 6291460
  7.3 37.0 %collective-permute-start.4 = (f32[9,145,128]{2,1,0:T(8,128)}, f32[9,145,128]{2,1,0:T(8,128)}, u32[]{:S(2)}, u32[]{:S(2)}) collective-permute-start(f32[9,145,128]{2,1,0:T(8,128)} %get-tuple-element.15), channel_id=1, source_target_pairs={{4,0},{5,1},{6,2},{7,3},{8,4},{9,5},{10,6},{11,7},{12,8},{13,9},{1... | collective-permute-start | bytes 2004488 | tf_op jit(solution)/shard_map/ppermute | solution.py:58
  8.6 14.0 %copy-start.4 = (s32[512]{0:T(512)S(1)}, s32[512]{0:T(512)}, u32[]{:S(2)}) copy-start(s32[512]{0:T(512)} %param.9) | copy-start | bytes 6148
  11.6 31.5 %collective-permute-start.2 = (f32[16,17,128]{2,1,0:T(8,128)S(1)}, f32[16,17,128]{2,1,0:T(8,128)}, u32[]{:S(2)}, u32[]{:S(2)}) collective-permute-start(f32[16,17,128]{2,1,0:T(8,128)S(1)} %bitcast.44), channel_id=1, source_target_pairs={{1,2},{2,1},{5,6},{6,5},{9,10},{10,9},{13,14},{14,13},{17,18},{18,... | collective-permute-start | bytes 417800 | tf_op jit(solution)/shard_map/ppermute | solution.py:58
  13.6 30.7 %collective-permute-start.3 = (f32[9,17,128]{2,1,0:T(8,128)}, f32[9,17,128]{2,1,0:T(8,128)}, u32[]{:S(2)}, u32[]{:S(2)}) collective-permute-start(f32[9,17,128]{2,1,0:T(8,128)} %get-tuple-element.25), channel_id=1, source_target_pairs={{5,2},{6,1},{9,6},{10,5},{13,10},{14,9},{21,18},{22,17},{25,22},{2... | collective-permute-start | bytes 235016 | tf_op jit(solution)/shard_map/ppermute | solution.py:58
  14.9 30.9 %collective-permute-start.1 = (f32[9,145,128]{2,1,0:T(8,128)}, f32[9,145,128]{2,1,0:T(8,128)}, u32[]{:S(2)}, u32[]{:S(2)}) collective-permute-start(f32[9,145,128]{2,1,0:T(8,128)} %get-tuple-element.14), channel_id=1, source_target_pairs={{0,4},{1,5},{2,6},{3,7},{4,8},{5,9},{6,10},{7,11},{8,12},{9,13},{1... | collective-permute-start | bytes 2004488 | tf_op jit(solution)/shard_map/ppermute | solution.py:58
  21.3 24.4 %collective-permute-start = (f32[9,17,128]{2,1,0:T(8,128)}, f32[9,17,128]{2,1,0:T(8,128)}, u32[]{:S(2)}, u32[]{:S(2)}) collective-permute-start(f32[9,17,128]{2,1,0:T(8,128)} %get-tuple-element.24), channel_id=1, source_target_pairs={{1,6},{2,5},{5,10},{6,9},{9,14},{10,13},{17,22},{18,21},{21,26},{2... | collective-permute-start | bytes 235016 | tf_op jit(solution)/shard_map/ppermute | solution.py:58
  22.9 1.5 %copy-start.2 = (s32[512]{0:T(512)}, s32[512]{0:T(512)S(1)}, u32[]{:S(2)}) copy-start(s32[512]{0:T(512)S(1)} %multiply_add_fusion) | copy-start | bytes 6148
  26.1 10.0 %copy-start.1 = (s32[2,8,8]{2,1,0:T(8,128)S(1)}, s32[2,8,8]{2,1,0:T(8,128)}, u32[]{:S(2)}) copy-start(s32[2,8,8]{2,1,0:T(8,128)} %param.8) | copy-start | bytes 1540
  27.1 29.3 %all-to-all-start = ((bf16[16,65,384]{2,1,0:T(8,128)(2,1)}), bf16[16,65,384]{2,1,0:T(8,128)(2,1)}, u32[]{:S(2)}, u32[]{:S(2)}) async-start(bf16[16,65,384]{2,1,0:T(8,128)(2,1)} %fusion.14), calls=%async_computation | async-start | bytes 1769472 | tf_op jit(solution)/shard_map/all_to_all | solution.py:233
  83.2 16.0 %collective-permute-start.6 = (bf16[16,1,128]{2,1,0:T(2,128)(2,1)}, bf16[16,1,128]{2,1,0:T(2,128)(2,1)S(1)}, u32[]{:S(2)}, u32[]{:S(2)}) collective-permute-start(bf16[16,1,128]{2,1,0:T(2,128)(2,1)} %get-tuple-element.21), channel_id=1, source_target_pairs={{1,0},{2,1},{3,2},{5,4},{6,5},{7,6},{9,8},{10,9},{11,10},{13,12},{... | collective-permute-start | bytes 12296 | tf_op jit(solution)/shard_map/ppermute | solution.py:58
  84.5 14.7 %collective-permute-start.5 = (bf16[16,1,128]{2,1,0:T(2,128)(2,1)}, bf16[16,1,128]{2,1,0:T(2,128)(2,1)S(1)}, u32[]{:S(2)}, u32[]{:S(2)}) collective-permute-start(bf16[16,1,128]{2,1,0:T(2,128)(2,1)} %get-tuple-element.20), channel_id=1, source_target_pairs={{0,1},{1,2},{2,3},{4,5},{5,6},{6,7},{8,9},{9,10},{10,11},{12,13},{... | collective-permute-start | bytes 12296 | tf_op jit(solution)/shard_map/ppermute | solution.py:58
  87.5 11.8 %collective-permute-start.8 = (bf16[1,128,128]{2,1,0:T(8,128)(2,1)S(1)}, bf16[1,128,128]{2,1,0:T(8,128)(2,1)S(1)}, u32[]{:S(2)}, u32[]{:S(2)}) collective-permute-start(bf16[1,128,128]{2,1,0:T(8,128)(2,1)S(1)} %get-tuple-element.23), channel_id=1, source_target_pairs={{4,0},{5,1},{6,2},{7,3},{8,4},{9,5},{10,6},{11,7},{12,8},{13,9},{1... | collective-permute-start | bytes 98312 | tf_op jit(solution)/shard_map/ppermute | solution.py:58
  88.8 10.5 %collective-permute-start.7 = (bf16[1,128,128]{2,1,0:T(8,128)(2,1)S(1)}, bf16[1,128,128]{2,1,0:T(8,128)(2,1)S(1)}, u32[]{:S(2)}, u32[]{:S(2)}) collective-permute-start(bf16[1,128,128]{2,1,0:T(8,128)(2,1)S(1)} %get-tuple-element.22), channel_id=1, source_target_pairs={{0,4},{1,5},{2,6},{3,7},{4,8},{5,9},{6,10},{7,11},{8,12},{9,13},{1... | collective-permute-start | bytes 98312 | tf_op jit(solution)/shard_map/ppermute | solution.py:58
  94.2 15.1 %all-to-all-start.1 = ((bf16[16,64,128]{2,1,0:T(8,128)(2,1)}), bf16[16,64,128]{2,1,0:T(8,128)(2,1)S(1)}, u32[]{:S(2)}, u32[]{:S(2)}) async-start(bf16[16,64,128]{2,1,0:T(8,128)(2,1)} %bitcast.16), calls=%async_computation.1 | async-start | bytes 524288 | tf_op jit(solution)/shard_map/all_to_all | solution.py:256
  99.7 9.6 %copy-start.3 = (s32[512]{0:T(512)S(1)}, s32[512]{0:T(512)}, u32[]{:S(2)}) copy-start(s32[512]{0:T(512)} %copy-done.2) | copy-start | bytes 6148

commit v5 on v4

--- a/solution.py
+++ b/solution.py
@@ -127,26 +127,24 @@
     coupling_t = jnp.where(row_leaf_ref[...] == leaf, coupling_t, jnp.zeros_like(coupling_t))
     coupling = cpl_ref[...]
     coupling = jnp.where(col_leaf_ref[...] == leaf, coupling, jnp.zeros_like(coupling))
-    current = cur_ref[...]
-    volt = acc_ref[...]
+    filament = jnp.dot(coupling_t, cur_ref[...], preferred_element_type=jnp.float32)
+    sources = []
+    for n in range(near_count):
+        code = codes_ref[leaf * near_count + n]
+        src_row = jnp.minimum(jnp.maximum(row + code // 3, 0), bord_ref.shape[0] - 1)
+        src_col = jnp.minimum(jnp.maximum(col + code % 3, 0), bord_ref.shape[1] - 1)
+        keep = scale_ref[leaf * near_count + n] > 0
+        tile = bord_ref[src_row, src_col]
+        sources.append(jnp.where(keep, tile, jnp.zeros_like(tile)))
     for c in range(components):
-        total = jnp.dot(
-            coupling_t[c * cells : (c + 1) * cells], current, preferred_element_type=jnp.float32
+        weights = jnp.concatenate([ind_ref[0, n, c] for n in range(near_count)], axis=1)
+        stacked = jnp.concatenate([s[c] for s in sources], axis=0)
+        total = filament[c * cells : (c + 1) * cells] + jnp.dot(
+            weights, stacked, preferred_element_type=jnp.float32
         )
-        for n in range(near_count):
-            code = codes_ref[leaf * near_count + n]
-            src_row = jnp.minimum(jnp.maximum(row + code // 3, 0), bord_ref.shape[0] - 1)
-            src_col = jnp.minimum(jnp.maximum(col + code % 3, 0), bord_ref.shape[1] - 1)
-            part = jnp.dot(
-                ind_ref[0, n, c], bord_ref[src_row, src_col, c], preferred_element_type=jnp.float32
-            )
-            total += part * scale_ref[leaf * near_count + n]
         field_ref[0, c] = total.astype(field_ref.dtype)
-        volt += jnp.dot(
-            coupling[:, c * cells : (c + 1) * cells],
-            bord_ref[row + 1, col + 1, c],
-            preferred_element_type=jnp.float32,
-        )
+    own = bord_ref[row + 1, col + 1].reshape(components * cells, -1)
+    volt = acc_ref[...] + jnp.dot(coupling, own, preferred_element_type=jnp.float32)
     acc_ref[...] = volt
 
     @pl.when(leaf == pl.num_programs(0) - 1)

time: 112 us -> 112 us (level)
  no operation moved by 1% of the time
where the time goes in v5:
time: 112 us; the launch traced here: 110 us
  starting transfers between devices  36.5 us (33%)
  local copies, waits for them, and re-layouts  28.4 us (25%)
  Pallas kernels  16.9 us (15%)
  waiting for transfers between devices  13.9 us (12%)
  other arithmetic  10.3 us (9%)
  matrix products  3.5 us (3%)
    ppermute x9, starting transfers between devices, send(): return lax.ppermute(value, AXES, pairs_by(fn))  22.6 us
    pallas_call x1, Pallas kernels, leaf_fields(): pl.pallas_call(leaf_kernel, grid_spec=grid_spec, out_shape=[jax.ShapeDtyp...  16.9 us
    all_to_all x1, starting transfers between devices, body(): got = lax.all_to_all(payload, AXES, split_axis=0, concat_axis=0, tiled=True)  8.91 us
    all_to_all x1, waiting for transfers between devices, body(): lax.all_to_all(induced.reshape(owners, capacity, port_count), AXES, split...  8.18 us
    unnamed x14, local copies, waits for them, and re-layouts  7.56 us
    all_to_all x1, waiting for transfers between devices, body(): got = lax.all_to_all(payload, AXES, split_axis=0, concat_axis=0, tiled=True)  5.73 us
    all_to_all x1, starting transfers between devices, body(): lax.all_to_all(induced.reshape(owners, capacity, port_count), AXES, split...  5 us
    select_n x3, other arithmetic, join(): jnp.where(left, jnp.concatenate([edge, core], 1), jnp.concatenate([core,...  4.09 us
  transfers between devices with their start and end apart: 11, of which 2 were waited for; matrix products, arithmetic and copies ran while one was open for 22% of the time, Pallas kernels for 0%

profile of v5, /device:TPU:0, one launch (start us, length us, event | category | flops | bytes accessed | tf_op | source)
XLA Modules:
  0.0 110.5 jit_solution(15268984571308572224)
XLA Ops:
  0.6 0.0 copy-start
  0.6 1.6 %copy-done = f32[128,16,256]{2,1,0:T(8,128)S(1)} copy-done((f32[128,16,256]{2,1,0:T(8,128)S(1)}, f32[128,16,256]{2,1,0:T(8,128)}, u32[]{:S(2)}) %copy-start) | copy-done | bytes 2097176
  2.2 1.9 %constant_dynamic-slice_fusion = f32[128,16,145]{2,1,0:T(8,128)} fusion(f32[128,16,256]{2,1,0:T(8,128)S(1)} %copy-done, s32[]{:T(128)S(6)} %select_n.75), kind=kLoop, calls=%fused_computation.84 | loop fusion | bytes 2375684 | tf_op jit(solution)/shard_map/dynamic-slice.1
  4.2 2.0 %copy.39 = f32[128,16,145]{0,2,1:T(8,128)S(1)} copy(f32[128,16,145]{2,1,0:T(8,128)} %constant_dynamic-slice_fusion) | data formatting | bytes 2375680
  6.1 1.2 %fusion.32 = (f32[9,145,128]{2,1,0:T(8,128)}, f32[9,145,128]{2,1,0:T(8,128)}) fusion(f32[16,145,128]{2,1,0:T(8,128)S(1)} %bitcast.30), kind=kLoop, calls=%fused_computation.89 | loop fusion | bytes 2672640 | tf_op jit(solution)/shard_map/slice | solution.py:78
  7.3 1.3 %collective-permute-start.4 = (f32[9,145,128]{2,1,0:T(8,128)}, f32[9,145,128]{2,1,0:T(8,128)}, u32[]{:S(2)}, u32[]{:S(2)}) collective-permute-start(f32[9,145,128]{2,1,0:T(8,128)} %get-tuple-element.15), channel_id=1, source_target_pairs={{4,0},{5,1},{6,2},{7,3},{8,4},{9,5},{10,6},{11,7},{12,8},{13,9},{1... | collective-permute-start | bytes 2004488 | tf_op jit(solution)/shard_map/ppermute | solution.py:58
  8.6 0.0 copy-start.4
  8.6 1.3 %constant_dynamic-slice_fusion.1 = f32[128,16,17]{2,1,0:T(8,128)} fusion(f32[128,16,256]{2,1,0:T(8,128)S(1)} %copy-done, s32[]{:T(128)S(6)} %select_n.74), kind=kLoop, calls=%fused_computation.85 | loop fusion | bytes 278532 | tf_op jit(solution)/shard_map/dynamic-slice
  9.9 1.6 %copy.38 = f32[128,16,17]{0,2,1:T(8,128)S(1)} copy(f32[128,16,17]{2,1,0:T(8,128)} %constant_dynamic-slice_fusion.1) | data formatting | bytes 278528
  11.6 1.3 %collective-permute-start.2 = (f32[16,17,128]{2,1,0:T(8,128)S(1)}, f32[16,17,128]{2,1,0:T(8,128)}, u32[]{:S(2)}, u32[]{:S(2)}) collective-permute-start(f32[16,17,128]{2,1,0:T(8,128)S(1)} %bitcast.44), channel_id=1, source_target_pairs={{1,2},{2,1},{5,6},{6,5},{9,10},{10,9},{13,14},{14,13},{17,18},{18,... | collective-permute-start | bytes 417800 | tf_op jit(solution)/shard_map/ppermute | solution.py:58
  12.9 0.7 fusion.36
  13.6 1.3 %collective-permute-start.3 = (f32[9,17,128]{2,1,0:T(8,128)}, f32[9,17,128]{2,1,0:T(8,128)}, u32[]{:S(2)}, u32[]{:S(2)}) collective-permute-start(f32[9,17,128]{2,1,0:T(8,128)} %get-tuple-element.25), channel_id=1, source_target_pairs={{5,2},{6,1},{9,6},{10,5},{13,10},{14,9},{21,18},{22,17},{25,22},{2... | collective-permute-start | bytes 235016 | tf_op jit(solution)/shard_map/ppermute | solution.py:58
  14.9 6.4 %collective-permute-start.1 = (f32[9,145,128]{2,1,0:T(8,128)}, f32[9,145,128]{2,1,0:T(8,128)}, u32[]{:S(2)}, u32[]{:S(2)}) collective-permute-start(f32[9,145,128]{2,1,0:T(8,128)} %get-tuple-element.14), channel_id=1, source_target_pairs={{0,4},{1,5},{2,6},{3,7},{4,8},{5,9},{6,10},{7,11},{8,12},{9,13},{1... | collective-permute-start | bytes 2004488 | tf_op jit(solution)/shard_map/ppermute | solution.py:58
  21.3 1.3 %collective-permute-start = (f32[9,17,128]{2,1,0:T(8,128)}, f32[9,17,128]{2,1,0:T(8,128)}, u32[]{:S(2)}, u32[]{:S(2)}) collective-permute-start(f32[9,17,128]{2,1,0:T(8,128)} %get-tuple-element.24), channel_id=1, source_target_pairs={{1,6},{2,5},{5,10},{6,9},{9,14},{10,13},{17,22},{18,21},{21,26},{2... | collective-permute-start | bytes 235016 | tf_op jit(solution)/shard_map/ppermute | solution.py:58
  22.6 0.2 convert_reduce_fusion
  22.9 0.5 fusion.3
  23.4 0.1 reshape.116
  23.5 1.0 copy.45
  24.5 1.6 %fusion.6 = bf16[1024,384]{1,0:T(8,128)(2,1)S(1)} fusion(s32[512]{0:T(512)S(1)} %multiply_add_fusion, bf16[512,128]{1,0:T(8,128)(2,1)} %param.10, bf16[512,256]{1,0:T(8,128)(2,1)S(1)} %bitcast.49), kind=kOutput, calls=%fused_computation.14 | convolution fusion | flops 404357120 | bytes 1181696 | tf_op jit(solution)/shard_map/dot_general | solution.py:222
  26.1 0.0 copy-start.1
  26.1 1.0 fusion.14
  27.1 8.9 %all-to-all-start = ((bf16[16,65,384]{2,1,0:T(8,128)(2,1)}), bf16[16,65,384]{2,1,0:T(8,128)(2,1)}, u32[]{:S(2)}, u32[]{:S(2)}) async-start(bf16[16,65,384]{2,1,0:T(8,128)(2,1)} %fusion.14), calls=%async_computation | async-start | bytes 1769472 | tf_op jit(solution)/shard_map/all_to_all | solution.py:231
  36.0 0.6 compare_select_fusion
  36.7 0.1 reshape.92
  36.8 1.4 %reshape.78.codes_ref = s32[128]{0:T(128)} reshape(s32[2,8,8]{2,1,0:T(8,128)} %param.8) | data formatting | bytes 1024 | tf_op jit(solution)/shard_map/reshape | solution.py:252
  38.1 1.3 %reshape.100 = s32[128]{0:T(128)} reshape(s32[2,8,8]{2,1,0:T(8,128)} %get-tuple-element.26) | data formatting | bytes 1024 | tf_op jit(solution)/shard_map/broadcast_in_dim | solution.py:248
  39.5 1.2 %gather_fusion = pred[128]{0:T(512)(128)(4,1)S(1)} fusion(pred[4]{0:T(512)(128)(4,1)S(1)} %or_and_fusion.1, s32[1024]{0:T(1024)S(1)} %pad_clamp_fusion.1), kind=kCustom, calls=%fused_computation | custom fusion | bytes 768 | tf_op jit(solution)/shard_map/gather | solution.py:248
  40.7 0.6 pad_clamp_fusion
  41.3 1.2 %gather_fusion.1 = pred[128]{0:T(512)(128)(4,1)S(1)} fusion(pred[10]{0:T(512)(128)(4,1)S(1)} %or_and_fusion, s32[1024]{0:T(1024)S(1)} %pad_clamp_fusion), kind=kCustom, calls=%fused_computation.1 | custom fusion | bytes 768 | tf_op jit(solution)/shard_map/gather | solution.py:248
  42.6 0.5 and_convert_fusion.scale_ref
  43.1 0.0 collective-permute-done.2
  43.1 1.2 %maximum_select_fusion = f32[16,162,128]{2,1,0:T(8,128)S(1)} fusion(f32[16,145,128]{2,1,0:T(8,128)S(1)} %bitcast.31, f32[16,17,128]{2,1,0:T(8,128)} %collective-permute-done.2, pred[]{:T(512)S(6)} %eq.35), kind=kLoop, calls=%fused_computation.15 | loop fusion | flops 995328 | bytes 2654209 | tf_op jit(solution)/shard_map/jit(_where)/select_n | solution.py:85
  44.3 0.0 collective-permute-done.4
  44.3 1.5 %maximum_select_fusion.2 = f32[9,162,128]{2,1,0:T(8,128)S(1)} fusion(f32[9,145,128]{2,1,0:T(8,128)} %collective-permute-done.4, f32[9,17,128]{2,1,0:T(8,128)} %collective-permute-done.3, pred[]{:T(512)S(6)} %eq.35), kind=kLoop, calls=%fused_computation.30 | loop fusion | flops 559872 | bytes 1492993 | tf_op jit(solution)/shard_map/jit(_where)/select_n | solution.py:85
  45.8 0.0 collective-permute-done
  45.8 1.5 %maximum_select_fusion.1 = f32[9,162,128]{2,1,0:T(8,128)S(1)} fusion(f32[9,145,128]{2,1,0:T(8,128)} %collective-permute-done.1, f32[9,17,128]{2,1,0:T(8,128)} %collective-permute-done, pred[]{:T(512)S(6)} %eq.35), kind=kLoop, calls=%fused_computation.29 | loop fusion | flops 559872 | bytes 1492993 | tf_op jit(solution)/shard_map/jit(_where)/select_n | solution.py:85
  47.2 0.2 pad_maximum_fusion
  47.4 0.7 fusion.1
  48.1 0.2 maximum_bitcast_fusion
  48.4 2.2 %copy.32 = bf16[4,10,2,8,16,128]{5,4,3,2,1,0:T(8,128)(2,1)} copy(bf16[4,10,2,8,16,128]{5,4,1,3,0,2:T(8,128)(2,1)S(1)} %maximum_bitcast_fusion) | data formatting | bytes 5242880 | tf_op jit(solution)/shard_map/transpose | solution.py:24
  50.6 5.7 %all-to-all-done = bf16[16,65,384]{2,1,0:T(8,128)(2,1)} async-done(((bf16[16,65,384]{2,1,0:T(8,128)(2,1)}), bf16[16,65,384]{2,1,0:T(8,128)(2,1)}, u32[]{:S(2)}, u32[]{:S(2)}) %all-to-all-start) | async-done | bytes 798752 | tf_op jit(solution)/shard_map/all_to_all | solution.py:231
  56.4 1.2 %slice.103 = bf16[16,64,384]{2,1,0:T(8,128)(2,1)S(1)} slice(bf16[16,65,384]{2,1,0:T(8,128)(2,1)} %all-to-all-done), slice={[0:16], [0:64], [0:384]} | slice | bytes 1572864 | tf_op jit(solution)/shard_map/slice | solution.py:232
  57.6 0.9 slice_bitcast_fusion
  58.4 0.7 slice.105.cur_ref
  59.2 0.8 fusion.31
  60.0 0.7 reshape.88.row_leaf_ref
  60.6 0.8 slice_convert_fusion
  61.4 1.3 %reshape.115.col_leaf_ref = s32[1024,1]{1,0:T(8,128)} reshape(s32[16,64]{1,0:T(8,128)S(1)} %bitcast.50) | data formatting | bytes 8192 | tf_op jit(solution)/shard_map/convert_element_type | solution.py:233
  62.7 1.0 copy.35.cpl_t_ref
  63.7 16.9 %shard_map.77 = (bf16[16,2,128,128]{3,2,1,0:T(8,128)(2,1)}, bf16[1024,128]{1,0:T(8,128)(2,1)}) custom-call(s32[128]{0:T(128)} %reshape.78.codes_ref, f32[128]{0:T(128)} %and_convert_fusion.scale_ref, bf16[4,10,2,128,128]{4,3,2,1,0:T(8,128)(2,1)} %bitcast.32, bf16[16,8,2,128,128]{4,3,2,1,0:T(8,128)(2,1)} %bitcast.33, s32[1,1024]{1,0:T(1,128)} %reshape.88.row_leaf_ref, ...), custom_call_target="tpu_custom_call" | custom-call | tf_op jit(solution)/shard_map/pallas_call | solution.py:180
  80.5 1.5 %copy.44 = bf16[2,8,2,8,16,128]{5,4,1,3,0,2:T(8,128)(2,1)S(1)} copy(bf16[2,8,2,8,16,128]{5,4,3,2,1,0:T(8,128)(2,1)} %bitcast.43) | data formatting | bytes 2097152 | tf_op jit(solution)/shard_map/reshape;reshape | solution.py:32
  82.0 0.3 fusion.33
  82.3 0.6 fusion.34
  83.0 1.3 %collective-permute-start.6 = (bf16[16,1,128]{2,1,0:T(2,128)(2,1)}, bf16[16,1,128]{2,1,0:T(2,128)(2,1)S(1)}, u32[]{:S(2)}, u32[]{:S(2)}) collective-permute-start(bf16[16,1,128]{2,1,0:T(2,128)(2,1)} %get-tuple-element.21), channel_id=1, source_target_pairs={{1,0},{2,1},{3,2},{5,4},{6,5},{7,6},{9,8},{10,9},{11,10},{13,12},{... | collective-permute-start | bytes 12296 | tf_op jit(solution)/shard_map/ppermute | solution.py:58
  84.3 3.0 %collective-permute-start.5 = (bf16[16,1,128]{2,1,0:T(2,128)(2,1)}, bf16[16,1,128]{2,1,0:T(2,128)(2,1)S(1)}, u32[]{:S(2)}, u32[]{:S(2)}) collective-permute-start(bf16[16,1,128]{2,1,0:T(2,128)(2,1)} %get-tuple-element.20), channel_id=1, source_target_pairs={{0,1},{1,2},{2,3},{4,5},{5,6},{6,7},{8,9},{9,10},{10,11},{12,13},{... | collective-permute-start | bytes 12296 | tf_op jit(solution)/shard_map/ppermute | solution.py:58
  87.3 1.3 %collective-permute-start.8 = (bf16[1,128,128]{2,1,0:T(8,128)(2,1)S(1)}, bf16[1,128,128]{2,1,0:T(8,128)(2,1)S(1)}, u32[]{:S(2)}, u32[]{:S(2)}) collective-permute-start(bf16[1,128,128]{2,1,0:T(8,128)(2,1)S(1)} %get-tuple-element.23), channel_id=1, source_target_pairs={{4,0},{5,1},{6,2},{7,3},{8,4},{9,5},{10,6},{11,7},{12,8},{13,9},{1... | collective-permute-start | bytes 98312 | tf_op jit(solution)/shard_map/ppermute | solution.py:58
  88.6 5.4 %collective-permute-start.7 = (bf16[1,128,128]{2,1,0:T(8,128)(2,1)S(1)}, bf16[1,128,128]{2,1,0:T(8,128)(2,1)S(1)}, u32[]{:S(2)}, u32[]{:S(2)}) collective-permute-start(bf16[1,128,128]{2,1,0:T(8,128)(2,1)S(1)} %get-tuple-element.22), channel_id=1, source_target_pairs={{0,4},{1,5},{2,6},{3,7},{4,8},{5,9},{6,10},{7,11},{8,12},{9,13},{1... | collective-permute-start | bytes 98312 | tf_op jit(solution)/shard_map/ppermute | solution.py:58
  94.0 5.0 %all-to-all-start.1 = ((bf16[16,64,128]{2,1,0:T(8,128)(2,1)}), bf16[16,64,128]{2,1,0:T(8,128)(2,1)S(1)}, u32[]{:S(2)}, u32[]{:S(2)}) async-start(bf16[16,64,128]{2,1,0:T(8,128)(2,1)} %bitcast.16), calls=%async_computation.1 | async-start | bytes 524288 | tf_op jit(solution)/shard_map/all_to_all | solution.py:254
  99.0 0.1 maximum_convert_fusion.1
  99.2 0.1 maximum_convert_fusion
  99.3 0.2 fusion.9
  99.5 1.4 %copy.37 = f32[128,16,128]{2,1,0:T(8,128)} copy(f32[128,16,128]{0,2,1:T(8,128)S(1)} %fusion.9) | data formatting | bytes 2097152
  100.8 8.2 %all-to-all-done.1 = bf16[16,64,128]{2,1,0:T(8,128)(2,1)S(1)} async-done(((bf16[16,64,128]{2,1,0:T(8,128)(2,1)}), bf16[16,64,128]{2,1,0:T(8,128)(2,1)S(1)}, u32[]{:S(2)}, u32[]{:S(2)}) %all-to-all-start.1) | async-done | bytes 262176 | tf_op jit(solution)/shard_map/all_to_all | solution.py:254
  109.0 1.4 %fusion.7 = bf16[512,128]{1,0:T(8,128)(2,1)} fusion(bf16[1024,128]{1,0:T(8,128)(2,1)S(1)} %bitcast.48, s32[512]{0:T(512)S(1)} %copy-done.3), kind=kOutput, calls=%fused_computation.16 | convolution fusion | flops 134807552 | bytes 395264 | tf_op jit(solution)/shard_map/dot_general | solution.py:257
  (20 shorter events, 0.1 us)
Async XLA Ops:
  0.6 1.6 %copy-start = (f32[128,16,256]{2,1,0:T(8,128)S(1)}, f32[128,16,256]{2,1,0:T(8,128)}, u32[]{:S(2)}) copy-start(f32[128,16,256]{2,1,0:T(8,128)} %param.6) | copy-start | bytes 6291460
  7.3 37.0 %collective-permute-start.4 = (f32[9,145,128]{2,1,0:T(8,128)}, f32[9,145,128]{2,1,0:T(8,128)}, u32[]{:S(2)}, u32[]{:S(2)}) collective-permute-start(f32[9,145,128]{2,1,0:T(8,128)} %get-tuple-element.15), channel_id=1, source_target_pairs={{4,0},{5,1},{6,2},{7,3},{8,4},{9,5},{10,6},{11,7},{12,8},{13,9},{1... | collective-permute-start | bytes 2004488 | tf_op jit(solution)/shard_map/ppermute | solution.py:58
  8.6 14.0 %copy-start.4 = (s32[512]{0:T(512)S(1)}, s32[512]{0:T(512)}, u32[]{:S(2)}) copy-start(s32[512]{0:T(512)} %param.9) | copy-start | bytes 6148
  11.6 31.5 %collective-permute-start.2 = (f32[16,17,128]{2,1,0:T(8,128)S(1)}, f32[16,17,128]{2,1,0:T(8,128)}, u32[]{:S(2)}, u32[]{:S(2)}) collective-permute-start(f32[16,17,128]{2,1,0:T(8,128)S(1)} %bitcast.44), channel_id=1, source_target_pairs={{1,2},{2,1},{5,6},{6,5},{9,10},{10,9},{13,14},{14,13},{17,18},{18,... | collective-permute-start | bytes 417800 | tf_op jit(solution)/shard_map/ppermute | solution.py:58
  13.6 30.7 %collective-permute-start.3 = (f32[9,17,128]{2,1,0:T(8,128)}, f32[9,17,128]{2,1,0:T(8,128)}, u32[]{:S(2)}, u32[]{:S(2)}) collective-permute-start(f32[9,17,128]{2,1,0:T(8,128)} %get-tuple-element.25), channel_id=1, source_target_pairs={{5,2},{6,1},{9,6},{10,5},{13,10},{14,9},{21,18},{22,17},{25,22},{2... | collective-permute-start | bytes 235016 | tf_op jit(solution)/shard_map/ppermute | solution.py:58
  14.9 30.9 %collective-permute-start.1 = (f32[9,145,128]{2,1,0:T(8,128)}, f32[9,145,128]{2,1,0:T(8,128)}, u32[]{:S(2)}, u32[]{:S(2)}) collective-permute-start(f32[9,145,128]{2,1,0:T(8,128)} %get-tuple-element.14), channel_id=1, source_target_pairs={{0,4},{1,5},{2,6},{3,7},{4,8},{5,9},{6,10},{7,11},{8,12},{9,13},{1... | collective-permute-start | bytes 2004488 | tf_op jit(solution)/shard_map/ppermute | solution.py:58
  21.3 24.4 %collective-permute-start = (f32[9,17,128]{2,1,0:T(8,128)}, f32[9,17,128]{2,1,0:T(8,128)}, u32[]{:S(2)}, u32[]{:S(2)}) collective-permute-start(f32[9,17,128]{2,1,0:T(8,128)} %get-tuple-element.24), channel_id=1, source_target_pairs={{1,6},{2,5},{5,10},{6,9},{9,14},{10,13},{17,22},{18,21},{21,26},{2... | collective-permute-start | bytes 235016 | tf_op jit(solution)/shard_map/ppermute | solution.py:58
  22.9 1.5 %copy-start.2 = (s32[512]{0:T(512)}, s32[512]{0:T(512)S(1)}, u32[]{:S(2)}) copy-start(s32[512]{0:T(512)S(1)} %multiply_add_fusion) | copy-start | bytes 6148
  26.1 10.0 %copy-start.1 = (s32[2,8,8]{2,1,0:T(8,128)S(1)}, s32[2,8,8]{2,1,0:T(8,128)}, u32[]{:S(2)}) copy-start(s32[2,8,8]{2,1,0:T(8,128)} %param.8) | copy-start | bytes 1540
  27.1 29.3 %all-to-all-start = ((bf16[16,65,384]{2,1,0:T(8,128)(2,1)}), bf16[16,65,384]{2,1,0:T(8,128)(2,1)}, u32[]{:S(2)}, u32[]{:S(2)}) async-start(bf16[16,65,384]{2,1,0:T(8,128)(2,1)} %fusion.14), calls=%async_computation | async-start | bytes 1769472 | tf_op jit(solution)/shard_map/all_to_all | solution.py:231
  83.0 16.0 %collective-permute-start.6 = (bf16[16,1,128]{2,1,0:T(2,128)(2,1)}, bf16[16,1,128]{2,1,0:T(2,128)(2,1)S(1)}, u32[]{:S(2)}, u32[]{:S(2)}) collective-permute-start(bf16[16,1,128]{2,1,0:T(2,128)(2,1)} %get-tuple-element.21), channel_id=1, source_target_pairs={{1,0},{2,1},{3,2},{5,4},{6,5},{7,6},{9,8},{10,9},{11,10},{13,12},{... | collective-permute-start | bytes 12296 | tf_op jit(solution)/shard_map/ppermute | solution.py:58
  84.3 14.7 %collective-permute-start.5 = (bf16[16,1,128]{2,1,0:T(2,128)(2,1)}, bf16[16,1,128]{2,1,0:T(2,128)(2,1)S(1)}, u32[]{:S(2)}, u32[]{:S(2)}) collective-permute-start(bf16[16,1,128]{2,1,0:T(2,128)(2,1)} %get-tuple-element.20), channel_id=1, source_target_pairs={{0,1},{1,2},{2,3},{4,5},{5,6},{6,7},{8,9},{9,10},{10,11},{12,13},{... | collective-permute-start | bytes 12296 | tf_op jit(solution)/shard_map/ppermute | solution.py:58
  87.3 11.8 %collective-permute-start.8 = (bf16[1,128,128]{2,1,0:T(8,128)(2,1)S(1)}, bf16[1,128,128]{2,1,0:T(8,128)(2,1)S(1)}, u32[]{:S(2)}, u32[]{:S(2)}) collective-permute-start(bf16[1,128,128]{2,1,0:T(8,128)(2,1)S(1)} %get-tuple-element.23), channel_id=1, source_target_pairs={{4,0},{5,1},{6,2},{7,3},{8,4},{9,5},{10,6},{11,7},{12,8},{13,9},{1... | collective-permute-start | bytes 98312 | tf_op jit(solution)/shard_map/ppermute | solution.py:58
  88.6 10.5 %collective-permute-start.7 = (bf16[1,128,128]{2,1,0:T(8,128)(2,1)S(1)}, bf16[1,128,128]{2,1,0:T(8,128)(2,1)S(1)}, u32[]{:S(2)}, u32[]{:S(2)}) collective-permute-start(bf16[1,128,128]{2,1,0:T(8,128)(2,1)S(1)} %get-tuple-element.22), channel_id=1, source_target_pairs={{0,4},{1,5},{2,6},{3,7},{4,8},{5,9},{6,10},{7,11},{8,12},{9,13},{1... | collective-permute-start | bytes 98312 | tf_op jit(solution)/shard_map/ppermute | solution.py:58
  94.0 15.1 %all-to-all-start.1 = ((bf16[16,64,128]{2,1,0:T(8,128)(2,1)}), bf16[16,64,128]{2,1,0:T(8,128)(2,1)S(1)}, u32[]{:S(2)}, u32[]{:S(2)}) async-start(bf16[16,64,128]{2,1,0:T(8,128)(2,1)} %bitcast.16), calls=%async_computation.1 | async-start | bytes 524288 | tf_op jit(solution)/shard_map/all_to_all | solution.py:254
  99.5 9.6 %copy-start.3 = (s32[512]{0:T(512)S(1)}, s32[512]{0:T(512)}, u32[]{:S(2)}) copy-start(s32[512]{0:T(512)} %copy-done.2) | copy-start | bytes 6148

commit v6 on v4

--- a/solution.py
+++ b/solution.py
@@ -108,50 +108,56 @@
 
 
 def leaf_kernel(
-    codes_ref, scale_ref, bord_ref, ind_ref, row_leaf_ref, col_leaf_ref, cpl_ref, cpl_t_ref,
-    cur_ref, field_ref, volt_ref, acc_ref,
+    codes_ref, scale_ref, bord_hbm, ind_hbm, row_leaf_ref, cpl_t_hbm, cur_hbm,
+    field_ref, volt_ref, bord_ref, ind_ref, cpl_t_ref, cur_ref, acc_ref, sems, ind_sems,
 ):
-    leaf = pl.program_id(0)
+    leaf_count = ind_ref.shape[0]
     leaf_cols = bord_ref.shape[1] - 2
     near_count = ind_ref.shape[1]
-    components = ind_ref.shape[2]
     cells = ind_ref.shape[3]
-    row = leaf // leaf_cols
-    col = leaf % leaf_cols
-
-    @pl.when(leaf == 0)
-    def _():
-        acc_ref[...] = jnp.zeros_like(acc_ref)
-
-    coupling_t = cpl_t_ref[...]
-    coupling_t = jnp.where(row_leaf_ref[...] == leaf, coupling_t, jnp.zeros_like(coupling_t))
-    coupling = cpl_ref[...]
-    coupling = jnp.where(col_leaf_ref[...] == leaf, coupling, jnp.zeros_like(coupling))
-    current = cur_ref[...]
-    volt = acc_ref[...]
-    for c in range(components):
-        total = jnp.dot(
-            coupling_t[c * cells : (c + 1) * cells], current, preferred_element_type=jnp.float32
-        )
+    first = [
+        pltpu.make_async_copy(bord_hbm, bord_ref, sems.at[0]),
+        pltpu.make_async_copy(cpl_t_hbm, cpl_t_ref, sems.at[1]),
+        pltpu.make_async_copy(cur_hbm, cur_ref, sems.at[2]),
+    ]
+    for copy in first:
+        copy.start()
+    for l in range(leaf_count):
+        pltpu.make_async_copy(ind_hbm.at[l], ind_ref.at[l], ind_sems.at[l]).start()
+    acc_ref[...] = jnp.zeros_like(acc_ref)
+    for copy in first:
+        copy.wait()
+
+    def one_leaf(leaf, carry):
+        pltpu.make_async_copy(ind_hbm.at[leaf], ind_ref.at[leaf], ind_sems.at[leaf]).wait()
+        row = leaf // leaf_cols
+        col = leaf % leaf_cols
+        coupling_t = cpl_t_ref[...]
+        coupling_t = jnp.where(row_leaf_ref[...] == leaf, coupling_t, jnp.zeros_like(coupling_t))
+        filament = jnp.dot(coupling_t, cur_ref[...], preferred_element_type=jnp.float32)
+        sources = []
         for n in range(near_count):
             code = codes_ref[leaf * near_count + n]
             src_row = jnp.minimum(jnp.maximum(row + code // 3, 0), bord_ref.shape[0] - 1)
             src_col = jnp.minimum(jnp.maximum(col + code % 3, 0), bord_ref.shape[1] - 1)
-            part = jnp.dot(
-                ind_ref[0, n, c], bord_ref[src_row, src_col, c], preferred_element_type=jnp.float32
+            keep = scale_ref[leaf * near_count + n] > 0
+            tile = bord_ref[src_row, src_col]
+            sources.append(jnp.where(keep, tile, jnp.zeros_like(tile)))
+        for c in range(2):
+            weights = jnp.concatenate([ind_ref[leaf, n, c] for n in range(near_count)], axis=1)
+            stacked = jnp.concatenate([s[c] for s in sources], axis=0)
+            total = filament[c * cells : (c + 1) * cells] + jnp.dot(
+                weights, stacked, preferred_element_type=jnp.float32
             )
-            total += part * scale_ref[leaf * near_count + n]
-        field_ref[0, c] = total.astype(field_ref.dtype)
-        volt += jnp.dot(
-            coupling[:, c * cells : (c + 1) * cells],
-            bord_ref[row + 1, col + 1, c],
-            preferred_element_type=jnp.float32,
+            field_ref[leaf, c] = total.astype(field_ref.dtype)
+        own = bord_ref[row + 1, col + 1].reshape(2 * cells, -1)
+        acc_ref[...] += lax.dot_general(
+            own, coupling_t, (((0,), (0,)), ((), ())), preferred_element_type=jnp.float32
         )
-    acc_ref[...] = volt
-
-    @pl.when(leaf == pl.num_programs(0) - 1)
-    def _():
-        volt_ref[...] = volt.astype(volt_ref.dtype)
+        return carry
+
+    lax.fori_loop(0, leaf_count, one_leaf, 0)
+    volt_ref[...] = acc_ref[...].astype(volt_ref.dtype)
 
 
 def leaf_fields(codes, scales, bordered, kernels, slot_leaf, coupling, current):
@@ -159,35 +165,27 @@
     slot_count, port_count = current.shape
     coupling_t = coupling.T
     row_leaf = slot_leaf.reshape(1, slot_count)
-    col_leaf = slot_leaf.reshape(slot_count, 1)
-    operands = (bordered, kernels, row_leaf, col_leaf, coupling, coupling_t, current)
-
-    def whole(shape):
-        return pl.BlockSpec(shape, lambda l, codes, scales: (0,) * len(shape))
-
-    in_specs = [whole(x.shape) for x in operands]
-    in_specs[1] = pl.BlockSpec(
-        (1, near_count, components, cells, cells), lambda l, codes, scales: (l, 0, 0, 0, 0)
-    )
-    grid_spec = pltpu.PrefetchScalarGridSpec(
-        num_scalar_prefetch=2,
-        grid=(leaf_count,),
-        in_specs=in_specs,
-        out_specs=[
-            pl.BlockSpec((1, components, cells, port_count), lambda l, codes, scales: (l, 0, 0, 0)),
-            whole((slot_count, port_count)),
-        ],
-        scratch_shapes=[pltpu.VMEM((slot_count, port_count), jnp.float32)],
-    )
+    smem = pl.BlockSpec(memory_space=pltpu.SMEM)
+    hbm = pl.BlockSpec(memory_space=pl.ANY)
+    vmem = pl.BlockSpec(memory_space=pltpu.VMEM)
     return pl.pallas_call(
         leaf_kernel,
-        grid_spec=grid_spec,
+        in_specs=[smem, smem, hbm, hbm, vmem, hbm, hbm],
+        out_specs=[vmem, vmem],
         out_shape=[
             jax.ShapeDtypeStruct((leaf_count, components, cells, port_count), jnp.bfloat16),
-            jax.ShapeDtypeStruct((slot_count, port_count), jnp.bfloat16),
+            jax.ShapeDtypeStruct((port_count, slot_count), jnp.bfloat16),
         ],
-        compiler_params=pltpu.CompilerParams(dimension_semantics=("arbitrary",)),
-    )(codes, scales, *operands)
+        scratch_shapes=[
+            pltpu.VMEM(bordered.shape, bordered.dtype),
+            pltpu.VMEM(kernels.shape, kernels.dtype),
+            pltpu.VMEM(coupling_t.shape, coupling_t.dtype),
+            pltpu.VMEM(current.shape, current.dtype),
+            pltpu.VMEM((port_count, slot_count), jnp.float32),
+            pltpu.SemaphoreType.DMA((3,)),
+            pltpu.SemaphoreType.DMA((leaf_count,)),
+        ],
+    )(codes, scales, bordered, kernels, row_leaf, coupling_t, current)
 
 
 def body(stream, inductance, near_lists, filament_leaf, filament_current, filament_coupling):
@@ -254,10 +252,10 @@
         near_lists.reshape(-1), scales, bordered, kernels, got_leaf, got_coupling, got_current
     )
     returned = lax.all_to_all(
-        induced.reshape(owners, capacity, port_count), AXES, split_axis=0, concat_axis=0, tiled=True
-    ).reshape(slot_count, port_count)
+        induced.reshape(port_count, owners, capacity), AXES, split_axis=1, concat_axis=1, tiled=True
+    ).reshape(port_count, slot_count)
     filament_voltage = lax.dot_general(
-        placement, returned, (((0,), (0,)), ((), ())), preferred_element_type=jnp.float32
+        placement, returned, (((0,), (1,)), ((), ())), preferred_element_type=jnp.float32
     ).astype(jnp.bfloat16)
 
     grid_field = from_leaves(total_field.reshape(leaf_rows, leaf_cols, 2, leaf_cells, port_count))

time: 112 us -> 110 us (0.982)
  starting transfers between devices: 36.5 us -> 40 us
  Pallas kernels: 17.1 us -> 13.9 us
  local copies, waits for them, and re-layouts: 28.4 us -> 27.1 us
    pallas_call x1, Pallas kernels: 17.1 us -> 13.9 us  [leaf_fields(): pl.pallas_call(leaf_kernel, in_specs=[smem, smem, hbm, hbm, vmem, hbm, hb...]
    all_to_all x1, starting transfers between devices: 5.04 us -> 7.69 us  [body(): lax.all_to_all(induced.reshape(port_count, owners, capacity), AXES, split...]
    all_to_all x1, starting transfers between devices: 8.91 us -> 11.6 us  [body(): got = lax.all_to_all(payload, AXES, split_axis=0, concat_axis=0, tiled=True)]
    ppermute x9, starting transfers between devices: 22.5 us -> 20.7 us  [send(): return lax.ppermute(value, AXES, pairs_by(fn))]
    convert_element_type x2 -> x1, local copies, waits for them, and re-layouts: 1.94 us -> 0.67 us  [body(): got_leaf = got[:, capacity, :capacity].reshape(slot_count).astype(jnp.int32)]
    unnamed x14 -> x16, local copies, waits for them, and re-layouts: 7.56 us -> 7.56 us
  transfers between devices with their start and end apart: 11 -> 11, of which waited for: 2 -> 2; matrix products, arithmetic and copies ran while one was open for 22% -> 23% of each run, Pallas kernels for 0% -> 0%
where the time goes in v6:
time: 110 us; the launch traced here: 109 us
  starting transfers between devices  40 us (36%)
  local copies, waits for them, and re-layouts  27.1 us (25%)
  waiting for transfers between devices  14 us (13%)
  Pallas kernels  13.9 us (13%)
  other arithmetic  9.55 us (9%)
  matrix products  3.51 us (3%)
    ppermute x9, starting transfers between devices, send(): return lax.ppermute(value, AXES, pairs_by(fn))  20.7 us
    pallas_call x1, Pallas kernels, leaf_fields(): pl.pallas_call(leaf_kernel, in_specs=[smem, smem, hbm, hbm, vmem, hbm, hb...  13.9 us
    all_to_all x1, starting transfers between devices, body(): got = lax.all_to_all(payload, AXES, split_axis=0, concat_axis=0, tiled=True)  11.6 us
    all_to_all x1, waiting for transfers between devices, body(): lax.all_to_all(induced.reshape(port_count, owners, capacity), AXES, split...  8.18 us
    all_to_all x1, starting transfers between devices, body(): lax.all_to_all(induced.reshape(port_count, owners, capacity), AXES, split...  7.69 us
    unnamed x16, local copies, waits for them, and re-layouts  7.56 us
    all_to_all x1, waiting for transfers between devices, body(): got = lax.all_to_all(payload, AXES, split_axis=0, concat_axis=0, tiled=True)  5.76 us
    select_n x3, other arithmetic, join(): jnp.where(left, jnp.concatenate([edge, core], 1), jnp.concatenate([core,...  4.09 us
  transfers between devices with their start and end apart: 11, of which 2 were waited for; matrix products, arithmetic and copies ran while one was open for 23% of the time, Pallas kernels for 0%

profile of v6, /device:TPU:0, one launch (start us, length us, event | category | flops | bytes accessed | tf_op | source)
XLA Modules:
  0.0 109.0 jit_solution(13334756970234777974)
XLA Ops:
  0.6 0.0 copy-start
  0.6 1.6 %copy-done = f32[128,16,256]{2,1,0:T(8,128)S(1)} copy-done((f32[128,16,256]{2,1,0:T(8,128)S(1)}, f32[128,16,256]{2,1,0:T(8,128)}, u32[]{:S(2)}) %copy-start) | copy-done | bytes 2097176
  2.2 1.9 %constant_dynamic-slice_fusion = f32[128,16,145]{2,1,0:T(8,128)} fusion(f32[128,16,256]{2,1,0:T(8,128)S(1)} %copy-done, s32[]{:T(128)S(6)} %select_n.75), kind=kLoop, calls=%fused_computation.86 | loop fusion | bytes 2375684 | tf_op jit(solution)/shard_map/dynamic-slice.1
  4.2 2.0 %copy.30 = f32[128,16,145]{0,2,1:T(8,128)S(1)} copy(f32[128,16,145]{2,1,0:T(8,128)} %constant_dynamic-slice_fusion) | data formatting | bytes 2375680
  6.1 1.2 %fusion.32 = (f32[9,145,128]{2,1,0:T(8,128)}, f32[9,145,128]{2,1,0:T(8,128)}) fusion(f32[16,145,128]{2,1,0:T(8,128)S(1)} %bitcast.29), kind=kLoop, calls=%fused_computation.89 | loop fusion | bytes 2672640 | tf_op jit(solution)/shard_map/slice | solution.py:78
  7.3 5.8 %collective-permute-start.1 = (f32[9,145,128]{2,1,0:T(8,128)}, f32[9,145,128]{2,1,0:T(8,128)}, u32[]{:S(2)}, u32[]{:S(2)}) collective-permute-start(f32[9,145,128]{2,1,0:T(8,128)} %get-tuple-element.12), channel_id=1, source_target_pairs={{0,4},{1,5},{2,6},{3,7},{4,8},{5,9},{6,10},{7,11},{8,12},{9,13},{1... | collective-permute-start | bytes 2004488 | tf_op jit(solution)/shard_map/ppermute | solution.py:58
  13.1 1.3 %constant_dynamic-slice_fusion.1 = f32[128,16,17]{2,1,0:T(8,128)} fusion(f32[128,16,256]{2,1,0:T(8,128)S(1)} %copy-done, s32[]{:T(128)S(6)} %select_n.74), kind=kLoop, calls=%fused_computation.87 | loop fusion | bytes 278532 | tf_op jit(solution)/shard_map/dynamic-slice
  14.4 1.6 %copy.29 = f32[128,16,17]{0,2,1:T(8,128)S(1)} copy(f32[128,16,17]{2,1,0:T(8,128)} %constant_dynamic-slice_fusion.1) | data formatting | bytes 278528
  16.0 1.3 %collective-permute-start.2 = (f32[16,17,128]{2,1,0:T(8,128)S(1)}, f32[16,17,128]{2,1,0:T(8,128)}, u32[]{:S(2)}, u32[]{:S(2)}) collective-permute-start(f32[16,17,128]{2,1,0:T(8,128)S(1)} %bitcast.43), channel_id=1, source_target_pairs={{1,2},{2,1},{5,6},{6,5},{9,10},{10,9},{13,14},{14,13},{17,18},{18,... | collective-permute-start | bytes 417800 | tf_op jit(solution)/shard_map/ppermute | solution.py:58
  17.4 0.7 fusion.36
  18.1 1.3 %collective-permute-start = (f32[9,17,128]{2,1,0:T(8,128)}, f32[9,17,128]{2,1,0:T(8,128)}, u32[]{:S(2)}, u32[]{:S(2)}) collective-permute-start(f32[9,17,128]{2,1,0:T(8,128)} %get-tuple-element.20), channel_id=1, source_target_pairs={{1,6},{2,5},{5,10},{6,9},{9,14},{10,13},{17,22},{18,21},{21,26},{2... | collective-permute-start | bytes 235016 | tf_op jit(solution)/shard_map/ppermute | solution.py:58
  19.4 1.3 %collective-permute-start.4 = (f32[9,145,128]{2,1,0:T(8,128)}, f32[9,145,128]{2,1,0:T(8,128)}, u32[]{:S(2)}, u32[]{:S(2)}) collective-permute-start(f32[9,145,128]{2,1,0:T(8,128)} %get-tuple-element.13), channel_id=1, source_target_pairs={{4,0},{5,1},{6,2},{7,3},{8,4},{9,5},{10,6},{11,7},{12,8},{13,9},{1... | collective-permute-start | bytes 2004488 | tf_op jit(solution)/shard_map/ppermute | solution.py:58
  20.7 1.3 %collective-permute-start.3 = (f32[9,17,128]{2,1,0:T(8,128)}, f32[9,17,128]{2,1,0:T(8,128)}, u32[]{:S(2)}, u32[]{:S(2)}) collective-permute-start(f32[9,17,128]{2,1,0:T(8,128)} %get-tuple-element.21), channel_id=1, source_target_pairs={{5,2},{6,1},{9,6},{10,5},{13,10},{14,9},{21,18},{22,17},{25,22},{2... | collective-permute-start | bytes 235016 | tf_op jit(solution)/shard_map/ppermute | solution.py:58
  22.0 0.2 convert_reduce_fusion
  22.3 0.5 fusion.3
  22.8 0.1 reshape.101
  22.8 1.0 copy.36
  23.8 1.6 %fusion.6 = bf16[1024,384]{1,0:T(8,128)(2,1)S(1)} fusion(s32[512]{0:T(512)S(1)} %multiply_add_fusion, bf16[512,128]{1,0:T(8,128)(2,1)} %param.10, bf16[512,256]{1,0:T(8,128)(2,1)S(1)} %bitcast.48), kind=kOutput, calls=%fused_computation.14 | convolution fusion | flops 404357120 | bytes 1181696 | tf_op jit(solution)/shard_map/dot_general | solution.py:222
  25.5 0.0 copy-start.2
  25.5 1.0 fusion.14
  26.5 11.6 %all-to-all-start = ((bf16[16,65,384]{2,1,0:T(8,128)(2,1)}), bf16[16,65,384]{2,1,0:T(8,128)(2,1)}, u32[]{:S(2)}, u32[]{:S(2)}) async-start(bf16[16,65,384]{2,1,0:T(8,128)(2,1)} %fusion.14), calls=%async_computation | async-start | bytes 1769472 | tf_op jit(solution)/shard_map/all_to_all | solution.py:231
  38.1 0.6 compare_select_fusion
  38.7 0.1 reshape.86
  38.8 1.3 %reshape.65.codes_ref = s32[128]{0:T(128)} reshape(s32[2,8,8]{2,1,0:T(8,128)} %param.8) | data formatting | bytes 1024 | tf_op jit(solution)/shard_map/reshape | solution.py:252
  40.1 1.3 %reshape.78 = s32[128]{0:T(128)} reshape(s32[2,8,8]{2,1,0:T(8,128)} %get-tuple-element.23) | data formatting | bytes 1024 | tf_op jit(solution)/shard_map/broadcast_in_dim | solution.py:248
  41.4 1.2 %gather_fusion.1 = pred[128]{0:T(512)(128)(4,1)S(1)} fusion(pred[10]{0:T(512)(128)(4,1)S(1)} %or_and_fusion, s32[1024]{0:T(1024)S(1)} %pad_clamp_fusion), kind=kCustom, calls=%fused_computation.1 | custom fusion | bytes 768 | tf_op jit(solution)/shard_map/gather | solution.py:248
  42.6 0.6 pad_clamp_fusion.1
  43.3 1.2 %gather_fusion = pred[128]{0:T(512)(128)(4,1)S(1)} fusion(pred[4]{0:T(512)(128)(4,1)S(1)} %or_and_fusion.1, s32[1024]{0:T(1024)S(1)} %pad_clamp_fusion.1), kind=kCustom, calls=%fused_computation | custom fusion | bytes 768 | tf_op jit(solution)/shard_map/gather | solution.py:248
  44.5 0.6 and_convert_fusion.scale_ref
  45.1 0.0 collective-permute-done.2
  45.1 1.2 %maximum_select_fusion = f32[16,162,128]{2,1,0:T(8,128)S(1)} fusion(f32[16,145,128]{2,1,0:T(8,128)S(1)} %bitcast.30, f32[16,17,128]{2,1,0:T(8,128)} %collective-permute-done.2, pred[]{:T(512)S(6)} %eq.35), kind=kLoop, calls=%fused_computation.15 | loop fusion | flops 995328 | bytes 2654209 | tf_op jit(solution)/shard_map/jit(_where)/select_n | solution.py:85
  46.3 0.0 collective-permute-done
  46.3 0.0 collective-permute-done.1
  46.3 1.5 %maximum_select_fusion.1 = f32[9,162,128]{2,1,0:T(8,128)S(1)} fusion(f32[9,145,128]{2,1,0:T(8,128)} %collective-permute-done.1, f32[9,17,128]{2,1,0:T(8,128)} %collective-permute-done, pred[]{:T(512)S(6)} %eq.35), kind=kLoop, calls=%fused_computation.29 | loop fusion | flops 559872 | bytes 1492993 | tf_op jit(solution)/shard_map/jit(_where)/select_n | solution.py:85
  47.7 0.0 collective-permute-done.3
  47.8 1.5 %maximum_select_fusion.2 = f32[9,162,128]{2,1,0:T(8,128)S(1)} fusion(f32[9,145,128]{2,1,0:T(8,128)} %collective-permute-done.4, f32[9,17,128]{2,1,0:T(8,128)} %collective-permute-done.3, pred[]{:T(512)S(6)} %eq.35), kind=kLoop, calls=%fused_computation.30 | loop fusion | flops 559872 | bytes 1492993 | tf_op jit(solution)/shard_map/jit(_where)/select_n | solution.py:85
  49.2 0.2 pad_maximum_fusion
  49.4 0.7 fusion.1
  50.1 0.2 maximum_bitcast_fusion
  50.4 2.2 %copy.23 = bf16[4,10,2,8,16,128]{5,4,3,2,1,0:T(8,128)(2,1)} copy(bf16[4,10,2,8,16,128]{5,4,1,3,0,2:T(8,128)(2,1)S(1)} %maximum_bitcast_fusion) | data formatting | bytes 5242880 | tf_op jit(solution)/shard_map/transpose | solution.py:24
  52.6 5.8 %all-to-all-done = bf16[16,65,384]{2,1,0:T(8,128)(2,1)} async-done(((bf16[16,65,384]{2,1,0:T(8,128)(2,1)}), bf16[16,65,384]{2,1,0:T(8,128)(2,1)}, u32[]{:S(2)}, u32[]{:S(2)}) %all-to-all-start) | async-done | bytes 798752 | tf_op jit(solution)/shard_map/all_to_all | solution.py:231
  58.4 1.2 %slice.103 = bf16[16,64,384]{2,1,0:T(8,128)(2,1)S(1)} slice(bf16[16,65,384]{2,1,0:T(8,128)(2,1)} %all-to-all-done), slice={[0:16], [0:64], [0:384]} | slice | bytes 1572864 | tf_op jit(solution)/shard_map/slice | solution.py:232
  59.7 0.7 slice.105.cur_hbm
  60.4 1.0 copy.25.cpl_t_hbm
  61.4 0.8 fusion.20
  62.2 0.7 reshape.75.row_leaf_ref
  62.8 13.9 %shard_map.77 = (bf16[16,2,128,128]{3,2,1,0:T(8,128)(2,1)}, bf16[128,1024]{1,0:T(8,128)(2,1)}) custom-call(s32[128]{0:T(128)} %reshape.65.codes_ref, f32[128]{0:T(128)} %and_convert_fusion.scale_ref, bf16[4,10,2,128,128]{4,3,2,1,0:T(8,128)(2,1)} %bitcast.31, bf16[16,8,2,128,128]{4,3,2,1,0:T(8,128)(2,1)} %bitcast.32, s32[1,1024]{1,0:T(1,128)} %reshape.75.row_leaf_ref, ...), custom_call_target="tpu_custom_call" | custom-call | tf_op jit(solution)/shard_map/pallas_call | solution.py:171
  76.8 1.5 %copy.35 = bf16[2,8,2,8,16,128]{5,4,1,3,0,2:T(8,128)(2,1)S(1)} copy(bf16[2,8,2,8,16,128]{5,4,3,2,1,0:T(8,128)(2,1)} %bitcast.42) | data formatting | bytes 2097152 | tf_op jit(solution)/shard_map/reshape;reshape | solution.py:32
  78.3 0.3 fusion.33
  78.6 0.6 fusion.34
  79.2 2.3 %collective-permute-start.5 = (bf16[16,1,128]{2,1,0:T(2,128)(2,1)}, bf16[16,1,128]{2,1,0:T(2,128)(2,1)S(1)}, u32[]{:S(2)}, u32[]{:S(2)}) collective-permute-start(bf16[16,1,128]{2,1,0:T(2,128)(2,1)} %get-tuple-element.16), channel_id=1, source_target_pairs={{0,1},{1,2},{2,3},{4,5},{5,6},{6,7},{8,9},{9,10},{10,11},{12,13},{... | collective-permute-start | bytes 12296 | tf_op jit(solution)/shard_map/ppermute | solution.py:58
  81.5 1.3 %collective-permute-start.6 = (bf16[16,1,128]{2,1,0:T(2,128)(2,1)}, bf16[16,1,128]{2,1,0:T(2,128)(2,1)S(1)}, u32[]{:S(2)}, u32[]{:S(2)}) collective-permute-start(bf16[16,1,128]{2,1,0:T(2,128)(2,1)} %get-tuple-element.17), channel_id=1, source_target_pairs={{1,0},{2,1},{3,2},{5,4},{6,5},{7,6},{9,8},{10,9},{11,10},{13,12},{... | collective-permute-start | bytes 12296 | tf_op jit(solution)/shard_map/ppermute | solution.py:58
  82.8 4.8 %collective-permute-start.7 = (bf16[1,128,128]{2,1,0:T(8,128)(2,1)S(1)}, bf16[1,128,128]{2,1,0:T(8,128)(2,1)S(1)}, u32[]{:S(2)}, u32[]{:S(2)}) collective-permute-start(bf16[1,128,128]{2,1,0:T(8,128)(2,1)S(1)} %get-tuple-element.18), channel_id=1, source_target_pairs={{0,4},{1,5},{2,6},{3,7},{4,8},{5,9},{6,10},{7,11},{8,12},{9,13},{1... | collective-permute-start | bytes 98312 | tf_op jit(solution)/shard_map/ppermute | solution.py:58
  87.7 1.3 %collective-permute-start.8 = (bf16[1,128,128]{2,1,0:T(8,128)(2,1)S(1)}, bf16[1,128,128]{2,1,0:T(8,128)(2,1)S(1)}, u32[]{:S(2)}, u32[]{:S(2)}) collective-permute-start(bf16[1,128,128]{2,1,0:T(8,128)(2,1)S(1)} %get-tuple-element.19), channel_id=1, source_target_pairs={{4,0},{5,1},{6,2},{7,3},{8,4},{9,5},{10,6},{11,7},{12,8},{13,9},{1... | collective-permute-start | bytes 98312 | tf_op jit(solution)/shard_map/ppermute | solution.py:58
  89.0 0.8 copy.27
  89.8 7.7 %all-to-all-start.1 = ((bf16[128,16,64]{0,2,1:T(8,128)(2,1)}), bf16[128,16,64]{0,2,1:T(8,128)(2,1)S(1)}, u32[]{:S(2)}, u32[]{:S(2)}) async-start(bf16[128,16,64]{0,2,1:T(8,128)(2,1)} %bitcast.16), calls=%async_computation.1 | async-start | bytes 524288 | tf_op jit(solution)/shard_map/all_to_all | solution.py:254
  97.5 0.0 collective-permute-done.5
  97.5 0.0 collective-permute-done.6
  97.6 0.1 maximum_convert_fusion.1
  97.7 0.1 maximum_convert_fusion
  97.8 0.2 fusion.9
  98.0 1.4 %copy.28 = f32[128,16,128]{2,1,0:T(8,128)} copy(f32[128,16,128]{0,2,1:T(8,128)S(1)} %fusion.9) | data formatting | bytes 2097152
  99.4 8.2 %all-to-all-done.1 = bf16[128,16,64]{0,2,1:T(8,128)(2,1)S(1)} async-done(((bf16[128,16,64]{0,2,1:T(8,128)(2,1)}), bf16[128,16,64]{0,2,1:T(8,128)(2,1)S(1)}, u32[]{:S(2)}, u32[]{:S(2)}) %all-to-all-start.1) | async-done | bytes 262176 | tf_op jit(solution)/shard_map/all_to_all | solution.py:254
  107.6 1.4 %fusion.7 = bf16[512,128]{1,0:T(8,128)(2,1)} fusion(bf16[128,1024]{0,1:T(8,128)(2,1)S(1)} %bitcast.47, s32[512]{0:T(512)S(1)} %copy-done.4), kind=kOutput, calls=%fused_computation.16 | convolution fusion | flops 134807552 | bytes 395264 | tf_op jit(solution)/shard_map/dot_general | solution.py:257
  (21 shorter events, 0.1 us)
Async XLA Ops:
  0.6 1.6 %copy-start = (f32[128,16,256]{2,1,0:T(8,128)S(1)}, f32[128,16,256]{2,1,0:T(8,128)}, u32[]{:S(2)}) copy-start(f32[128,16,256]{2,1,0:T(8,128)} %param.6) | copy-start | bytes 6291460
  7.3 39.0 %collective-permute-start.1 = (f32[9,145,128]{2,1,0:T(8,128)}, f32[9,145,128]{2,1,0:T(8,128)}, u32[]{:S(2)}, u32[]{:S(2)}) collective-permute-start(f32[9,145,128]{2,1,0:T(8,128)} %get-tuple-element.12), channel_id=1, source_target_pairs={{0,4},{1,5},{2,6},{3,7},{4,8},{5,9},{6,10},{7,11},{8,12},{9,13},{1... | collective-permute-start | bytes 2004488 | tf_op jit(solution)/shard_map/ppermute | solution.py:58
  13.1 8.9 %copy-start.5 = (s32[512]{0:T(512)S(1)}, s32[512]{0:T(512)}, u32[]{:S(2)}) copy-start(s32[512]{0:T(512)} %param.9) | copy-start | bytes 6148
  16.0 29.0 %collective-permute-start.2 = (f32[16,17,128]{2,1,0:T(8,128)S(1)}, f32[16,17,128]{2,1,0:T(8,128)}, u32[]{:S(2)}, u32[]{:S(2)}) collective-permute-start(f32[16,17,128]{2,1,0:T(8,128)S(1)} %bitcast.43), channel_id=1, source_target_pairs={{1,2},{2,1},{5,6},{6,5},{9,10},{10,9},{13,14},{14,13},{17,18},{18,... | collective-permute-start | bytes 417800 | tf_op jit(solution)/shard_map/ppermute | solution.py:58
  18.1 28.2 %collective-permute-start = (f32[9,17,128]{2,1,0:T(8,128)}, f32[9,17,128]{2,1,0:T(8,128)}, u32[]{:S(2)}, u32[]{:S(2)}) collective-permute-start(f32[9,17,128]{2,1,0:T(8,128)} %get-tuple-element.20), channel_id=1, source_target_pairs={{1,6},{2,5},{5,10},{6,9},{9,14},{10,13},{17,22},{18,21},{21,26},{2... | collective-permute-start | bytes 235016 | tf_op jit(solution)/shard_map/ppermute | solution.py:58
  19.4 28.4 %collective-permute-start.4 = (f32[9,145,128]{2,1,0:T(8,128)}, f32[9,145,128]{2,1,0:T(8,128)}, u32[]{:S(2)}, u32[]{:S(2)}) collective-permute-start(f32[9,145,128]{2,1,0:T(8,128)} %get-tuple-element.13), channel_id=1, source_target_pairs={{4,0},{5,1},{6,2},{7,3},{8,4},{9,5},{10,6},{11,7},{12,8},{13,9},{1... | collective-permute-start | bytes 2004488 | tf_op jit(solution)/shard_map/ppermute | solution.py:58
  20.7 27.1 %collective-permute-start.3 = (f32[9,17,128]{2,1,0:T(8,128)}, f32[9,17,128]{2,1,0:T(8,128)}, u32[]{:S(2)}, u32[]{:S(2)}) collective-permute-start(f32[9,17,128]{2,1,0:T(8,128)} %get-tuple-element.21), channel_id=1, source_target_pairs={{5,2},{6,1},{9,6},{10,5},{13,10},{14,9},{21,18},{22,17},{25,22},{2... | collective-permute-start | bytes 235016 | tf_op jit(solution)/shard_map/ppermute | solution.py:58
  22.3 1.6 %copy-start.3 = (s32[512]{0:T(512)}, s32[512]{0:T(512)S(1)}, u32[]{:S(2)}) copy-start(s32[512]{0:T(512)S(1)} %multiply_add_fusion) | copy-start | bytes 6148
  25.5 12.6 %copy-start.2 = (s32[2,8,8]{2,1,0:T(8,128)S(1)}, s32[2,8,8]{2,1,0:T(8,128)}, u32[]{:S(2)}) copy-start(s32[2,8,8]{2,1,0:T(8,128)} %param.8) | copy-start | bytes 1540
  26.5 31.9 %all-to-all-start = ((bf16[16,65,384]{2,1,0:T(8,128)(2,1)}), bf16[16,65,384]{2,1,0:T(8,128)(2,1)}, u32[]{:S(2)}, u32[]{:S(2)}) async-start(bf16[16,65,384]{2,1,0:T(8,128)(2,1)} %fusion.14), calls=%async_computation | async-start | bytes 1769472 | tf_op jit(solution)/shard_map/all_to_all | solution.py:231
  76.8 12.2 %copy-start.1 = (bf16[128,1024]{1,0:T(8,128)(2,1)S(1)}, bf16[128,1024]{1,0:T(8,128)(2,1)}, u32[]{:S(2)}) copy-start(bf16[128,1024]{1,0:T(8,128)(2,1)} %get-tuple-element.5) | copy-start | bytes 786436
  79.2 18.3 %collective-permute-start.5 = (bf16[16,1,128]{2,1,0:T(2,128)(2,1)}, bf16[16,1,128]{2,1,0:T(2,128)(2,1)S(1)}, u32[]{:S(2)}, u32[]{:S(2)}) collective-permute-start(bf16[16,1,128]{2,1,0:T(2,128)(2,1)} %get-tuple-element.16), channel_id=1, source_target_pairs={{0,1},{1,2},{2,3},{4,5},{5,6},{6,7},{8,9},{9,10},{10,11},{12,13},{... | collective-permute-start | bytes 12296 | tf_op jit(solution)/shard_map/ppermute | solution.py:58
  81.5 16.0 %collective-permute-start.6 = (bf16[16,1,128]{2,1,0:T(2,128)(2,1)}, bf16[16,1,128]{2,1,0:T(2,128)(2,1)S(1)}, u32[]{:S(2)}, u32[]{:S(2)}) collective-permute-start(bf16[16,1,128]{2,1,0:T(2,128)(2,1)} %get-tuple-element.17), channel_id=1, source_target_pairs={{1,0},{2,1},{3,2},{5,4},{6,5},{7,6},{9,8},{10,9},{11,10},{13,12},{... | collective-permute-start | bytes 12296 | tf_op jit(solution)/shard_map/ppermute | solution.py:58
  82.8 14.9 %collective-permute-start.7 = (bf16[1,128,128]{2,1,0:T(8,128)(2,1)S(1)}, bf16[1,128,128]{2,1,0:T(8,128)(2,1)S(1)}, u32[]{:S(2)}, u32[]{:S(2)}) collective-permute-start(bf16[1,128,128]{2,1,0:T(8,128)(2,1)S(1)} %get-tuple-element.18), channel_id=1, source_target_pairs={{0,4},{1,5},{2,6},{3,7},{4,8},{5,9},{6,10},{7,11},{8,12},{9,13},{1... | collective-permute-start | bytes 98312 | tf_op jit(solution)/shard_map/ppermute | solution.py:58
  87.7 10.0 %collective-permute-start.8 = (bf16[1,128,128]{2,1,0:T(8,128)(2,1)S(1)}, bf16[1,128,128]{2,1,0:T(8,128)(2,1)S(1)}, u32[]{:S(2)}, u32[]{:S(2)}) collective-permute-start(bf16[1,128,128]{2,1,0:T(8,128)(2,1)S(1)} %get-tuple-element.19), channel_id=1, source_target_pairs={{4,0},{5,1},{6,2},{7,3},{8,4},{9,5},{10,6},{11,7},{12,8},{13,9},{1... | collective-permute-start | bytes 98312 | tf_op jit(solution)/shard_map/ppermute | solution.py:58
  89.8 17.7 %all-to-all-start.1 = ((bf16[128,16,64]{0,2,1:T(8,128)(2,1)}), bf16[128,16,64]{0,2,1:T(8,128)(2,1)S(1)}, u32[]{:S(2)}, u32[]{:S(2)}) async-start(bf16[128,16,64]{0,2,1:T(8,128)(2,1)} %bitcast.16), calls=%async_computation.1 | async-start | bytes 524288 | tf_op jit(solution)/shard_map/all_to_all | solution.py:254
  98.0 9.6 %copy-start.4 = (s32[512]{0:T(512)S(1)}, s32[512]{0:T(512)}, u32[]{:S(2)}) copy-start(s32[512]{0:T(512)} %copy-done.3) | copy-start | bytes 6148

commit v7 on v6

--- a/solution.py
+++ b/solution.py
@@ -79,12 +79,11 @@
     v_bot = send(mid[:hr], lambda x, y, z: (x - 1, y, z))
     d_top = send(side[rows - hr :], lambda x, y, z: sideways(x, y, z, 1))
     d_bot = send(side[:hr], lambda x, y, z: sideways(x, y, z, -1))
-    left = gz == 0
-
-    def join(core, edge):
-        return jnp.where(left, jnp.concatenate([edge, core], 1), jnp.concatenate([core, edge], 1))
-
-    return jnp.concatenate([join(v_top, d_top), join(mid, h_got), join(v_bot, d_bot)], 0)
+
+    core = jnp.concatenate([v_top, mid, v_bot], 0)
+    edge = jnp.concatenate([d_top, h_got, d_bot], 0)
+    both = jnp.concatenate([edge, core, edge], 1)
+    return lax.dynamic_slice_in_dim(both, gz * hc, mid_w + hc, 1)
 
 
 def field_halo(grid_field):
@@ -137,10 +136,10 @@
         filament = jnp.dot(coupling_t, cur_ref[...], preferred_element_type=jnp.float32)
         sources = []
         for n in range(near_count):
-            code = codes_ref[leaf * near_count + n]
+            code = codes_ref[leaf, n]
             src_row = jnp.minimum(jnp.maximum(row + code // 3, 0), bord_ref.shape[0] - 1)
             src_col = jnp.minimum(jnp.maximum(col + code % 3, 0), bord_ref.shape[1] - 1)
-            keep = scale_ref[leaf * near_count + n] > 0
+            keep = scale_ref[leaf, n] > 0
             tile = bord_ref[src_row, src_col]
             sources.append(jnp.where(keep, tile, jnp.zeros_like(tile)))
         for c in range(2):
@@ -157,7 +156,7 @@
         return carry
 
     lax.fori_loop(0, leaf_count, one_leaf, 0)
-    volt_ref[...] = acc_ref[...].astype(volt_ref.dtype)
+    volt_ref[...] = acc_ref[...].T.astype(volt_ref.dtype)
 
 
 def leaf_fields(codes, scales, bordered, kernels, slot_leaf, coupling, current):
@@ -174,7 +173,7 @@
         out_specs=[vmem, vmem],
         out_shape=[
             jax.ShapeDtypeStruct((leaf_count, components, cells, port_count), jnp.bfloat16),
-            jax.ShapeDtypeStruct((port_count, slot_count), jnp.bfloat16),
+            jax.ShapeDtypeStruct((slot_count, port_count), jnp.bfloat16),
         ],
         scratch_shapes=[
             pltpu.VMEM(bordered.shape, bordered.dtype),
@@ -237,25 +236,24 @@
     window = stream_window(stream.transpose(1, 2, 0), half_cols)
     currents = plane_curl(window).astype(jnp.bfloat16)
     bordered = to_leaves(currents)
-    ring_rows = jnp.arange(leaf_rows + 2, dtype=jnp.int32)
-    ring_cols = jnp.arange(leaf_cols + 2, dtype=jnp.int32)
-    row_ok = ((ring_rows > 0) | (gx > 0)) & ((ring_rows < leaf_rows + 1) | (gx < nx - 1))
-    col_ok = ((ring_cols > 0) | (col_index > 0)) & (
-        (ring_cols < leaf_cols + 1) | (col_index < ny * nz - 1)
-    )
     src_row = jnp.arange(leaf_rows, dtype=jnp.int32)[:, None, None] + near_lists // 3
     src_col = jnp.arange(leaf_cols, dtype=jnp.int32)[None, :, None] + near_lists % 3
-    scales = (row_ok[src_row] & col_ok[src_col]).astype(jnp.float32).reshape(-1)
+    row_ok = ((src_row > 0) | (gx > 0)) & ((src_row < leaf_rows + 1) | (gx < nx - 1))
+    col_ok = ((src_col > 0) | (col_index > 0)) & (
+        (src_col < leaf_cols + 1) | (col_index < ny * nz - 1)
+    )
+    scales = (row_ok & col_ok).astype(jnp.int32).reshape(leaf_count, near_count)
 
     kernels = inductance.reshape(leaf_count, near_count, 2, leaf_cells, leaf_cells)
+    codes = near_lists.reshape(leaf_count, near_count)
     total_field, induced = leaf_fields(
-        near_lists.reshape(-1), scales, bordered, kernels, got_leaf, got_coupling, got_current
+        codes, scales, bordered, kernels, got_leaf, got_coupling, got_current
     )
     returned = lax.all_to_all(
-        induced.reshape(port_count, owners, capacity), AXES, split_axis=1, concat_axis=1, tiled=True
-    ).reshape(port_count, slot_count)
+        induced.reshape(owners, capacity, port_count), AXES, split_axis=0, concat_axis=0, tiled=True
+    ).reshape(slot_count, port_count)
     filament_voltage = lax.dot_general(
-        placement, returned, (((0,), (1,)), ((), ())), preferred_element_type=jnp.float32
+        placement, returned, (((0,), (0,)), ((), ())), preferred_element_type=jnp.float32
     ).astype(jnp.bfloat16)
 
     grid_field = from_leaves(total_field.reshape(leaf_rows, leaf_cols, 2, leaf_cells, port_count))

time: 110 us -> 107 us (0.973)
  local copies, waits for them, and re-layouts: 27.1 us -> 21.1 us
  waiting for transfers between devices: 14 us -> 16.9 us
  starting transfers between devices: 40 us -> 42.8 us
  other arithmetic: 9.55 us -> 7.63 us
    ppermute x9, starting transfers between devices: 20.7 us -> 29.2 us  [send(): return lax.ppermute(value, AXES, pairs_by(fn))]
    select_n x4 -> x0, other arithmetic: 4.71 us -> none  [the longest x3 4.09 us: join(): jnp.where(left, jnp.concatenate([edge, core], 1), jnp.concatenate([core,...]
    all_to_all x1, starting transfers between devices: 11.6 us -> 7.15 us  [body(): got = lax.all_to_all(payload, AXES, split_axis=0, concat_axis=0, tiled=True)]
    ppermute x9, waiting for transfers between devices: 0.02 us -> 4.03 us  [send(): return lax.ppermute(value, AXES, pairs_by(fn))]
    concatenate x1, other arithmetic: 0.2 us -> 3.56 us  [stream_window(): both = jnp.concatenate([edge, core, edge], 1)]
    gather x2 -> x0, local copies, waits for them, and re-layouts: 2.46 us -> none  [body(): scales = (row_ok[src_row] & col_ok[src_col]).astype(jnp.float32).reshape(-1)]
    broadcast_in_dim x2 -> x0, local copies, waits for them, and re-layouts: 1.4 us -> none  [body(): scales = (row_ok[src_row] & col_ok[src_col]).astype(jnp.float32).reshape(-1)]
    all_to_all x1, starting transfers between devices: 7.69 us -> 6.36 us  [body(): lax.all_to_all(induced.reshape(owners, capacity, port_count), AXES, split...]
  transfers between devices with their start and end apart: 11 -> 11, of which waited for: 2 -> 3; matrix products, arithmetic and copies ran while one was open for 23% -> 15% of each run, Pallas kernels for 0% -> 0%
where the time goes in v7:
time: 107 us; the launch traced here: 106 us
  starting transfers between devices  42.8 us (40%)
  local copies, waits for them, and re-layouts  21.1 us (20%)
  waiting for transfers between devices  16.9 us (16%)
  Pallas kernels  14.1 us (13%)
  other arithmetic  7.63 us (7%)
  matrix products  2.61 us (2%)
    ppermute x9, starting transfers between devices, send(): return lax.ppermute(value, AXES, pairs_by(fn))  29.2 us
    pallas_call x1, Pallas kernels, leaf_fields(): pl.pallas_call(leaf_kernel, in_specs=[smem, smem, hbm, hbm, vmem, hbm, hb...  14.1 us
    all_to_all x1, waiting for transfers between devices, body(): lax.all_to_all(induced.reshape(owners, capacity, port_count), AXES, split...  8.18 us
    unnamed x16, local copies, waits for them, and re-layouts  7.57 us
    all_to_all x1, starting transfers between devices, body(): got = lax.all_to_all(payload, AXES, split_axis=0, concat_axis=0, tiled=True)  7.15 us
    all_to_all x1, starting transfers between devices, body(): lax.all_to_all(induced.reshape(owners, capacity, port_count), AXES, split...  6.36 us
    all_to_all x1, waiting for transfers between devices, body(): got = lax.all_to_all(payload, AXES, split_axis=0, concat_axis=0, tiled=True)  4.73 us
    ppermute x9, waiting for transfers between devices, send(): return lax.ppermute(value, AXES, pairs_by(fn))  4.03 us
  transfers between devices with their start and end apart: 11, of which 3 were waited for; matrix products, arithmetic and copies ran while one was open for 15% of the time, Pallas kernels for 0%

profile of v7, /device:TPU:0, one launch (start us, length us, event | category | flops | bytes accessed | tf_op | source)
XLA Modules:
  0.0 106.1 jit_solution(2172052843241385742)
XLA Ops:
  0.6 0.0 copy-start
  0.6 1.6 %copy-done = f32[128,16,256]{2,1,0:T(8,128)S(1)} copy-done((f32[128,16,256]{2,1,0:T(8,128)S(1)}, f32[128,16,256]{2,1,0:T(8,128)}, u32[]{:S(2)}) %copy-start) | copy-done | bytes 2097176
  2.2 1.9 %constant_dynamic-slice_fusion = f32[128,16,145]{2,1,0:T(8,128)} fusion(f32[128,16,256]{2,1,0:T(8,128)S(1)} %copy-done, s32[]{:T(128)S(6)} %select_n.49), kind=kLoop, calls=%fused_computation.74 | loop fusion | bytes 2375684 | tf_op jit(solution)/shard_map/dynamic-slice.1
  4.2 0.0 copy-start.4
  4.2 2.0 %copy.42 = f32[128,16,145]{0,2,1:T(8,128)S(1)} copy(f32[128,16,145]{2,1,0:T(8,128)} %constant_dynamic-slice_fusion) | data formatting | bytes 2375680
  6.1 0.0 copy-start.5
  6.2 1.2 %fusion.40 = (f32[9,145,128]{2,1,0:T(8,128)}, f32[9,145,128]{2,1,0:T(8,128)}) fusion(f32[16,145,128]{2,1,0:T(8,128)S(1)} %bitcast.32), kind=kLoop, calls=%fused_computation.93 | loop fusion | bytes 2672640 | tf_op jit(solution)/shard_map/slice | solution.py:79
  7.3 5.8 %collective-permute-start.3 = (f32[9,145,128]{2,1,0:T(8,128)}, f32[9,145,128]{2,1,0:T(8,128)}, u32[]{:S(2)}, u32[]{:S(2)}) collective-permute-start(f32[9,145,128]{2,1,0:T(8,128)} %get-tuple-element.13), channel_id=1, source_target_pairs={{0,4},{1,5},{2,6},{3,7},{4,8},{5,9},{6,10},{7,11},{8,12},{9,13},{1... | collective-permute-start | bytes 2004488 | tf_op jit(solution)/shard_map/ppermute | solution.py:58
  13.1 1.3 %collective-permute-start.4 = (f32[9,145,128]{2,1,0:T(8,128)}, f32[9,145,128]{2,1,0:T(8,128)}, u32[]{:S(2)}, u32[]{:S(2)}) collective-permute-start(f32[9,145,128]{2,1,0:T(8,128)} %get-tuple-element.12), channel_id=1, source_target_pairs={{4,0},{5,1},{6,2},{7,3},{8,4},{9,5},{10,6},{11,7},{12,8},{13,9},{1... | collective-permute-start | bytes 2004488 | tf_op jit(solution)/shard_map/ppermute | solution.py:58
  14.4 0.0 copy-done.4
  14.4 0.2 convert_reduce_fusion
  14.7 0.0 copy-start.2
  14.7 0.5 fusion.11
  15.2 0.1 reshape.80
  15.3 1.0 copy.48
  16.2 0.0 copy-done.5
  16.3 0.7 fusion.14
  17.0 1.1 fusion.22
  18.0 0.0 copy-done.2
  18.0 7.2 %all-to-all-start = ((bf16[16,65,384]{2,1,0:T(8,128)(2,1)}), bf16[16,65,384]{2,1,0:T(8,128)(2,1)}, u32[]{:S(2)}, u32[]{:S(2)}) async-start(bf16[16,65,384]{2,1,0:T(8,128)(2,1)} %fusion.22), calls=%async_computation | async-start | bytes 1769472 | tf_op jit(solution)/shard_map/all_to_all | solution.py:230
  25.2 1.3 %constant_dynamic-slice_fusion.1 = f32[128,16,17]{2,1,0:T(8,128)} fusion(f32[128,16,256]{2,1,0:T(8,128)S(1)} %copy-done, s32[]{:T(128)S(6)} %select_n.48), kind=kLoop, calls=%fused_computation.75 | loop fusion | bytes 278532 | tf_op jit(solution)/shard_map/dynamic-slice
  26.5 1.6 %copy.41 = f32[128,16,17]{0,2,1:T(8,128)S(1)} copy(f32[128,16,17]{2,1,0:T(8,128)} %constant_dynamic-slice_fusion.1) | data formatting | bytes 278528
  28.2 1.3 %collective-permute-start.1 = (f32[16,17,128]{2,1,0:T(8,128)S(1)}, f32[16,17,128]{2,1,0:T(8,128)}, u32[]{:S(2)}, u32[]{:S(2)}) collective-permute-start(f32[16,17,128]{2,1,0:T(8,128)S(1)} %bitcast.46), channel_id=1, source_target_pairs={{1,2},{2,1},{5,6},{6,5},{9,10},{10,9},{13,14},{14,13},{17,18},{18,... | collective-permute-start | bytes 417800 | tf_op jit(solution)/shard_map/ppermute | solution.py:58
  29.5 0.7 fusion.44
  30.2 1.3 %collective-permute-start = (f32[9,17,128]{2,1,0:T(8,128)}, f32[9,17,128]{2,1,0:T(8,128)}, u32[]{:S(2)}, u32[]{:S(2)}) collective-permute-start(f32[9,17,128]{2,1,0:T(8,128)} %get-tuple-element.21), channel_id=1, source_target_pairs={{1,6},{2,5},{5,10},{6,9},{9,14},{10,13},{17,22},{18,21},{21,26},{2... | collective-permute-start | bytes 235016 | tf_op jit(solution)/shard_map/ppermute | solution.py:58
  31.5 1.3 %collective-permute-start.2 = (f32[9,17,128]{2,1,0:T(8,128)}, f32[9,17,128]{2,1,0:T(8,128)}, u32[]{:S(2)}, u32[]{:S(2)}) collective-permute-start(f32[9,17,128]{2,1,0:T(8,128)} %get-tuple-element.20), channel_id=1, source_target_pairs={{5,2},{6,1},{9,6},{10,5},{13,10},{14,9},{21,18},{22,17},{25,22},{2... | collective-permute-start | bytes 235016 | tf_op jit(solution)/shard_map/ppermute | solution.py:58
  32.8 0.0 copy-done.1
  32.8 0.6 convert_bitcast_fusion.scale_ref
  33.4 0.0 collective-permute-done
  33.4 0.0 collective-permute-done.2
  33.4 0.0 collective-permute-done.1
  33.4 0.0 collective-permute-done.3
  33.4 4.0 %collective-permute-done.4 = f32[9,145,128]{2,1,0:T(8,128)} collective-permute-done((f32[9,145,128]{2,1,0:T(8,128)}, f32[9,145,128]{2,1,0:T(8,128)}, u32[]{:S(2)}, u32[]{:S(2)}) %collective-permute-start.4) | collective-permute-done | bytes 668192 | tf_op jit(solution)/shard_map/ppermute | solution.py:58
  37.4 3.6 %fusion.3 = f32[34,162,128]{2,1,0:T(8,128)S(1)} fusion(s32[]{:T(128)S(6)} %select_n.50, f32[9,17,128]{2,1,0:T(8,128)} %collective-permute-done, f32[16,17,128]{2,1,0:T(8,128)} %collective-permute-done.1, f32[9,17,128]{2,1,0:T(8,128)} %collective-permute-done.2, f32[9,145,128]{2,1,0:T(8,128)} %collective-permute-done.3, f32[16,145,128]{2,1,0:T(8,128)S(1)} %bitcast.33, ...), kind=kLoop, calls=%fused_computation.12 | loop fusion | flops 5640192 | bytes 5640196 | tf_op jit(solution)/shard_map/concatenate | solution.py:85
  41.0 0.7 fusion.9
  41.7 0.2 maximum_bitcast_fusion
  41.9 2.2 %copy.32 = bf16[4,10,2,8,16,128]{5,4,3,2,1,0:T(8,128)(2,1)} copy(bf16[4,10,2,8,16,128]{5,4,1,3,0,2:T(8,128)(2,1)S(1)} %maximum_bitcast_fusion) | data formatting | bytes 5242880 | tf_op jit(solution)/shard_map/transpose | solution.py:24
  44.2 4.7 %all-to-all-done = bf16[16,65,384]{2,1,0:T(8,128)(2,1)} async-done(((bf16[16,65,384]{2,1,0:T(8,128)(2,1)}), bf16[16,65,384]{2,1,0:T(8,128)(2,1)}, u32[]{:S(2)}, u32[]{:S(2)}) %all-to-all-start) | async-done | bytes 798752 | tf_op jit(solution)/shard_map/all_to_all | solution.py:230
  48.9 1.2 %slice.99 = bf16[16,64,384]{2,1,0:T(8,128)(2,1)S(1)} slice(bf16[16,65,384]{2,1,0:T(8,128)(2,1)} %all-to-all-done), slice={[0:16], [0:64], [0:384]} | slice | bytes 1572864 | tf_op jit(solution)/shard_map/slice | solution.py:231
  50.2 0.7 slice.101.cur_hbm
  50.9 1.0 copy.36.cpl_t_hbm
  51.9 0.8 fusion.28
  52.7 0.7 reshape.77.row_leaf_ref
  53.4 14.1 %shard_map.77 = (bf16[16,2,128,128]{3,2,1,0:T(8,128)(2,1)}, bf16[1024,128]{1,0:T(8,128)(2,1)}) custom-call(s32[16,8]{1,0:T(8,128)} %bitcast.52, s32[16,8]{1,0:T(8,128)} %convert_bitcast_fusion.scale_ref, bf16[4,10,2,128,128]{4,3,2,1,0:T(8,128)(2,1)} %bitcast.34, bf16[16,8,2,128,128]{4,3,2,1,0:T(8,128)(2,1)} %bitcast.35, s32[1,1024]{1,0:T(1,128)} %reshape.77.row_leaf_ref, ...), custom_call_target="tpu_custom_call" | custom-call | tf_op jit(solution)/shard_map/pallas_call | solution.py:170
  67.5 1.5 %copy.47 = bf16[2,8,2,8,16,128]{5,4,1,3,0,2:T(8,128)(2,1)S(1)} copy(bf16[2,8,2,8,16,128]{5,4,3,2,1,0:T(8,128)(2,1)} %bitcast.45) | data formatting | bytes 2097152 | tf_op jit(solution)/shard_map/reshape;reshape | solution.py:32
  69.0 0.3 fusion.41
  69.3 0.6 fusion.42
  69.9 5.6 %collective-permute-start.5 = (bf16[16,1,128]{2,1,0:T(2,128)(2,1)}, bf16[16,1,128]{2,1,0:T(2,128)(2,1)S(1)}, u32[]{:S(2)}, u32[]{:S(2)}) collective-permute-start(bf16[16,1,128]{2,1,0:T(2,128)(2,1)} %get-tuple-element.16), channel_id=1, source_target_pairs={{0,1},{1,2},{2,3},{4,5},{5,6},{6,7},{8,9},{9,10},{10,11},{12,13},{... | collective-permute-start | bytes 12296 | tf_op jit(solution)/shard_map/ppermute | solution.py:58
  75.5 1.3 %collective-permute-start.6 = (bf16[16,1,128]{2,1,0:T(2,128)(2,1)}, bf16[16,1,128]{2,1,0:T(2,128)(2,1)S(1)}, u32[]{:S(2)}, u32[]{:S(2)}) collective-permute-start(bf16[16,1,128]{2,1,0:T(2,128)(2,1)} %get-tuple-element.17), channel_id=1, source_target_pairs={{1,0},{2,1},{3,2},{5,4},{6,5},{7,6},{9,8},{10,9},{11,10},{13,12},{... | collective-permute-start | bytes 12296 | tf_op jit(solution)/shard_map/ppermute | solution.py:58
  76.8 10.1 %collective-permute-start.7 = (bf16[1,128,128]{2,1,0:T(8,128)(2,1)S(1)}, bf16[1,128,128]{2,1,0:T(8,128)(2,1)S(1)}, u32[]{:S(2)}, u32[]{:S(2)}) collective-permute-start(bf16[1,128,128]{2,1,0:T(8,128)(2,1)S(1)} %get-tuple-element.18), channel_id=1, source_target_pairs={{0,4},{1,5},{2,6},{3,7},{4,8},{5,9},{6,10},{7,11},{8,12},{9,13},{1... | collective-permute-start | bytes 98312 | tf_op jit(solution)/shard_map/ppermute | solution.py:58
  86.9 1.3 %collective-permute-start.8 = (bf16[1,128,128]{2,1,0:T(8,128)(2,1)S(1)}, bf16[1,128,128]{2,1,0:T(8,128)(2,1)S(1)}, u32[]{:S(2)}, u32[]{:S(2)}) collective-permute-start(bf16[1,128,128]{2,1,0:T(8,128)(2,1)S(1)} %get-tuple-element.19), channel_id=1, source_target_pairs={{4,0},{5,1},{6,2},{7,3},{8,4},{9,5},{10,6},{11,7},{12,8},{13,9},{1... | collective-permute-start | bytes 98312 | tf_op jit(solution)/shard_map/ppermute | solution.py:58
  88.2 6.4 %all-to-all-start.1 = ((bf16[16,64,128]{2,1,0:T(8,128)(2,1)}), bf16[16,64,128]{2,1,0:T(8,128)(2,1)S(1)}, u32[]{:S(2)}, u32[]{:S(2)}) async-start(bf16[16,64,128]{2,1,0:T(8,128)(2,1)} %bitcast.18), calls=%async_computation.1 | async-start | bytes 524288 | tf_op jit(solution)/shard_map/all_to_all | solution.py:252
  94.6 0.0 collective-permute-done.5
  94.6 0.0 collective-permute-done.6
  94.6 0.1 maximum_convert_fusion.1
  94.8 0.0 collective-permute-done.7
  94.8 0.0 collective-permute-done.8
  94.8 0.1 maximum_convert_fusion
  94.9 0.0 copy-start.3
  94.9 0.2 fusion.17
  95.1 1.4 %copy.38 = f32[128,16,128]{2,1,0:T(8,128)} copy(f32[128,16,128]{0,2,1:T(8,128)S(1)} %fusion.17) | data formatting | bytes 2097152
  96.5 8.2 %all-to-all-done.1 = bf16[16,64,128]{2,1,0:T(8,128)(2,1)S(1)} async-done(((bf16[16,64,128]{2,1,0:T(8,128)(2,1)}), bf16[16,64,128]{2,1,0:T(8,128)(2,1)S(1)}, u32[]{:S(2)}, u32[]{:S(2)}) %all-to-all-start.1) | async-done | bytes 262176 | tf_op jit(solution)/shard_map/all_to_all | solution.py:252
  104.6 0.0 copy-done.3
  104.6 1.4 %fusion.15 = bf16[512,128]{1,0:T(8,128)(2,1)} fusion(bf16[1024,128]{1,0:T(8,128)(2,1)S(1)} %bitcast.50, s32[512]{0:T(512)S(1)} %copy-done.3), kind=kOutput, calls=%fused_computation.29 | convolution fusion | flops 134807552 | bytes 395264 | tf_op jit(solution)/shard_map/dot_general | solution.py:255
  (7 shorter events, 0.1 us)
Async XLA Ops:
  0.6 1.6 %copy-start = (f32[128,16,256]{2,1,0:T(8,128)S(1)}, f32[128,16,256]{2,1,0:T(8,128)}, u32[]{:S(2)}) copy-start(f32[128,16,256]{2,1,0:T(8,128)} %param.6) | copy-start | bytes 6291460
  4.2 10.2 %copy-start.4 = (s32[512]{0:T(512)S(1)}, s32[512]{0:T(512)}, u32[]{:S(2)}) copy-start(s32[512]{0:T(512)} %param.9) | copy-start | bytes 6148
  6.1 10.1 %copy-start.5 = (bf16[512,128]{1,0:T(8,128)(2,1)S(1)}, bf16[512,128]{1,0:T(8,128)(2,1)}, u32[]{:S(2)}) copy-start(bf16[512,128]{1,0:T(8,128)(2,1)} %param.10) | copy-start | bytes 393220
  7.3 26.1 %collective-permute-start.3 = (f32[9,145,128]{2,1,0:T(8,128)}, f32[9,145,128]{2,1,0:T(8,128)}, u32[]{:S(2)}, u32[]{:S(2)}) collective-permute-start(f32[9,145,128]{2,1,0:T(8,128)} %get-tuple-element.13), channel_id=1, source_target_pairs={{0,4},{1,5},{2,6},{3,7},{4,8},{5,9},{6,10},{7,11},{8,12},{9,13},{1... | collective-permute-start | bytes 2004488 | tf_op jit(solution)/shard_map/ppermute | solution.py:58
  13.1 24.3 %collective-permute-start.4 = (f32[9,145,128]{2,1,0:T(8,128)}, f32[9,145,128]{2,1,0:T(8,128)}, u32[]{:S(2)}, u32[]{:S(2)}) collective-permute-start(f32[9,145,128]{2,1,0:T(8,128)} %get-tuple-element.12), channel_id=1, source_target_pairs={{4,0},{5,1},{6,2},{7,3},{8,4},{9,5},{10,6},{11,7},{12,8},{13,9},{1... | collective-permute-start | bytes 2004488 | tf_op jit(solution)/shard_map/ppermute | solution.py:58
  14.7 3.3 %copy-start.2 = (s32[512]{0:T(512)}, s32[512]{0:T(512)S(1)}, u32[]{:S(2)}) copy-start(s32[512]{0:T(512)S(1)} %multiply_add_fusion) | copy-start | bytes 6148
  18.0 14.7 %copy-start.1 = (s32[2,8,8]{2,1,0:T(8,128)S(1)}, s32[2,8,8]{2,1,0:T(8,128)}, u32[]{:S(2)}) copy-start(s32[2,8,8]{2,1,0:T(8,128)} %param.8) | copy-start | bytes 1540
  18.0 30.9 %all-to-all-start = ((bf16[16,65,384]{2,1,0:T(8,128)(2,1)}), bf16[16,65,384]{2,1,0:T(8,128)(2,1)}, u32[]{:S(2)}, u32[]{:S(2)}) async-start(bf16[16,65,384]{2,1,0:T(8,128)(2,1)} %fusion.22), calls=%async_computation | async-start | bytes 1769472 | tf_op jit(solution)/shard_map/all_to_all | solution.py:230
  28.2 5.2 %collective-permute-start.1 = (f32[16,17,128]{2,1,0:T(8,128)S(1)}, f32[16,17,128]{2,1,0:T(8,128)}, u32[]{:S(2)}, u32[]{:S(2)}) collective-permute-start(f32[16,17,128]{2,1,0:T(8,128)S(1)} %bitcast.46), channel_id=1, source_target_pairs={{1,2},{2,1},{5,6},{6,5},{9,10},{10,9},{13,14},{14,13},{17,18},{18,... | collective-permute-start | bytes 417800 | tf_op jit(solution)/shard_map/ppermute | solution.py:58
  30.2 3.2 %collective-permute-start = (f32[9,17,128]{2,1,0:T(8,128)}, f32[9,17,128]{2,1,0:T(8,128)}, u32[]{:S(2)}, u32[]{:S(2)}) collective-permute-start(f32[9,17,128]{2,1,0:T(8,128)} %get-tuple-element.21), channel_id=1, source_target_pairs={{1,6},{2,5},{5,10},{6,9},{9,14},{10,13},{17,22},{18,21},{21,26},{2... | collective-permute-start | bytes 235016 | tf_op jit(solution)/shard_map/ppermute | solution.py:58
  31.5 1.9 %collective-permute-start.2 = (f32[9,17,128]{2,1,0:T(8,128)}, f32[9,17,128]{2,1,0:T(8,128)}, u32[]{:S(2)}, u32[]{:S(2)}) collective-permute-start(f32[9,17,128]{2,1,0:T(8,128)} %get-tuple-element.20), channel_id=1, source_target_pairs={{5,2},{6,1},{9,6},{10,5},{13,10},{14,9},{21,18},{22,17},{25,22},{2... | collective-permute-start | bytes 235016 | tf_op jit(solution)/shard_map/ppermute | solution.py:58
  69.9 24.7 %collective-permute-start.5 = (bf16[16,1,128]{2,1,0:T(2,128)(2,1)}, bf16[16,1,128]{2,1,0:T(2,128)(2,1)S(1)}, u32[]{:S(2)}, u32[]{:S(2)}) collective-permute-start(bf16[16,1,128]{2,1,0:T(2,128)(2,1)} %get-tuple-element.16), channel_id=1, source_target_pairs={{0,1},{1,2},{2,3},{4,5},{5,6},{6,7},{8,9},{9,10},{10,11},{12,13},{... | collective-permute-start | bytes 12296 | tf_op jit(solution)/shard_map/ppermute | solution.py:58
  75.5 19.1 %collective-permute-start.6 = (bf16[16,1,128]{2,1,0:T(2,128)(2,1)}, bf16[16,1,128]{2,1,0:T(2,128)(2,1)S(1)}, u32[]{:S(2)}, u32[]{:S(2)}) collective-permute-start(bf16[16,1,128]{2,1,0:T(2,128)(2,1)} %get-tuple-element.17), channel_id=1, source_target_pairs={{1,0},{2,1},{3,2},{5,4},{6,5},{7,6},{9,8},{10,9},{11,10},{13,12},{... | collective-permute-start | bytes 12296 | tf_op jit(solution)/shard_map/ppermute | solution.py:58
  76.8 17.9 %collective-permute-start.7 = (bf16[1,128,128]{2,1,0:T(8,128)(2,1)S(1)}, bf16[1,128,128]{2,1,0:T(8,128)(2,1)S(1)}, u32[]{:S(2)}, u32[]{:S(2)}) collective-permute-start(bf16[1,128,128]{2,1,0:T(8,128)(2,1)S(1)} %get-tuple-element.18), channel_id=1, source_target_pairs={{0,4},{1,5},{2,6},{3,7},{4,8},{5,9},{6,10},{7,11},{8,12},{9,13},{1... | collective-permute-start | bytes 98312 | tf_op jit(solution)/shard_map/ppermute | solution.py:58
  86.9 7.8 %collective-permute-start.8 = (bf16[1,128,128]{2,1,0:T(8,128)(2,1)S(1)}, bf16[1,128,128]{2,1,0:T(8,128)(2,1)S(1)}, u32[]{:S(2)}, u32[]{:S(2)}) collective-permute-start(bf16[1,128,128]{2,1,0:T(8,128)(2,1)S(1)} %get-tuple-element.19), channel_id=1, source_target_pairs={{4,0},{5,1},{6,2},{7,3},{8,4},{9,5},{10,6},{11,7},{12,8},{13,9},{1... | collective-permute-start | bytes 98312 | tf_op jit(solution)/shard_map/ppermute | solution.py:58
  88.2 16.4 %all-to-all-start.1 = ((bf16[16,64,128]{2,1,0:T(8,128)(2,1)}), bf16[16,64,128]{2,1,0:T(8,128)(2,1)S(1)}, u32[]{:S(2)}, u32[]{:S(2)}) async-start(bf16[16,64,128]{2,1,0:T(8,128)(2,1)} %bitcast.18), calls=%async_computation.1 | async-start | bytes 524288 | tf_op jit(solution)/shard_map/all_to_all | solution.py:252
  94.9 9.8 %copy-start.3 = (s32[512]{0:T(512)S(1)}, s32[512]{0:T(512)}, u32[]{:S(2)}) copy-start(s32[512]{0:T(512)} %copy-done.2) | copy-start | bytes 6148

commit v8 on v7

--- a/solution.py
+++ b/solution.py
@@ -67,7 +67,7 @@
     return None
 
 
-def stream_window(stream, half):
+def stream_window(stream, half, ready):
     gz = lax.axis_index("gz")
     rows, width = stream.shape[0], stream.shape[1]
     hr, hc = LEAF_R + 1, LEAF_C + 1
@@ -80,10 +80,13 @@
     d_top = send(side[rows - hr :], lambda x, y, z: sideways(x, y, z, 1))
     d_bot = send(side[:hr], lambda x, y, z: sideways(x, y, z, -1))
 
+    (v_top, v_bot, d_top, d_bot, h_got), ready = lax.optimization_barrier(
+        ((v_top, v_bot, d_top, d_bot, h_got), ready)
+    )
     core = jnp.concatenate([v_top, mid, v_bot], 0)
     edge = jnp.concatenate([d_top, h_got, d_bot], 0)
     both = jnp.concatenate([edge, core, edge], 1)
-    return lax.dynamic_slice_in_dim(both, gz * hc, mid_w + hc, 1)
+    return lax.dynamic_slice_in_dim(both, gz * hc, mid_w + hc, 1), ready
 
 
 def field_halo(grid_field):
@@ -159,11 +162,9 @@
     volt_ref[...] = acc_ref[...].T.astype(volt_ref.dtype)
 
 
-def leaf_fields(codes, scales, bordered, kernels, slot_leaf, coupling, current):
+def leaf_fields(codes, scales, bordered, kernels, row_leaf, coupling_t, current):
     leaf_count, near_count, components, cells, _ = kernels.shape
     slot_count, port_count = current.shape
-    coupling_t = coupling.T
-    row_leaf = slot_leaf.reshape(1, slot_count)
     smem = pl.BlockSpec(memory_space=pltpu.SMEM)
     hbm = pl.BlockSpec(memory_space=pl.ANY)
     vmem = pl.BlockSpec(memory_space=pltpu.VMEM)
@@ -230,10 +231,13 @@
     got = lax.all_to_all(payload, AXES, split_axis=0, concat_axis=0, tiled=True)
     got_rows = got[:, :capacity].reshape(slot_count, row_width)
     got_leaf = got[:, capacity, :capacity].reshape(slot_count).astype(jnp.int32)
-    got_coupling = got_rows[:, : 2 * leaf_cells]
+    got_coupling_t = got_rows[:, : 2 * leaf_cells].T
     got_current = got_rows[:, 2 * leaf_cells :]
-
-    window = stream_window(stream.transpose(1, 2, 0), half_cols)
+    got_leaf = got_leaf.reshape(1, slot_count)
+
+    window, (got_leaf, got_coupling_t, got_current) = stream_window(
+        stream.transpose(1, 2, 0), half_cols, (got_leaf, got_coupling_t, got_current)
+    )
     currents = plane_curl(window).astype(jnp.bfloat16)
     bordered = to_leaves(currents)
     src_row = jnp.arange(leaf_rows, dtype=jnp.int32)[:, None, None] + near_lists // 3
@@ -247,7 +251,7 @@
     kernels = inductance.reshape(leaf_count, near_count, 2, leaf_cells, leaf_cells)
     codes = near_lists.reshape(leaf_count, near_count)
     total_field, induced = leaf_fields(
-        codes, scales, bordered, kernels, got_leaf, got_coupling, got_current
+        codes, scales, bordered, kernels, got_leaf, got_coupling_t, got_current
     )
     returned = lax.all_to_all(
         induced.reshape(owners, capacity, port_count), AXES, split_axis=0, concat_axis=0, tiled=True

time: 107 us -> 104 us (0.972)
  starting transfers between devices: 42.8 us -> 38 us
    ppermute x9, starting transfers between devices: 29.2 us -> 23.9 us  [send(): return lax.ppermute(value, AXES, pairs_by(fn))]
    ppermute x9, waiting for transfers between devices: 4.03 us -> 7.91 us  [send(): return lax.ppermute(value, AXES, pairs_by(fn))]
    all_to_all x1, waiting for transfers between devices: 4.73 us -> 1.55 us  [body(): got = lax.all_to_all(payload, AXES, split_axis=0, concat_axis=0, tiled=True)]
    unnamed x16 -> x14, local copies, waits for them, and re-layouts: 7.57 us -> 5.98 us
  transfers between devices with their start and end apart: 11 -> 11, of which waited for: 3 -> 4; matrix products, arithmetic and copies ran while one was open for 15% -> 15% of each run, Pallas kernels for 0% -> 0%
where the time goes in v8:
time: 104 us; the launch traced here: 103 us
  starting transfers between devices  38 us (37%)
  local copies, waits for them, and re-layouts  20.3 us (20%)
  waiting for transfers between devices  17.6 us (17%)
  Pallas kernels  14.1 us (14%)
  other arithmetic  8.44 us (8%)
  matrix products  3.5 us (3%)
    ppermute x9, starting transfers between devices, send(): return lax.ppermute(value, AXES, pairs_by(fn))  23.9 us
    pallas_call x1, Pallas kernels, leaf_fields(): pl.pallas_call(leaf_kernel, in_specs=[smem, smem, hbm, hbm, vmem, hbm, hb...  14.1 us
    all_to_all x1, waiting for transfers between devices, body(): lax.all_to_all(induced.reshape(owners, capacity, port_count), AXES, split...  8.18 us
    ppermute x9, waiting for transfers between devices, send(): return lax.ppermute(value, AXES, pairs_by(fn))  7.91 us
    all_to_all x1, starting transfers between devices, body(): got = lax.all_to_all(payload, AXES, split_axis=0, concat_axis=0, tiled=True)  7.4 us
    all_to_all x1, starting transfers between devices, body(): lax.all_to_all(induced.reshape(owners, capacity, port_count), AXES, split...  6.71 us
    unnamed x14, local copies, waits for them, and re-layouts  5.98 us
    concatenate x1, other arithmetic, stream_window(): both = jnp.concatenate([edge, core, edge], 1)  3.56 us
  transfers between devices with their start and end apart: 11, of which 4 were waited for; matrix products, arithmetic and copies ran while one was open for 15% of the time, Pallas kernels for 0%

profile of v8, /device:TPU:0, one launch (start us, length us, event | category | flops | bytes accessed | tf_op | source)
XLA Modules:
  0.0 102.9 jit_solution(12774779570014052219)
XLA Ops:
  0.6 0.0 copy-start
  0.6 0.9 fusion.31
  1.5 0.2 convert_reduce_fusion
  1.8 0.0 copy-start.3
  1.8 0.5 fusion.11
  2.2 0.1 reshape.80
  2.3 1.0 copy.48
  3.3 1.6 %fusion.14 = bf16[1024,384]{1,0:T(8,128)(2,1)S(1)} fusion(s32[512]{0:T(512)S(1)} %multiply_add_fusion, bf16[512,128]{1,0:T(8,128)(2,1)} %param.10, bf16[512,256]{1,0:T(8,128)(2,1)S(1)} %bitcast.51), kind=kOutput, calls=%fused_computation.28 | convolution fusion | flops 404357120 | bytes 1181696 | tf_op jit(solution)/shard_map/dot_general | solution.py:222
  4.9 1.0 fusion.22
  6.0 0.0 copy-done.3
  6.0 7.4 %all-to-all-start = ((bf16[16,65,384]{2,1,0:T(8,128)(2,1)}), bf16[16,65,384]{2,1,0:T(8,128)(2,1)}, u32[]{:S(2)}, u32[]{:S(2)}) async-start(bf16[16,65,384]{2,1,0:T(8,128)(2,1)} %fusion.22), calls=%async_computation | async-start | bytes 1769472 | tf_op jit(solution)/shard_map/all_to_all | solution.py:231
  13.4 0.0 copy-done
  13.4 2.0 %constant_dynamic-slice_fusion.1 = f32[128,16,145]{2,1,0:T(8,128)} fusion(f32[128,16,256]{2,1,0:T(8,128)S(1)} %copy-done, s32[]{:T(128)S(6)} %select_n.48), kind=kLoop, calls=%fused_computation.75 | loop fusion | bytes 2375684 | tf_op jit(solution)/shard_map/dynamic-slice
  15.3 2.0 %copy.41 = f32[128,16,145]{0,2,1:T(8,128)S(1)} copy(f32[128,16,145]{2,1,0:T(8,128)} %constant_dynamic-slice_fusion.1) | data formatting | bytes 2375680
  17.3 0.0 copy-start.2
  17.3 1.2 %fusion.40 = (f32[9,145,128]{2,1,0:T(8,128)}, f32[9,145,128]{2,1,0:T(8,128)}) fusion(f32[16,145,128]{2,1,0:T(8,128)S(1)} %bitcast.32), kind=kLoop, calls=%fused_computation.93 | loop fusion | bytes 2672640 | tf_op jit(solution)/shard_map/slice | solution.py:79
  18.5 4.6 %collective-permute-start = (f32[9,145,128]{2,1,0:T(8,128)}, f32[9,145,128]{2,1,0:T(8,128)}, u32[]{:S(2)}, u32[]{:S(2)}) collective-permute-start(f32[9,145,128]{2,1,0:T(8,128)} %get-tuple-element.29), channel_id=1, source_target_pairs={{0,4},{1,5},{2,6},{3,7},{4,8},{5,9},{6,10},{7,11},{8,12},{9,13},{1... | collective-permute-start | bytes 2004488 | tf_op jit(solution)/shard_map/ppermute | solution.py:58
  23.1 1.3 %collective-permute-start.1 = (f32[9,145,128]{2,1,0:T(8,128)}, f32[9,145,128]{2,1,0:T(8,128)}, u32[]{:S(2)}, u32[]{:S(2)}) collective-permute-start(f32[9,145,128]{2,1,0:T(8,128)} %get-tuple-element.28), channel_id=1, source_target_pairs={{4,0},{5,1},{6,2},{7,3},{8,4},{9,5},{10,6},{11,7},{12,8},{13,9},{1... | collective-permute-start | bytes 2004488 | tf_op jit(solution)/shard_map/ppermute | solution.py:58
  24.4 1.3 %constant_dynamic-slice_fusion = f32[128,16,17]{2,1,0:T(8,128)} fusion(f32[128,16,256]{2,1,0:T(8,128)S(1)} %copy-done, s32[]{:T(128)S(6)} %select_n.49), kind=kLoop, calls=%fused_computation.74 | loop fusion | bytes 278532 | tf_op jit(solution)/shard_map/dynamic-slice.1
  25.7 1.6 %copy.42 = f32[128,16,17]{0,2,1:T(8,128)S(1)} copy(f32[128,16,17]{2,1,0:T(8,128)} %constant_dynamic-slice_fusion) | data formatting | bytes 278528
  27.4 1.3 %collective-permute-start.4 = (f32[16,17,128]{2,1,0:T(8,128)S(1)}, f32[16,17,128]{2,1,0:T(8,128)}, u32[]{:S(2)}, u32[]{:S(2)}) collective-permute-start(f32[16,17,128]{2,1,0:T(8,128)S(1)} %bitcast.46), channel_id=1, source_target_pairs={{1,2},{2,1},{5,6},{6,5},{9,10},{10,9},{13,14},{14,13},{17,18},{18,... | collective-permute-start | bytes 417800 | tf_op jit(solution)/shard_map/ppermute | solution.py:58
  28.7 0.7 fusion.44
  29.4 1.3 %collective-permute-start.2 = (f32[9,17,128]{2,1,0:T(8,128)}, f32[9,17,128]{2,1,0:T(8,128)}, u32[]{:S(2)}, u32[]{:S(2)}) collective-permute-start(f32[9,17,128]{2,1,0:T(8,128)} %get-tuple-element.37), channel_id=1, source_target_pairs={{1,6},{2,5},{5,10},{6,9},{9,14},{10,13},{17,22},{18,21},{21,26},{2... | collective-permute-start | bytes 235016 | tf_op jit(solution)/shard_map/ppermute | solution.py:58
  30.7 1.3 %collective-permute-start.3 = (f32[9,17,128]{2,1,0:T(8,128)}, f32[9,17,128]{2,1,0:T(8,128)}, u32[]{:S(2)}, u32[]{:S(2)}) collective-permute-start(f32[9,17,128]{2,1,0:T(8,128)} %get-tuple-element.36), channel_id=1, source_target_pairs={{5,2},{6,1},{9,6},{10,5},{13,10},{14,9},{21,18},{22,17},{25,22},{2... | collective-permute-start | bytes 235016 | tf_op jit(solution)/shard_map/ppermute | solution.py:58
  32.0 0.0 copy-done.2
  32.0 0.6 convert_bitcast_fusion.scale_ref
  32.6 1.5 %all-to-all-done = bf16[16,65,384]{2,1,0:T(8,128)(2,1)} async-done(((bf16[16,65,384]{2,1,0:T(8,128)(2,1)}), bf16[16,65,384]{2,1,0:T(8,128)(2,1)}, u32[]{:S(2)}, u32[]{:S(2)}) %all-to-all-start) | async-done | bytes 798752 | tf_op jit(solution)/shard_map/all_to_all | solution.py:231
  34.2 1.2 %slice.95 = bf16[16,64,384]{2,1,0:T(8,128)(2,1)S(1)} slice(bf16[16,65,384]{2,1,0:T(8,128)(2,1)} %all-to-all-done), slice={[0:16], [0:64], [0:384]} | slice | bytes 1572864 | tf_op jit(solution)/shard_map/slice | solution.py:232
  35.4 0.8 slice_bitcast_fusion
  36.2 0.7 slice.97.cur_hbm
  36.9 0.8 fusion.28
  37.7 0.7 reshape.77.row_leaf_ref
  38.4 0.0 collective-permute-done.2
  38.4 0.0 collective-permute-done.3
  38.4 0.0 collective-permute-done.4
  38.4 5.6 %collective-permute-done = f32[9,145,128]{2,1,0:T(8,128)} collective-permute-done((f32[9,145,128]{2,1,0:T(8,128)}, f32[9,145,128]{2,1,0:T(8,128)}, u32[]{:S(2)}, u32[]{:S(2)}) %collective-permute-start) | collective-permute-done | bytes 668192 | tf_op jit(solution)/shard_map/ppermute | solution.py:58
  44.0 2.3 %collective-permute-done.1 = f32[9,145,128]{2,1,0:T(8,128)} collective-permute-done((f32[9,145,128]{2,1,0:T(8,128)}, f32[9,145,128]{2,1,0:T(8,128)}, u32[]{:S(2)}, u32[]{:S(2)}) %collective-permute-start.1) | collective-permute-done | bytes 668192 | tf_op jit(solution)/shard_map/ppermute | solution.py:58
  46.3 3.6 %fusion.3 = f32[34,162,128]{2,1,0:T(8,128)S(1)} fusion(s32[]{:T(128)S(6)} %select_n.56, f32[9,17,128]{2,1,0:T(8,128)} %collective-permute-done.2, f32[16,17,128]{2,1,0:T(8,128)} %collective-permute-done.4, f32[9,17,128]{2,1,0:T(8,128)} %collective-permute-done.3, f32[9,145,128]{2,1,0:T(8,128)} %collective-permute-done, f32[16,145,128]{2,1,0:T(8,128)S(1)} %bitcast.33, ...), kind=kLoop, calls=%fused_computation.12 | loop fusion | flops 5640192 | bytes 5640196 | tf_op jit(solution)/shard_map/concatenate | solution.py:88
  49.9 0.7 fusion.9
  50.5 0.2 maximum_bitcast_fusion
  50.8 0.0 copy-start.1
  50.8 2.2 %copy.33 = bf16[4,10,2,8,16,128]{5,4,3,2,1,0:T(8,128)(2,1)} copy(bf16[4,10,2,8,16,128]{5,4,1,3,0,2:T(8,128)(2,1)S(1)} %maximum_bitcast_fusion) | data formatting | bytes 5242880 | tf_op jit(solution)/shard_map/transpose | solution.py:24
  53.1 0.0 copy-done.1
  53.1 1.0 copy.36.cpl_t_hbm
  54.1 14.1 %shard_map.77 = (bf16[16,2,128,128]{3,2,1,0:T(8,128)(2,1)}, bf16[1024,128]{1,0:T(8,128)(2,1)}) custom-call(s32[16,8]{1,0:T(8,128)} %bitcast.52, s32[16,8]{1,0:T(8,128)} %convert_bitcast_fusion.scale_ref, bf16[4,10,2,128,128]{4,3,2,1,0:T(8,128)(2,1)} %bitcast.34, bf16[16,8,2,128,128]{4,3,2,1,0:T(8,128)(2,1)} %bitcast.35, s32[1,1024]{1,0:T(1,128)} %reshape.77.row_leaf_ref, ...), custom_call_target="tpu_custom_call" | custom-call | tf_op jit(solution)/shard_map/pallas_call | solution.py:171
  68.2 1.5 %copy.47 = bf16[2,8,2,8,16,128]{5,4,1,3,0,2:T(8,128)(2,1)S(1)} copy(bf16[2,8,2,8,16,128]{5,4,3,2,1,0:T(8,128)(2,1)} %bitcast.45) | data formatting | bytes 2097152 | tf_op jit(solution)/shard_map/reshape;reshape | solution.py:32
  69.7 0.3 fusion.41
  70.0 0.6 fusion.42
  70.6 3.8 %collective-permute-start.5 = (bf16[16,1,128]{2,1,0:T(2,128)(2,1)}, bf16[16,1,128]{2,1,0:T(2,128)(2,1)S(1)}, u32[]{:S(2)}, u32[]{:S(2)}) collective-permute-start(bf16[16,1,128]{2,1,0:T(2,128)(2,1)} %get-tuple-element.32), channel_id=1, source_target_pairs={{0,1},{1,2},{2,3},{4,5},{5,6},{6,7},{8,9},{9,10},{10,11},{12,13},{... | collective-permute-start | bytes 12296 | tf_op jit(solution)/shard_map/ppermute | solution.py:58
  74.4 1.3 %collective-permute-start.6 = (bf16[16,1,128]{2,1,0:T(2,128)(2,1)}, bf16[16,1,128]{2,1,0:T(2,128)(2,1)S(1)}, u32[]{:S(2)}, u32[]{:S(2)}) collective-permute-start(bf16[16,1,128]{2,1,0:T(2,128)(2,1)} %get-tuple-element.33), channel_id=1, source_target_pairs={{1,0},{2,1},{3,2},{5,4},{6,5},{7,6},{9,8},{10,9},{11,10},{13,12},{... | collective-permute-start | bytes 12296 | tf_op jit(solution)/shard_map/ppermute | solution.py:58
  75.8 7.6 %collective-permute-start.7 = (bf16[1,128,128]{2,1,0:T(8,128)(2,1)S(1)}, bf16[1,128,128]{2,1,0:T(8,128)(2,1)S(1)}, u32[]{:S(2)}, u32[]{:S(2)}) collective-permute-start(bf16[1,128,128]{2,1,0:T(8,128)(2,1)S(1)} %get-tuple-element.34), channel_id=1, source_target_pairs={{0,4},{1,5},{2,6},{3,7},{4,8},{5,9},{6,10},{7,11},{8,12},{9,13},{1... | collective-permute-start | bytes 98312 | tf_op jit(solution)/shard_map/ppermute | solution.py:58
  83.4 1.3 %collective-permute-start.8 = (bf16[1,128,128]{2,1,0:T(8,128)(2,1)S(1)}, bf16[1,128,128]{2,1,0:T(8,128)(2,1)S(1)}, u32[]{:S(2)}, u32[]{:S(2)}) collective-permute-start(bf16[1,128,128]{2,1,0:T(8,128)(2,1)S(1)} %get-tuple-element.35), channel_id=1, source_target_pairs={{4,0},{5,1},{6,2},{7,3},{8,4},{9,5},{10,6},{11,7},{12,8},{13,9},{1... | collective-permute-start | bytes 98312 | tf_op jit(solution)/shard_map/ppermute | solution.py:58
  84.7 6.7 %all-to-all-start.1 = ((bf16[16,64,128]{2,1,0:T(8,128)(2,1)}), bf16[16,64,128]{2,1,0:T(8,128)(2,1)S(1)}, u32[]{:S(2)}, u32[]{:S(2)}) async-start(bf16[16,64,128]{2,1,0:T(8,128)(2,1)} %bitcast.18), calls=%async_computation.1 | async-start | bytes 524288 | tf_op jit(solution)/shard_map/all_to_all | solution.py:256
  91.4 0.0 collective-permute-done.5
  91.4 0.0 collective-permute-done.6
  91.4 0.1 maximum_convert_fusion.1
  91.6 0.0 collective-permute-done.7
  91.6 0.0 collective-permute-done.8
  91.6 0.1 maximum_convert_fusion
  91.7 0.0 copy-start.4
  91.7 0.2 fusion.17
  91.9 1.4 %copy.38 = f32[128,16,128]{2,1,0:T(8,128)} copy(f32[128,16,128]{0,2,1:T(8,128)S(1)} %fusion.17) | data formatting | bytes 2097152
  93.3 8.2 %all-to-all-done.1 = bf16[16,64,128]{2,1,0:T(8,128)(2,1)S(1)} async-done(((bf16[16,64,128]{2,1,0:T(8,128)(2,1)}), bf16[16,64,128]{2,1,0:T(8,128)(2,1)S(1)}, u32[]{:S(2)}, u32[]{:S(2)}) %all-to-all-start.1) | async-done | bytes 262176 | tf_op jit(solution)/shard_map/all_to_all | solution.py:256
  101.5 1.4 %fusion.15 = bf16[512,128]{1,0:T(8,128)(2,1)} fusion(bf16[1024,128]{1,0:T(8,128)(2,1)S(1)} %bitcast.50, s32[512]{0:T(512)S(1)} %copy-done.4), kind=kOutput, calls=%fused_computation.29 | convolution fusion | flops 134807552 | bytes 395264 | tf_op jit(solution)/shard_map/dot_general | solution.py:259
  (5 shorter events, 0.0 us)
Async XLA Ops:
  0.6 12.8 %copy-start = (f32[128,16,256]{2,1,0:T(8,128)S(1)}, f32[128,16,256]{2,1,0:T(8,128)}, u32[]{:S(2)}) copy-start(f32[128,16,256]{2,1,0:T(8,128)} %param.6) | copy-start | bytes 6291460
  1.8 4.2 %copy-start.3 = (s32[512]{0:T(512)}, s32[512]{0:T(512)S(1)}, u32[]{:S(2)}) copy-start(s32[512]{0:T(512)S(1)} %multiply_add_fusion) | copy-start | bytes 6148
  6.0 28.2 %all-to-all-start = ((bf16[16,65,384]{2,1,0:T(8,128)(2,1)}), bf16[16,65,384]{2,1,0:T(8,128)(2,1)}, u32[]{:S(2)}, u32[]{:S(2)}) async-start(bf16[16,65,384]{2,1,0:T(8,128)(2,1)} %fusion.22), calls=%async_computation | async-start | bytes 1769472 | tf_op jit(solution)/shard_map/all_to_all | solution.py:231
  17.3 14.7 %copy-start.2 = (s32[2,8,8]{2,1,0:T(8,128)S(1)}, s32[2,8,8]{2,1,0:T(8,128)}, u32[]{:S(2)}) copy-start(s32[2,8,8]{2,1,0:T(8,128)} %param.8) | copy-start | bytes 1540
  18.5 25.5 %collective-permute-start = (f32[9,145,128]{2,1,0:T(8,128)}, f32[9,145,128]{2,1,0:T(8,128)}, u32[]{:S(2)}, u32[]{:S(2)}) collective-permute-start(f32[9,145,128]{2,1,0:T(8,128)} %get-tuple-element.29), channel_id=1, source_target_pairs={{0,4},{1,5},{2,6},{3,7},{4,8},{5,9},{6,10},{7,11},{8,12},{9,13},{1... | collective-permute-start | bytes 2004488 | tf_op jit(solution)/shard_map/ppermute | solution.py:58
  23.1 23.2 %collective-permute-start.1 = (f32[9,145,128]{2,1,0:T(8,128)}, f32[9,145,128]{2,1,0:T(8,128)}, u32[]{:S(2)}, u32[]{:S(2)}) collective-permute-start(f32[9,145,128]{2,1,0:T(8,128)} %get-tuple-element.28), channel_id=1, source_target_pairs={{4,0},{5,1},{6,2},{7,3},{8,4},{9,5},{10,6},{11,7},{12,8},{13,9},{1... | collective-permute-start | bytes 2004488 | tf_op jit(solution)/shard_map/ppermute | solution.py:58
  27.4 11.0 %collective-permute-start.4 = (f32[16,17,128]{2,1,0:T(8,128)S(1)}, f32[16,17,128]{2,1,0:T(8,128)}, u32[]{:S(2)}, u32[]{:S(2)}) collective-permute-start(f32[16,17,128]{2,1,0:T(8,128)S(1)} %bitcast.46), channel_id=1, source_target_pairs={{1,2},{2,1},{5,6},{6,5},{9,10},{10,9},{13,14},{14,13},{17,18},{18,... | collective-permute-start | bytes 417800 | tf_op jit(solution)/shard_map/ppermute | solution.py:58
  29.4 9.0 %collective-permute-start.2 = (f32[9,17,128]{2,1,0:T(8,128)}, f32[9,17,128]{2,1,0:T(8,128)}, u32[]{:S(2)}, u32[]{:S(2)}) collective-permute-start(f32[9,17,128]{2,1,0:T(8,128)} %get-tuple-element.37), channel_id=1, source_target_pairs={{1,6},{2,5},{5,10},{6,9},{9,14},{10,13},{17,22},{18,21},{21,26},{2... | collective-permute-start | bytes 235016 | tf_op jit(solution)/shard_map/ppermute | solution.py:58
  30.7 7.7 %collective-permute-start.3 = (f32[9,17,128]{2,1,0:T(8,128)}, f32[9,17,128]{2,1,0:T(8,128)}, u32[]{:S(2)}, u32[]{:S(2)}) collective-permute-start(f32[9,17,128]{2,1,0:T(8,128)} %get-tuple-element.36), channel_id=1, source_target_pairs={{5,2},{6,1},{9,6},{10,5},{13,10},{14,9},{21,18},{22,17},{25,22},{2... | collective-permute-start | bytes 235016 | tf_op jit(solution)/shard_map/ppermute | solution.py:58
  50.8 2.3 %copy-start.1 = (bf16[256,1024]{0,1:T(8,128)(2,1)S(1)}, bf16[256,1024]{0,1:T(8,128)(2,1)}, u32[]{:S(2)}) copy-start(bf16[256,1024]{0,1:T(8,128)(2,1)} %slice_bitcast_fusion) | copy-start | bytes 1572868
  70.6 20.8 %collective-permute-start.5 = (bf16[16,1,128]{2,1,0:T(2,128)(2,1)}, bf16[16,1,128]{2,1,0:T(2,128)(2,1)S(1)}, u32[]{:S(2)}, u32[]{:S(2)}) collective-permute-start(bf16[16,1,128]{2,1,0:T(2,128)(2,1)} %get-tuple-element.32), channel_id=1, source_target_pairs={{0,1},{1,2},{2,3},{4,5},{5,6},{6,7},{8,9},{9,10},{10,11},{12,13},{... | collective-permute-start | bytes 12296 | tf_op jit(solution)/shard_map/ppermute | solution.py:58
  74.4 17.0 %collective-permute-start.6 = (bf16[16,1,128]{2,1,0:T(2,128)(2,1)}, bf16[16,1,128]{2,1,0:T(2,128)(2,1)S(1)}, u32[]{:S(2)}, u32[]{:S(2)}) collective-permute-start(bf16[16,1,128]{2,1,0:T(2,128)(2,1)} %get-tuple-element.33), channel_id=1, source_target_pairs={{1,0},{2,1},{3,2},{5,4},{6,5},{7,6},{9,8},{10,9},{11,10},{13,12},{... | collective-permute-start | bytes 12296 | tf_op jit(solution)/shard_map/ppermute | solution.py:58
  75.8 15.8 %collective-permute-start.7 = (bf16[1,128,128]{2,1,0:T(8,128)(2,1)S(1)}, bf16[1,128,128]{2,1,0:T(8,128)(2,1)S(1)}, u32[]{:S(2)}, u32[]{:S(2)}) collective-permute-start(bf16[1,128,128]{2,1,0:T(8,128)(2,1)S(1)} %get-tuple-element.34), channel_id=1, source_target_pairs={{0,4},{1,5},{2,6},{3,7},{4,8},{5,9},{6,10},{7,11},{8,12},{9,13},{1... | collective-permute-start | bytes 98312 | tf_op jit(solution)/shard_map/ppermute | solution.py:58
  83.4 8.2 %collective-permute-start.8 = (bf16[1,128,128]{2,1,0:T(8,128)(2,1)S(1)}, bf16[1,128,128]{2,1,0:T(8,128)(2,1)S(1)}, u32[]{:S(2)}, u32[]{:S(2)}) collective-permute-start(bf16[1,128,128]{2,1,0:T(8,128)(2,1)S(1)} %get-tuple-element.35), channel_id=1, source_target_pairs={{4,0},{5,1},{6,2},{7,3},{8,4},{9,5},{10,6},{11,7},{12,8},{13,9},{1... | collective-permute-start | bytes 98312 | tf_op jit(solution)/shard_map/ppermute | solution.py:58
  84.7 16.8 %all-to-all-start.1 = ((bf16[16,64,128]{2,1,0:T(8,128)(2,1)}), bf16[16,64,128]{2,1,0:T(8,128)(2,1)S(1)}, u32[]{:S(2)}, u32[]{:S(2)}) async-start(bf16[16,64,128]{2,1,0:T(8,128)(2,1)} %bitcast.18), calls=%async_computation.1 | async-start | bytes 524288 | tf_op jit(solution)/shard_map/all_to_all | solution.py:256
  91.7 9.8 %copy-start.4 = (s32[512]{0:T(512)S(1)}, s32[512]{0:T(512)}, u32[]{:S(2)}) copy-start(s32[512]{0:T(512)} %copy-done.3) | copy-start | bytes 6148

commit v9 on v8

--- a/solution.py
+++ b/solution.py
@@ -151,7 +151,9 @@
             total = filament[c * cells : (c + 1) * cells] + jnp.dot(
                 weights, stacked, preferred_element_type=jnp.float32
             )
-            field_ref[leaf, c] = total.astype(field_ref.dtype)
+            field_ref[c, pl.ds(row * LEAF_R, LEAF_R), pl.ds(pl.multiple_of(col * LEAF_C, LEAF_C), LEAF_C)] = (
+                total.reshape(LEAF_R, LEAF_C, -1).astype(field_ref.dtype)
+            )
         own = bord_ref[row + 1, col + 1].reshape(2 * cells, -1)
         acc_ref[...] += lax.dot_general(
             own, coupling_t, (((0,), (0,)), ((), ())), preferred_element_type=jnp.float32
@@ -164,6 +166,8 @@
 
 def leaf_fields(codes, scales, bordered, kernels, row_leaf, coupling_t, current):
     leaf_count, near_count, components, cells, _ = kernels.shape
+    leaf_rows = bordered.shape[0] - 2
+    leaf_cols = bordered.shape[1] - 2
     slot_count, port_count = current.shape
     smem = pl.BlockSpec(memory_space=pltpu.SMEM)
     hbm = pl.BlockSpec(memory_space=pl.ANY)
@@ -173,7 +177,9 @@
         in_specs=[smem, smem, hbm, hbm, vmem, hbm, hbm],
         out_specs=[vmem, vmem],
         out_shape=[
-            jax.ShapeDtypeStruct((leaf_count, components, cells, port_count), jnp.bfloat16),
+            jax.ShapeDtypeStruct(
+                (components, leaf_rows * LEAF_R, leaf_cols * LEAF_C, port_count), jnp.bfloat16
+            ),
             jax.ShapeDtypeStruct((slot_count, port_count), jnp.bfloat16),
         ],
         scratch_shapes=[
@@ -260,8 +266,7 @@
         placement, returned, (((0,), (0,)), ((), ())), preferred_element_type=jnp.float32
     ).astype(jnp.bfloat16)
 
-    grid_field = from_leaves(total_field.reshape(leaf_rows, leaf_cols, 2, leaf_cells, port_count))
-    loop_voltage = field_halo(grid_field).transpose(2, 0, 1)
+    loop_voltage = field_halo(total_field).transpose(2, 0, 1)
     return (loop_voltage, filament_voltage)
 
 

time: 104 us -> 104 us (level)
    another operation x3 -> x2, local copies, waits for them, and re-layouts: 4.76 us -> 3.26 us
    squeeze x0 -> x1, local copies, waits for them, and re-layouts: none -> 1.27 us  [field_halo(): x_field = grid_field[0]]
  transfers between devices with their start and end apart: 11 -> 11, of which waited for: 4 -> 4; matrix products, arithmetic and copies ran while one was open for 15% -> 16% of each run, Pallas kernels for 0% -> 0%
where the time goes in v9:
time: 104 us; the launch traced here: 103 us
  starting transfers between devices  38 us (37%)
  local copies, waits for them, and re-layouts  20.6 us (20%)
  waiting for transfers between devices  17.6 us (17%)
  Pallas kernels  14.1 us (14%)
  other arithmetic  8.44 us (8%)
  matrix products  3.5 us (3%)
    ppermute x9, starting transfers between devices, send(): return lax.ppermute(value, AXES, pairs_by(fn))  23.9 us
    pallas_call x1, Pallas kernels, leaf_fields(): pl.pallas_call(leaf_kernel, in_specs=[smem, smem, hbm, hbm, vmem, hbm, hb...  14.1 us
    all_to_all x1, waiting for transfers between devices, body(): lax.all_to_all(induced.reshape(owners, capacity, port_count), AXES, split...  8.18 us
    ppermute x9, waiting for transfers between devices, send(): return lax.ppermute(value, AXES, pairs_by(fn))  7.91 us
    all_to_all x1, starting transfers between devices, body(): got = lax.all_to_all(payload, AXES, split_axis=0, concat_axis=0, tiled=True)  7.4 us
    all_to_all x1, starting transfers between devices, body(): lax.all_to_all(induced.reshape(owners, capacity, port_count), AXES, split...  6.71 us
    unnamed x14, local copies, waits for them, and re-layouts  5.98 us
    concatenate x1, other arithmetic, stream_window(): both = jnp.concatenate([edge, core, edge], 1)  3.56 us
  transfers between devices with their start and end apart: 11, of which 4 were waited for; matrix products, arithmetic and copies ran while one was open for 16% of the time, Pallas kernels for 0%

profile of v9, /device:TPU:0, one launch (start us, length us, event | category | flops | bytes accessed | tf_op | source)
XLA Modules:
  0.0 103.1 jit_solution(11219420847587105109)
XLA Ops:
  0.6 0.0 copy-start
  0.6 0.9 fusion.31
  1.5 0.2 convert_reduce_fusion
  1.8 0.0 copy-start.3
  1.8 0.5 fusion.11
  2.2 0.1 reshape.77
  2.3 1.0 copy.43
  3.3 1.6 %fusion.14 = bf16[1024,384]{1,0:T(8,128)(2,1)S(1)} fusion(s32[512]{0:T(512)S(1)} %multiply_add_fusion, bf16[512,128]{1,0:T(8,128)(2,1)} %param.10, bf16[512,256]{1,0:T(8,128)(2,1)S(1)} %bitcast.48), kind=kOutput, calls=%fused_computation.28 | convolution fusion | flops 404357120 | bytes 1181696 | tf_op jit(solution)/shard_map/dot_general | solution.py:228
  4.9 1.0 fusion.22
  6.0 0.0 copy-done.3
  6.0 7.4 %all-to-all-start = ((bf16[16,65,384]{2,1,0:T(8,128)(2,1)}), bf16[16,65,384]{2,1,0:T(8,128)(2,1)}, u32[]{:S(2)}, u32[]{:S(2)}) async-start(bf16[16,65,384]{2,1,0:T(8,128)(2,1)} %fusion.22), calls=%async_computation | async-start | bytes 1769472 | tf_op jit(solution)/shard_map/all_to_all | solution.py:237
  13.4 0.0 copy-done
  13.4 2.0 %constant_dynamic-slice_fusion.1 = f32[128,16,145]{2,1,0:T(8,128)} fusion(f32[128,16,256]{2,1,0:T(8,128)S(1)} %copy-done, s32[]{:T(128)S(6)} %select_n.48), kind=kLoop, calls=%fused_computation.78 | loop fusion | bytes 2375684 | tf_op jit(solution)/shard_map/dynamic-slice
  15.3 2.0 %copy.38 = f32[128,16,145]{0,2,1:T(8,128)S(1)} copy(f32[128,16,145]{2,1,0:T(8,128)} %constant_dynamic-slice_fusion.1) | data formatting | bytes 2375680
  17.3 0.0 copy-start.2
  17.3 1.2 %fusion.40 = (f32[9,145,128]{2,1,0:T(8,128)}, f32[9,145,128]{2,1,0:T(8,128)}) fusion(f32[16,145,128]{2,1,0:T(8,128)S(1)} %bitcast.34), kind=kLoop, calls=%fused_computation.96 | loop fusion | bytes 2672640 | tf_op jit(solution)/shard_map/slice | solution.py:79
  18.5 4.6 %collective-permute-start = (f32[9,145,128]{2,1,0:T(8,128)}, f32[9,145,128]{2,1,0:T(8,128)}, u32[]{:S(2)}, u32[]{:S(2)}) collective-permute-start(f32[9,145,128]{2,1,0:T(8,128)} %get-tuple-element.31), channel_id=1, source_target_pairs={{0,4},{1,5},{2,6},{3,7},{4,8},{5,9},{6,10},{7,11},{8,12},{9,13},{1... | collective-permute-start | bytes 2004488 | tf_op jit(solution)/shard_map/ppermute | solution.py:58
  23.1 1.3 %collective-permute-start.1 = (f32[9,145,128]{2,1,0:T(8,128)}, f32[9,145,128]{2,1,0:T(8,128)}, u32[]{:S(2)}, u32[]{:S(2)}) collective-permute-start(f32[9,145,128]{2,1,0:T(8,128)} %get-tuple-element.30), channel_id=1, source_target_pairs={{4,0},{5,1},{6,2},{7,3},{8,4},{9,5},{10,6},{11,7},{12,8},{13,9},{1... | collective-permute-start | bytes 2004488 | tf_op jit(solution)/shard_map/ppermute | solution.py:58
  24.4 1.3 %constant_dynamic-slice_fusion = f32[128,16,17]{2,1,0:T(8,128)} fusion(f32[128,16,256]{2,1,0:T(8,128)S(1)} %copy-done, s32[]{:T(128)S(6)} %select_n.49), kind=kLoop, calls=%fused_computation.77 | loop fusion | bytes 278532 | tf_op jit(solution)/shard_map/dynamic-slice.1
  25.7 1.6 %copy.39 = f32[128,16,17]{0,2,1:T(8,128)S(1)} copy(f32[128,16,17]{2,1,0:T(8,128)} %constant_dynamic-slice_fusion) | data formatting | bytes 278528
  27.4 1.3 %collective-permute-start.4 = (f32[16,17,128]{2,1,0:T(8,128)S(1)}, f32[16,17,128]{2,1,0:T(8,128)}, u32[]{:S(2)}, u32[]{:S(2)}) collective-permute-start(f32[16,17,128]{2,1,0:T(8,128)S(1)} %bitcast.42), channel_id=1, source_target_pairs={{1,2},{2,1},{5,6},{6,5},{9,10},{10,9},{13,14},{14,13},{17,18},{18,... | collective-permute-start | bytes 417800 | tf_op jit(solution)/shard_map/ppermute | solution.py:58
  28.7 0.7 fusion.42
  29.4 1.3 %collective-permute-start.2 = (f32[9,17,128]{2,1,0:T(8,128)}, f32[9,17,128]{2,1,0:T(8,128)}, u32[]{:S(2)}, u32[]{:S(2)}) collective-permute-start(f32[9,17,128]{2,1,0:T(8,128)} %get-tuple-element.39), channel_id=1, source_target_pairs={{1,6},{2,5},{5,10},{6,9},{9,14},{10,13},{17,22},{18,21},{21,26},{2... | collective-permute-start | bytes 235016 | tf_op jit(solution)/shard_map/ppermute | solution.py:58
  30.7 1.3 %collective-permute-start.3 = (f32[9,17,128]{2,1,0:T(8,128)}, f32[9,17,128]{2,1,0:T(8,128)}, u32[]{:S(2)}, u32[]{:S(2)}) collective-permute-start(f32[9,17,128]{2,1,0:T(8,128)} %get-tuple-element.38), channel_id=1, source_target_pairs={{5,2},{6,1},{9,6},{10,5},{13,10},{14,9},{21,18},{22,17},{25,22},{2... | collective-permute-start | bytes 235016 | tf_op jit(solution)/shard_map/ppermute | solution.py:58
  32.0 0.0 copy-done.2
  32.0 0.6 convert_bitcast_fusion.scale_ref
  32.6 1.5 %all-to-all-done = bf16[16,65,384]{2,1,0:T(8,128)(2,1)} async-done(((bf16[16,65,384]{2,1,0:T(8,128)(2,1)}), bf16[16,65,384]{2,1,0:T(8,128)(2,1)}, u32[]{:S(2)}, u32[]{:S(2)}) %all-to-all-start) | async-done | bytes 798752 | tf_op jit(solution)/shard_map/all_to_all | solution.py:237
  34.2 1.2 %slice.103 = bf16[16,64,384]{2,1,0:T(8,128)(2,1)S(1)} slice(bf16[16,65,384]{2,1,0:T(8,128)(2,1)} %all-to-all-done), slice={[0:16], [0:64], [0:384]} | slice | bytes 1572864 | tf_op jit(solution)/shard_map/slice | solution.py:238
  35.4 0.8 slice_bitcast_fusion
  36.2 0.7 slice.105.cur_hbm
  36.9 0.8 fusion.28
  37.7 0.7 reshape.74.row_leaf_ref
  38.4 0.0 collective-permute-done.2
  38.4 0.0 collective-permute-done.3
  38.4 0.0 collective-permute-done.4
  38.4 5.6 %collective-permute-done = f32[9,145,128]{2,1,0:T(8,128)} collective-permute-done((f32[9,145,128]{2,1,0:T(8,128)}, f32[9,145,128]{2,1,0:T(8,128)}, u32[]{:S(2)}, u32[]{:S(2)}) %collective-permute-start) | collective-permute-done | bytes 668192 | tf_op jit(solution)/shard_map/ppermute | solution.py:58
  44.0 2.3 %collective-permute-done.1 = f32[9,145,128]{2,1,0:T(8,128)} collective-permute-done((f32[9,145,128]{2,1,0:T(8,128)}, f32[9,145,128]{2,1,0:T(8,128)}, u32[]{:S(2)}, u32[]{:S(2)}) %collective-permute-start.1) | collective-permute-done | bytes 668192 | tf_op jit(solution)/shard_map/ppermute | solution.py:58
  46.3 3.6 %fusion.3 = f32[34,162,128]{2,1,0:T(8,128)S(1)} fusion(s32[]{:T(128)S(6)} %select_n.56, f32[9,17,128]{2,1,0:T(8,128)} %collective-permute-done.2, f32[16,17,128]{2,1,0:T(8,128)} %collective-permute-done.4, f32[9,17,128]{2,1,0:T(8,128)} %collective-permute-done.3, f32[9,145,128]{2,1,0:T(8,128)} %collective-permute-done, f32[16,145,128]{2,1,0:T(8,128)S(1)} %bitcast.35, ...), kind=kLoop, calls=%fused_computation.12 | loop fusion | flops 5640192 | bytes 5640196 | tf_op jit(solution)/shard_map/concatenate | solution.py:88
  49.9 0.7 fusion.9
  50.5 0.2 maximum_bitcast_fusion
  50.8 0.0 copy-start.1
  50.8 2.2 %copy.31 = bf16[4,10,2,8,16,128]{5,4,3,2,1,0:T(8,128)(2,1)} copy(bf16[4,10,2,8,16,128]{5,4,1,3,0,2:T(8,128)(2,1)S(1)} %maximum_bitcast_fusion) | data formatting | bytes 5242880 | tf_op jit(solution)/shard_map/transpose | solution.py:24
  53.1 0.0 copy-done.1
  53.1 1.0 copy.34.cpl_t_hbm
  54.1 14.1 %shard_map.77 = (bf16[2,16,128,128]{3,2,1,0:T(8,128)(2,1)}, bf16[1024,128]{1,0:T(8,128)(2,1)}) custom-call(s32[16,8]{1,0:T(8,128)} %bitcast.49, s32[16,8]{1,0:T(8,128)} %convert_bitcast_fusion.scale_ref, bf16[4,10,2,128,128]{4,3,2,1,0:T(8,128)(2,1)} %bitcast.36, bf16[16,8,2,128,128]{4,3,2,1,0:T(8,128)(2,1)} %bitcast.37, s32[1,1024]{1,0:T(1,128)} %reshape.74.row_leaf_ref, ...), custom_call_target="tpu_custom_call" | custom-call | tf_op jit(solution)/shard_map/pallas_call | solution.py:175
  68.2 1.3 %slice_bitcast_fusion.2 = (bf16[16,128,128]{2,1,0:T(8,128)(2,1)S(1)}, bf16[16,128,128]{2,1,0:T(8,128)(2,1)S(1)}) fusion(bf16[2,16,128,128]{3,2,1,0:T(8,128)(2,1)} %get-tuple-element.20), kind=kLoop, calls=%fused_computation.45 | loop fusion | bytes 2097152 | tf_op jit(solution)/shard_map/squeeze | solution.py:93
  69.5 0.6 fusion.41
  70.1 3.8 %collective-permute-start.5 = (bf16[16,1,128]{2,1,0:T(2,128)(2,1)}, bf16[16,1,128]{2,1,0:T(2,128)(2,1)S(1)}, u32[]{:S(2)}, u32[]{:S(2)}) collective-permute-start(bf16[16,1,128]{2,1,0:T(2,128)(2,1)} %get-tuple-element.36), channel_id=1, source_target_pairs={{0,1},{1,2},{2,3},{4,5},{5,6},{6,7},{8,9},{9,10},{10,11},{12,13},{... | collective-permute-start | bytes 12296 | tf_op jit(solution)/shard_map/ppermute | solution.py:58
  73.9 1.3 %collective-permute-start.6 = (bf16[16,1,128]{2,1,0:T(2,128)(2,1)}, bf16[16,1,128]{2,1,0:T(2,128)(2,1)S(1)}, u32[]{:S(2)}, u32[]{:S(2)}) collective-permute-start(bf16[16,1,128]{2,1,0:T(2,128)(2,1)} %get-tuple-element.37), channel_id=1, source_target_pairs={{1,0},{2,1},{3,2},{5,4},{6,5},{7,6},{9,8},{10,9},{11,10},{13,12},{... | collective-permute-start | bytes 12296 | tf_op jit(solution)/shard_map/ppermute | solution.py:58
  75.2 0.8 slice_bitcast_fusion.4
  76.0 7.6 %collective-permute-start.7 = (bf16[1,128,128]{2,1,0:T(8,128)(2,1)S(1)}, bf16[1,128,128]{2,1,0:T(8,128)(2,1)S(1)}, u32[]{:S(2)}, u32[]{:S(2)}) collective-permute-start(bf16[1,128,128]{2,1,0:T(8,128)(2,1)S(1)} %get-tuple-element.34), channel_id=1, source_target_pairs={{0,4},{1,5},{2,6},{3,7},{4,8},{5,9},{6,10},{7,11},{8,12},{9,13},{1... | collective-permute-start | bytes 98312 | tf_op jit(solution)/shard_map/ppermute | solution.py:58
  83.6 1.3 %collective-permute-start.8 = (bf16[1,128,128]{2,1,0:T(8,128)(2,1)S(1)}, bf16[1,128,128]{2,1,0:T(8,128)(2,1)S(1)}, u32[]{:S(2)}, u32[]{:S(2)}) collective-permute-start(bf16[1,128,128]{2,1,0:T(8,128)(2,1)S(1)} %get-tuple-element.35), channel_id=1, source_target_pairs={{4,0},{5,1},{6,2},{7,3},{8,4},{9,5},{10,6},{11,7},{12,8},{13,9},{1... | collective-permute-start | bytes 98312 | tf_op jit(solution)/shard_map/ppermute | solution.py:58
  84.9 6.7 %all-to-all-start.1 = ((bf16[16,64,128]{2,1,0:T(8,128)(2,1)}), bf16[16,64,128]{2,1,0:T(8,128)(2,1)S(1)}, u32[]{:S(2)}, u32[]{:S(2)}) async-start(bf16[16,64,128]{2,1,0:T(8,128)(2,1)} %bitcast.46), calls=%async_computation.1 | async-start | bytes 524288 | tf_op jit(solution)/shard_map/all_to_all | solution.py:262
  91.6 0.0 collective-permute-done.5
  91.7 0.0 collective-permute-done.6
  91.7 0.1 maximum_convert_fusion.1
  91.8 0.0 collective-permute-done.7
  91.8 0.0 collective-permute-done.8
  91.8 0.1 maximum_convert_fusion
  91.9 0.2 fusion.17
  92.1 1.4 %copy.35 = f32[128,16,128]{2,1,0:T(8,128)} copy(f32[128,16,128]{0,2,1:T(8,128)S(1)} %fusion.17) | data formatting | bytes 2097152
  93.5 8.2 %all-to-all-done.1 = bf16[16,64,128]{2,1,0:T(8,128)(2,1)S(1)} async-done(((bf16[16,64,128]{2,1,0:T(8,128)(2,1)}), bf16[16,64,128]{2,1,0:T(8,128)(2,1)S(1)}, u32[]{:S(2)}, u32[]{:S(2)}) %all-to-all-start.1) | async-done | bytes 262176 | tf_op jit(solution)/shard_map/all_to_all | solution.py:262
  101.7 0.0 copy-done.4
  101.7 1.4 %fusion.15 = bf16[512,128]{1,0:T(8,128)(2,1)} fusion(bf16[1024,128]{1,0:T(8,128)(2,1)S(1)} %bitcast.47, s32[512]{0:T(512)S(1)} %copy-done.4), kind=kOutput, calls=%fused_computation.29 | convolution fusion | flops 134807552 | bytes 395264 | tf_op jit(solution)/shard_map/dot_general | solution.py:265
  (4 shorter events, 0.0 us)
Async XLA Ops:
  0.6 12.8 %copy-start = (f32[128,16,256]{2,1,0:T(8,128)S(1)}, f32[128,16,256]{2,1,0:T(8,128)}, u32[]{:S(2)}) copy-start(f32[128,16,256]{2,1,0:T(8,128)} %param.6) | copy-start | bytes 6291460
  1.8 4.2 %copy-start.3 = (s32[512]{0:T(512)}, s32[512]{0:T(512)S(1)}, u32[]{:S(2)}) copy-start(s32[512]{0:T(512)S(1)} %multiply_add_fusion) | copy-start | bytes 6148
  6.0 28.2 %all-to-all-start = ((bf16[16,65,384]{2,1,0:T(8,128)(2,1)}), bf16[16,65,384]{2,1,0:T(8,128)(2,1)}, u32[]{:S(2)}, u32[]{:S(2)}) async-start(bf16[16,65,384]{2,1,0:T(8,128)(2,1)} %fusion.22), calls=%async_computation | async-start | bytes 1769472 | tf_op jit(solution)/shard_map/all_to_all | solution.py:237
  17.3 14.7 %copy-start.2 = (s32[2,8,8]{2,1,0:T(8,128)S(1)}, s32[2,8,8]{2,1,0:T(8,128)}, u32[]{:S(2)}) copy-start(s32[2,8,8]{2,1,0:T(8,128)} %param.8) | copy-start | bytes 1540
  18.5 25.5 %collective-permute-start = (f32[9,145,128]{2,1,0:T(8,128)}, f32[9,145,128]{2,1,0:T(8,128)}, u32[]{:S(2)}, u32[]{:S(2)}) collective-permute-start(f32[9,145,128]{2,1,0:T(8,128)} %get-tuple-element.31), channel_id=1, source_target_pairs={{0,4},{1,5},{2,6},{3,7},{4,8},{5,9},{6,10},{7,11},{8,12},{9,13},{1... | collective-permute-start | bytes 2004488 | tf_op jit(solution)/shard_map/ppermute | solution.py:58
  23.1 23.2 %collective-permute-start.1 = (f32[9,145,128]{2,1,0:T(8,128)}, f32[9,145,128]{2,1,0:T(8,128)}, u32[]{:S(2)}, u32[]{:S(2)}) collective-permute-start(f32[9,145,128]{2,1,0:T(8,128)} %get-tuple-element.30), channel_id=1, source_target_pairs={{4,0},{5,1},{6,2},{7,3},{8,4},{9,5},{10,6},{11,7},{12,8},{13,9},{1... | collective-permute-start | bytes 2004488 | tf_op jit(solution)/shard_map/ppermute | solution.py:58
  27.4 11.0 %collective-permute-start.4 = (f32[16,17,128]{2,1,0:T(8,128)S(1)}, f32[16,17,128]{2,1,0:T(8,128)}, u32[]{:S(2)}, u32[]{:S(2)}) collective-permute-start(f32[16,17,128]{2,1,0:T(8,128)S(1)} %bitcast.42), channel_id=1, source_target_pairs={{1,2},{2,1},{5,6},{6,5},{9,10},{10,9},{13,14},{14,13},{17,18},{18,... | collective-permute-start | bytes 417800 | tf_op jit(solution)/shard_map/ppermute | solution.py:58
  29.4 9.0 %collective-permute-start.2 = (f32[9,17,128]{2,1,0:T(8,128)}, f32[9,17,128]{2,1,0:T(8,128)}, u32[]{:S(2)}, u32[]{:S(2)}) collective-permute-start(f32[9,17,128]{2,1,0:T(8,128)} %get-tuple-element.39), channel_id=1, source_target_pairs={{1,6},{2,5},{5,10},{6,9},{9,14},{10,13},{17,22},{18,21},{21,26},{2... | collective-permute-start | bytes 235016 | tf_op jit(solution)/shard_map/ppermute | solution.py:58
  30.7 7.7 %collective-permute-start.3 = (f32[9,17,128]{2,1,0:T(8,128)}, f32[9,17,128]{2,1,0:T(8,128)}, u32[]{:S(2)}, u32[]{:S(2)}) collective-permute-start(f32[9,17,128]{2,1,0:T(8,128)} %get-tuple-element.38), channel_id=1, source_target_pairs={{5,2},{6,1},{9,6},{10,5},{13,10},{14,9},{21,18},{22,17},{25,22},{2... | collective-permute-start | bytes 235016 | tf_op jit(solution)/shard_map/ppermute | solution.py:58
  50.8 2.3 %copy-start.1 = (bf16[256,1024]{0,1:T(8,128)(2,1)S(1)}, bf16[256,1024]{0,1:T(8,128)(2,1)}, u32[]{:S(2)}) copy-start(bf16[256,1024]{0,1:T(8,128)(2,1)} %slice_bitcast_fusion) | copy-start | bytes 1572868
  70.1 21.6 %collective-permute-start.5 = (bf16[16,1,128]{2,1,0:T(2,128)(2,1)}, bf16[16,1,128]{2,1,0:T(2,128)(2,1)S(1)}, u32[]{:S(2)}, u32[]{:S(2)}) collective-permute-start(bf16[16,1,128]{2,1,0:T(2,128)(2,1)} %get-tuple-element.36), channel_id=1, source_target_pairs={{0,1},{1,2},{2,3},{4,5},{5,6},{6,7},{8,9},{9,10},{10,11},{12,13},{... | collective-permute-start | bytes 12296 | tf_op jit(solution)/shard_map/ppermute | solution.py:58
  73.9 17.7 %collective-permute-start.6 = (bf16[16,1,128]{2,1,0:T(2,128)(2,1)}, bf16[16,1,128]{2,1,0:T(2,128)(2,1)S(1)}, u32[]{:S(2)}, u32[]{:S(2)}) collective-permute-start(bf16[16,1,128]{2,1,0:T(2,128)(2,1)} %get-tuple-element.37), channel_id=1, source_target_pairs={{1,0},{2,1},{3,2},{5,4},{6,5},{7,6},{9,8},{10,9},{11,10},{13,12},{... | collective-permute-start | bytes 12296 | tf_op jit(solution)/shard_map/ppermute | solution.py:58
  76.0 15.8 %collective-permute-start.7 = (bf16[1,128,128]{2,1,0:T(8,128)(2,1)S(1)}, bf16[1,128,128]{2,1,0:T(8,128)(2,1)S(1)}, u32[]{:S(2)}, u32[]{:S(2)}) collective-permute-start(bf16[1,128,128]{2,1,0:T(8,128)(2,1)S(1)} %get-tuple-element.34), channel_id=1, source_target_pairs={{0,4},{1,5},{2,6},{3,7},{4,8},{5,9},{6,10},{7,11},{8,12},{9,13},{1... | collective-permute-start | bytes 98312 | tf_op jit(solution)/shard_map/ppermute | solution.py:58
  83.6 8.2 %collective-permute-start.8 = (bf16[1,128,128]{2,1,0:T(8,128)(2,1)S(1)}, bf16[1,128,128]{2,1,0:T(8,128)(2,1)S(1)}, u32[]{:S(2)}, u32[]{:S(2)}) collective-permute-start(bf16[1,128,128]{2,1,0:T(8,128)(2,1)S(1)} %get-tuple-element.35), channel_id=1, source_target_pairs={{4,0},{5,1},{6,2},{7,3},{8,4},{9,5},{10,6},{11,7},{12,8},{13,9},{1... | collective-permute-start | bytes 98312 | tf_op jit(solution)/shard_map/ppermute | solution.py:58
  84.9 16.8 %all-to-all-start.1 = ((bf16[16,64,128]{2,1,0:T(8,128)(2,1)}), bf16[16,64,128]{2,1,0:T(8,128)(2,1)S(1)}, u32[]{:S(2)}, u32[]{:S(2)}) async-start(bf16[16,64,128]{2,1,0:T(8,128)(2,1)} %bitcast.46), calls=%async_computation.1 | async-start | bytes 524288 | tf_op jit(solution)/shard_map/all_to_all | solution.py:262
  91.9 9.8 %copy-start.4 = (s32[512]{0:T(512)S(1)}, s32[512]{0:T(512)}, u32[]{:S(2)}) copy-start(s32[512]{0:T(512)} %copy-done.3) | copy-start | bytes 6148

commit v10 on v9

--- a/solution.py
+++ b/solution.py
@@ -114,9 +114,16 @@
     field_ref, volt_ref, bord_ref, ind_ref, cpl_t_ref, cur_ref, acc_ref, sems, ind_sems,
 ):
     leaf_count = ind_ref.shape[0]
-    leaf_cols = bord_ref.shape[1] - 2
+    leaf_rows = bord_ref.shape[1] // LEAF_R - 2
+    leaf_cols = bord_ref.shape[2] // LEAF_C - 2
     near_count = ind_ref.shape[1]
     cells = ind_ref.shape[3]
+
+    def tile(r, q):
+        rows = pl.ds(r * LEAF_R, LEAF_R)
+        cols = pl.ds(pl.multiple_of(q * LEAF_C, LEAF_C), LEAF_C)
+        return bord_ref[:, rows, cols, :].reshape(2, cells, -1)
+
     first = [
         pltpu.make_async_copy(bord_hbm, bord_ref, sems.at[0]),
         pltpu.make_async_copy(cpl_t_hbm, cpl_t_ref, sems.at[1]),
@@ -140,11 +147,11 @@
         sources = []
         for n in range(near_count):
             code = codes_ref[leaf, n]
-            src_row = jnp.minimum(jnp.maximum(row + code // 3, 0), bord_ref.shape[0] - 1)
-            src_col = jnp.minimum(jnp.maximum(col + code % 3, 0), bord_ref.shape[1] - 1)
+            src_row = jnp.minimum(jnp.maximum(row + code // 3, 0), leaf_rows + 1)
+            src_col = jnp.minimum(jnp.maximum(col + code % 3, 0), leaf_cols + 1)
             keep = scale_ref[leaf, n] > 0
-            tile = bord_ref[src_row, src_col]
-            sources.append(jnp.where(keep, tile, jnp.zeros_like(tile)))
+            block = tile(src_row, src_col)
+            sources.append(jnp.where(keep, block, jnp.zeros_like(block)))
         for c in range(2):
             weights = jnp.concatenate([ind_ref[leaf, n, c] for n in range(near_count)], axis=1)
             stacked = jnp.concatenate([s[c] for s in sources], axis=0)
@@ -154,7 +161,7 @@
             field_ref[c, pl.ds(row * LEAF_R, LEAF_R), pl.ds(pl.multiple_of(col * LEAF_C, LEAF_C), LEAF_C)] = (
                 total.reshape(LEAF_R, LEAF_C, -1).astype(field_ref.dtype)
             )
-        own = bord_ref[row + 1, col + 1].reshape(2 * cells, -1)
+        own = tile(row + 1, col + 1).reshape(2 * cells, -1)
         acc_ref[...] += lax.dot_general(
             own, coupling_t, (((0,), (0,)), ((), ())), preferred_element_type=jnp.float32
         )
@@ -166,8 +173,8 @@
 
 def leaf_fields(codes, scales, bordered, kernels, row_leaf, coupling_t, current):
     leaf_count, near_count, components, cells, _ = kernels.shape
-    leaf_rows = bordered.shape[0] - 2
-    leaf_cols = bordered.shape[1] - 2
+    leaf_rows = bordered.shape[1] // LEAF_R - 2
+    leaf_cols = bordered.shape[2] // LEAF_C - 2
     slot_count, port_count = current.shape
     smem = pl.BlockSpec(memory_space=pltpu.SMEM)
     hbm = pl.BlockSpec(memory_space=pl.ANY)
@@ -244,8 +251,7 @@
     window, (got_leaf, got_coupling_t, got_current) = stream_window(
         stream.transpose(1, 2, 0), half_cols, (got_leaf, got_coupling_t, got_current)
     )
-    currents = plane_curl(window).astype(jnp.bfloat16)
-    bordered = to_leaves(currents)
+    bordered = plane_curl(window).astype(jnp.bfloat16)
     src_row = jnp.arange(leaf_rows, dtype=jnp.int32)[:, None, None] + near_lists // 3
     src_col = jnp.arange(leaf_cols, dtype=jnp.int32)[None, :, None] + near_lists % 3
     row_ok = ((src_row > 0) | (gx > 0)) & ((src_row < leaf_rows + 1) | (gx < nx - 1))

time: 104 us -> 107 us (1.029)
  other arithmetic: 8.44 us -> 12.3 us
  local copies, waits for them, and re-layouts: 20.6 us -> 19.3 us
    another operation x1 -> x2, other arithmetic: 0.69 us -> 4.78 us  [plane_curl(): return jnp.stack([along_y, along_x])]
    transpose x1 -> x0, local copies, waits for them, and re-layouts: 2.24 us -> none  [to_leaves(): blocks = blocks.transpose(1, 3, 0, 2, 4, 5)]
    unnamed x14 -> x12, local copies, waits for them, and re-layouts: 5.98 us -> 5.98 us
  transfers between devices with their start and end apart: 11 -> 11, of which waited for: 4 -> 4; matrix products, arithmetic and copies ran while one was open for 16% -> 15% of each run, Pallas kernels for 0% -> 0%
where the time goes in v10:
time: 107 us; the launch traced here: 106 us
  starting transfers between devices  38 us (36%)
  local copies, waits for them, and re-layouts  19.3 us (18%)
  waiting for transfers between devices  17.6 us (16%)
  Pallas kernels  14.3 us (13%)
  other arithmetic  12.3 us (11%)
  matrix products  3.5 us (3%)
    ppermute x9, starting transfers between devices, send(): return lax.ppermute(value, AXES, pairs_by(fn))  23.9 us
    pallas_call x1, Pallas kernels, leaf_fields(): pl.pallas_call(leaf_kernel, in_specs=[smem, smem, hbm, hbm, vmem, hbm, hb...  14.3 us
    all_to_all x1, waiting for transfers between devices, body(): lax.all_to_all(induced.reshape(owners, capacity, port_count), AXES, split...  8.18 us
    ppermute x9, waiting for transfers between devices, send(): return lax.ppermute(value, AXES, pairs_by(fn))  7.91 us
    all_to_all x1, starting transfers between devices, body(): got = lax.all_to_all(payload, AXES, split_axis=0, concat_axis=0, tiled=True)  7.4 us
    all_to_all x1, starting transfers between devices, body(): lax.all_to_all(induced.reshape(owners, capacity, port_count), AXES, split...  6.72 us
    unnamed x12, local copies, waits for them, and re-layouts  5.98 us
    another operation x2, other arithmetic, plane_curl(): return jnp.stack([along_y, along_x])  4.78 us
  transfers between devices with their start and end apart: 11, of which 4 were waited for; matrix products, arithmetic and copies ran while one was open for 15% of the time, Pallas kernels for 0%

profile of v10, /device:TPU:0, one launch (start us, length us, event | category | flops | bytes accessed | tf_op | source)
XLA Modules:
  0.0 105.9 jit_solution(15370899367103004148)
XLA Ops:
  0.6 0.0 copy-start
  0.6 0.9 fusion.33
  1.5 0.2 convert_reduce_fusion
  1.8 0.0 copy-start.2
  1.8 0.5 fusion.11
  2.2 0.1 reshape.66
  2.3 1.0 copy.41
  3.3 1.6 %fusion.14 = bf16[1024,384]{1,0:T(8,128)(2,1)S(1)} fusion(s32[512]{0:T(512)S(1)} %multiply_add_fusion, bf16[512,128]{1,0:T(8,128)(2,1)} %param.10, bf16[512,256]{1,0:T(8,128)(2,1)S(1)} %bitcast.44), kind=kOutput, calls=%fused_computation.28 | convolution fusion | flops 404357120 | bytes 1181696 | tf_op jit(solution)/shard_map/dot_general | solution.py:235
  4.9 1.0 fusion.24
  5.9 0.0 copy-done.2
  5.9 7.4 %all-to-all-start = ((bf16[16,65,384]{2,1,0:T(8,128)(2,1)}), bf16[16,65,384]{2,1,0:T(8,128)(2,1)}, u32[]{:S(2)}, u32[]{:S(2)}) async-start(bf16[16,65,384]{2,1,0:T(8,128)(2,1)} %fusion.24), calls=%async_computation | async-start | bytes 1769472 | tf_op jit(solution)/shard_map/all_to_all | solution.py:244
  13.4 0.0 copy-done
  13.4 1.9 %constant_dynamic-slice_fusion.1 = f32[128,16,145]{2,1,0:T(8,128)} fusion(f32[128,16,256]{2,1,0:T(8,128)S(1)} %copy-done, s32[]{:T(128)S(6)} %select_n.48), kind=kLoop, calls=%fused_computation.80 | loop fusion | bytes 2375684 | tf_op jit(solution)/shard_map/dynamic-slice
  15.3 2.0 %copy.36 = f32[128,16,145]{0,2,1:T(8,128)S(1)} copy(f32[128,16,145]{2,1,0:T(8,128)} %constant_dynamic-slice_fusion.1) | data formatting | bytes 2375680
  17.3 0.0 copy-start.1
  17.3 1.2 %fusion.42 = (f32[9,145,128]{2,1,0:T(8,128)}, f32[9,145,128]{2,1,0:T(8,128)}) fusion(f32[16,145,128]{2,1,0:T(8,128)S(1)} %bitcast.33), kind=kLoop, calls=%fused_computation.98 | loop fusion | bytes 2672640 | tf_op jit(solution)/shard_map/slice | solution.py:79
  18.5 4.6 %collective-permute-start = (f32[9,145,128]{2,1,0:T(8,128)}, f32[9,145,128]{2,1,0:T(8,128)}, u32[]{:S(2)}, u32[]{:S(2)}) collective-permute-start(f32[9,145,128]{2,1,0:T(8,128)} %get-tuple-element.31), channel_id=1, source_target_pairs={{0,4},{1,5},{2,6},{3,7},{4,8},{5,9},{6,10},{7,11},{8,12},{9,13},{1... | collective-permute-start | bytes 2004488 | tf_op jit(solution)/shard_map/ppermute | solution.py:58
  23.1 1.3 %collective-permute-start.1 = (f32[9,145,128]{2,1,0:T(8,128)}, f32[9,145,128]{2,1,0:T(8,128)}, u32[]{:S(2)}, u32[]{:S(2)}) collective-permute-start(f32[9,145,128]{2,1,0:T(8,128)} %get-tuple-element.30), channel_id=1, source_target_pairs={{4,0},{5,1},{6,2},{7,3},{8,4},{9,5},{10,6},{11,7},{12,8},{13,9},{1... | collective-permute-start | bytes 2004488 | tf_op jit(solution)/shard_map/ppermute | solution.py:58
  24.4 1.3 %constant_dynamic-slice_fusion = f32[128,16,17]{2,1,0:T(8,128)} fusion(f32[128,16,256]{2,1,0:T(8,128)S(1)} %copy-done, s32[]{:T(128)S(6)} %select_n.49), kind=kLoop, calls=%fused_computation.79 | loop fusion | bytes 278532 | tf_op jit(solution)/shard_map/dynamic-slice.1
  25.7 1.6 %copy.37 = f32[128,16,17]{0,2,1:T(8,128)S(1)} copy(f32[128,16,17]{2,1,0:T(8,128)} %constant_dynamic-slice_fusion) | data formatting | bytes 278528
  27.3 1.3 %collective-permute-start.4 = (f32[16,17,128]{2,1,0:T(8,128)S(1)}, f32[16,17,128]{2,1,0:T(8,128)}, u32[]{:S(2)}, u32[]{:S(2)}) collective-permute-start(f32[16,17,128]{2,1,0:T(8,128)S(1)} %bitcast.38), channel_id=1, source_target_pairs={{1,2},{2,1},{5,6},{6,5},{9,10},{10,9},{13,14},{14,13},{17,18},{18,... | collective-permute-start | bytes 417800 | tf_op jit(solution)/shard_map/ppermute | solution.py:58
  28.7 0.7 fusion.44
  29.4 1.3 %collective-permute-start.2 = (f32[9,17,128]{2,1,0:T(8,128)}, f32[9,17,128]{2,1,0:T(8,128)}, u32[]{:S(2)}, u32[]{:S(2)}) collective-permute-start(f32[9,17,128]{2,1,0:T(8,128)} %get-tuple-element.39), channel_id=1, source_target_pairs={{1,6},{2,5},{5,10},{6,9},{9,14},{10,13},{17,22},{18,21},{21,26},{2... | collective-permute-start | bytes 235016 | tf_op jit(solution)/shard_map/ppermute | solution.py:58
  30.7 1.3 %collective-permute-start.3 = (f32[9,17,128]{2,1,0:T(8,128)}, f32[9,17,128]{2,1,0:T(8,128)}, u32[]{:S(2)}, u32[]{:S(2)}) collective-permute-start(f32[9,17,128]{2,1,0:T(8,128)} %get-tuple-element.38), channel_id=1, source_target_pairs={{5,2},{6,1},{9,6},{10,5},{13,10},{14,9},{21,18},{22,17},{25,22},{2... | collective-permute-start | bytes 235016 | tf_op jit(solution)/shard_map/ppermute | solution.py:58
  32.0 0.0 copy-done.1
  32.0 0.6 convert_bitcast_fusion.scale_ref
  32.6 1.5 %all-to-all-done = bf16[16,65,384]{2,1,0:T(8,128)(2,1)} async-done(((bf16[16,65,384]{2,1,0:T(8,128)(2,1)}), bf16[16,65,384]{2,1,0:T(8,128)(2,1)}, u32[]{:S(2)}, u32[]{:S(2)}) %all-to-all-start) | async-done | bytes 798752 | tf_op jit(solution)/shard_map/all_to_all | solution.py:244
  34.1 1.2 %slice.103 = bf16[16,64,384]{2,1,0:T(8,128)(2,1)S(1)} slice(bf16[16,65,384]{2,1,0:T(8,128)(2,1)} %all-to-all-done), slice={[0:16], [0:64], [0:384]} | slice | bytes 1572864 | tf_op jit(solution)/shard_map/slice | solution.py:245
  35.4 0.8 slice_bitcast_fusion
  36.2 0.7 slice.105.cur_hbm
  36.9 0.8 fusion.30
  37.7 0.7 reshape.63.row_leaf_ref
  38.3 0.0 collective-permute-done.2
  38.3 0.0 collective-permute-done.3
  38.4 0.0 collective-permute-done.4
  38.4 5.7 %collective-permute-done = f32[9,145,128]{2,1,0:T(8,128)} collective-permute-done((f32[9,145,128]{2,1,0:T(8,128)}, f32[9,145,128]{2,1,0:T(8,128)}, u32[]{:S(2)}, u32[]{:S(2)}) %collective-permute-start) | collective-permute-done | bytes 668192 | tf_op jit(solution)/shard_map/ppermute | solution.py:58
  44.0 2.2 %collective-permute-done.1 = f32[9,145,128]{2,1,0:T(8,128)} collective-permute-done((f32[9,145,128]{2,1,0:T(8,128)}, f32[9,145,128]{2,1,0:T(8,128)}, u32[]{:S(2)}, u32[]{:S(2)}) %collective-permute-start.1) | collective-permute-done | bytes 668192 | tf_op jit(solution)/shard_map/ppermute | solution.py:58
  46.2 3.6 %fusion.3 = f32[34,162,128]{2,1,0:T(8,128)S(1)} fusion(s32[]{:T(128)S(6)} %select_n.56, f32[9,17,128]{2,1,0:T(8,128)} %collective-permute-done.2, f32[16,17,128]{2,1,0:T(8,128)} %collective-permute-done.4, f32[9,17,128]{2,1,0:T(8,128)} %collective-permute-done.3, f32[9,145,128]{2,1,0:T(8,128)} %collective-permute-done, f32[16,145,128]{2,1,0:T(8,128)S(1)} %bitcast.34, ...), kind=kLoop, calls=%fused_computation.12 | loop fusion | flops 5640192 | bytes 5640196 | tf_op jit(solution)/shard_map/concatenate | solution.py:88
  49.8 1.7 %fusion.15 = (bf16[1,32,160,128]{3,2,1,0:T(8,128)(2,1)S(1)}, bf16[1,32,160,128]{3,2,1,0:T(8,128)(2,1)}) fusion(f32[34,162,128]{2,1,0:T(8,128)S(1)} %fusion.3), kind=kLoop, calls=%fused_computation.29 | loop fusion | flops 2621440 | bytes 13107200 | tf_op jit(solution)/shard_map/stack | solution.py:16
  51.5 2.0 %copy.32.cpl_t_hbm = bf16[256,1024]{1,0:T(8,128)(2,1)} copy(bf16[256,1024]{0,1:T(8,128)(2,1)} %slice_bitcast_fusion) | data formatting | bytes 1048576 | tf_op jit(solution)/shard_map/optimization_barrier | solution.py:83
  53.6 3.0 %pad_maximum_fusion.bord_hbm = bf16[2,32,160,128]{3,2,1,0:T(8,128)(2,1)} fusion(bf16[1,32,160,128]{3,2,1,0:T(8,128)(2,1)} %get-tuple-element.29, bf16[1,32,160,128]{3,2,1,0:T(8,128)(2,1)S(1)} %get-tuple-element.28), kind=kLoop, calls=%fused_computation.21 | loop fusion | flops 1310720 | bytes 5242880 | tf_op jit(solution)/shard_map/stack | solution.py:16
  56.6 14.3 %shard_map.77 = (bf16[2,16,128,128]{3,2,1,0:T(8,128)(2,1)}, bf16[1024,128]{1,0:T(8,128)(2,1)}) custom-call(s32[16,8]{1,0:T(8,128)} %bitcast.45, s32[16,8]{1,0:T(8,128)} %convert_bitcast_fusion.scale_ref, bf16[2,32,160,128]{3,2,1,0:T(8,128)(2,1)} %pad_maximum_fusion.bord_hbm, bf16[16,8,2,128,128]{4,3,2,1,0:T(8,128)(2,1)} %bitcast.35, ...), custom_call_target="tpu_custom_call" | custom-call | tf_op jit(solution)/shard_map/pallas_call | solution.py:182
  70.9 1.3 %slice_bitcast_fusion.2 = (bf16[16,128,128]{2,1,0:T(8,128)(2,1)S(1)}, bf16[16,128,128]{2,1,0:T(8,128)(2,1)S(1)}) fusion(bf16[2,16,128,128]{3,2,1,0:T(8,128)(2,1)} %get-tuple-element.20), kind=kLoop, calls=%fused_computation.47 | loop fusion | bytes 2097152 | tf_op jit(solution)/shard_map/squeeze | solution.py:93
  72.2 0.6 fusion.43
  72.8 3.8 %collective-permute-start.5 = (bf16[16,1,128]{2,1,0:T(2,128)(2,1)}, bf16[16,1,128]{2,1,0:T(2,128)(2,1)S(1)}, u32[]{:S(2)}, u32[]{:S(2)}) collective-permute-start(bf16[16,1,128]{2,1,0:T(2,128)(2,1)} %get-tuple-element.36), channel_id=1, source_target_pairs={{0,1},{1,2},{2,3},{4,5},{5,6},{6,7},{8,9},{9,10},{10,11},{12,13},{... | collective-permute-start | bytes 12296 | tf_op jit(solution)/shard_map/ppermute | solution.py:58
  76.6 1.3 %collective-permute-start.6 = (bf16[16,1,128]{2,1,0:T(2,128)(2,1)}, bf16[16,1,128]{2,1,0:T(2,128)(2,1)S(1)}, u32[]{:S(2)}, u32[]{:S(2)}) collective-permute-start(bf16[16,1,128]{2,1,0:T(2,128)(2,1)} %get-tuple-element.37), channel_id=1, source_target_pairs={{1,0},{2,1},{3,2},{5,4},{6,5},{7,6},{9,8},{10,9},{11,10},{13,12},{... | collective-permute-start | bytes 12296 | tf_op jit(solution)/shard_map/ppermute | solution.py:58
  77.9 0.8 slice_bitcast_fusion.4
  78.7 7.7 %collective-permute-start.7 = (bf16[1,128,128]{2,1,0:T(8,128)(2,1)S(1)}, bf16[1,128,128]{2,1,0:T(8,128)(2,1)S(1)}, u32[]{:S(2)}, u32[]{:S(2)}) collective-permute-start(bf16[1,128,128]{2,1,0:T(8,128)(2,1)S(1)} %get-tuple-element.34), channel_id=1, source_target_pairs={{0,4},{1,5},{2,6},{3,7},{4,8},{5,9},{6,10},{7,11},{8,12},{9,13},{1... | collective-permute-start | bytes 98312 | tf_op jit(solution)/shard_map/ppermute | solution.py:58
  86.3 1.3 %collective-permute-start.8 = (bf16[1,128,128]{2,1,0:T(8,128)(2,1)S(1)}, bf16[1,128,128]{2,1,0:T(8,128)(2,1)S(1)}, u32[]{:S(2)}, u32[]{:S(2)}) collective-permute-start(bf16[1,128,128]{2,1,0:T(8,128)(2,1)S(1)} %get-tuple-element.35), channel_id=1, source_target_pairs={{4,0},{5,1},{6,2},{7,3},{8,4},{9,5},{10,6},{11,7},{12,8},{13,9},{1... | collective-permute-start | bytes 98312 | tf_op jit(solution)/shard_map/ppermute | solution.py:58
  87.6 6.7 %all-to-all-start.1 = ((bf16[16,64,128]{2,1,0:T(8,128)(2,1)}), bf16[16,64,128]{2,1,0:T(8,128)(2,1)S(1)}, u32[]{:S(2)}, u32[]{:S(2)}) async-start(bf16[16,64,128]{2,1,0:T(8,128)(2,1)} %bitcast.42), calls=%async_computation.1 | async-start | bytes 524288 | tf_op jit(solution)/shard_map/all_to_all | solution.py:268
  94.4 0.0 collective-permute-done.5
  94.4 0.0 collective-permute-done.6
  94.4 0.1 maximum_convert_fusion.1
  94.5 0.0 collective-permute-done.7
  94.5 0.0 collective-permute-done.8
  94.6 0.1 maximum_convert_fusion
  94.7 0.0 copy-start.3
  94.7 0.2 fusion.19
  94.9 1.4 %copy.33 = f32[128,16,128]{2,1,0:T(8,128)} copy(f32[128,16,128]{0,2,1:T(8,128)S(1)} %fusion.19) | data formatting | bytes 2097152
  96.2 8.2 %all-to-all-done.1 = bf16[16,64,128]{2,1,0:T(8,128)(2,1)S(1)} async-done(((bf16[16,64,128]{2,1,0:T(8,128)(2,1)}), bf16[16,64,128]{2,1,0:T(8,128)(2,1)S(1)}, u32[]{:S(2)}, u32[]{:S(2)}) %all-to-all-start.1) | async-done | bytes 262176 | tf_op jit(solution)/shard_map/all_to_all | solution.py:268
  104.4 0.0 copy-done.3
  104.4 1.4 %fusion.17 = bf16[512,128]{1,0:T(8,128)(2,1)} fusion(bf16[1024,128]{1,0:T(8,128)(2,1)S(1)} %bitcast.43, s32[512]{0:T(512)S(1)} %copy-done.3), kind=kOutput, calls=%fused_computation.31 | convolution fusion | flops 134807552 | bytes 395264 | tf_op jit(solution)/shard_map/dot_general | solution.py:271
  (3 shorter events, 0.0 us)
Async XLA Ops:
  0.6 12.7 %copy-start = (f32[128,16,256]{2,1,0:T(8,128)S(1)}, f32[128,16,256]{2,1,0:T(8,128)}, u32[]{:S(2)}) copy-start(f32[128,16,256]{2,1,0:T(8,128)} %param.6) | copy-start | bytes 6291460
  1.8 4.2 %copy-start.2 = (s32[512]{0:T(512)}, s32[512]{0:T(512)S(1)}, u32[]{:S(2)}) copy-start(s32[512]{0:T(512)S(1)} %multiply_add_fusion) | copy-start | bytes 6148
  5.9 28.2 %all-to-all-start = ((bf16[16,65,384]{2,1,0:T(8,128)(2,1)}), bf16[16,65,384]{2,1,0:T(8,128)(2,1)}, u32[]{:S(2)}, u32[]{:S(2)}) async-start(bf16[16,65,384]{2,1,0:T(8,128)(2,1)} %fusion.24), calls=%async_computation | async-start | bytes 1769472 | tf_op jit(solution)/shard_map/all_to_all | solution.py:244
  17.3 14.7 %copy-start.1 = (s32[2,8,8]{2,1,0:T(8,128)S(1)}, s32[2,8,8]{2,1,0:T(8,128)}, u32[]{:S(2)}) copy-start(s32[2,8,8]{2,1,0:T(8,128)} %param.8) | copy-start | bytes 1540
  18.5 25.6 %collective-permute-start = (f32[9,145,128]{2,1,0:T(8,128)}, f32[9,145,128]{2,1,0:T(8,128)}, u32[]{:S(2)}, u32[]{:S(2)}) collective-permute-start(f32[9,145,128]{2,1,0:T(8,128)} %get-tuple-element.31), channel_id=1, source_target_pairs={{0,4},{1,5},{2,6},{3,7},{4,8},{5,9},{6,10},{7,11},{8,12},{9,13},{1... | collective-permute-start | bytes 2004488 | tf_op jit(solution)/shard_map/ppermute | solution.py:58
  23.1 23.1 %collective-permute-start.1 = (f32[9,145,128]{2,1,0:T(8,128)}, f32[9,145,128]{2,1,0:T(8,128)}, u32[]{:S(2)}, u32[]{:S(2)}) collective-permute-start(f32[9,145,128]{2,1,0:T(8,128)} %get-tuple-element.30), channel_id=1, source_target_pairs={{4,0},{5,1},{6,2},{7,3},{8,4},{9,5},{10,6},{11,7},{12,8},{13,9},{1... | collective-permute-start | bytes 2004488 | tf_op jit(solution)/shard_map/ppermute | solution.py:58
  27.3 11.0 %collective-permute-start.4 = (f32[16,17,128]{2,1,0:T(8,128)S(1)}, f32[16,17,128]{2,1,0:T(8,128)}, u32[]{:S(2)}, u32[]{:S(2)}) collective-permute-start(f32[16,17,128]{2,1,0:T(8,128)S(1)} %bitcast.38), channel_id=1, source_target_pairs={{1,2},{2,1},{5,6},{6,5},{9,10},{10,9},{13,14},{14,13},{17,18},{18,... | collective-permute-start | bytes 417800 | tf_op jit(solution)/shard_map/ppermute | solution.py:58
  29.4 9.0 %collective-permute-start.2 = (f32[9,17,128]{2,1,0:T(8,128)}, f32[9,17,128]{2,1,0:T(8,128)}, u32[]{:S(2)}, u32[]{:S(2)}) collective-permute-start(f32[9,17,128]{2,1,0:T(8,128)} %get-tuple-element.39), channel_id=1, source_target_pairs={{1,6},{2,5},{5,10},{6,9},{9,14},{10,13},{17,22},{18,21},{21,26},{2... | collective-permute-start | bytes 235016 | tf_op jit(solution)/shard_map/ppermute | solution.py:58
  30.7 7.7 %collective-permute-start.3 = (f32[9,17,128]{2,1,0:T(8,128)}, f32[9,17,128]{2,1,0:T(8,128)}, u32[]{:S(2)}, u32[]{:S(2)}) collective-permute-start(f32[9,17,128]{2,1,0:T(8,128)} %get-tuple-element.38), channel_id=1, source_target_pairs={{5,2},{6,1},{9,6},{10,5},{13,10},{14,9},{21,18},{22,17},{25,22},{2... | collective-permute-start | bytes 235016 | tf_op jit(solution)/shard_map/ppermute | solution.py:58
  72.8 21.6 %collective-permute-start.5 = (bf16[16,1,128]{2,1,0:T(2,128)(2,1)}, bf16[16,1,128]{2,1,0:T(2,128)(2,1)S(1)}, u32[]{:S(2)}, u32[]{:S(2)}) collective-permute-start(bf16[16,1,128]{2,1,0:T(2,128)(2,1)} %get-tuple-element.36), channel_id=1, source_target_pairs={{0,1},{1,2},{2,3},{4,5},{5,6},{6,7},{8,9},{9,10},{10,11},{12,13},{... | collective-permute-start | bytes 12296 | tf_op jit(solution)/shard_map/ppermute | solution.py:58
  76.6 17.8 %collective-permute-start.6 = (bf16[16,1,128]{2,1,0:T(2,128)(2,1)}, bf16[16,1,128]{2,1,0:T(2,128)(2,1)S(1)}, u32[]{:S(2)}, u32[]{:S(2)}) collective-permute-start(bf16[16,1,128]{2,1,0:T(2,128)(2,1)} %get-tuple-element.37), channel_id=1, source_target_pairs={{1,0},{2,1},{3,2},{5,4},{6,5},{7,6},{9,8},{10,9},{11,10},{13,12},{... | collective-permute-start | bytes 12296 | tf_op jit(solution)/shard_map/ppermute | solution.py:58
  78.7 15.9 %collective-permute-start.7 = (bf16[1,128,128]{2,1,0:T(8,128)(2,1)S(1)}, bf16[1,128,128]{2,1,0:T(8,128)(2,1)S(1)}, u32[]{:S(2)}, u32[]{:S(2)}) collective-permute-start(bf16[1,128,128]{2,1,0:T(8,128)(2,1)S(1)} %get-tuple-element.34), channel_id=1, source_target_pairs={{0,4},{1,5},{2,6},{3,7},{4,8},{5,9},{6,10},{7,11},{8,12},{9,13},{1... | collective-permute-start | bytes 98312 | tf_op jit(solution)/shard_map/ppermute | solution.py:58
  86.3 8.2 %collective-permute-start.8 = (bf16[1,128,128]{2,1,0:T(8,128)(2,1)S(1)}, bf16[1,128,128]{2,1,0:T(8,128)(2,1)S(1)}, u32[]{:S(2)}, u32[]{:S(2)}) collective-permute-start(bf16[1,128,128]{2,1,0:T(8,128)(2,1)S(1)} %get-tuple-element.35), channel_id=1, source_target_pairs={{4,0},{5,1},{6,2},{7,3},{8,4},{9,5},{10,6},{11,7},{12,8},{13,9},{1... | collective-permute-start | bytes 98312 | tf_op jit(solution)/shard_map/ppermute | solution.py:58
  87.6 16.8 %all-to-all-start.1 = ((bf16[16,64,128]{2,1,0:T(8,128)(2,1)}), bf16[16,64,128]{2,1,0:T(8,128)(2,1)S(1)}, u32[]{:S(2)}, u32[]{:S(2)}) async-start(bf16[16,64,128]{2,1,0:T(8,128)(2,1)} %bitcast.42), calls=%async_computation.1 | async-start | bytes 524288 | tf_op jit(solution)/shard_map/all_to_all | solution.py:268
  94.7 9.8 %copy-start.3 = (s32[512]{0:T(512)S(1)}, s32[512]{0:T(512)}, u32[]{:S(2)}) copy-start(s32[512]{0:T(512)} %copy-done.2) | copy-start | bytes 6148

commit v11 on v9

--- a/solution.py
+++ b/solution.py
@@ -75,18 +75,13 @@
     mid = lax.dynamic_slice_in_dim(stream, gz * (width - mid_w), mid_w, 1)
     side = lax.dynamic_slice_in_dim(stream, gz * (width - hc), hc, 1)
     h_got = send(side, lambda x, y, z: sideways(x, y, z, 0))
-    v_top = send(mid[rows - hr :], lambda x, y, z: (x + 1, y, z))
-    v_bot = send(mid[:hr], lambda x, y, z: (x - 1, y, z))
-    d_top = send(side[rows - hr :], lambda x, y, z: sideways(x, y, z, 1))
-    d_bot = send(side[:hr], lambda x, y, z: sideways(x, y, z, -1))
-
-    (v_top, v_bot, d_top, d_bot, h_got), ready = lax.optimization_barrier(
-        ((v_top, v_bot, d_top, d_bot, h_got), ready)
-    )
-    core = jnp.concatenate([v_top, mid, v_bot], 0)
-    edge = jnp.concatenate([d_top, h_got, d_bot], 0)
-    both = jnp.concatenate([edge, core, edge], 1)
-    return lax.dynamic_slice_in_dim(both, gz * hc, mid_w + hc, 1), ready
+    wide = lax.dynamic_slice_in_dim(
+        jnp.concatenate([h_got, mid, h_got], 1), gz * hc, mid_w + hc, 1
+    )
+    v_top = send(wide[rows - hr :], lambda x, y, z: (x + 1, y, z))
+    v_bot = send(wide[:hr], lambda x, y, z: (x - 1, y, z))
+    (v_top, v_bot), ready = lax.optimization_barrier(((v_top, v_bot), ready))
+    return jnp.concatenate([v_top, wide, v_bot], 0), ready
 
 
 def field_halo(grid_field):

time: 104 us -> 102 us (0.981)
  starting transfers between devices: 38 us -> 33.9 us
  waiting for transfers between devices: 17.6 us -> 19.4 us
    ppermute x9 -> x7, starting transfers between devices: 23.9 us -> 19 us  [send(): return lax.ppermute(value, AXES, pairs_by(fn))]
    all_to_all x1, waiting for transfers between devices: 1.55 us -> 3.76 us  [body(): got = lax.all_to_all(payload, AXES, split_axis=0, concat_axis=0, tiled=True)]
    unnamed x14 -> x18, local copies, waits for them, and re-layouts: 5.98 us -> 7.17 us
    transpose x1, local copies, waits for them, and re-layouts: 0.83 us -> 1.88 us  [body(): got_coupling_t = got_rows[:, :2 * leaf_cells].T]
    ppermute x9 -> x7, waiting for transfers between devices: 7.91 us -> 7.49 us  [send(): return lax.ppermute(value, AXES, pairs_by(fn))]
    concatenate x1 -> x2, other arithmetic: 3.56 us -> 3.47 us  [the longest x1 1.91 us: stream_window(): jnp.concatenate([h_got, mid, h_got], 1)]
  transfers between devices with their start and end apart: 11 -> 9, of which waited for: 4 -> 4; matrix products, arithmetic and copies ran while one was open for 16% -> 17% of each run, Pallas kernels for 0% -> 0%
where the time goes in v11:
time: 102 us; the launch traced here: 101 us
  starting transfers between devices  33.9 us (33%)
  local copies, waits for them, and re-layouts  21.1 us (21%)
  waiting for transfers between devices  19.4 us (19%)
  Pallas kernels  14.1 us (14%)
  other arithmetic  8.33 us (8%)
  matrix products  3.5 us (3%)
    ppermute x7, starting transfers between devices, send(): return lax.ppermute(value, AXES, pairs_by(fn))  19 us
    pallas_call x1, Pallas kernels, leaf_fields(): pl.pallas_call(leaf_kernel, in_specs=[smem, smem, hbm, hbm, vmem, hbm, hb...  14.1 us
    all_to_all x1, waiting for transfers between devices, body(): lax.all_to_all(induced.reshape(owners, capacity, port_count), AXES, split...  8.18 us
    all_to_all x1, starting transfers between devices, body(): lax.all_to_all(induced.reshape(owners, capacity, port_count), AXES, split...  7.52 us
    ppermute x7, waiting for transfers between devices, send(): return lax.ppermute(value, AXES, pairs_by(fn))  7.49 us
    all_to_all x1, starting transfers between devices, body(): got = lax.all_to_all(payload, AXES, split_axis=0, concat_axis=0, tiled=True)  7.4 us
    unnamed x18, local copies, waits for them, and re-layouts  7.17 us
    all_to_all x1, waiting for transfers between devices, body(): got = lax.all_to_all(payload, AXES, split_axis=0, concat_axis=0, tiled=True)  3.76 us
  transfers between devices with their start and end apart: 9, of which 4 were waited for; matrix products, arithmetic and copies ran while one was open for 17% of the time, Pallas kernels for 0%

profile of v11, /device:TPU:0, one launch (start us, length us, event | category | flops | bytes accessed | tf_op | source)
XLA Modules:
  0.0 101.4 jit_solution(7470322856028575194)
XLA Ops:
  0.6 0.0 copy-start
  0.6 0.9 fusion.25
  1.5 0.2 convert_reduce_fusion
  1.8 0.0 copy-start.5
  1.8 0.5 fusion.3
  2.2 0.1 reshape.77
  2.3 1.0 copy.43
  3.3 1.6 %fusion.6 = bf16[1024,384]{1,0:T(8,128)(2,1)S(1)} fusion(s32[512]{0:T(512)S(1)} %multiply_add_fusion, bf16[512,128]{1,0:T(8,128)(2,1)} %param.10, bf16[512,256]{1,0:T(8,128)(2,1)S(1)} %bitcast.44), kind=kOutput, calls=%fused_computation.15 | convolution fusion | flops 404357120 | bytes 1181696 | tf_op jit(solution)/shard_map/dot_general | solution.py:223
  4.9 1.0 fusion.16
  5.9 0.0 copy-done.5
  5.9 7.4 %all-to-all-start = ((bf16[16,65,384]{2,1,0:T(8,128)(2,1)}), bf16[16,65,384]{2,1,0:T(8,128)(2,1)}, u32[]{:S(2)}, u32[]{:S(2)}) async-start(bf16[16,65,384]{2,1,0:T(8,128)(2,1)} %fusion.16), calls=%async_computation | async-start | bytes 1769472 | tf_op jit(solution)/shard_map/all_to_all | solution.py:232
  13.4 0.0 copy-done
  13.4 0.3 constant_dynamic-slice_fusion.1
  13.7 0.4 copy.38
  14.2 0.7 collective-permute-start
  14.8 1.9 %constant_dynamic-slice_fusion = f32[128,16,145]{2,1,0:T(8,128)} fusion(f32[128,16,256]{2,1,0:T(8,128)S(1)} %copy-done, s32[]{:T(128)S(6)} %select_n.49), kind=kLoop, calls=%fused_computation.79 | loop fusion | bytes 2375684 | tf_op jit(solution)/shard_map/dynamic-slice.1
  16.7 2.8 %copy.39 = f32[128,16,145]{0,2,1:T(8,128)} copy(f32[128,16,145]{2,1,0:T(8,128)} %constant_dynamic-slice_fusion) | data formatting | bytes 2375680
  19.5 0.0 collective-permute-done
  19.5 0.7 copy-done.3
  20.2 1.9 %fusion.8 = f32[16,162,128]{2,1,0:T(8,128)S(1)} fusion(s32[]{:T(128)S(6)} %select_n.50, f32[16,17,128]{2,1,0:T(8,128)} %copy-done.3, f32[16,145,128]{2,1,0:T(8,128)} %bitcast.38), kind=kLoop, calls=%fused_computation.17 | loop fusion | flops 663552 | bytes 2654212 | tf_op jit(solution)/shard_map/concatenate | solution.py:79
  22.1 0.0 copy-start.4
  22.1 1.2 %fusion.34 = (f32[9,162,128]{2,1,0:T(8,128)}, f32[9,162,128]{2,1,0:T(8,128)}) fusion(f32[16,162,128]{2,1,0:T(8,128)S(1)} %fusion.8), kind=kLoop, calls=%fused_computation.85 | loop fusion | bytes 2985984 | tf_op jit(solution)/shard_map/slice | solution.py:82
  23.4 4.6 %collective-permute-start.1 = (f32[9,162,128]{2,1,0:T(8,128)}, f32[9,162,128]{2,1,0:T(8,128)}, u32[]{:S(2)}, u32[]{:S(2)}) collective-permute-start(f32[9,162,128]{2,1,0:T(8,128)} %get-tuple-element.25), channel_id=1, source_target_pairs={{0,4},{1,5},{2,6},{3,7},{4,8},{5,9},{6,10},{7,11},{8,12},{9,13},{1... | collective-permute-start | bytes 2239496 | tf_op jit(solution)/shard_map/ppermute | solution.py:58
  28.0 1.3 %collective-permute-start.2 = (f32[9,162,128]{2,1,0:T(8,128)}, f32[9,162,128]{2,1,0:T(8,128)}, u32[]{:S(2)}, u32[]{:S(2)}) collective-permute-start(f32[9,162,128]{2,1,0:T(8,128)} %get-tuple-element.24), channel_id=1, source_target_pairs={{4,0},{5,1},{6,2},{7,3},{8,4},{9,5},{10,6},{11,7},{12,8},{13,9},{1... | collective-permute-start | bytes 2239496 | tf_op jit(solution)/shard_map/ppermute | solution.py:58
  29.3 0.0 copy-done.4
  29.3 0.6 convert_bitcast_fusion.scale_ref
  30.0 3.8 %all-to-all-done = bf16[16,65,384]{2,1,0:T(8,128)(2,1)} async-done(((bf16[16,65,384]{2,1,0:T(8,128)(2,1)}), bf16[16,65,384]{2,1,0:T(8,128)(2,1)}, u32[]{:S(2)}, u32[]{:S(2)}) %all-to-all-start) | async-done | bytes 798752 | tf_op jit(solution)/shard_map/all_to_all | solution.py:232
  33.7 1.2 %slice.93 = bf16[16,64,384]{2,1,0:T(8,128)(2,1)S(1)} slice(bf16[16,65,384]{2,1,0:T(8,128)(2,1)} %all-to-all-done), slice={[0:16], [0:64], [0:384]} | slice | bytes 1572864 | tf_op jit(solution)/shard_map/slice | solution.py:233
  34.9 0.0 copy-start.1
  35.0 0.9 copy-done.1
  35.8 0.7 slice.95.cur_hbm
  36.5 0.8 fusion.22
  37.3 0.7 reshape.74.row_leaf_ref
  38.0 1.9 %slice_bitcast_fusion = bf16[256,1024]{0,1:T(8,128)(2,1)} fusion(bf16[1024,384]{1,0:T(8,128)(2,1)} %bitcast.40), kind=kLoop, calls=%fused_computation.32 | loop fusion | bytes 1048576 | tf_op jit(solution)/shard_map/transpose | solution.py:235
  39.9 1.7 %collective-permute-done.1 = f32[9,162,128]{2,1,0:T(8,128)} collective-permute-done((f32[9,162,128]{2,1,0:T(8,128)}, f32[9,162,128]{2,1,0:T(8,128)}, u32[]{:S(2)}, u32[]{:S(2)}) %collective-permute-start.1) | collective-permute-done | bytes 746528 | tf_op jit(solution)/shard_map/ppermute | solution.py:58
  41.5 5.8 %collective-permute-done.2 = f32[9,162,128]{2,1,0:T(8,128)} collective-permute-done((f32[9,162,128]{2,1,0:T(8,128)}, f32[9,162,128]{2,1,0:T(8,128)}, u32[]{:S(2)}, u32[]{:S(2)}) %collective-permute-start.2) | collective-permute-done | bytes 746528 | tf_op jit(solution)/shard_map/ppermute | solution.py:58
  47.4 1.6 %pad_maximum_fusion = f32[34,162,128]{2,1,0:T(8,128)S(1)} fusion(f32[9,162,128]{2,1,0:T(8,128)} %collective-permute-done.2, f32[16,162,128]{2,1,0:T(8,128)S(1)} %fusion.8, f32[9,162,128]{2,1,0:T(8,128)} %collective-permute-done.1), kind=kLoop, calls=%fused_computation | loop fusion | flops 1410048 | bytes 5640192 | tf_op jit(solution)/shard_map/concatenate | solution.py:84
  48.9 0.7 fusion.1
  49.6 0.2 maximum_bitcast_fusion
  49.9 0.0 copy-start.2
  49.9 2.2 %copy.31 = bf16[4,10,2,8,16,128]{5,4,3,2,1,0:T(8,128)(2,1)} copy(bf16[4,10,2,8,16,128]{5,4,1,3,0,2:T(8,128)(2,1)S(1)} %maximum_bitcast_fusion) | data formatting | bytes 5242880 | tf_op jit(solution)/shard_map/transpose | solution.py:24
  52.1 0.0 copy-done.2
  52.1 1.0 copy.34.cpl_t_hbm
  53.1 14.1 %shard_map.77 = (bf16[2,16,128,128]{3,2,1,0:T(8,128)(2,1)}, bf16[1024,128]{1,0:T(8,128)(2,1)}) custom-call(s32[16,8]{1,0:T(8,128)} %bitcast.46, s32[16,8]{1,0:T(8,128)} %convert_bitcast_fusion.scale_ref, bf16[4,10,2,128,128]{4,3,2,1,0:T(8,128)(2,1)} %bitcast.34, bf16[16,8,2,128,128]{4,3,2,1,0:T(8,128)(2,1)} %bitcast.35, s32[1,1024]{1,0:T(1,128)} %reshape.74.row_leaf_ref, ...), custom_call_target="tpu_custom_call" | custom-call | tf_op jit(solution)/shard_map/pallas_call | solution.py:170
  67.2 1.3 %slice_bitcast_fusion.2 = (bf16[16,128,128]{2,1,0:T(8,128)(2,1)S(1)}, bf16[16,128,128]{2,1,0:T(8,128)(2,1)S(1)}) fusion(bf16[2,16,128,128]{3,2,1,0:T(8,128)(2,1)} %get-tuple-element.14), kind=kLoop, calls=%fused_computation.34 | loop fusion | bytes 2097152 | tf_op jit(solution)/shard_map/squeeze | solution.py:88
  68.5 0.6 fusion.35
  69.1 5.1 %collective-permute-start.3 = (bf16[16,1,128]{2,1,0:T(2,128)(2,1)}, bf16[16,1,128]{2,1,0:T(2,128)(2,1)S(1)}, u32[]{:S(2)}, u32[]{:S(2)}) collective-permute-start(bf16[16,1,128]{2,1,0:T(2,128)(2,1)} %get-tuple-element.30), channel_id=1, source_target_pairs={{0,1},{1,2},{2,3},{4,5},{5,6},{6,7},{8,9},{9,10},{10,11},{12,13},{... | collective-permute-start | bytes 12296 | tf_op jit(solution)/shard_map/ppermute | solution.py:58
  74.2 1.3 %collective-permute-start.4 = (bf16[16,1,128]{2,1,0:T(2,128)(2,1)}, bf16[16,1,128]{2,1,0:T(2,128)(2,1)S(1)}, u32[]{:S(2)}, u32[]{:S(2)}) collective-permute-start(bf16[16,1,128]{2,1,0:T(2,128)(2,1)} %get-tuple-element.31), channel_id=1, source_target_pairs={{1,0},{2,1},{3,2},{5,4},{6,5},{7,6},{9,8},{10,9},{11,10},{13,12},{... | collective-permute-start | bytes 12296 | tf_op jit(solution)/shard_map/ppermute | solution.py:58
  75.5 0.8 slice_bitcast_fusion.4
  76.3 4.7 %collective-permute-start.5 = (bf16[1,128,128]{2,1,0:T(8,128)(2,1)S(1)}, bf16[1,128,128]{2,1,0:T(8,128)(2,1)S(1)}, u32[]{:S(2)}, u32[]{:S(2)}) collective-permute-start(bf16[1,128,128]{2,1,0:T(8,128)(2,1)S(1)} %get-tuple-element.28), channel_id=1, source_target_pairs={{0,4},{1,5},{2,6},{3,7},{4,8},{5,9},{6,10},{7,11},{8,12},{9,13},{1... | collective-permute-start | bytes 98312 | tf_op jit(solution)/shard_map/ppermute | solution.py:58
  81.1 1.3 %collective-permute-start.6 = (bf16[1,128,128]{2,1,0:T(8,128)(2,1)S(1)}, bf16[1,128,128]{2,1,0:T(8,128)(2,1)S(1)}, u32[]{:S(2)}, u32[]{:S(2)}) collective-permute-start(bf16[1,128,128]{2,1,0:T(8,128)(2,1)S(1)} %get-tuple-element.29), channel_id=1, source_target_pairs={{4,0},{5,1},{6,2},{7,3},{8,4},{9,5},{10,6},{11,7},{12,8},{13,9},{1... | collective-permute-start | bytes 98312 | tf_op jit(solution)/shard_map/ppermute | solution.py:58
  82.4 7.5 %all-to-all-start.1 = ((bf16[16,64,128]{2,1,0:T(8,128)(2,1)}), bf16[16,64,128]{2,1,0:T(8,128)(2,1)S(1)}, u32[]{:S(2)}, u32[]{:S(2)}) async-start(bf16[16,64,128]{2,1,0:T(8,128)(2,1)} %bitcast.18), calls=%async_computation.1 | async-start | bytes 524288 | tf_op jit(solution)/shard_map/all_to_all | solution.py:257
  89.9 0.0 collective-permute-done.3
  89.9 0.0 collective-permute-done.4
  89.9 0.1 maximum_convert_fusion.1
  90.1 0.0 collective-permute-done.5
  90.1 0.0 collective-permute-done.6
  90.1 0.1 maximum_convert_fusion
  90.2 0.2 fusion.11
  90.4 0.0 copy-start.6
  90.4 1.4 %copy.35 = f32[128,16,128]{2,1,0:T(8,128)} copy(f32[128,16,128]{0,2,1:T(8,128)S(1)} %fusion.11) | data formatting | bytes 2097152
  91.8 8.2 %all-to-all-done.1 = bf16[16,64,128]{2,1,0:T(8,128)(2,1)S(1)} async-done(((bf16[16,64,128]{2,1,0:T(8,128)(2,1)}), bf16[16,64,128]{2,1,0:T(8,128)(2,1)S(1)}, u32[]{:S(2)}, u32[]{:S(2)}) %all-to-all-start.1) | async-done | bytes 262176 | tf_op jit(solution)/shard_map/all_to_all | solution.py:257
  100.0 0.0 copy-done.6
  100.0 1.4 %fusion.9 = bf16[512,128]{1,0:T(8,128)(2,1)} fusion(bf16[1024,128]{1,0:T(8,128)(2,1)S(1)} %bitcast.43, s32[512]{0:T(512)S(1)} %copy-done.6), kind=kOutput, calls=%fused_computation.18 | convolution fusion | flops 134807552 | bytes 395264 | tf_op jit(solution)/shard_map/dot_general | solution.py:260
  (4 shorter events, 0.0 us)
Async XLA Ops:
  0.6 12.7 %copy-start = (f32[128,16,256]{2,1,0:T(8,128)S(1)}, f32[128,16,256]{2,1,0:T(8,128)}, u32[]{:S(2)}) copy-start(f32[128,16,256]{2,1,0:T(8,128)} %param.6) | copy-start | bytes 6291460
  1.8 4.2 %copy-start.5 = (s32[512]{0:T(512)}, s32[512]{0:T(512)S(1)}, u32[]{:S(2)}) copy-start(s32[512]{0:T(512)S(1)} %multiply_add_fusion) | copy-start | bytes 6148
  5.9 27.8 %all-to-all-start = ((bf16[16,65,384]{2,1,0:T(8,128)(2,1)}), bf16[16,65,384]{2,1,0:T(8,128)(2,1)}, u32[]{:S(2)}, u32[]{:S(2)}) async-start(bf16[16,65,384]{2,1,0:T(8,128)(2,1)} %fusion.16), calls=%async_computation | async-start | bytes 1769472 | tf_op jit(solution)/shard_map/all_to_all | solution.py:232
  14.2 5.4 %collective-permute-start = (f32[16,17,128]{2,1,0:T(8,128)S(1)}, f32[16,17,128]{2,1,0:T(8,128)S(1)}, u32[]{:S(2)}, u32[]{:S(2)}) collective-permute-start(f32[16,17,128]{2,1,0:T(8,128)S(1)} %bitcast.45), channel_id=1, source_target_pairs={{1,2},{2,1},{5,6},{6,5},{9,10},{10,9},{13,14},{14,13},{17,18},{18,... | collective-permute-start | bytes 417800 | tf_op jit(solution)/shard_map/ppermute | solution.py:58
  19.5 0.7 copy-start.3
  22.1 7.2 %copy-start.4 = (s32[2,8,8]{2,1,0:T(8,128)S(1)}, s32[2,8,8]{2,1,0:T(8,128)}, u32[]{:S(2)}) copy-start(s32[2,8,8]{2,1,0:T(8,128)} %param.8) | copy-start | bytes 1540
  23.4 18.2 %collective-permute-start.1 = (f32[9,162,128]{2,1,0:T(8,128)}, f32[9,162,128]{2,1,0:T(8,128)}, u32[]{:S(2)}, u32[]{:S(2)}) collective-permute-start(f32[9,162,128]{2,1,0:T(8,128)} %get-tuple-element.25), channel_id=1, source_target_pairs={{0,4},{1,5},{2,6},{3,7},{4,8},{5,9},{6,10},{7,11},{8,12},{9,13},{1... | collective-permute-start | bytes 2239496 | tf_op jit(solution)/shard_map/ppermute | solution.py:58
  28.0 19.3 %collective-permute-start.2 = (f32[9,162,128]{2,1,0:T(8,128)}, f32[9,162,128]{2,1,0:T(8,128)}, u32[]{:S(2)}, u32[]{:S(2)}) collective-permute-start(f32[9,162,128]{2,1,0:T(8,128)} %get-tuple-element.24), channel_id=1, source_target_pairs={{4,0},{5,1},{6,2},{7,3},{8,4},{9,5},{10,6},{11,7},{12,8},{13,9},{1... | collective-permute-start | bytes 2239496 | tf_op jit(solution)/shard_map/ppermute | solution.py:58
  34.9 0.9 copy-start.1
  49.9 2.2 %copy-start.2 = (bf16[256,1024]{0,1:T(8,128)(2,1)S(1)}, bf16[256,1024]{0,1:T(8,128)(2,1)}, u32[]{:S(2)}) copy-start(bf16[256,1024]{0,1:T(8,128)(2,1)} %slice_bitcast_fusion) | copy-start | bytes 1572868
  69.1 20.8 %collective-permute-start.3 = (bf16[16,1,128]{2,1,0:T(2,128)(2,1)}, bf16[16,1,128]{2,1,0:T(2,128)(2,1)S(1)}, u32[]{:S(2)}, u32[]{:S(2)}) collective-permute-start(bf16[16,1,128]{2,1,0:T(2,128)(2,1)} %get-tuple-element.30), channel_id=1, source_target_pairs={{0,1},{1,2},{2,3},{4,5},{5,6},{6,7},{8,9},{9,10},{10,11},{12,13},{... | collective-permute-start | bytes 12296 | tf_op jit(solution)/shard_map/ppermute | solution.py:58
  74.2 15.7 %collective-permute-start.4 = (bf16[16,1,128]{2,1,0:T(2,128)(2,1)}, bf16[16,1,128]{2,1,0:T(2,128)(2,1)S(1)}, u32[]{:S(2)}, u32[]{:S(2)}) collective-permute-start(bf16[16,1,128]{2,1,0:T(2,128)(2,1)} %get-tuple-element.31), channel_id=1, source_target_pairs={{1,0},{2,1},{3,2},{5,4},{6,5},{7,6},{9,8},{10,9},{11,10},{13,12},{... | collective-permute-start | bytes 12296 | tf_op jit(solution)/shard_map/ppermute | solution.py:58
  76.3 13.7 %collective-permute-start.5 = (bf16[1,128,128]{2,1,0:T(8,128)(2,1)S(1)}, bf16[1,128,128]{2,1,0:T(8,128)(2,1)S(1)}, u32[]{:S(2)}, u32[]{:S(2)}) collective-permute-start(bf16[1,128,128]{2,1,0:T(8,128)(2,1)S(1)} %get-tuple-element.28), channel_id=1, source_target_pairs={{0,4},{1,5},{2,6},{3,7},{4,8},{5,9},{6,10},{7,11},{8,12},{9,13},{1... | collective-permute-start | bytes 98312 | tf_op jit(solution)/shard_map/ppermute | solution.py:58
  81.1 9.0 %collective-permute-start.6 = (bf16[1,128,128]{2,1,0:T(8,128)(2,1)S(1)}, bf16[1,128,128]{2,1,0:T(8,128)(2,1)S(1)}, u32[]{:S(2)}, u32[]{:S(2)}) collective-permute-start(bf16[1,128,128]{2,1,0:T(8,128)(2,1)S(1)} %get-tuple-element.29), channel_id=1, source_target_pairs={{4,0},{5,1},{6,2},{7,3},{8,4},{9,5},{10,6},{11,7},{12,8},{13,9},{1... | collective-permute-start | bytes 98312 | tf_op jit(solution)/shard_map/ppermute | solution.py:58
  82.4 17.6 %all-to-all-start.1 = ((bf16[16,64,128]{2,1,0:T(8,128)(2,1)}), bf16[16,64,128]{2,1,0:T(8,128)(2,1)S(1)}, u32[]{:S(2)}, u32[]{:S(2)}) async-start(bf16[16,64,128]{2,1,0:T(8,128)(2,1)} %bitcast.18), calls=%async_computation.1 | async-start | bytes 524288 | tf_op jit(solution)/shard_map/all_to_all | solution.py:257
  90.4 9.6 %copy-start.6 = (s32[512]{0:T(512)S(1)}, s32[512]{0:T(512)}, u32[]{:S(2)}) copy-start(s32[512]{0:T(512)} %copy-done.5) | copy-start | bytes 6148

commit v12 on v11

--- a/solution.py
+++ b/solution.py
@@ -106,7 +106,7 @@
 
 def leaf_kernel(
     codes_ref, scale_ref, bord_hbm, ind_hbm, row_leaf_ref, cpl_t_hbm, cur_hbm,
-    field_ref, volt_ref, bord_ref, ind_ref, cpl_t_ref, cur_ref, acc_ref, sems, ind_sems,
+    field_ref, bord_ref, ind_ref, cpl_t_ref, cur_ref, sems, ind_sems,
 ):
     leaf_count = ind_ref.shape[0]
     leaf_cols = bord_ref.shape[1] - 2
@@ -121,7 +121,6 @@
         copy.start()
     for l in range(leaf_count):
         pltpu.make_async_copy(ind_hbm.at[l], ind_ref.at[l], ind_sems.at[l]).start()
-    acc_ref[...] = jnp.zeros_like(acc_ref)
     for copy in first:
         copy.wait()
 
@@ -149,13 +148,29 @@
             field_ref[c, pl.ds(row * LEAF_R, LEAF_R), pl.ds(pl.multiple_of(col * LEAF_C, LEAF_C), LEAF_C)] = (
                 total.reshape(LEAF_R, LEAF_C, -1).astype(field_ref.dtype)
             )
+        return carry
+
+    lax.fori_loop(0, leaf_count, one_leaf, 0)
+
+
+def induced_kernel(bord_ref, row_leaf_ref, cpl_t_ref, volt_ref, acc_ref):
+    leaf_rows = bord_ref.shape[0] - 2
+    leaf_cols = bord_ref.shape[1] - 2
+    cells = bord_ref.shape[3]
+    acc_ref[...] = jnp.zeros_like(acc_ref)
+
+    def one_leaf(leaf, carry):
+        row = leaf // leaf_cols
+        col = leaf % leaf_cols
+        coupling_t = cpl_t_ref[...]
+        coupling_t = jnp.where(row_leaf_ref[...] == leaf, coupling_t, jnp.zeros_like(coupling_t))
         own = bord_ref[row + 1, col + 1].reshape(2 * cells, -1)
         acc_ref[...] += lax.dot_general(
             own, coupling_t, (((0,), (0,)), ((), ())), preferred_element_type=jnp.float32
         )
         return carry
 
-    lax.fori_loop(0, leaf_count, one_leaf, 0)
+    lax.fori_loop(0, leaf_rows * leaf_cols, one_leaf, 0)
     volt_ref[...] = acc_ref[...].T.astype(volt_ref.dtype)
 
 
@@ -167,26 +182,31 @@
     smem = pl.BlockSpec(memory_space=pltpu.SMEM)
     hbm = pl.BlockSpec(memory_space=pl.ANY)
     vmem = pl.BlockSpec(memory_space=pltpu.VMEM)
-    return pl.pallas_call(
+    field = pl.pallas_call(
         leaf_kernel,
         in_specs=[smem, smem, hbm, hbm, vmem, hbm, hbm],
-        out_specs=[vmem, vmem],
-        out_shape=[
-            jax.ShapeDtypeStruct(
-                (components, leaf_rows * LEAF_R, leaf_cols * LEAF_C, port_count), jnp.bfloat16
-            ),
-            jax.ShapeDtypeStruct((slot_count, port_count), jnp.bfloat16),
-        ],
+        out_specs=vmem,
+        out_shape=jax.ShapeDtypeStruct(
+            (components, leaf_rows * LEAF_R, leaf_cols * LEAF_C, port_count), jnp.bfloat16
+        ),
         scratch_shapes=[
             pltpu.VMEM(bordered.shape, bordered.dtype),
             pltpu.VMEM(kernels.shape, kernels.dtype),
             pltpu.VMEM(coupling_t.shape, coupling_t.dtype),
             pltpu.VMEM(current.shape, current.dtype),
-            pltpu.VMEM((port_count, slot_count), jnp.float32),
             pltpu.SemaphoreType.DMA((3,)),
             pltpu.SemaphoreType.DMA((leaf_count,)),
         ],
     )(codes, scales, bordered, kernels, row_leaf, coupling_t, current)
+    field, bordered = lax.optimization_barrier((field, bordered))
+    volt = pl.pallas_call(
+        induced_kernel,
+        in_specs=[vmem, vmem, vmem],
+        out_specs=vmem,
+        out_shape=jax.ShapeDtypeStruct((slot_count, port_count), jnp.bfloat16),
+        scratch_shapes=[pltpu.VMEM((port_count, slot_count), jnp.float32)],
+    )(bordered, row_leaf, coupling_t)
+    return field, volt
 
 
 def body(stream, inductance, near_lists, filament_leaf, filament_current, filament_coupling):

time: 102 us -> 102 us (level)
  Pallas kernels: 14.1 us -> 20 us
  waiting for transfers between devices: 19.4 us -> 15.5 us
  local copies, waits for them, and re-layouts: 21.1 us -> 19.7 us
    all_to_all x1, waiting for transfers between devices: 8.18 us -> 0.01 us  [body(): lax.all_to_all(induced.reshape(owners, capacity, port_count), AXES, split...]
    pallas_call x0 -> x1, Pallas kernels: none -> 6.94 us  [leaf_fields(): pl.pallas_call(induced_kernel, in_specs=[vmem, vmem, vmem], out_specs=vme...]
    ppermute x7, waiting for transfers between devices: 7.49 us -> 11.8 us  [send(): return lax.ppermute(value, AXES, pairs_by(fn))]
    transpose x1 -> x0, local copies, waits for them, and re-layouts: 1.88 us -> none  [body(): got_coupling_t = got_rows[:, :2 * leaf_cells].T]
    unnamed x18 -> x11, local copies, waits for them, and re-layouts: 7.17 us -> 8.35 us
    pallas_call x1, Pallas kernels: 14.1 us -> 13.1 us  [leaf_fields(): pl.pallas_call(leaf_kernel, in_specs=[smem, smem, hbm, hbm, vmem, hbm, hb...]
  transfers between devices with their start and end apart: 9 -> 9, of which waited for: 4 -> 5; matrix products, arithmetic and copies ran while one was open for 17% -> 18% of each run, Pallas kernels for 0% -> 7%
where the time goes in v12:
time: 102 us; the launch traced here: 101 us
  starting transfers between devices  33.2 us (33%)
  Pallas kernels  20 us (20%)
  local copies, waits for them, and re-layouts  19.7 us (19%)
  waiting for transfers between devices  15.5 us (15%)
  other arithmetic  8.33 us (8%)
  matrix products  3.5 us (3%)
    ppermute x7, starting transfers between devices, send(): return lax.ppermute(value, AXES, pairs_by(fn))  18.1 us
    pallas_call x1, Pallas kernels, leaf_fields(): pl.pallas_call(leaf_kernel, in_specs=[smem, smem, hbm, hbm, vmem, hbm, hb...  13.1 us
    ppermute x7, waiting for transfers between devices, send(): return lax.ppermute(value, AXES, pairs_by(fn))  11.8 us
    unnamed x11, local copies, waits for them, and re-layouts  8.35 us
    all_to_all x1, starting transfers between devices, body(): lax.all_to_all(induced.reshape(owners, capacity, port_count), AXES, split...  7.7 us
    all_to_all x1, starting transfers between devices, body(): got = lax.all_to_all(payload, AXES, split_axis=0, concat_axis=0, tiled=True)  7.4 us
    pallas_call x1, Pallas kernels, leaf_fields(): pl.pallas_call(induced_kernel, in_specs=[vmem, vmem, vmem], out_specs=vme...  6.94 us
    all_to_all x1, waiting for transfers between devices, body(): got = lax.all_to_all(payload, AXES, split_axis=0, concat_axis=0, tiled=True)  3.72 us
  transfers between devices with their start and end apart: 9, of which 5 were waited for; matrix products, arithmetic and copies ran while one was open for 18% of the time, Pallas kernels for 7%

profile of v12, /device:TPU:0, one launch (start us, length us, event | category | flops | bytes accessed | tf_op | source)
XLA Modules:
  0.0 101.1 jit_solution(4853293291414315892)
XLA Ops:
  0.6 0.0 copy-start
  0.6 0.9 fusion.25
  1.5 0.2 convert_reduce_fusion
  1.8 0.5 fusion.3
  2.2 0.1 reshape.77
  2.3 1.0 copy.46
  3.3 1.6 %fusion.6 = bf16[1024,384]{1,0:T(8,128)(2,1)S(1)} fusion(s32[512]{0:T(512)S(1)} %multiply_add_fusion, bf16[512,128]{1,0:T(8,128)(2,1)} %param.10, bf16[512,256]{1,0:T(8,128)(2,1)S(1)} %bitcast.47), kind=kOutput, calls=%fused_computation.15 | convolution fusion | flops 404357120 | bytes 1181696 | tf_op jit(solution)/shard_map/dot_general | solution.py:243
  4.9 1.0 fusion.16
  5.9 7.4 %all-to-all-start = ((bf16[16,65,384]{2,1,0:T(8,128)(2,1)}), bf16[16,65,384]{2,1,0:T(8,128)(2,1)}, u32[]{:S(2)}, u32[]{:S(2)}) async-start(bf16[16,65,384]{2,1,0:T(8,128)(2,1)} %fusion.16), calls=%async_computation | async-start | bytes 1769472 | tf_op jit(solution)/shard_map/all_to_all | solution.py:252
  13.3 0.0 copy-done
  13.4 0.3 constant_dynamic-slice_fusion.1
  13.7 0.4 copy.40
  14.2 0.7 collective-permute-start
  14.8 1.9 %constant_dynamic-slice_fusion = f32[128,16,145]{2,1,0:T(8,128)} fusion(f32[128,16,256]{2,1,0:T(8,128)S(1)} %copy-done, s32[]{:T(128)S(6)} %select_n.49), kind=kLoop, calls=%fused_computation.78 | loop fusion | bytes 2375684 | tf_op jit(solution)/shard_map/dynamic-slice.1
  16.8 2.8 %copy.41 = f32[128,16,145]{0,2,1:T(8,128)} copy(f32[128,16,145]{2,1,0:T(8,128)} %constant_dynamic-slice_fusion) | data formatting | bytes 2375680
  19.6 0.0 collective-permute-done
  19.6 0.0 copy-start.1
  19.6 0.7 copy-done.1
  20.2 1.9 %fusion.8 = f32[16,162,128]{2,1,0:T(8,128)S(1)} fusion(s32[]{:T(128)S(6)} %select_n.50, f32[16,17,128]{2,1,0:T(8,128)} %copy-done.1, f32[16,145,128]{2,1,0:T(8,128)} %bitcast.38), kind=kLoop, calls=%fused_computation.17 | loop fusion | flops 663552 | bytes 2654212 | tf_op jit(solution)/shard_map/concatenate | solution.py:79
  22.2 0.0 copy-start.2
  22.2 1.2 %fusion.34 = (f32[9,162,128]{2,1,0:T(8,128)}, f32[9,162,128]{2,1,0:T(8,128)}) fusion(f32[16,162,128]{2,1,0:T(8,128)S(1)} %fusion.8), kind=kLoop, calls=%fused_computation.84 | loop fusion | bytes 2985984 | tf_op jit(solution)/shard_map/slice | solution.py:82
  23.4 4.7 %collective-permute-start.1 = (f32[9,162,128]{2,1,0:T(8,128)}, f32[9,162,128]{2,1,0:T(8,128)}, u32[]{:S(2)}, u32[]{:S(2)}) collective-permute-start(f32[9,162,128]{2,1,0:T(8,128)} %get-tuple-element.25), channel_id=1, source_target_pairs={{0,4},{1,5},{2,6},{3,7},{4,8},{5,9},{6,10},{7,11},{8,12},{9,13},{1... | collective-permute-start | bytes 2239496 | tf_op jit(solution)/shard_map/ppermute | solution.py:58
  28.0 1.3 %collective-permute-start.2 = (f32[9,162,128]{2,1,0:T(8,128)}, f32[9,162,128]{2,1,0:T(8,128)}, u32[]{:S(2)}, u32[]{:S(2)}) collective-permute-start(f32[9,162,128]{2,1,0:T(8,128)} %get-tuple-element.24), channel_id=1, source_target_pairs={{4,0},{5,1},{6,2},{7,3},{8,4},{9,5},{10,6},{11,7},{12,8},{13,9},{1... | collective-permute-start | bytes 2239496 | tf_op jit(solution)/shard_map/ppermute | solution.py:58
  29.3 0.0 copy-done.2
  29.4 0.6 convert_bitcast_fusion.scale_ref
  30.0 3.7 %all-to-all-done = bf16[16,65,384]{2,1,0:T(8,128)(2,1)} async-done(((bf16[16,65,384]{2,1,0:T(8,128)(2,1)}), bf16[16,65,384]{2,1,0:T(8,128)(2,1)}, u32[]{:S(2)}, u32[]{:S(2)}) %all-to-all-start) | async-done | bytes 798752 | tf_op jit(solution)/shard_map/all_to_all | solution.py:252
  33.7 1.2 %slice.93 = bf16[16,64,384]{2,1,0:T(8,128)(2,1)S(1)} slice(bf16[16,65,384]{2,1,0:T(8,128)(2,1)} %all-to-all-done), slice={[0:16], [0:64], [0:384]} | slice | bytes 1572864 | tf_op jit(solution)/shard_map/slice | solution.py:253
  34.9 0.8 slice.94
  35.7 0.7 slice.95.cur_hbm
  36.5 2.1 %copy.42 = bf16[1024,256]{0,1:T(8,128)(2,1)} copy(bf16[1024,256]{1,0:T(8,128)(2,1)} %slice.94) | data formatting | bytes 1048576
  38.5 0.8 fusion.22
  39.3 0.7 reshape.74.row_leaf_ref
  40.0 1.6 %collective-permute-done.1 = f32[9,162,128]{2,1,0:T(8,128)} collective-permute-done((f32[9,162,128]{2,1,0:T(8,128)}, f32[9,162,128]{2,1,0:T(8,128)}, u32[]{:S(2)}, u32[]{:S(2)}) %collective-permute-start.1) | collective-permute-done | bytes 746528 | tf_op jit(solution)/shard_map/ppermute | solution.py:58
  41.5 5.8 %collective-permute-done.2 = f32[9,162,128]{2,1,0:T(8,128)} collective-permute-done((f32[9,162,128]{2,1,0:T(8,128)}, f32[9,162,128]{2,1,0:T(8,128)}, u32[]{:S(2)}, u32[]{:S(2)}) %collective-permute-start.2) | collective-permute-done | bytes 746528 | tf_op jit(solution)/shard_map/ppermute | solution.py:58
  47.4 1.6 %pad_maximum_fusion = f32[34,162,128]{2,1,0:T(8,128)S(1)} fusion(f32[9,162,128]{2,1,0:T(8,128)} %collective-permute-done.2, f32[16,162,128]{2,1,0:T(8,128)S(1)} %fusion.8, f32[9,162,128]{2,1,0:T(8,128)} %collective-permute-done.1), kind=kLoop, calls=%fused_computation | loop fusion | flops 1410048 | bytes 5640192 | tf_op jit(solution)/shard_map/concatenate | solution.py:84
  48.9 0.7 fusion.1
  49.6 0.2 maximum_bitcast_fusion
  49.9 2.2 %copy.34 = bf16[4,10,2,8,16,128]{5,4,3,2,1,0:T(8,128)(2,1)} copy(bf16[4,10,2,8,16,128]{5,4,1,3,0,2:T(8,128)(2,1)S(1)} %maximum_bitcast_fusion) | data formatting | bytes 5242880 | tf_op jit(solution)/shard_map/transpose | solution.py:24
  52.1 13.1 %shard_map.77 = bf16[2,16,128,128]{3,2,1,0:T(8,128)(2,1)} custom-call(s32[16,8]{1,0:T(8,128)} %bitcast.49, s32[16,8]{1,0:T(8,128)} %convert_bitcast_fusion.scale_ref, bf16[4,10,2,128,128]{4,3,2,1,0:T(8,128)(2,1)} %bitcast.33, bf16[16,8,2,128,128]{4,3,2,1,0:T(8,128)(2,1)} %bitcast.35, s32[1,1024]{1,0:T(1,128)} %reshape.74.row_leaf_ref, ...), custom_call_target="tpu_custom_call" | custom-call | tf_op jit(solution)/shard_map/pallas_call | solution.py:185
  65.2 1.3 %slice_bitcast_fusion.1 = (bf16[16,128,128]{2,1,0:T(8,128)(2,1)S(1)}, bf16[16,128,128]{2,1,0:T(8,128)(2,1)S(1)}) fusion(bf16[2,16,128,128]{3,2,1,0:T(8,128)(2,1)} %shard_map.77), kind=kLoop, calls=%fused_computation.33 | loop fusion | bytes 2097152 | tf_op jit(solution)/shard_map/squeeze | solution.py:88
  66.5 5.1 %collective-permute-start.3 = (bf16[16,1,128]{2,1,0:T(2,128)(2,1)S(1)}, bf16[16,1,128]{2,1,0:T(2,128)(2,1)S(1)}, u32[]{:S(2)}, u32[]{:S(2)}) collective-permute-start(bf16[16,1,128]{2,1,0:T(2,128)(2,1)S(1)} %get-tuple-element.30), channel_id=1, source_target_pairs={{0,1},{1,2},{2,3},{4,5},{5,6},{6,7},{8,9},{9,10},{10,11},{12,13},{... | collective-permute-start | bytes 12296 | tf_op jit(solution)/shard_map/ppermute | solution.py:58
  71.6 1.3 %collective-permute-start.4 = (bf16[16,1,128]{2,1,0:T(2,128)(2,1)S(1)}, bf16[16,1,128]{2,1,0:T(2,128)(2,1)S(1)}, u32[]{:S(2)}, u32[]{:S(2)}) collective-permute-start(bf16[16,1,128]{2,1,0:T(2,128)(2,1)S(1)} %get-tuple-element.31), channel_id=1, source_target_pairs={{1,0},{2,1},{3,2},{5,4},{6,5},{7,6},{9,8},{10,9},{11,10},{13,12},{... | collective-permute-start | bytes 12296 | tf_op jit(solution)/shard_map/ppermute | solution.py:58
  72.9 0.8 slice_bitcast_fusion.3
  73.7 6.9 %shard_map.78 = bf16[1024,128]{1,0:T(8,128)(2,1)} custom-call(bf16[4,10,2,128,128]{4,3,2,1,0:T(8,128)(2,1)} %bitcast.34, s32[1,1024]{1,0:T(1,128)} %reshape.74.row_leaf_ref, bf16[256,1024]{1,0:T(8,128)(2,1)} %bitcast.40), custom_call_target="tpu_custom_call" | custom-call | tf_op jit(solution)/shard_map/pallas_call | solution.py:202
  80.6 7.7 %all-to-all-start.1 = ((bf16[16,64,128]{2,1,0:T(8,128)(2,1)}), bf16[16,64,128]{2,1,0:T(8,128)(2,1)S(1)}, u32[]{:S(2)}, u32[]{:S(2)}) async-start(bf16[16,64,128]{2,1,0:T(8,128)(2,1)} %bitcast.43), calls=%async_computation.1 | async-start | bytes 524288 | tf_op jit(solution)/shard_map/all_to_all | solution.py:277
  88.3 3.8 %collective-permute-start.5 = (bf16[1,128,128]{2,1,0:T(8,128)(2,1)S(1)}, bf16[1,128,128]{2,1,0:T(8,128)(2,1)S(1)}, u32[]{:S(2)}, u32[]{:S(2)}) collective-permute-start(bf16[1,128,128]{2,1,0:T(8,128)(2,1)S(1)} %get-tuple-element.28), channel_id=1, source_target_pairs={{0,4},{1,5},{2,6},{3,7},{4,8},{5,9},{6,10},{7,11},{8,12},{9,13},{1... | collective-permute-start | bytes 98312 | tf_op jit(solution)/shard_map/ppermute | solution.py:58
  92.2 1.3 %collective-permute-start.6 = (bf16[1,128,128]{2,1,0:T(8,128)(2,1)S(1)}, bf16[1,128,128]{2,1,0:T(8,128)(2,1)S(1)}, u32[]{:S(2)}, u32[]{:S(2)}) collective-permute-start(bf16[1,128,128]{2,1,0:T(8,128)(2,1)S(1)} %get-tuple-element.29), channel_id=1, source_target_pairs={{4,0},{5,1},{6,2},{7,3},{8,4},{9,5},{10,6},{11,7},{12,8},{13,9},{1... | collective-permute-start | bytes 98312 | tf_op jit(solution)/shard_map/ppermute | solution.py:58
  93.5 0.0 collective-permute-done.3
  93.5 0.0 collective-permute-done.4
  93.5 0.1 maximum_convert_fusion.1
  93.6 0.7 collective-permute-done.5
  94.3 3.7 %collective-permute-done.6 = bf16[1,128,128]{2,1,0:T(8,128)(2,1)S(1)} collective-permute-done((bf16[1,128,128]{2,1,0:T(8,128)(2,1)S(1)}, bf16[1,128,128]{2,1,0:T(8,128)(2,1)S(1)}, u32[]{:S(2)}, u32[]{:S(2)}) %collective-permute-start.6) | collective-permute-done | bytes 32800 | tf_op jit(solution)/shard_map/ppermute | solution.py:58
  98.0 0.1 maximum_convert_fusion
  98.1 0.2 fusion.11
  98.3 1.4 %copy.37 = f32[128,16,128]{2,1,0:T(8,128)} copy(f32[128,16,128]{0,2,1:T(8,128)S(1)} %fusion.11) | data formatting | bytes 2097152
  99.7 0.0 all-to-all-done.1
  99.7 1.4 %fusion.9 = bf16[512,128]{1,0:T(8,128)(2,1)} fusion(bf16[1024,128]{1,0:T(8,128)(2,1)S(1)} %bitcast.46, s32[512]{0:T(512)S(1)} %multiply_add_fusion), kind=kOutput, calls=%fused_computation.18 | convolution fusion | flops 134807552 | bytes 395264 | tf_op jit(solution)/shard_map/dot_general | solution.py:280
  (4 shorter events, 0.0 us)
Async XLA Ops:
  0.6 12.7 %copy-start = (f32[128,16,256]{2,1,0:T(8,128)S(1)}, f32[128,16,256]{2,1,0:T(8,128)}, u32[]{:S(2)}) copy-start(f32[128,16,256]{2,1,0:T(8,128)} %param.6) | copy-start | bytes 6291460
  5.9 27.8 %all-to-all-start = ((bf16[16,65,384]{2,1,0:T(8,128)(2,1)}), bf16[16,65,384]{2,1,0:T(8,128)(2,1)}, u32[]{:S(2)}, u32[]{:S(2)}) async-start(bf16[16,65,384]{2,1,0:T(8,128)(2,1)} %fusion.16), calls=%async_computation | async-start | bytes 1769472 | tf_op jit(solution)/shard_map/all_to_all | solution.py:252
  14.2 5.4 %collective-permute-start = (f32[16,17,128]{2,1,0:T(8,128)S(1)}, f32[16,17,128]{2,1,0:T(8,128)S(1)}, u32[]{:S(2)}, u32[]{:S(2)}) collective-permute-start(f32[16,17,128]{2,1,0:T(8,128)S(1)} %bitcast.48), channel_id=1, source_target_pairs={{1,2},{2,1},{5,6},{6,5},{9,10},{10,9},{13,14},{14,13},{17,18},{18,... | collective-permute-start | bytes 417800 | tf_op jit(solution)/shard_map/ppermute | solution.py:58
  19.6 0.7 copy-start.1
  22.2 7.2 %copy-start.2 = (s32[2,8,8]{2,1,0:T(8,128)S(1)}, s32[2,8,8]{2,1,0:T(8,128)}, u32[]{:S(2)}) copy-start(s32[2,8,8]{2,1,0:T(8,128)} %param.8) | copy-start | bytes 1540
  23.4 18.1 %collective-permute-start.1 = (f32[9,162,128]{2,1,0:T(8,128)}, f32[9,162,128]{2,1,0:T(8,128)}, u32[]{:S(2)}, u32[]{:S(2)}) collective-permute-start(f32[9,162,128]{2,1,0:T(8,128)} %get-tuple-element.25), channel_id=1, source_target_pairs={{0,4},{1,5},{2,6},{3,7},{4,8},{5,9},{6,10},{7,11},{8,12},{9,13},{1... | collective-permute-start | bytes 2239496 | tf_op jit(solution)/shard_map/ppermute | solution.py:58
  28.0 19.3 %collective-permute-start.2 = (f32[9,162,128]{2,1,0:T(8,128)}, f32[9,162,128]{2,1,0:T(8,128)}, u32[]{:S(2)}, u32[]{:S(2)}) collective-permute-start(f32[9,162,128]{2,1,0:T(8,128)} %get-tuple-element.24), channel_id=1, source_target_pairs={{4,0},{5,1},{6,2},{7,3},{8,4},{9,5},{10,6},{11,7},{12,8},{13,9},{1... | collective-permute-start | bytes 2239496 | tf_op jit(solution)/shard_map/ppermute | solution.py:58
  66.5 27.0 %collective-permute-start.3 = (bf16[16,1,128]{2,1,0:T(2,128)(2,1)S(1)}, bf16[16,1,128]{2,1,0:T(2,128)(2,1)S(1)}, u32[]{:S(2)}, u32[]{:S(2)}) collective-permute-start(bf16[16,1,128]{2,1,0:T(2,128)(2,1)S(1)} %get-tuple-element.30), channel_id=1, source_target_pairs={{0,1},{1,2},{2,3},{4,5},{5,6},{6,7},{8,9},{9,10},{10,11},{12,13},{... | collective-permute-start | bytes 12296 | tf_op jit(solution)/shard_map/ppermute | solution.py:58
  71.6 21.9 %collective-permute-start.4 = (bf16[16,1,128]{2,1,0:T(2,128)(2,1)S(1)}, bf16[16,1,128]{2,1,0:T(2,128)(2,1)S(1)}, u32[]{:S(2)}, u32[]{:S(2)}) collective-permute-start(bf16[16,1,128]{2,1,0:T(2,128)(2,1)S(1)} %get-tuple-element.31), channel_id=1, source_target_pairs={{1,0},{2,1},{3,2},{5,4},{6,5},{7,6},{9,8},{10,9},{11,10},{13,12},{... | collective-permute-start | bytes 12296 | tf_op jit(solution)/shard_map/ppermute | solution.py:58
  80.6 19.1 %all-to-all-start.1 = ((bf16[16,64,128]{2,1,0:T(8,128)(2,1)}), bf16[16,64,128]{2,1,0:T(8,128)(2,1)S(1)}, u32[]{:S(2)}, u32[]{:S(2)}) async-start(bf16[16,64,128]{2,1,0:T(8,128)(2,1)} %bitcast.43), calls=%async_computation.1 | async-start | bytes 524288 | tf_op jit(solution)/shard_map/all_to_all | solution.py:277
  88.3 6.0 %collective-permute-start.5 = (bf16[1,128,128]{2,1,0:T(8,128)(2,1)S(1)}, bf16[1,128,128]{2,1,0:T(8,128)(2,1)S(1)}, u32[]{:S(2)}, u32[]{:S(2)}) collective-permute-start(bf16[1,128,128]{2,1,0:T(8,128)(2,1)S(1)} %get-tuple-element.28), channel_id=1, source_target_pairs={{0,4},{1,5},{2,6},{3,7},{4,8},{5,9},{6,10},{7,11},{8,12},{9,13},{1... | collective-permute-start | bytes 98312 | tf_op jit(solution)/shard_map/ppermute | solution.py:58
  92.2 5.9 %collective-permute-start.6 = (bf16[1,128,128]{2,1,0:T(8,128)(2,1)S(1)}, bf16[1,128,128]{2,1,0:T(8,128)(2,1)S(1)}, u32[]{:S(2)}, u32[]{:S(2)}) collective-permute-start(bf16[1,128,128]{2,1,0:T(8,128)(2,1)S(1)} %get-tuple-element.29), channel_id=1, source_target_pairs={{4,0},{5,1},{6,2},{7,3},{8,4},{9,5},{10,6},{11,7},{12,8},{13,9},{1... | collective-permute-start | bytes 98312 | tf_op jit(solution)/shard_map/ppermute | solution.py:58

commit v13 on v12

--- a/solution.py
+++ b/solution.py
@@ -104,9 +104,31 @@
     return x_pad[:, :-2] - x_pad[:, 2:] + (y_pad[2:] - y_pad[:-2])
 
 
+def filament_kernel(row_leaf_ref, cpl_t_ref, cur_ref, fil_ref):
+    def one_leaf(leaf, carry):
+        coupling_t = cpl_t_ref[...]
+        coupling_t = jnp.where(row_leaf_ref[...] == leaf, coupling_t, jnp.zeros_like(coupling_t))
+        fil_ref[leaf] = jnp.dot(coupling_t, cur_ref[...], preferred_element_type=jnp.float32)
+        return carry
+
+    lax.fori_loop(0, fil_ref.shape[0], one_leaf, 0)
+
+
+def filament_field(row_leaf, coupling_t, current, leaf_count):
+    vmem = pl.BlockSpec(memory_space=pltpu.VMEM)
+    return pl.pallas_call(
+        filament_kernel,
+        in_specs=[vmem, vmem, vmem],
+        out_specs=vmem,
+        out_shape=jax.ShapeDtypeStruct(
+            (leaf_count, coupling_t.shape[0], current.shape[1]), jnp.float32
+        ),
+    )(row_leaf, coupling_t, current)
+
+
 def leaf_kernel(
-    codes_ref, scale_ref, bord_hbm, ind_hbm, row_leaf_ref, cpl_t_hbm, cur_hbm,
-    field_ref, bord_ref, ind_ref, cpl_t_ref, cur_ref, sems, ind_sems,
+    codes_ref, scale_ref, bord_hbm, ind_hbm, fil_hbm,
+    field_ref, bord_ref, ind_ref, fil_ref, sems, ind_sems,
 ):
     leaf_count = ind_ref.shape[0]
     leaf_cols = bord_ref.shape[1] - 2
@@ -114,8 +136,7 @@
     cells = ind_ref.shape[3]
     first = [
         pltpu.make_async_copy(bord_hbm, bord_ref, sems.at[0]),
-        pltpu.make_async_copy(cpl_t_hbm, cpl_t_ref, sems.at[1]),
-        pltpu.make_async_copy(cur_hbm, cur_ref, sems.at[2]),
+        pltpu.make_async_copy(fil_hbm, fil_ref, sems.at[1]),
     ]
     for copy in first:
         copy.start()
@@ -128,9 +149,7 @@
         pltpu.make_async_copy(ind_hbm.at[leaf], ind_ref.at[leaf], ind_sems.at[leaf]).wait()
         row = leaf // leaf_cols
         col = leaf % leaf_cols
-        coupling_t = cpl_t_ref[...]
-        coupling_t = jnp.where(row_leaf_ref[...] == leaf, coupling_t, jnp.zeros_like(coupling_t))
-        filament = jnp.dot(coupling_t, cur_ref[...], preferred_element_type=jnp.float32)
+        filament = fil_ref[leaf]
         sources = []
         for n in range(near_count):
             code = codes_ref[leaf, n]
@@ -174,17 +193,18 @@
     volt_ref[...] = acc_ref[...].T.astype(volt_ref.dtype)
 
 
-def leaf_fields(codes, scales, bordered, kernels, row_leaf, coupling_t, current):
+def leaf_fields(codes, scales, bordered, kernels, filament, row_leaf, coupling_t):
     leaf_count, near_count, components, cells, _ = kernels.shape
     leaf_rows = bordered.shape[0] - 2
     leaf_cols = bordered.shape[1] - 2
-    slot_count, port_count = current.shape
+    port_count = bordered.shape[-1]
+    slot_count = coupling_t.shape[1]
     smem = pl.BlockSpec(memory_space=pltpu.SMEM)
     hbm = pl.BlockSpec(memory_space=pl.ANY)
     vmem = pl.BlockSpec(memory_space=pltpu.VMEM)
     field = pl.pallas_call(
         leaf_kernel,
-        in_specs=[smem, smem, hbm, hbm, vmem, hbm, hbm],
+        in_specs=[smem, smem, hbm, hbm, hbm],
         out_specs=vmem,
         out_shape=jax.ShapeDtypeStruct(
             (components, leaf_rows * LEAF_R, leaf_cols * LEAF_C, port_count), jnp.bfloat16
@@ -192,12 +212,11 @@
         scratch_shapes=[
             pltpu.VMEM(bordered.shape, bordered.dtype),
             pltpu.VMEM(kernels.shape, kernels.dtype),
-            pltpu.VMEM(coupling_t.shape, coupling_t.dtype),
-            pltpu.VMEM(current.shape, current.dtype),
-            pltpu.SemaphoreType.DMA((3,)),
+            pltpu.VMEM(filament.shape, filament.dtype),
+            pltpu.SemaphoreType.DMA((2,)),
             pltpu.SemaphoreType.DMA((leaf_count,)),
         ],
-    )(codes, scales, bordered, kernels, row_leaf, coupling_t, current)
+    )(codes, scales, bordered, kernels, filament)
     field, bordered = lax.optimization_barrier((field, bordered))
     volt = pl.pallas_call(
         induced_kernel,
@@ -255,9 +274,10 @@
     got_coupling_t = got_rows[:, : 2 * leaf_cells].T
     got_current = got_rows[:, 2 * leaf_cells :]
     got_leaf = got_leaf.reshape(1, slot_count)
-
-    window, (got_leaf, got_coupling_t, got_current) = stream_window(
-        stream.transpose(1, 2, 0), half_cols, (got_leaf, got_coupling_t, got_current)
+    filament = filament_field(got_leaf, got_coupling_t, got_current, leaf_count)
+
+    window, (got_leaf, got_coupling_t, filament) = stream_window(
+        stream.transpose(1, 2, 0), half_cols, (got_leaf, got_coupling_t, filament)
     )
     currents = plane_curl(window).astype(jnp.bfloat16)
     bordered = to_leaves(currents)
@@ -272,7 +292,7 @@
     kernels = inductance.reshape(leaf_count, near_count, 2, leaf_cells, leaf_cells)
     codes = near_lists.reshape(leaf_count, near_count)
     total_field, induced = leaf_fields(
-        codes, scales, bordered, kernels, got_leaf, got_coupling_t, got_current
+        codes, scales, bordered, kernels, filament, got_leaf, got_coupling_t
     )
     returned = lax.all_to_all(
         induced.reshape(owners, capacity, port_count), AXES, split_axis=0, concat_axis=0, tiled=True

time: 102 us -> 102 us (level)
  waiting for transfers between devices: 15.5 us -> 8.45 us
  Pallas kernels: 20 us -> 26.5 us
    ppermute x7, waiting for transfers between devices: 11.8 us -> 4.8 us  [send(): return lax.ppermute(value, AXES, pairs_by(fn))]
    pallas_call x1 -> x2, Pallas kernels: 13.1 us -> 19.5 us  [the longest x1 12.5 us: leaf_fields(): pl.pallas_call(leaf_kernel, in_specs=[smem, smem, hbm, hbm, hbm], out_spe...]
  transfers between devices with their start and end apart: 9 -> 9, of which waited for: 5 -> 4; matrix products, arithmetic and copies ran while one was open for 18% -> 18% of each run, Pallas kernels for 7% -> 14%
where the time goes in v13:
time: 102 us; the launch traced here: 101 us
  starting transfers between devices  33.2 us (33%)
  Pallas kernels  26.5 us (26%)
  local copies, waits for them, and re-layouts  19.7 us (19%)
  waiting for transfers between devices  8.45 us (8%)
  other arithmetic  8.33 us (8%)
  matrix products  3.5 us (3%)
    ppermute x7, starting transfers between devices, send(): return lax.ppermute(value, AXES, pairs_by(fn))  18.2 us
    pallas_call x1, Pallas kernels, leaf_fields(): pl.pallas_call(leaf_kernel, in_specs=[smem, smem, hbm, hbm, hbm], out_spe...  12.5 us
    unnamed x11, local copies, waits for them, and re-layouts  8.34 us
    all_to_all x1, starting transfers between devices, body(): lax.all_to_all(induced.reshape(owners, capacity, port_count), AXES, split...  7.67 us
    all_to_all x1, starting transfers between devices, body(): got = lax.all_to_all(payload, AXES, split_axis=0, concat_axis=0, tiled=True)  7.4 us
    pallas_call x1, Pallas kernels, filament_field(): pl.pallas_call(filament_kernel, in_specs=[vmem, vmem, vmem], out_specs=vm...  7.02 us
    pallas_call x1, Pallas kernels, leaf_fields(): pl.pallas_call(induced_kernel, in_specs=[vmem, vmem, vmem], out_specs=vme...  6.94 us
    ppermute x7, waiting for transfers between devices, send(): return lax.ppermute(value, AXES, pairs_by(fn))  4.8 us
  transfers between devices with their start and end apart: 9, of which 4 were waited for; matrix products, arithmetic and copies ran while one was open for 18% of the time, Pallas kernels for 14%

profile of v13, /device:TPU:0, one launch (start us, length us, event | category | flops | bytes accessed | tf_op | source)
XLA Modules:
  0.0 100.6 jit_solution(5449344468934374270)
XLA Ops:
  0.6 0.0 copy-start
  0.6 0.9 fusion.25
  1.5 0.2 convert_reduce_fusion
  1.8 0.5 fusion.3
  2.2 0.1 reshape.77
  2.3 1.0 copy.46
  3.3 1.6 %fusion.6 = bf16[1024,384]{1,0:T(8,128)(2,1)S(1)} fusion(s32[512]{0:T(512)S(1)} %multiply_add_fusion, bf16[512,128]{1,0:T(8,128)(2,1)} %param.10, bf16[512,256]{1,0:T(8,128)(2,1)S(1)} %bitcast.47), kind=kOutput, calls=%fused_computation.15 | convolution fusion | flops 404357120 | bytes 1181696 | tf_op jit(solution)/shard_map/dot_general | solution.py:262
  4.9 1.0 fusion.16
  5.9 7.4 %all-to-all-start = ((bf16[16,65,384]{2,1,0:T(8,128)(2,1)}), bf16[16,65,384]{2,1,0:T(8,128)(2,1)}, u32[]{:S(2)}, u32[]{:S(2)}) async-start(bf16[16,65,384]{2,1,0:T(8,128)(2,1)} %fusion.16), calls=%async_computation | async-start | bytes 1769472 | tf_op jit(solution)/shard_map/all_to_all | solution.py:271
  13.3 0.0 copy-done
  13.4 0.3 constant_dynamic-slice_fusion.1
  13.7 0.4 copy.40
  14.2 0.7 collective-permute-start
  14.8 2.0 %constant_dynamic-slice_fusion = f32[128,16,145]{2,1,0:T(8,128)} fusion(f32[128,16,256]{2,1,0:T(8,128)S(1)} %copy-done, s32[]{:T(128)S(6)} %select_n.49), kind=kLoop, calls=%fused_computation.78 | loop fusion | bytes 2375684 | tf_op jit(solution)/shard_map/dynamic-slice.1
  16.8 2.8 %copy.41 = f32[128,16,145]{0,2,1:T(8,128)} copy(f32[128,16,145]{2,1,0:T(8,128)} %constant_dynamic-slice_fusion) | data formatting | bytes 2375680
  19.6 0.0 collective-permute-done
  19.6 0.0 copy-start.1
  19.6 0.7 copy-done.1
  20.2 1.9 %fusion.8 = f32[16,162,128]{2,1,0:T(8,128)S(1)} fusion(s32[]{:T(128)S(6)} %select_n.50, f32[16,17,128]{2,1,0:T(8,128)} %copy-done.1, f32[16,145,128]{2,1,0:T(8,128)} %bitcast.38), kind=kLoop, calls=%fused_computation.17 | loop fusion | flops 663552 | bytes 2654212 | tf_op jit(solution)/shard_map/concatenate | solution.py:79
  22.2 0.0 copy-start.2
  22.2 1.3 %fusion.34 = (f32[9,162,128]{2,1,0:T(8,128)}, f32[9,162,128]{2,1,0:T(8,128)}) fusion(f32[16,162,128]{2,1,0:T(8,128)S(1)} %fusion.8), kind=kLoop, calls=%fused_computation.84 | loop fusion | bytes 2985984 | tf_op jit(solution)/shard_map/slice | solution.py:82
  23.4 4.7 %collective-permute-start.1 = (f32[9,162,128]{2,1,0:T(8,128)}, f32[9,162,128]{2,1,0:T(8,128)}, u32[]{:S(2)}, u32[]{:S(2)}) collective-permute-start(f32[9,162,128]{2,1,0:T(8,128)} %get-tuple-element.25), channel_id=1, source_target_pairs={{0,4},{1,5},{2,6},{3,7},{4,8},{5,9},{6,10},{7,11},{8,12},{9,13},{1... | collective-permute-start | bytes 2239496 | tf_op jit(solution)/shard_map/ppermute | solution.py:58
  28.1 1.3 %collective-permute-start.2 = (f32[9,162,128]{2,1,0:T(8,128)}, f32[9,162,128]{2,1,0:T(8,128)}, u32[]{:S(2)}, u32[]{:S(2)}) collective-permute-start(f32[9,162,128]{2,1,0:T(8,128)} %get-tuple-element.24), channel_id=1, source_target_pairs={{4,0},{5,1},{6,2},{7,3},{8,4},{9,5},{10,6},{11,7},{12,8},{13,9},{1... | collective-permute-start | bytes 2239496 | tf_op jit(solution)/shard_map/ppermute | solution.py:58
  29.4 0.0 copy-done.2
  29.4 0.6 convert_bitcast_fusion.scale_ref
  30.0 3.7 %all-to-all-done = bf16[16,65,384]{2,1,0:T(8,128)(2,1)} async-done(((bf16[16,65,384]{2,1,0:T(8,128)(2,1)}), bf16[16,65,384]{2,1,0:T(8,128)(2,1)}, u32[]{:S(2)}, u32[]{:S(2)}) %all-to-all-start) | async-done | bytes 798752 | tf_op jit(solution)/shard_map/all_to_all | solution.py:271
  33.7 1.2 %slice.93 = bf16[16,64,384]{2,1,0:T(8,128)(2,1)S(1)} slice(bf16[16,65,384]{2,1,0:T(8,128)(2,1)} %all-to-all-done), slice={[0:16], [0:64], [0:384]} | slice | bytes 1572864 | tf_op jit(solution)/shard_map/slice | solution.py:272
  34.9 0.8 slice.94
  35.7 0.7 slice.95.cur_ref
  36.5 2.0 %copy.42 = bf16[1024,256]{0,1:T(8,128)(2,1)} copy(bf16[1024,256]{1,0:T(8,128)(2,1)} %slice.94) | data formatting | bytes 1048576
  38.5 0.8 fusion.22
  39.3 0.7 reshape.74.row_leaf_ref
  40.0 7.0 %shard_map.77.fil_hbm = f32[16,256,128]{2,1,0:T(8,128)} custom-call(s32[1,1024]{1,0:T(1,128)} %reshape.74.row_leaf_ref, bf16[256,1024]{1,0:T(8,128)(2,1)} %bitcast.39, bf16[1024,128]{1,0:T(8,128)(2,1)} %slice.95.cur_ref), custom_call_target="tpu_custom_call" | custom-call | tf_op jit(solution)/shard_map/pallas_call | solution.py:119
  47.0 0.0 collective-permute-done.1
  47.0 0.4 collective-permute-done.2
  47.4 1.6 %pad_maximum_fusion = f32[34,162,128]{2,1,0:T(8,128)S(1)} fusion(f32[9,162,128]{2,1,0:T(8,128)} %collective-permute-done.2, f32[16,162,128]{2,1,0:T(8,128)S(1)} %fusion.8, f32[9,162,128]{2,1,0:T(8,128)} %collective-permute-done.1), kind=kLoop, calls=%fused_computation | loop fusion | flops 1410048 | bytes 5640192 | tf_op jit(solution)/shard_map/concatenate | solution.py:84
  48.9 0.7 fusion.1
  49.6 0.2 maximum_bitcast_fusion
  49.9 2.3 %copy.34 = bf16[4,10,2,8,16,128]{5,4,3,2,1,0:T(8,128)(2,1)} copy(bf16[4,10,2,8,16,128]{5,4,1,3,0,2:T(8,128)(2,1)S(1)} %maximum_bitcast_fusion) | data formatting | bytes 5242880 | tf_op jit(solution)/shard_map/transpose | solution.py:24
  52.1 12.5 %shard_map.78 = bf16[2,16,128,128]{3,2,1,0:T(8,128)(2,1)} custom-call(s32[16,8]{1,0:T(8,128)} %bitcast.49, s32[16,8]{1,0:T(8,128)} %convert_bitcast_fusion.scale_ref, bf16[4,10,2,128,128]{4,3,2,1,0:T(8,128)(2,1)} %bitcast.33, bf16[16,8,2,128,128]{4,3,2,1,0:T(8,128)(2,1)} %bitcast.35, f32[16,256,128]{2,1,0:T(8,128)} %shard_map.77.fil_hbm), custom_call_target="tpu_custom_call" | custom-call | tf_op jit(solution)/shard_map/pallas_call | solution.py:205
  64.7 1.3 %slice_bitcast_fusion.1 = (bf16[16,128,128]{2,1,0:T(8,128)(2,1)S(1)}, bf16[16,128,128]{2,1,0:T(8,128)(2,1)S(1)}) fusion(bf16[2,16,128,128]{3,2,1,0:T(8,128)(2,1)} %shard_map.78), kind=kLoop, calls=%fused_computation.33 | loop fusion | bytes 2097152 | tf_op jit(solution)/shard_map/squeeze | solution.py:88
  66.0 5.1 %collective-permute-start.3 = (bf16[16,1,128]{2,1,0:T(2,128)(2,1)S(1)}, bf16[16,1,128]{2,1,0:T(2,128)(2,1)S(1)}, u32[]{:S(2)}, u32[]{:S(2)}) collective-permute-start(bf16[16,1,128]{2,1,0:T(2,128)(2,1)S(1)} %get-tuple-element.30), channel_id=1, source_target_pairs={{0,1},{1,2},{2,3},{4,5},{5,6},{6,7},{8,9},{9,10},{10,11},{12,13},{... | collective-permute-start | bytes 12296 | tf_op jit(solution)/shard_map/ppermute | solution.py:58
  71.1 1.3 %collective-permute-start.4 = (bf16[16,1,128]{2,1,0:T(2,128)(2,1)S(1)}, bf16[16,1,128]{2,1,0:T(2,128)(2,1)S(1)}, u32[]{:S(2)}, u32[]{:S(2)}) collective-permute-start(bf16[16,1,128]{2,1,0:T(2,128)(2,1)S(1)} %get-tuple-element.31), channel_id=1, source_target_pairs={{1,0},{2,1},{3,2},{5,4},{6,5},{7,6},{9,8},{10,9},{11,10},{13,12},{... | collective-permute-start | bytes 12296 | tf_op jit(solution)/shard_map/ppermute | solution.py:58
  72.4 0.8 slice_bitcast_fusion.3
  73.2 6.9 %shard_map.79 = bf16[1024,128]{1,0:T(8,128)(2,1)} custom-call(bf16[4,10,2,128,128]{4,3,2,1,0:T(8,128)(2,1)} %bitcast.34, s32[1,1024]{1,0:T(1,128)} %reshape.74.row_leaf_ref, bf16[256,1024]{1,0:T(8,128)(2,1)} %bitcast.40), custom_call_target="tpu_custom_call" | custom-call | tf_op jit(solution)/shard_map/pallas_call | solution.py:221
  80.1 7.7 %all-to-all-start.1 = ((bf16[16,64,128]{2,1,0:T(8,128)(2,1)}), bf16[16,64,128]{2,1,0:T(8,128)(2,1)S(1)}, u32[]{:S(2)}, u32[]{:S(2)}) async-start(bf16[16,64,128]{2,1,0:T(8,128)(2,1)} %bitcast.43), calls=%async_computation.1 | async-start | bytes 524288 | tf_op jit(solution)/shard_map/all_to_all | solution.py:297
  87.8 3.8 %collective-permute-start.5 = (bf16[1,128,128]{2,1,0:T(8,128)(2,1)S(1)}, bf16[1,128,128]{2,1,0:T(8,128)(2,1)S(1)}, u32[]{:S(2)}, u32[]{:S(2)}) collective-permute-start(bf16[1,128,128]{2,1,0:T(8,128)(2,1)S(1)} %get-tuple-element.28), channel_id=1, source_target_pairs={{0,4},{1,5},{2,6},{3,7},{4,8},{5,9},{6,10},{7,11},{8,12},{9,13},{1... | collective-permute-start | bytes 98312 | tf_op jit(solution)/shard_map/ppermute | solution.py:58
  91.6 1.3 %collective-permute-start.6 = (bf16[1,128,128]{2,1,0:T(8,128)(2,1)S(1)}, bf16[1,128,128]{2,1,0:T(8,128)(2,1)S(1)}, u32[]{:S(2)}, u32[]{:S(2)}) collective-permute-start(bf16[1,128,128]{2,1,0:T(8,128)(2,1)S(1)} %get-tuple-element.29), channel_id=1, source_target_pairs={{4,0},{5,1},{6,2},{7,3},{8,4},{9,5},{10,6},{11,7},{12,8},{13,9},{1... | collective-permute-start | bytes 98312 | tf_op jit(solution)/shard_map/ppermute | solution.py:58
  92.9 0.0 collective-permute-done.3
  93.0 0.0 collective-permute-done.4
  93.0 0.1 maximum_convert_fusion.1
  93.1 0.7 collective-permute-done.5
  93.8 3.7 %collective-permute-done.6 = bf16[1,128,128]{2,1,0:T(8,128)(2,1)S(1)} collective-permute-done((bf16[1,128,128]{2,1,0:T(8,128)(2,1)S(1)}, bf16[1,128,128]{2,1,0:T(8,128)(2,1)S(1)}, u32[]{:S(2)}, u32[]{:S(2)}) %collective-permute-start.6) | collective-permute-done | bytes 32800 | tf_op jit(solution)/shard_map/ppermute | solution.py:58
  97.5 0.1 maximum_convert_fusion
  97.6 0.2 fusion.11
  97.8 1.4 %copy.37 = f32[128,16,128]{2,1,0:T(8,128)} copy(f32[128,16,128]{0,2,1:T(8,128)S(1)} %fusion.11) | data formatting | bytes 2097152
  99.2 0.0 all-to-all-done.1
  99.2 1.4 %fusion.9 = bf16[512,128]{1,0:T(8,128)(2,1)} fusion(bf16[1024,128]{1,0:T(8,128)(2,1)S(1)} %bitcast.46, s32[512]{0:T(512)S(1)} %multiply_add_fusion), kind=kOutput, calls=%fused_computation.18 | convolution fusion | flops 134807552 | bytes 395264 | tf_op jit(solution)/shard_map/dot_general | solution.py:300
  (4 shorter events, 0.0 us)
Async XLA Ops:
  0.6 12.7 %copy-start = (f32[128,16,256]{2,1,0:T(8,128)S(1)}, f32[128,16,256]{2,1,0:T(8,128)}, u32[]{:S(2)}) copy-start(f32[128,16,256]{2,1,0:T(8,128)} %param.6) | copy-start | bytes 6291460
  5.9 27.8 %all-to-all-start = ((bf16[16,65,384]{2,1,0:T(8,128)(2,1)}), bf16[16,65,384]{2,1,0:T(8,128)(2,1)}, u32[]{:S(2)}, u32[]{:S(2)}) async-start(bf16[16,65,384]{2,1,0:T(8,128)(2,1)} %fusion.16), calls=%async_computation | async-start | bytes 1769472 | tf_op jit(solution)/shard_map/all_to_all | solution.py:271
  14.2 5.4 %collective-permute-start = (f32[16,17,128]{2,1,0:T(8,128)S(1)}, f32[16,17,128]{2,1,0:T(8,128)S(1)}, u32[]{:S(2)}, u32[]{:S(2)}) collective-permute-start(f32[16,17,128]{2,1,0:T(8,128)S(1)} %bitcast.48), channel_id=1, source_target_pairs={{1,2},{2,1},{5,6},{6,5},{9,10},{10,9},{13,14},{14,13},{17,18},{18,... | collective-permute-start | bytes 417800 | tf_op jit(solution)/shard_map/ppermute | solution.py:58
  19.6 0.7 copy-start.1
  22.2 7.3 %copy-start.2 = (s32[2,8,8]{2,1,0:T(8,128)S(1)}, s32[2,8,8]{2,1,0:T(8,128)}, u32[]{:S(2)}) copy-start(s32[2,8,8]{2,1,0:T(8,128)} %param.8) | copy-start | bytes 1540
  23.4 23.6 %collective-permute-start.1 = (f32[9,162,128]{2,1,0:T(8,128)}, f32[9,162,128]{2,1,0:T(8,128)}, u32[]{:S(2)}, u32[]{:S(2)}) collective-permute-start(f32[9,162,128]{2,1,0:T(8,128)} %get-tuple-element.25), channel_id=1, source_target_pairs={{0,4},{1,5},{2,6},{3,7},{4,8},{5,9},{6,10},{7,11},{8,12},{9,13},{1... | collective-permute-start | bytes 2239496 | tf_op jit(solution)/shard_map/ppermute | solution.py:58
  28.1 19.3 %collective-permute-start.2 = (f32[9,162,128]{2,1,0:T(8,128)}, f32[9,162,128]{2,1,0:T(8,128)}, u32[]{:S(2)}, u32[]{:S(2)}) collective-permute-start(f32[9,162,128]{2,1,0:T(8,128)} %get-tuple-element.24), channel_id=1, source_target_pairs={{4,0},{5,1},{6,2},{7,3},{8,4},{9,5},{10,6},{11,7},{12,8},{13,9},{1... | collective-permute-start | bytes 2239496 | tf_op jit(solution)/shard_map/ppermute | solution.py:58
  66.0 27.0 %collective-permute-start.3 = (bf16[16,1,128]{2,1,0:T(2,128)(2,1)S(1)}, bf16[16,1,128]{2,1,0:T(2,128)(2,1)S(1)}, u32[]{:S(2)}, u32[]{:S(2)}) collective-permute-start(bf16[16,1,128]{2,1,0:T(2,128)(2,1)S(1)} %get-tuple-element.30), channel_id=1, source_target_pairs={{0,1},{1,2},{2,3},{4,5},{5,6},{6,7},{8,9},{9,10},{10,11},{12,13},{... | collective-permute-start | bytes 12296 | tf_op jit(solution)/shard_map/ppermute | solution.py:58
  71.1 21.8 %collective-permute-start.4 = (bf16[16,1,128]{2,1,0:T(2,128)(2,1)S(1)}, bf16[16,1,128]{2,1,0:T(2,128)(2,1)S(1)}, u32[]{:S(2)}, u32[]{:S(2)}) collective-permute-start(bf16[16,1,128]{2,1,0:T(2,128)(2,1)S(1)} %get-tuple-element.31), channel_id=1, source_target_pairs={{1,0},{2,1},{3,2},{5,4},{6,5},{7,6},{9,8},{10,9},{11,10},{13,12},{... | collective-permute-start | bytes 12296 | tf_op jit(solution)/shard_map/ppermute | solution.py:58
  80.1 19.0 %all-to-all-start.1 = ((bf16[16,64,128]{2,1,0:T(8,128)(2,1)}), bf16[16,64,128]{2,1,0:T(8,128)(2,1)S(1)}, u32[]{:S(2)}, u32[]{:S(2)}) async-start(bf16[16,64,128]{2,1,0:T(8,128)(2,1)} %bitcast.43), calls=%async_computation.1 | async-start | bytes 524288 | tf_op jit(solution)/shard_map/all_to_all | solution.py:297
  87.8 6.0 %collective-permute-start.5 = (bf16[1,128,128]{2,1,0:T(8,128)(2,1)S(1)}, bf16[1,128,128]{2,1,0:T(8,128)(2,1)S(1)}, u32[]{:S(2)}, u32[]{:S(2)}) collective-permute-start(bf16[1,128,128]{2,1,0:T(8,128)(2,1)S(1)} %get-tuple-element.28), channel_id=1, source_target_pairs={{0,4},{1,5},{2,6},{3,7},{4,8},{5,9},{6,10},{7,11},{8,12},{9,13},{1... | collective-permute-start | bytes 98312 | tf_op jit(solution)/shard_map/ppermute | solution.py:58
  91.6 5.9 %collective-permute-start.6 = (bf16[1,128,128]{2,1,0:T(8,128)(2,1)S(1)}, bf16[1,128,128]{2,1,0:T(8,128)(2,1)S(1)}, u32[]{:S(2)}, u32[]{:S(2)}) collective-permute-start(bf16[1,128,128]{2,1,0:T(8,128)(2,1)S(1)} %get-tuple-element.29), channel_id=1, source_target_pairs={{4,0},{5,1},{6,2},{7,3},{8,4},{9,5},{10,6},{11,7},{12,8},{13,9},{1... | collective-permute-start | bytes 98312 | tf_op jit(solution)/shard_map/ppermute | solution.py:58

commit v14 on v13

--- a/solution.py
+++ b/solution.py
@@ -172,24 +172,29 @@
     lax.fori_loop(0, leaf_count, one_leaf, 0)
 
 
-def induced_kernel(bord_ref, row_leaf_ref, cpl_t_ref, volt_ref, acc_ref):
-    leaf_rows = bord_ref.shape[0] - 2
-    leaf_cols = bord_ref.shape[1] - 2
-    cells = bord_ref.shape[3]
+def induced_kernel(bord_hbm, row_leaf_ref, cpl_t_ref, volt_ref, own_ref, acc_ref, sems):
+    leaf_rows = own_ref.shape[0]
+    leaf_cols = own_ref.shape[1] - 2
+    cells = own_ref.shape[3]
+    copies = [
+        pltpu.make_async_copy(bord_hbm.at[r + 1], own_ref.at[r], sems.at[r]) for r in range(leaf_rows)
+    ]
+    for copy in copies:
+        copy.start()
     acc_ref[...] = jnp.zeros_like(acc_ref)
 
-    def one_leaf(leaf, carry):
-        row = leaf // leaf_cols
-        col = leaf % leaf_cols
+    def one_leaf(row, col):
         coupling_t = cpl_t_ref[...]
+        leaf = row * leaf_cols + col
         coupling_t = jnp.where(row_leaf_ref[...] == leaf, coupling_t, jnp.zeros_like(coupling_t))
-        own = bord_ref[row + 1, col + 1].reshape(2 * cells, -1)
+        own = own_ref[row, col + 1].reshape(2 * cells, -1)
         acc_ref[...] += lax.dot_general(
             own, coupling_t, (((0,), (0,)), ((), ())), preferred_element_type=jnp.float32
         )
-        return carry
-
-    lax.fori_loop(0, leaf_rows * leaf_cols, one_leaf, 0)
+
+    for r in range(leaf_rows):
+        copies[r].wait()
+        lax.fori_loop(0, leaf_cols, lambda col, carry: (one_leaf(r, col), carry)[1], 0)
     volt_ref[...] = acc_ref[...].T.astype(volt_ref.dtype)
 
 
@@ -220,10 +225,14 @@
     field, bordered = lax.optimization_barrier((field, bordered))
     volt = pl.pallas_call(
         induced_kernel,
-        in_specs=[vmem, vmem, vmem],
+        in_specs=[hbm, vmem, vmem],
         out_specs=vmem,
         out_shape=jax.ShapeDtypeStruct((slot_count, port_count), jnp.bfloat16),
-        scratch_shapes=[pltpu.VMEM((port_count, slot_count), jnp.float32)],
+        scratch_shapes=[
+            pltpu.VMEM((leaf_rows,) + bordered.shape[1:], bordered.dtype),
+            pltpu.VMEM((port_count, slot_count), jnp.float32),
+            pltpu.SemaphoreType.DMA((leaf_rows,)),
+        ],
     )(bordered, row_leaf, coupling_t)
     return field, volt
 

time: 102 us -> 102 us (level)
  no operation moved by 1% of the time
where the time goes in v14:
time: 102 us; the launch traced here: 101 us
  starting transfers between devices  33.3 us (33%)
  Pallas kernels  26.6 us (26%)
  local copies, waits for them, and re-layouts  19.7 us (19%)
  waiting for transfers between devices  8.45 us (8%)
  other arithmetic  8.33 us (8%)
  matrix products  3.5 us (3%)
    ppermute x7, starting transfers between devices, send(): return lax.ppermute(value, AXES, pairs_by(fn))  18.2 us
    pallas_call x1, Pallas kernels, leaf_fields(): pl.pallas_call(leaf_kernel, in_specs=[smem, smem, hbm, hbm, hbm], out_spe...  12.5 us
    unnamed x11, local copies, waits for them, and re-layouts  8.34 us
    all_to_all x1, starting transfers between devices, body(): lax.all_to_all(induced.reshape(owners, capacity, port_count), AXES, split...  7.68 us
    all_to_all x1, starting transfers between devices, body(): got = lax.all_to_all(payload, AXES, split_axis=0, concat_axis=0, tiled=True)  7.4 us
    pallas_call x1, Pallas kernels, leaf_fields(): pl.pallas_call(induced_kernel, in_specs=[hbm, vmem, vmem], out_specs=vmem...  7.09 us
    pallas_call x1, Pallas kernels, filament_field(): pl.pallas_call(filament_kernel, in_specs=[vmem, vmem, vmem], out_specs=vm...  7.02 us
    ppermute x7, waiting for transfers between devices, send(): return lax.ppermute(value, AXES, pairs_by(fn))  4.8 us
  transfers between devices with their start and end apart: 9, of which 4 were waited for; matrix products, arithmetic and copies ran while one was open for 18% of the time, Pallas kernels for 14%

profile of v14, /device:TPU:0, one launch (start us, length us, event | category | flops | bytes accessed | tf_op | source)
XLA Modules:
  0.0 100.8 jit_solution(1011333128522871508)
XLA Ops:
  0.6 0.0 copy-start
  0.6 0.9 fusion.25
  1.5 0.2 convert_reduce_fusion
  1.8 0.5 fusion.3
  2.2 0.1 reshape.77
  2.3 1.0 copy.46
  3.3 1.6 %fusion.6 = bf16[1024,384]{1,0:T(8,128)(2,1)S(1)} fusion(s32[512]{0:T(512)S(1)} %multiply_add_fusion, bf16[512,128]{1,0:T(8,128)(2,1)} %param.10, bf16[512,256]{1,0:T(8,128)(2,1)S(1)} %bitcast.47), kind=kOutput, calls=%fused_computation.15 | convolution fusion | flops 404357120 | bytes 1181696 | tf_op jit(solution)/shard_map/dot_general | solution.py:271
  4.9 1.0 fusion.16
  5.9 7.4 %all-to-all-start = ((bf16[16,65,384]{2,1,0:T(8,128)(2,1)}), bf16[16,65,384]{2,1,0:T(8,128)(2,1)}, u32[]{:S(2)}, u32[]{:S(2)}) async-start(bf16[16,65,384]{2,1,0:T(8,128)(2,1)} %fusion.16), calls=%async_computation | async-start | bytes 1769472 | tf_op jit(solution)/shard_map/all_to_all | solution.py:280
  13.3 0.0 copy-done
  13.4 0.3 constant_dynamic-slice_fusion.1
  13.7 0.4 copy.40
  14.2 0.7 collective-permute-start
  14.8 2.0 %constant_dynamic-slice_fusion = f32[128,16,145]{2,1,0:T(8,128)} fusion(f32[128,16,256]{2,1,0:T(8,128)S(1)} %copy-done, s32[]{:T(128)S(6)} %select_n.49), kind=kLoop, calls=%fused_computation.78 | loop fusion | bytes 2375684 | tf_op jit(solution)/shard_map/dynamic-slice.1
  16.8 2.8 %copy.41 = f32[128,16,145]{0,2,1:T(8,128)} copy(f32[128,16,145]{2,1,0:T(8,128)} %constant_dynamic-slice_fusion) | data formatting | bytes 2375680
  19.6 0.0 collective-permute-done
  19.6 0.0 copy-start.1
  19.6 0.7 copy-done.1
  20.2 1.9 %fusion.8 = f32[16,162,128]{2,1,0:T(8,128)S(1)} fusion(s32[]{:T(128)S(6)} %select_n.50, f32[16,17,128]{2,1,0:T(8,128)} %copy-done.1, f32[16,145,128]{2,1,0:T(8,128)} %bitcast.38), kind=kLoop, calls=%fused_computation.17 | loop fusion | flops 663552 | bytes 2654212 | tf_op jit(solution)/shard_map/concatenate | solution.py:79
  22.2 0.0 copy-start.2
  22.2 1.3 %fusion.34 = (f32[9,162,128]{2,1,0:T(8,128)}, f32[9,162,128]{2,1,0:T(8,128)}) fusion(f32[16,162,128]{2,1,0:T(8,128)S(1)} %fusion.8), kind=kLoop, calls=%fused_computation.84 | loop fusion | bytes 2985984 | tf_op jit(solution)/shard_map/slice | solution.py:82
  23.4 4.7 %collective-permute-start.1 = (f32[9,162,128]{2,1,0:T(8,128)}, f32[9,162,128]{2,1,0:T(8,128)}, u32[]{:S(2)}, u32[]{:S(2)}) collective-permute-start(f32[9,162,128]{2,1,0:T(8,128)} %get-tuple-element.25), channel_id=1, source_target_pairs={{0,4},{1,5},{2,6},{3,7},{4,8},{5,9},{6,10},{7,11},{8,12},{9,13},{1... | collective-permute-start | bytes 2239496 | tf_op jit(solution)/shard_map/ppermute | solution.py:58
  28.1 1.3 %collective-permute-start.2 = (f32[9,162,128]{2,1,0:T(8,128)}, f32[9,162,128]{2,1,0:T(8,128)}, u32[]{:S(2)}, u32[]{:S(2)}) collective-permute-start(f32[9,162,128]{2,1,0:T(8,128)} %get-tuple-element.24), channel_id=1, source_target_pairs={{4,0},{5,1},{6,2},{7,3},{8,4},{9,5},{10,6},{11,7},{12,8},{13,9},{1... | collective-permute-start | bytes 2239496 | tf_op jit(solution)/shard_map/ppermute | solution.py:58
  29.4 0.0 copy-done.2
  29.4 0.6 convert_bitcast_fusion.scale_ref
  30.0 3.7 %all-to-all-done = bf16[16,65,384]{2,1,0:T(8,128)(2,1)} async-done(((bf16[16,65,384]{2,1,0:T(8,128)(2,1)}), bf16[16,65,384]{2,1,0:T(8,128)(2,1)}, u32[]{:S(2)}, u32[]{:S(2)}) %all-to-all-start) | async-done | bytes 798752 | tf_op jit(solution)/shard_map/all_to_all | solution.py:280
  33.7 1.2 %slice.93 = bf16[16,64,384]{2,1,0:T(8,128)(2,1)S(1)} slice(bf16[16,65,384]{2,1,0:T(8,128)(2,1)} %all-to-all-done), slice={[0:16], [0:64], [0:384]} | slice | bytes 1572864 | tf_op jit(solution)/shard_map/slice | solution.py:281
  34.9 0.8 slice.94
  35.7 0.7 slice.95.cur_ref
  36.5 2.0 %copy.42 = bf16[1024,256]{0,1:T(8,128)(2,1)} copy(bf16[1024,256]{1,0:T(8,128)(2,1)} %slice.94) | data formatting | bytes 1048576
  38.5 0.8 fusion.22
  39.3 0.7 reshape.74.row_leaf_ref
  40.0 7.0 %shard_map.77.fil_hbm = f32[16,256,128]{2,1,0:T(8,128)} custom-call(s32[1,1024]{1,0:T(1,128)} %reshape.74.row_leaf_ref, bf16[256,1024]{1,0:T(8,128)(2,1)} %bitcast.39, bf16[1024,128]{1,0:T(8,128)(2,1)} %slice.95.cur_ref), custom_call_target="tpu_custom_call" | custom-call | tf_op jit(solution)/shard_map/pallas_call | solution.py:119
  47.0 0.0 collective-permute-done.1
  47.0 0.4 collective-permute-done.2
  47.4 1.6 %pad_maximum_fusion = f32[34,162,128]{2,1,0:T(8,128)S(1)} fusion(f32[9,162,128]{2,1,0:T(8,128)} %collective-permute-done.2, f32[16,162,128]{2,1,0:T(8,128)S(1)} %fusion.8, f32[9,162,128]{2,1,0:T(8,128)} %collective-permute-done.1), kind=kLoop, calls=%fused_computation | loop fusion | flops 1410048 | bytes 5640192 | tf_op jit(solution)/shard_map/concatenate | solution.py:84
  48.9 0.7 fusion.1
  49.6 0.2 maximum_bitcast_fusion
  49.9 2.3 %copy.34 = bf16[4,10,2,8,16,128]{5,4,3,2,1,0:T(8,128)(2,1)} copy(bf16[4,10,2,8,16,128]{5,4,1,3,0,2:T(8,128)(2,1)S(1)} %maximum_bitcast_fusion) | data formatting | bytes 5242880 | tf_op jit(solution)/shard_map/transpose | solution.py:24
  52.1 12.5 %shard_map.78 = bf16[2,16,128,128]{3,2,1,0:T(8,128)(2,1)} custom-call(s32[16,8]{1,0:T(8,128)} %bitcast.49, s32[16,8]{1,0:T(8,128)} %convert_bitcast_fusion.scale_ref, bf16[4,10,2,128,128]{4,3,2,1,0:T(8,128)(2,1)} %bitcast.33, bf16[16,8,2,128,128]{4,3,2,1,0:T(8,128)(2,1)} %bitcast.35, f32[16,256,128]{2,1,0:T(8,128)} %shard_map.77.fil_hbm), custom_call_target="tpu_custom_call" | custom-call | tf_op jit(solution)/shard_map/pallas_call | solution.py:210
  64.7 1.3 %slice_bitcast_fusion.1 = (bf16[16,128,128]{2,1,0:T(8,128)(2,1)S(1)}, bf16[16,128,128]{2,1,0:T(8,128)(2,1)S(1)}) fusion(bf16[2,16,128,128]{3,2,1,0:T(8,128)(2,1)} %shard_map.78), kind=kLoop, calls=%fused_computation.33 | loop fusion | bytes 2097152 | tf_op jit(solution)/shard_map/squeeze | solution.py:88
  66.0 5.1 %collective-permute-start.3 = (bf16[16,1,128]{2,1,0:T(2,128)(2,1)S(1)}, bf16[16,1,128]{2,1,0:T(2,128)(2,1)S(1)}, u32[]{:S(2)}, u32[]{:S(2)}) collective-permute-start(bf16[16,1,128]{2,1,0:T(2,128)(2,1)S(1)} %get-tuple-element.30), channel_id=1, source_target_pairs={{0,1},{1,2},{2,3},{4,5},{5,6},{6,7},{8,9},{9,10},{10,11},{12,13},{... | collective-permute-start | bytes 12296 | tf_op jit(solution)/shard_map/ppermute | solution.py:58
  71.1 1.3 %collective-permute-start.4 = (bf16[16,1,128]{2,1,0:T(2,128)(2,1)S(1)}, bf16[16,1,128]{2,1,0:T(2,128)(2,1)S(1)}, u32[]{:S(2)}, u32[]{:S(2)}) collective-permute-start(bf16[16,1,128]{2,1,0:T(2,128)(2,1)S(1)} %get-tuple-element.31), channel_id=1, source_target_pairs={{1,0},{2,1},{3,2},{5,4},{6,5},{7,6},{9,8},{10,9},{11,10},{13,12},{... | collective-permute-start | bytes 12296 | tf_op jit(solution)/shard_map/ppermute | solution.py:58
  72.4 0.8 slice_bitcast_fusion.3
  73.2 7.1 %shard_map.79 = bf16[1024,128]{1,0:T(8,128)(2,1)} custom-call(bf16[4,10,2,128,128]{4,3,2,1,0:T(8,128)(2,1)} %bitcast.34, s32[1,1024]{1,0:T(1,128)} %reshape.74.row_leaf_ref, bf16[256,1024]{1,0:T(8,128)(2,1)} %bitcast.40), custom_call_target="tpu_custom_call" | custom-call | tf_op jit(solution)/shard_map/pallas_call | solution.py:226
  80.3 7.7 %all-to-all-start.1 = ((bf16[16,64,128]{2,1,0:T(8,128)(2,1)}), bf16[16,64,128]{2,1,0:T(8,128)(2,1)S(1)}, u32[]{:S(2)}, u32[]{:S(2)}) async-start(bf16[16,64,128]{2,1,0:T(8,128)(2,1)} %bitcast.43), calls=%async_computation.1 | async-start | bytes 524288 | tf_op jit(solution)/shard_map/all_to_all | solution.py:306
  88.0 3.8 %collective-permute-start.5 = (bf16[1,128,128]{2,1,0:T(8,128)(2,1)S(1)}, bf16[1,128,128]{2,1,0:T(8,128)(2,1)S(1)}, u32[]{:S(2)}, u32[]{:S(2)}) collective-permute-start(bf16[1,128,128]{2,1,0:T(8,128)(2,1)S(1)} %get-tuple-element.28), channel_id=1, source_target_pairs={{0,4},{1,5},{2,6},{3,7},{4,8},{5,9},{6,10},{7,11},{8,12},{9,13},{1... | collective-permute-start | bytes 98312 | tf_op jit(solution)/shard_map/ppermute | solution.py:58
  91.8 1.3 %collective-permute-start.6 = (bf16[1,128,128]{2,1,0:T(8,128)(2,1)S(1)}, bf16[1,128,128]{2,1,0:T(8,128)(2,1)S(1)}, u32[]{:S(2)}, u32[]{:S(2)}) collective-permute-start(bf16[1,128,128]{2,1,0:T(8,128)(2,1)S(1)} %get-tuple-element.29), channel_id=1, source_target_pairs={{4,0},{5,1},{6,2},{7,3},{8,4},{9,5},{10,6},{11,7},{12,8},{13,9},{1... | collective-permute-start | bytes 98312 | tf_op jit(solution)/shard_map/ppermute | solution.py:58
  93.1 0.0 collective-permute-done.3
  93.1 0.0 collective-permute-done.4
  93.1 0.1 maximum_convert_fusion.1
  93.3 0.7 collective-permute-done.5
  93.9 3.7 %collective-permute-done.6 = bf16[1,128,128]{2,1,0:T(8,128)(2,1)S(1)} collective-permute-done((bf16[1,128,128]{2,1,0:T(8,128)(2,1)S(1)}, bf16[1,128,128]{2,1,0:T(8,128)(2,1)S(1)}, u32[]{:S(2)}, u32[]{:S(2)}) %collective-permute-start.6) | collective-permute-done | bytes 32800 | tf_op jit(solution)/shard_map/ppermute | solution.py:58
  97.7 0.1 maximum_convert_fusion
  97.8 0.2 fusion.11
  98.0 1.4 %copy.37 = f32[128,16,128]{2,1,0:T(8,128)} copy(f32[128,16,128]{0,2,1:T(8,128)S(1)} %fusion.11) | data formatting | bytes 2097152
  99.3 0.0 all-to-all-done.1
  99.4 1.4 %fusion.9 = bf16[512,128]{1,0:T(8,128)(2,1)} fusion(bf16[1024,128]{1,0:T(8,128)(2,1)S(1)} %bitcast.46, s32[512]{0:T(512)S(1)} %multiply_add_fusion), kind=kOutput, calls=%fused_computation.18 | convolution fusion | flops 134807552 | bytes 395264 | tf_op jit(solution)/shard_map/dot_general | solution.py:309
  (4 shorter events, 0.0 us)
Async XLA Ops:
  0.6 12.7 %copy-start = (f32[128,16,256]{2,1,0:T(8,128)S(1)}, f32[128,16,256]{2,1,0:T(8,128)}, u32[]{:S(2)}) copy-start(f32[128,16,256]{2,1,0:T(8,128)} %param.6) | copy-start | bytes 6291460
  5.9 27.8 %all-to-all-start = ((bf16[16,65,384]{2,1,0:T(8,128)(2,1)}), bf16[16,65,384]{2,1,0:T(8,128)(2,1)}, u32[]{:S(2)}, u32[]{:S(2)}) async-start(bf16[16,65,384]{2,1,0:T(8,128)(2,1)} %fusion.16), calls=%async_computation | async-start | bytes 1769472 | tf_op jit(solution)/shard_map/all_to_all | solution.py:280
  14.2 5.4 %collective-permute-start = (f32[16,17,128]{2,1,0:T(8,128)S(1)}, f32[16,17,128]{2,1,0:T(8,128)S(1)}, u32[]{:S(2)}, u32[]{:S(2)}) collective-permute-start(f32[16,17,128]{2,1,0:T(8,128)S(1)} %bitcast.48), channel_id=1, source_target_pairs={{1,2},{2,1},{5,6},{6,5},{9,10},{10,9},{13,14},{14,13},{17,18},{18,... | collective-permute-start | bytes 417800 | tf_op jit(solution)/shard_map/ppermute | solution.py:58
  19.6 0.7 copy-start.1
  22.2 7.3 %copy-start.2 = (s32[2,8,8]{2,1,0:T(8,128)S(1)}, s32[2,8,8]{2,1,0:T(8,128)}, u32[]{:S(2)}) copy-start(s32[2,8,8]{2,1,0:T(8,128)} %param.8) | copy-start | bytes 1540
  23.4 23.6 %collective-permute-start.1 = (f32[9,162,128]{2,1,0:T(8,128)}, f32[9,162,128]{2,1,0:T(8,128)}, u32[]{:S(2)}, u32[]{:S(2)}) collective-permute-start(f32[9,162,128]{2,1,0:T(8,128)} %get-tuple-element.25), channel_id=1, source_target_pairs={{0,4},{1,5},{2,6},{3,7},{4,8},{5,9},{6,10},{7,11},{8,12},{9,13},{1... | collective-permute-start | bytes 2239496 | tf_op jit(solution)/shard_map/ppermute | solution.py:58
  28.1 19.3 %collective-permute-start.2 = (f32[9,162,128]{2,1,0:T(8,128)}, f32[9,162,128]{2,1,0:T(8,128)}, u32[]{:S(2)}, u32[]{:S(2)}) collective-permute-start(f32[9,162,128]{2,1,0:T(8,128)} %get-tuple-element.24), channel_id=1, source_target_pairs={{4,0},{5,1},{6,2},{7,3},{8,4},{9,5},{10,6},{11,7},{12,8},{13,9},{1... | collective-permute-start | bytes 2239496 | tf_op jit(solution)/shard_map/ppermute | solution.py:58
  66.0 27.2 %collective-permute-start.3 = (bf16[16,1,128]{2,1,0:T(2,128)(2,1)S(1)}, bf16[16,1,128]{2,1,0:T(2,128)(2,1)S(1)}, u32[]{:S(2)}, u32[]{:S(2)}) collective-permute-start(bf16[16,1,128]{2,1,0:T(2,128)(2,1)S(1)} %get-tuple-element.30), channel_id=1, source_target_pairs={{0,1},{1,2},{2,3},{4,5},{5,6},{6,7},{8,9},{9,10},{10,11},{12,13},{... | collective-permute-start | bytes 12296 | tf_op jit(solution)/shard_map/ppermute | solution.py:58
  71.1 22.0 %collective-permute-start.4 = (bf16[16,1,128]{2,1,0:T(2,128)(2,1)S(1)}, bf16[16,1,128]{2,1,0:T(2,128)(2,1)S(1)}, u32[]{:S(2)}, u32[]{:S(2)}) collective-permute-start(bf16[16,1,128]{2,1,0:T(2,128)(2,1)S(1)} %get-tuple-element.31), channel_id=1, source_target_pairs={{1,0},{2,1},{3,2},{5,4},{6,5},{7,6},{9,8},{10,9},{11,10},{13,12},{... | collective-permute-start | bytes 12296 | tf_op jit(solution)/shard_map/ppermute | solution.py:58
  80.3 19.1 %all-to-all-start.1 = ((bf16[16,64,128]{2,1,0:T(8,128)(2,1)}), bf16[16,64,128]{2,1,0:T(8,128)(2,1)S(1)}, u32[]{:S(2)}, u32[]{:S(2)}) async-start(bf16[16,64,128]{2,1,0:T(8,128)(2,1)} %bitcast.43), calls=%async_computation.1 | async-start | bytes 524288 | tf_op jit(solution)/shard_map/all_to_all | solution.py:306
  88.0 6.0 %collective-permute-start.5 = (bf16[1,128,128]{2,1,0:T(8,128)(2,1)S(1)}, bf16[1,128,128]{2,1,0:T(8,128)(2,1)S(1)}, u32[]{:S(2)}, u32[]{:S(2)}) collective-permute-start(bf16[1,128,128]{2,1,0:T(8,128)(2,1)S(1)} %get-tuple-element.28), channel_id=1, source_target_pairs={{0,4},{1,5},{2,6},{3,7},{4,8},{5,9},{6,10},{7,11},{8,12},{9,13},{1... | collective-permute-start | bytes 98312 | tf_op jit(solution)/shard_map/ppermute | solution.py:58
  91.8 5.9 %collective-permute-start.6 = (bf16[1,128,128]{2,1,0:T(8,128)(2,1)S(1)}, bf16[1,128,128]{2,1,0:T(8,128)(2,1)S(1)}, u32[]{:S(2)}, u32[]{:S(2)}) collective-permute-start(bf16[1,128,128]{2,1,0:T(8,128)(2,1)S(1)} %get-tuple-element.29), channel_id=1, source_target_pairs={{4,0},{5,1},{6,2},{7,3},{8,4},{9,5},{10,6},{11,7},{12,8},{13,9},{1... | collective-permute-start | bytes 98312 | tf_op jit(solution)/shard_map/ppermute | solution.py:58

commit v15 on v14

--- a/solution.py
+++ b/solution.py
@@ -172,7 +172,7 @@
     lax.fori_loop(0, leaf_count, one_leaf, 0)
 
 
-def induced_kernel(bord_hbm, row_leaf_ref, cpl_t_ref, volt_ref, own_ref, acc_ref, sems):
+def induced_kernel(bord_hbm, col_leaf_ref, cpl_ref, volt_ref, own_ref, acc_ref, sems):
     leaf_rows = own_ref.shape[0]
     leaf_cols = own_ref.shape[1] - 2
     cells = own_ref.shape[3]
@@ -184,26 +184,24 @@
     acc_ref[...] = jnp.zeros_like(acc_ref)
 
     def one_leaf(row, col):
-        coupling_t = cpl_t_ref[...]
+        coupling = cpl_ref[...]
         leaf = row * leaf_cols + col
-        coupling_t = jnp.where(row_leaf_ref[...] == leaf, coupling_t, jnp.zeros_like(coupling_t))
+        coupling = jnp.where(col_leaf_ref[...] == leaf, coupling, jnp.zeros_like(coupling))
         own = own_ref[row, col + 1].reshape(2 * cells, -1)
-        acc_ref[...] += lax.dot_general(
-            own, coupling_t, (((0,), (0,)), ((), ())), preferred_element_type=jnp.float32
-        )
+        acc_ref[...] += jnp.dot(coupling, own, preferred_element_type=jnp.float32)
 
     for r in range(leaf_rows):
         copies[r].wait()
         lax.fori_loop(0, leaf_cols, lambda col, carry: (one_leaf(r, col), carry)[1], 0)
-    volt_ref[...] = acc_ref[...].T.astype(volt_ref.dtype)
-
-
-def leaf_fields(codes, scales, bordered, kernels, filament, row_leaf, coupling_t):
+    volt_ref[...] = acc_ref[...].astype(volt_ref.dtype)
+
+
+def leaf_fields(codes, scales, bordered, kernels, filament, col_leaf, coupling):
     leaf_count, near_count, components, cells, _ = kernels.shape
     leaf_rows = bordered.shape[0] - 2
     leaf_cols = bordered.shape[1] - 2
     port_count = bordered.shape[-1]
-    slot_count = coupling_t.shape[1]
+    slot_count = coupling.shape[0]
     smem = pl.BlockSpec(memory_space=pltpu.SMEM)
     hbm = pl.BlockSpec(memory_space=pl.ANY)
     vmem = pl.BlockSpec(memory_space=pltpu.VMEM)
@@ -230,10 +228,10 @@
         out_shape=jax.ShapeDtypeStruct((slot_count, port_count), jnp.bfloat16),
         scratch_shapes=[
             pltpu.VMEM((leaf_rows,) + bordered.shape[1:], bordered.dtype),
-            pltpu.VMEM((port_count, slot_count), jnp.float32),
+            pltpu.VMEM((slot_count, port_count), jnp.float32),
             pltpu.SemaphoreType.DMA((leaf_rows,)),
         ],
-    )(bordered, row_leaf, coupling_t)
+    )(bordered, col_leaf, coupling)
     return field, volt
 
 
@@ -282,11 +280,13 @@
     got_leaf = got[:, capacity, :capacity].reshape(slot_count).astype(jnp.int32)
     got_coupling_t = got_rows[:, : 2 * leaf_cells].T
     got_current = got_rows[:, 2 * leaf_cells :]
+    got_coupling = got_rows[:, : 2 * leaf_cells]
+    col_leaf = got_leaf.reshape(slot_count, 1)
     got_leaf = got_leaf.reshape(1, slot_count)
     filament = filament_field(got_leaf, got_coupling_t, got_current, leaf_count)
 
-    window, (got_leaf, got_coupling_t, filament) = stream_window(
-        stream.transpose(1, 2, 0), half_cols, (got_leaf, got_coupling_t, filament)
+    window, (col_leaf, got_coupling, filament) = stream_window(
+        stream.transpose(1, 2, 0), half_cols, (col_leaf, got_coupling, filament)
     )
     currents = plane_curl(window).astype(jnp.bfloat16)
     bordered = to_leaves(currents)
@@ -301,7 +301,7 @@
     kernels = inductance.reshape(leaf_count, near_count, 2, leaf_cells, leaf_cells)
     codes = near_lists.reshape(leaf_count, near_count)
     total_field, induced = leaf_fields(
-        codes, scales, bordered, kernels, filament, got_leaf, got_coupling_t
+        codes, scales, bordered, kernels, filament, col_leaf, got_coupling
     )
     returned = lax.all_to_all(
         induced.reshape(owners, capacity, port_count), AXES, split_axis=0, concat_axis=0, tiled=True

time: 102 us -> 104 us (1.020)
  Pallas kernels: 26.6 us -> 28.3 us
  local copies, waits for them, and re-layouts: 19.7 us -> 21 us
    transpose x0 -> x2, local copies, waits for them, and re-layouts: none -> 3.09 us  [body(): got_coupling_t = got_rows[:, :2 * leaf_cells].T]
    unnamed x11 -> x10, local copies, waits for them, and re-layouts: 8.34 us -> 6.28 us
    pallas_call x1, Pallas kernels: 7.09 us -> 8.72 us  [leaf_fields(): pl.pallas_call(induced_kernel, in_specs=[hbm, vmem, vmem], out_specs=vmem...]
  transfers between devices with their start and end apart: 9 -> 9, of which waited for: 4 -> 3; matrix products, arithmetic and copies ran while one was open for 18% -> 20% of each run, Pallas kernels for 14% -> 15%
where the time goes in v15:
time: 104 us; the launch traced here: 103 us
  starting transfers between devices  32.6 us (31%)
  Pallas kernels  28.3 us (27%)
  local copies, waits for them, and re-layouts  21 us (20%)
  other arithmetic  9.1 us (9%)
  waiting for transfers between devices  8.1 us (8%)
  matrix products  3.5 us (3%)
    ppermute x7, starting transfers between devices, send(): return lax.ppermute(value, AXES, pairs_by(fn))  17.4 us
    pallas_call x1, Pallas kernels, leaf_fields(): pl.pallas_call(leaf_kernel, in_specs=[smem, smem, hbm, hbm, hbm], out_spe...  12.5 us
    pallas_call x1, Pallas kernels, leaf_fields(): pl.pallas_call(induced_kernel, in_specs=[hbm, vmem, vmem], out_specs=vmem...  8.72 us
    all_to_all x1, starting transfers between devices, body(): lax.all_to_all(induced.reshape(owners, capacity, port_count), AXES, split...  7.71 us
    all_to_all x1, starting transfers between devices, body(): got = lax.all_to_all(payload, AXES, split_axis=0, concat_axis=0, tiled=True)  7.4 us
    pallas_call x1, Pallas kernels, filament_field(): pl.pallas_call(filament_kernel, in_specs=[vmem, vmem, vmem], out_specs=vm...  7.05 us
    unnamed x10, local copies, waits for them, and re-layouts  6.28 us
    ppermute x7, waiting for transfers between devices, send(): return lax.ppermute(value, AXES, pairs_by(fn))  4.43 us
  transfers between devices with their start and end apart: 9, of which 3 were waited for; matrix products, arithmetic and copies ran while one was open for 20% of the time, Pallas kernels for 15%

profile of v15, /device:TPU:0, one launch (start us, length us, event | category | flops | bytes accessed | tf_op | source)
XLA Modules:
  0.0 103.5 jit_solution(8971570283261614923)
XLA Ops:
  0.6 0.0 copy-start
  0.6 0.9 fusion.24
  1.5 0.2 convert_reduce_fusion
  1.8 0.5 fusion.3
  2.2 0.1 reshape.91
  2.3 1.0 copy.57
  3.3 1.6 %fusion.6 = bf16[1024,384]{1,0:T(8,128)(2,1)S(1)} fusion(s32[512]{0:T(512)S(1)} %multiply_add_fusion, bf16[512,128]{1,0:T(8,128)(2,1)} %param.10, bf16[512,256]{1,0:T(8,128)(2,1)S(1)} %bitcast.47), kind=kOutput, calls=%fused_computation.15 | convolution fusion | flops 404357120 | bytes 1181696 | tf_op jit(solution)/shard_map/dot_general | solution.py:269
  4.9 1.0 fusion.16
  5.9 7.4 %all-to-all-start = ((bf16[16,65,384]{2,1,0:T(8,128)(2,1)}), bf16[16,65,384]{2,1,0:T(8,128)(2,1)}, u32[]{:S(2)}, u32[]{:S(2)}) async-start(bf16[16,65,384]{2,1,0:T(8,128)(2,1)} %fusion.16), calls=%async_computation | async-start | bytes 1769472 | tf_op jit(solution)/shard_map/all_to_all | solution.py:278
  13.3 0.0 copy-done
  13.4 0.3 constant_dynamic-slice_fusion.1
  13.7 0.4 copy.52
  14.2 0.7 collective-permute-start
  14.8 1.9 %constant_dynamic-slice_fusion = f32[128,16,145]{2,1,0:T(8,128)} fusion(f32[128,16,256]{2,1,0:T(8,128)S(1)} %copy-done, s32[]{:T(128)S(6)} %select_n.49), kind=kLoop, calls=%fused_computation.77 | loop fusion | bytes 2375684 | tf_op jit(solution)/shard_map/dynamic-slice.1
  16.8 2.8 %copy.53 = f32[128,16,145]{0,2,1:T(8,128)} copy(f32[128,16,145]{2,1,0:T(8,128)} %constant_dynamic-slice_fusion) | data formatting | bytes 2375680
  19.6 0.0 collective-permute-done
  19.6 0.0 copy-start.1
  19.6 0.7 copy-done.1
  20.2 1.9 %fusion.8 = f32[16,162,128]{2,1,0:T(8,128)S(1)} fusion(s32[]{:T(128)S(6)} %select_n.50, f32[16,17,128]{2,1,0:T(8,128)} %copy-done.1, f32[16,145,128]{2,1,0:T(8,128)} %bitcast.40), kind=kLoop, calls=%fused_computation.17 | loop fusion | flops 663552 | bytes 2654212 | tf_op jit(solution)/shard_map/concatenate | solution.py:79
  22.2 0.0 copy-start.2
  22.2 1.3 %fusion.34 = (f32[9,162,128]{2,1,0:T(8,128)}, f32[9,162,128]{2,1,0:T(8,128)}) fusion(f32[16,162,128]{2,1,0:T(8,128)S(1)} %fusion.8), kind=kLoop, calls=%fused_computation.85 | loop fusion | bytes 2985984 | tf_op jit(solution)/shard_map/slice | solution.py:82
  23.4 4.7 %collective-permute-start.1 = (f32[9,162,128]{2,1,0:T(8,128)}, f32[9,162,128]{2,1,0:T(8,128)}, u32[]{:S(2)}, u32[]{:S(2)}) collective-permute-start(f32[9,162,128]{2,1,0:T(8,128)} %get-tuple-element.27), channel_id=1, source_target_pairs={{0,4},{1,5},{2,6},{3,7},{4,8},{5,9},{6,10},{7,11},{8,12},{9,13},{1... | collective-permute-start | bytes 2239496 | tf_op jit(solution)/shard_map/ppermute | solution.py:58
  28.1 1.3 %collective-permute-start.2 = (f32[9,162,128]{2,1,0:T(8,128)}, f32[9,162,128]{2,1,0:T(8,128)}, u32[]{:S(2)}, u32[]{:S(2)}) collective-permute-start(f32[9,162,128]{2,1,0:T(8,128)} %get-tuple-element.26), channel_id=1, source_target_pairs={{4,0},{5,1},{6,2},{7,3},{8,4},{9,5},{10,6},{11,7},{12,8},{13,9},{1... | collective-permute-start | bytes 2239496 | tf_op jit(solution)/shard_map/ppermute | solution.py:58
  29.4 0.0 copy-done.2
  29.4 0.6 convert_bitcast_fusion.scale_ref
  30.0 3.7 %all-to-all-done = bf16[16,65,384]{2,1,0:T(8,128)(2,1)} async-done(((bf16[16,65,384]{2,1,0:T(8,128)(2,1)}), bf16[16,65,384]{2,1,0:T(8,128)(2,1)}, u32[]{:S(2)}, u32[]{:S(2)}) %all-to-all-start) | async-done | bytes 798752 | tf_op jit(solution)/shard_map/all_to_all | solution.py:278
  33.7 1.2 %slice.94 = bf16[16,64,384]{2,1,0:T(8,128)(2,1)S(1)} slice(bf16[16,65,384]{2,1,0:T(8,128)(2,1)} %all-to-all-done), slice={[0:16], [0:64], [0:384]} | slice | bytes 1572864 | tf_op jit(solution)/shard_map/slice | solution.py:279
  34.9 0.7 slice.96.cur_ref
  35.6 1.0 slice_bitcast_fusion.4
  36.7 2.1 %copy.44.cpl_t_ref = bf16[256,1024]{1,0:T(8,128)(2,1)} copy(bf16[256,1024]{0,1:T(8,128)(2,1)} %get-tuple-element.32) | data formatting | bytes 1048576 | tf_op jit(solution)/shard_map/transpose | solution.py:281
  38.7 0.8 slice_convert_fusion
  39.5 0.7 reshape.88.row_leaf_ref
  40.2 0.8 fusion.33
  41.0 0.1 reshape.87
  41.0 7.0 %shard_map.77.fil_hbm = f32[16,256,128]{2,1,0:T(8,128)} custom-call(s32[1,1024]{1,0:T(1,128)} %reshape.88.row_leaf_ref, bf16[256,1024]{1,0:T(8,128)(2,1)} %copy.44.cpl_t_ref, bf16[1024,128]{1,0:T(8,128)(2,1)} %slice.96.cur_ref), custom_call_target="tpu_custom_call" | custom-call | tf_op jit(solution)/shard_map/pallas_call | solution.py:119
  48.1 0.0 collective-permute-done.1
  48.1 0.0 collective-permute-done.2
  48.1 1.6 %pad_maximum_fusion = f32[34,162,128]{2,1,0:T(8,128)S(1)} fusion(f32[9,162,128]{2,1,0:T(8,128)} %collective-permute-done.2, f32[16,162,128]{2,1,0:T(8,128)S(1)} %fusion.8, f32[9,162,128]{2,1,0:T(8,128)} %collective-permute-done.1), kind=kLoop, calls=%fused_computation | loop fusion | flops 1410048 | bytes 5640192 | tf_op jit(solution)/shard_map/concatenate | solution.py:84
  49.6 0.7 fusion.1
  50.3 0.2 maximum_bitcast_fusion
  50.6 2.2 %copy.45 = bf16[4,10,2,8,16,128]{5,4,3,2,1,0:T(8,128)(2,1)} copy(bf16[4,10,2,8,16,128]{5,4,1,3,0,2:T(8,128)(2,1)S(1)} %maximum_bitcast_fusion) | data formatting | bytes 5242880 | tf_op jit(solution)/shard_map/transpose | solution.py:24
  52.8 12.5 %shard_map.78 = bf16[2,16,128,128]{3,2,1,0:T(8,128)(2,1)} custom-call(s32[16,8]{1,0:T(8,128)} %bitcast.49, s32[16,8]{1,0:T(8,128)} %convert_bitcast_fusion.scale_ref, bf16[4,10,2,128,128]{4,3,2,1,0:T(8,128)(2,1)} %bitcast.35, bf16[16,8,2,128,128]{4,3,2,1,0:T(8,128)(2,1)} %bitcast.37, f32[16,256,128]{2,1,0:T(8,128)} %shard_map.77.fil_hbm), custom_call_target="tpu_custom_call" | custom-call | tf_op jit(solution)/shard_map/pallas_call | solution.py:208
  65.4 1.3 %slice_bitcast_fusion.1 = (bf16[16,128,128]{2,1,0:T(8,128)(2,1)S(1)}, bf16[16,128,128]{2,1,0:T(8,128)(2,1)S(1)}) fusion(bf16[2,16,128,128]{3,2,1,0:T(8,128)(2,1)} %shard_map.78), kind=kLoop, calls=%fused_computation.33 | loop fusion | bytes 2097152 | tf_op jit(solution)/shard_map/squeeze | solution.py:88
  66.7 4.4 %collective-permute-start.3 = (bf16[16,1,128]{2,1,0:T(2,128)(2,1)S(1)}, bf16[16,1,128]{2,1,0:T(2,128)(2,1)S(1)}, u32[]{:S(2)}, u32[]{:S(2)}) collective-permute-start(bf16[16,1,128]{2,1,0:T(2,128)(2,1)S(1)} %get-tuple-element.34), channel_id=1, source_target_pairs={{0,1},{1,2},{2,3},{4,5},{5,6},{6,7},{8,9},{9,10},{10,11},{12,13},{... | collective-permute-start | bytes 12296 | tf_op jit(solution)/shard_map/ppermute | solution.py:58
  71.1 1.3 %collective-permute-start.4 = (bf16[16,1,128]{2,1,0:T(2,128)(2,1)S(1)}, bf16[16,1,128]{2,1,0:T(2,128)(2,1)S(1)}, u32[]{:S(2)}, u32[]{:S(2)}) collective-permute-start(bf16[16,1,128]{2,1,0:T(2,128)(2,1)S(1)} %get-tuple-element.35), channel_id=1, source_target_pairs={{1,0},{2,1},{3,2},{5,4},{6,5},{7,6},{9,8},{10,9},{11,10},{13,12},{... | collective-permute-start | bytes 12296 | tf_op jit(solution)/shard_map/ppermute | solution.py:58
  72.4 0.8 slice_bitcast_fusion.3
  73.2 1.0 copy.48.col_leaf_ref
  74.2 8.7 %shard_map.79 = bf16[1024,128]{1,0:T(8,128)(2,1)} custom-call(bf16[4,10,2,128,128]{4,3,2,1,0:T(8,128)(2,1)} %bitcast.36, s32[1024,1]{1,0:T(8,128)} %copy.48.col_leaf_ref, bf16[1024,256]{1,0:T(8,128)(2,1)} %get-tuple-element.15.cpl_ref), custom_call_target="tpu_custom_call" | custom-call | tf_op jit(solution)/shard_map/pallas_call | solution.py:224
  82.9 7.7 %all-to-all-start.1 = ((bf16[16,64,128]{2,1,0:T(8,128)(2,1)}), bf16[16,64,128]{2,1,0:T(8,128)(2,1)S(1)}, u32[]{:S(2)}, u32[]{:S(2)}) async-start(bf16[16,64,128]{2,1,0:T(8,128)(2,1)} %bitcast.43), calls=%async_computation.1 | async-start | bytes 524288 | tf_op jit(solution)/shard_map/all_to_all | solution.py:306
  90.7 3.8 %collective-permute-start.5 = (bf16[1,128,128]{2,1,0:T(8,128)(2,1)S(1)}, bf16[1,128,128]{2,1,0:T(8,128)(2,1)S(1)}, u32[]{:S(2)}, u32[]{:S(2)}) collective-permute-start(bf16[1,128,128]{2,1,0:T(8,128)(2,1)S(1)} %get-tuple-element.30), channel_id=1, source_target_pairs={{0,4},{1,5},{2,6},{3,7},{4,8},{5,9},{6,10},{7,11},{8,12},{9,13},{1... | collective-permute-start | bytes 98312 | tf_op jit(solution)/shard_map/ppermute | solution.py:58
  94.5 1.3 %collective-permute-start.6 = (bf16[1,128,128]{2,1,0:T(8,128)(2,1)S(1)}, bf16[1,128,128]{2,1,0:T(8,128)(2,1)S(1)}, u32[]{:S(2)}, u32[]{:S(2)}) collective-permute-start(bf16[1,128,128]{2,1,0:T(8,128)(2,1)S(1)} %get-tuple-element.31), channel_id=1, source_target_pairs={{4,0},{5,1},{6,2},{7,3},{8,4},{9,5},{10,6},{11,7},{12,8},{13,9},{1... | collective-permute-start | bytes 98312 | tf_op jit(solution)/shard_map/ppermute | solution.py:58
  95.8 0.0 collective-permute-done.3
  95.8 0.0 collective-permute-done.4
  95.8 0.1 maximum_convert_fusion.1
  95.9 0.7 collective-permute-done.5
  96.6 3.7 %collective-permute-done.6 = bf16[1,128,128]{2,1,0:T(8,128)(2,1)S(1)} collective-permute-done((bf16[1,128,128]{2,1,0:T(8,128)(2,1)S(1)}, bf16[1,128,128]{2,1,0:T(8,128)(2,1)S(1)}, u32[]{:S(2)}, u32[]{:S(2)}) %collective-permute-start.6) | collective-permute-done | bytes 32800 | tf_op jit(solution)/shard_map/ppermute | solution.py:58
  100.4 0.1 maximum_convert_fusion
  100.5 0.2 fusion.11
  100.6 1.4 %copy.49 = f32[128,16,128]{2,1,0:T(8,128)} copy(f32[128,16,128]{0,2,1:T(8,128)S(1)} %fusion.11) | data formatting | bytes 2097152
  102.0 0.0 all-to-all-done.1
  102.0 1.4 %fusion.9 = bf16[512,128]{1,0:T(8,128)(2,1)} fusion(bf16[1024,128]{1,0:T(8,128)(2,1)S(1)} %bitcast.46, s32[512]{0:T(512)S(1)} %multiply_add_fusion), kind=kOutput, calls=%fused_computation.18 | convolution fusion | flops 134807552 | bytes 395264 | tf_op jit(solution)/shard_map/dot_general | solution.py:309
  (4 shorter events, 0.0 us)
Async XLA Ops:
  0.6 12.7 %copy-start = (f32[128,16,256]{2,1,0:T(8,128)S(1)}, f32[128,16,256]{2,1,0:T(8,128)}, u32[]{:S(2)}) copy-start(f32[128,16,256]{2,1,0:T(8,128)} %param.6) | copy-start | bytes 6291460
  5.9 27.8 %all-to-all-start = ((bf16[16,65,384]{2,1,0:T(8,128)(2,1)}), bf16[16,65,384]{2,1,0:T(8,128)(2,1)}, u32[]{:S(2)}, u32[]{:S(2)}) async-start(bf16[16,65,384]{2,1,0:T(8,128)(2,1)} %fusion.16), calls=%async_computation | async-start | bytes 1769472 | tf_op jit(solution)/shard_map/all_to_all | solution.py:278
  14.2 5.4 %collective-permute-start = (f32[16,17,128]{2,1,0:T(8,128)S(1)}, f32[16,17,128]{2,1,0:T(8,128)S(1)}, u32[]{:S(2)}, u32[]{:S(2)}) collective-permute-start(f32[16,17,128]{2,1,0:T(8,128)S(1)} %bitcast.48), channel_id=1, source_target_pairs={{1,2},{2,1},{5,6},{6,5},{9,10},{10,9},{13,14},{14,13},{17,18},{18,... | collective-permute-start | bytes 417800 | tf_op jit(solution)/shard_map/ppermute | solution.py:58
  19.6 0.7 copy-start.1
  22.2 7.2 %copy-start.2 = (s32[2,8,8]{2,1,0:T(8,128)S(1)}, s32[2,8,8]{2,1,0:T(8,128)}, u32[]{:S(2)}) copy-start(s32[2,8,8]{2,1,0:T(8,128)} %param.8) | copy-start | bytes 1540
  23.4 24.6 %collective-permute-start.1 = (f32[9,162,128]{2,1,0:T(8,128)}, f32[9,162,128]{2,1,0:T(8,128)}, u32[]{:S(2)}, u32[]{:S(2)}) collective-permute-start(f32[9,162,128]{2,1,0:T(8,128)} %get-tuple-element.27), channel_id=1, source_target_pairs={{0,4},{1,5},{2,6},{3,7},{4,8},{5,9},{6,10},{7,11},{8,12},{9,13},{1... | collective-permute-start | bytes 2239496 | tf_op jit(solution)/shard_map/ppermute | solution.py:58
  28.1 20.0 %collective-permute-start.2 = (f32[9,162,128]{2,1,0:T(8,128)}, f32[9,162,128]{2,1,0:T(8,128)}, u32[]{:S(2)}, u32[]{:S(2)}) collective-permute-start(f32[9,162,128]{2,1,0:T(8,128)} %get-tuple-element.26), channel_id=1, source_target_pairs={{4,0},{5,1},{6,2},{7,3},{8,4},{9,5},{10,6},{11,7},{12,8},{13,9},{1... | collective-permute-start | bytes 2239496 | tf_op jit(solution)/shard_map/ppermute | solution.py:58
  66.7 29.1 %collective-permute-start.3 = (bf16[16,1,128]{2,1,0:T(2,128)(2,1)S(1)}, bf16[16,1,128]{2,1,0:T(2,128)(2,1)S(1)}, u32[]{:S(2)}, u32[]{:S(2)}) collective-permute-start(bf16[16,1,128]{2,1,0:T(2,128)(2,1)S(1)} %get-tuple-element.34), channel_id=1, source_target_pairs={{0,1},{1,2},{2,3},{4,5},{5,6},{6,7},{8,9},{9,10},{10,11},{12,13},{... | collective-permute-start | bytes 12296 | tf_op jit(solution)/shard_map/ppermute | solution.py:58
  71.1 24.7 %collective-permute-start.4 = (bf16[16,1,128]{2,1,0:T(2,128)(2,1)S(1)}, bf16[16,1,128]{2,1,0:T(2,128)(2,1)S(1)}, u32[]{:S(2)}, u32[]{:S(2)}) collective-permute-start(bf16[16,1,128]{2,1,0:T(2,128)(2,1)S(1)} %get-tuple-element.35), channel_id=1, source_target_pairs={{1,0},{2,1},{3,2},{5,4},{6,5},{7,6},{9,8},{10,9},{11,10},{13,12},{... | collective-permute-start | bytes 12296 | tf_op jit(solution)/shard_map/ppermute | solution.py:58
  82.9 19.1 %all-to-all-start.1 = ((bf16[16,64,128]{2,1,0:T(8,128)(2,1)}), bf16[16,64,128]{2,1,0:T(8,128)(2,1)S(1)}, u32[]{:S(2)}, u32[]{:S(2)}) async-start(bf16[16,64,128]{2,1,0:T(8,128)(2,1)} %bitcast.43), calls=%async_computation.1 | async-start | bytes 524288 | tf_op jit(solution)/shard_map/all_to_all | solution.py:306
  90.7 6.0 %collective-permute-start.5 = (bf16[1,128,128]{2,1,0:T(8,128)(2,1)S(1)}, bf16[1,128,128]{2,1,0:T(8,128)(2,1)S(1)}, u32[]{:S(2)}, u32[]{:S(2)}) collective-permute-start(bf16[1,128,128]{2,1,0:T(8,128)(2,1)S(1)} %get-tuple-element.30), channel_id=1, source_target_pairs={{0,4},{1,5},{2,6},{3,7},{4,8},{5,9},{6,10},{7,11},{8,12},{9,13},{1... | collective-permute-start | bytes 98312 | tf_op jit(solution)/shard_map/ppermute | solution.py:58
  94.5 5.9 %collective-permute-start.6 = (bf16[1,128,128]{2,1,0:T(8,128)(2,1)S(1)}, bf16[1,128,128]{2,1,0:T(8,128)(2,1)S(1)}, u32[]{:S(2)}, u32[]{:S(2)}) collective-permute-start(bf16[1,128,128]{2,1,0:T(8,128)(2,1)S(1)} %get-tuple-element.31), channel_id=1, source_target_pairs={{4,0},{5,1},{6,2},{7,3},{8,4},{9,5},{10,6},{11,7},{12,8},{13,9},{1... | collective-permute-start | bytes 98312 | tf_op jit(solution)/shard_map/ppermute | solution.py:58

commit v16 on v14

--- a/solution.py
+++ b/solution.py
@@ -128,27 +128,38 @@
 
 def leaf_kernel(
     codes_ref, scale_ref, bord_hbm, ind_hbm, fil_hbm,
-    field_ref, bord_ref, ind_ref, fil_ref, sems, ind_sems,
+    field_ref, bord_ref, ind_ref, fil_ref, sems, fil_sems, ind_sems,
 ):
     leaf_count = ind_ref.shape[0]
     leaf_cols = bord_ref.shape[1] - 2
     near_count = ind_ref.shape[1]
     cells = ind_ref.shape[3]
-    first = [
-        pltpu.make_async_copy(bord_hbm, bord_ref, sems.at[0]),
-        pltpu.make_async_copy(fil_hbm, fil_ref, sems.at[1]),
-    ]
-    for copy in first:
-        copy.start()
+    ring_rows = bord_ref.shape[0]
+
+    def row_copy(r):
+        return pltpu.make_async_copy(bord_hbm.at[r], bord_ref.at[r], sems.at[r])
+
+    def fil_copy(l):
+        return pltpu.make_async_copy(fil_hbm.at[l], fil_ref.at[l], fil_sems.at[l])
+
+    for r in range(ring_rows):
+        row_copy(r).start()
     for l in range(leaf_count):
+        fil_copy(l).start()
         pltpu.make_async_copy(ind_hbm.at[l], ind_ref.at[l], ind_sems.at[l]).start()
-    for copy in first:
-        copy.wait()
+    for r in range(3):
+        row_copy(r).wait()
 
     def one_leaf(leaf, carry):
-        pltpu.make_async_copy(ind_hbm.at[leaf], ind_ref.at[leaf], ind_sems.at[leaf]).wait()
         row = leaf // leaf_cols
         col = leaf % leaf_cols
+
+        @pl.when((col == 0) & (row > 0))
+        def _():
+            row_copy(row + 2).wait()
+
+        fil_copy(leaf).wait()
+        pltpu.make_async_copy(ind_hbm.at[leaf], ind_ref.at[leaf], ind_sems.at[leaf]).wait()
         filament = fil_ref[leaf]
         sources = []
         for n in range(near_count):
@@ -218,7 +229,8 @@
             pltpu.VMEM(bordered.shape, bordered.dtype),
             pltpu.VMEM(kernels.shape, kernels.dtype),
             pltpu.VMEM(filament.shape, filament.dtype),
-            pltpu.SemaphoreType.DMA((2,)),
+            pltpu.SemaphoreType.DMA((leaf_rows + 2,)),
+            pltpu.SemaphoreType.DMA((leaf_count,)),
             pltpu.SemaphoreType.DMA((leaf_count,)),
         ],
     )(codes, scales, bordered, kernels, filament)

time: 102 us -> 101 us (level)
  no operation moved by 1% of the time
where the time goes in v16:
time: 101 us; the launch traced here: 100 us
  starting transfers between devices  33.3 us (33%)
  Pallas kernels  26.3 us (26%)
  local copies, waits for them, and re-layouts  19.7 us (20%)
  waiting for transfers between devices  8.45 us (8%)
  other arithmetic  8.33 us (8%)
  matrix products  3.5 us (3%)
    ppermute x7, starting transfers between devices, send(): return lax.ppermute(value, AXES, pairs_by(fn))  18.2 us
    pallas_call x1, Pallas kernels, leaf_fields(): pl.pallas_call(leaf_kernel, in_specs=[smem, smem, hbm, hbm, hbm], out_spe...  12.2 us
    unnamed x11, local copies, waits for them, and re-layouts  8.34 us
    all_to_all x1, starting transfers between devices, body(): lax.all_to_all(induced.reshape(owners, capacity, port_count), AXES, split...  7.68 us
    all_to_all x1, starting transfers between devices, body(): got = lax.all_to_all(payload, AXES, split_axis=0, concat_axis=0, tiled=True)  7.4 us
    pallas_call x1, Pallas kernels, leaf_fields(): pl.pallas_call(induced_kernel, in_specs=[hbm, vmem, vmem], out_specs=vmem...  7.09 us
    pallas_call x1, Pallas kernels, filament_field(): pl.pallas_call(filament_kernel, in_specs=[vmem, vmem, vmem], out_specs=vm...  7.02 us
    ppermute x7, waiting for transfers between devices, send(): return lax.ppermute(value, AXES, pairs_by(fn))  4.8 us
  transfers between devices with their start and end apart: 9, of which 4 were waited for; matrix products, arithmetic and copies ran while one was open for 18% of the time, Pallas kernels for 14%

profile of v16, /device:TPU:0, one launch (start us, length us, event | category | flops | bytes accessed | tf_op | source)
XLA Modules:
  0.0 100.5 jit_solution(14003157150887094582)
XLA Ops:
  0.6 0.0 copy-start
  0.6 0.9 fusion.25
  1.5 0.2 convert_reduce_fusion
  1.8 0.5 fusion.3
  2.2 0.1 reshape.77
  2.3 1.0 copy.46
  3.3 1.6 %fusion.6 = bf16[1024,384]{1,0:T(8,128)(2,1)S(1)} fusion(s32[512]{0:T(512)S(1)} %multiply_add_fusion, bf16[512,128]{1,0:T(8,128)(2,1)} %param.10, bf16[512,256]{1,0:T(8,128)(2,1)S(1)} %bitcast.47), kind=kOutput, calls=%fused_computation.15 | convolution fusion | flops 404357120 | bytes 1181696 | tf_op jit(solution)/shard_map/dot_general | solution.py:283
  4.9 1.0 fusion.16
  5.9 7.4 %all-to-all-start = ((bf16[16,65,384]{2,1,0:T(8,128)(2,1)}), bf16[16,65,384]{2,1,0:T(8,128)(2,1)}, u32[]{:S(2)}, u32[]{:S(2)}) async-start(bf16[16,65,384]{2,1,0:T(8,128)(2,1)} %fusion.16), calls=%async_computation | async-start | bytes 1769472 | tf_op jit(solution)/shard_map/all_to_all | solution.py:292
  13.3 0.0 copy-done
  13.4 0.3 constant_dynamic-slice_fusion.1
  13.7 0.4 copy.40
  14.2 0.7 collective-permute-start
  14.8 2.0 %constant_dynamic-slice_fusion = f32[128,16,145]{2,1,0:T(8,128)} fusion(f32[128,16,256]{2,1,0:T(8,128)S(1)} %copy-done, s32[]{:T(128)S(6)} %select_n.49), kind=kLoop, calls=%fused_computation.78 | loop fusion | bytes 2375684 | tf_op jit(solution)/shard_map/dynamic-slice.1
  16.8 2.8 %copy.41 = f32[128,16,145]{0,2,1:T(8,128)} copy(f32[128,16,145]{2,1,0:T(8,128)} %constant_dynamic-slice_fusion) | data formatting | bytes 2375680
  19.6 0.0 collective-permute-done
  19.6 0.0 copy-start.1
  19.6 0.7 copy-done.1
  20.2 1.9 %fusion.8 = f32[16,162,128]{2,1,0:T(8,128)S(1)} fusion(s32[]{:T(128)S(6)} %select_n.50, f32[16,17,128]{2,1,0:T(8,128)} %copy-done.1, f32[16,145,128]{2,1,0:T(8,128)} %bitcast.38), kind=kLoop, calls=%fused_computation.17 | loop fusion | flops 663552 | bytes 2654212 | tf_op jit(solution)/shard_map/concatenate | solution.py:79
  22.2 0.0 copy-start.2
  22.2 1.3 %fusion.34 = (f32[9,162,128]{2,1,0:T(8,128)}, f32[9,162,128]{2,1,0:T(8,128)}) fusion(f32[16,162,128]{2,1,0:T(8,128)S(1)} %fusion.8), kind=kLoop, calls=%fused_computation.84 | loop fusion | bytes 2985984 | tf_op jit(solution)/shard_map/slice | solution.py:82
  23.4 4.7 %collective-permute-start.1 = (f32[9,162,128]{2,1,0:T(8,128)}, f32[9,162,128]{2,1,0:T(8,128)}, u32[]{:S(2)}, u32[]{:S(2)}) collective-permute-start(f32[9,162,128]{2,1,0:T(8,128)} %get-tuple-element.25), channel_id=1, source_target_pairs={{0,4},{1,5},{2,6},{3,7},{4,8},{5,9},{6,10},{7,11},{8,12},{9,13},{1... | collective-permute-start | bytes 2239496 | tf_op jit(solution)/shard_map/ppermute | solution.py:58
  28.1 1.3 %collective-permute-start.2 = (f32[9,162,128]{2,1,0:T(8,128)}, f32[9,162,128]{2,1,0:T(8,128)}, u32[]{:S(2)}, u32[]{:S(2)}) collective-permute-start(f32[9,162,128]{2,1,0:T(8,128)} %get-tuple-element.24), channel_id=1, source_target_pairs={{4,0},{5,1},{6,2},{7,3},{8,4},{9,5},{10,6},{11,7},{12,8},{13,9},{1... | collective-permute-start | bytes 2239496 | tf_op jit(solution)/shard_map/ppermute | solution.py:58
  29.4 0.0 copy-done.2
  29.4 0.6 convert_bitcast_fusion.scale_ref
  30.0 3.7 %all-to-all-done = bf16[16,65,384]{2,1,0:T(8,128)(2,1)} async-done(((bf16[16,65,384]{2,1,0:T(8,128)(2,1)}), bf16[16,65,384]{2,1,0:T(8,128)(2,1)}, u32[]{:S(2)}, u32[]{:S(2)}) %all-to-all-start) | async-done | bytes 798752 | tf_op jit(solution)/shard_map/all_to_all | solution.py:292
  33.7 1.2 %slice.93 = bf16[16,64,384]{2,1,0:T(8,128)(2,1)S(1)} slice(bf16[16,65,384]{2,1,0:T(8,128)(2,1)} %all-to-all-done), slice={[0:16], [0:64], [0:384]} | slice | bytes 1572864 | tf_op jit(solution)/shard_map/slice | solution.py:293
  34.9 0.8 slice.94
  35.7 0.7 slice.95.cur_ref
  36.5 2.0 %copy.42 = bf16[1024,256]{0,1:T(8,128)(2,1)} copy(bf16[1024,256]{1,0:T(8,128)(2,1)} %slice.94) | data formatting | bytes 1048576
  38.5 0.8 fusion.22
  39.3 0.7 reshape.74.row_leaf_ref
  40.0 7.0 %shard_map.77.fil_hbm = f32[16,256,128]{2,1,0:T(8,128)} custom-call(s32[1,1024]{1,0:T(1,128)} %reshape.74.row_leaf_ref, bf16[256,1024]{1,0:T(8,128)(2,1)} %bitcast.39, bf16[1024,128]{1,0:T(8,128)(2,1)} %slice.95.cur_ref), custom_call_target="tpu_custom_call" | custom-call | tf_op jit(solution)/shard_map/pallas_call | solution.py:119
  47.0 0.0 collective-permute-done.1
  47.0 0.4 collective-permute-done.2
  47.4 1.6 %pad_maximum_fusion = f32[34,162,128]{2,1,0:T(8,128)S(1)} fusion(f32[9,162,128]{2,1,0:T(8,128)} %collective-permute-done.2, f32[16,162,128]{2,1,0:T(8,128)S(1)} %fusion.8, f32[9,162,128]{2,1,0:T(8,128)} %collective-permute-done.1), kind=kLoop, calls=%fused_computation | loop fusion | flops 1410048 | bytes 5640192 | tf_op jit(solution)/shard_map/concatenate | solution.py:84
  48.9 0.7 fusion.1
  49.6 0.2 maximum_bitcast_fusion
  49.9 2.3 %copy.34 = bf16[4,10,2,8,16,128]{5,4,3,2,1,0:T(8,128)(2,1)} copy(bf16[4,10,2,8,16,128]{5,4,1,3,0,2:T(8,128)(2,1)S(1)} %maximum_bitcast_fusion) | data formatting | bytes 5242880 | tf_op jit(solution)/shard_map/transpose | solution.py:24
  52.1 12.2 %shard_map.78 = bf16[2,16,128,128]{3,2,1,0:T(8,128)(2,1)} custom-call(s32[16,8]{1,0:T(8,128)} %bitcast.49, s32[16,8]{1,0:T(8,128)} %convert_bitcast_fusion.scale_ref, bf16[4,10,2,128,128]{4,3,2,1,0:T(8,128)(2,1)} %bitcast.33, bf16[16,8,2,128,128]{4,3,2,1,0:T(8,128)(2,1)} %bitcast.35, f32[16,256,128]{2,1,0:T(8,128)} %shard_map.77.fil_hbm), custom_call_target="tpu_custom_call" | custom-call | tf_op jit(solution)/shard_map/pallas_call | solution.py:221
  64.3 1.3 %slice_bitcast_fusion.1 = (bf16[16,128,128]{2,1,0:T(8,128)(2,1)S(1)}, bf16[16,128,128]{2,1,0:T(8,128)(2,1)S(1)}) fusion(bf16[2,16,128,128]{3,2,1,0:T(8,128)(2,1)} %shard_map.78), kind=kLoop, calls=%fused_computation.33 | loop fusion | bytes 2097152 | tf_op jit(solution)/shard_map/squeeze | solution.py:88
  65.6 5.2 %collective-permute-start.3 = (bf16[16,1,128]{2,1,0:T(2,128)(2,1)S(1)}, bf16[16,1,128]{2,1,0:T(2,128)(2,1)S(1)}, u32[]{:S(2)}, u32[]{:S(2)}) collective-permute-start(bf16[16,1,128]{2,1,0:T(2,128)(2,1)S(1)} %get-tuple-element.30), channel_id=1, source_target_pairs={{0,1},{1,2},{2,3},{4,5},{5,6},{6,7},{8,9},{9,10},{10,11},{12,13},{... | collective-permute-start | bytes 12296 | tf_op jit(solution)/shard_map/ppermute | solution.py:58
  70.8 1.3 %collective-permute-start.4 = (bf16[16,1,128]{2,1,0:T(2,128)(2,1)S(1)}, bf16[16,1,128]{2,1,0:T(2,128)(2,1)S(1)}, u32[]{:S(2)}, u32[]{:S(2)}) collective-permute-start(bf16[16,1,128]{2,1,0:T(2,128)(2,1)S(1)} %get-tuple-element.31), channel_id=1, source_target_pairs={{1,0},{2,1},{3,2},{5,4},{6,5},{7,6},{9,8},{10,9},{11,10},{13,12},{... | collective-permute-start | bytes 12296 | tf_op jit(solution)/shard_map/ppermute | solution.py:58
  72.1 0.8 slice_bitcast_fusion.3
  72.9 7.1 %shard_map.79 = bf16[1024,128]{1,0:T(8,128)(2,1)} custom-call(bf16[4,10,2,128,128]{4,3,2,1,0:T(8,128)(2,1)} %bitcast.34, s32[1,1024]{1,0:T(1,128)} %reshape.74.row_leaf_ref, bf16[256,1024]{1,0:T(8,128)(2,1)} %bitcast.40), custom_call_target="tpu_custom_call" | custom-call | tf_op jit(solution)/shard_map/pallas_call | solution.py:238
  80.0 7.7 %all-to-all-start.1 = ((bf16[16,64,128]{2,1,0:T(8,128)(2,1)}), bf16[16,64,128]{2,1,0:T(8,128)(2,1)S(1)}, u32[]{:S(2)}, u32[]{:S(2)}) async-start(bf16[16,64,128]{2,1,0:T(8,128)(2,1)} %bitcast.43), calls=%async_computation.1 | async-start | bytes 524288 | tf_op jit(solution)/shard_map/all_to_all | solution.py:318
  87.7 3.8 %collective-permute-start.5 = (bf16[1,128,128]{2,1,0:T(8,128)(2,1)S(1)}, bf16[1,128,128]{2,1,0:T(8,128)(2,1)S(1)}, u32[]{:S(2)}, u32[]{:S(2)}) collective-permute-start(bf16[1,128,128]{2,1,0:T(8,128)(2,1)S(1)} %get-tuple-element.28), channel_id=1, source_target_pairs={{0,4},{1,5},{2,6},{3,7},{4,8},{5,9},{6,10},{7,11},{8,12},{9,13},{1... | collective-permute-start | bytes 98312 | tf_op jit(solution)/shard_map/ppermute | solution.py:58
  91.5 1.3 %collective-permute-start.6 = (bf16[1,128,128]{2,1,0:T(8,128)(2,1)S(1)}, bf16[1,128,128]{2,1,0:T(8,128)(2,1)S(1)}, u32[]{:S(2)}, u32[]{:S(2)}) collective-permute-start(bf16[1,128,128]{2,1,0:T(8,128)(2,1)S(1)} %get-tuple-element.29), channel_id=1, source_target_pairs={{4,0},{5,1},{6,2},{7,3},{8,4},{9,5},{10,6},{11,7},{12,8},{13,9},{1... | collective-permute-start | bytes 98312 | tf_op jit(solution)/shard_map/ppermute | solution.py:58
  92.8 0.0 collective-permute-done.3
  92.8 0.0 collective-permute-done.4
  92.8 0.1 maximum_convert_fusion.1
  93.0 0.7 collective-permute-done.5
  93.6 3.7 %collective-permute-done.6 = bf16[1,128,128]{2,1,0:T(8,128)(2,1)S(1)} collective-permute-done((bf16[1,128,128]{2,1,0:T(8,128)(2,1)S(1)}, bf16[1,128,128]{2,1,0:T(8,128)(2,1)S(1)}, u32[]{:S(2)}, u32[]{:S(2)}) %collective-permute-start.6) | collective-permute-done | bytes 32800 | tf_op jit(solution)/shard_map/ppermute | solution.py:58
  97.4 0.1 maximum_convert_fusion
  97.5 0.2 fusion.11
  97.7 1.4 %copy.37 = f32[128,16,128]{2,1,0:T(8,128)} copy(f32[128,16,128]{0,2,1:T(8,128)S(1)} %fusion.11) | data formatting | bytes 2097152
  99.0 0.0 all-to-all-done.1
  99.0 1.4 %fusion.9 = bf16[512,128]{1,0:T(8,128)(2,1)} fusion(bf16[1024,128]{1,0:T(8,128)(2,1)S(1)} %bitcast.46, s32[512]{0:T(512)S(1)} %multiply_add_fusion), kind=kOutput, calls=%fused_computation.18 | convolution fusion | flops 134807552 | bytes 395264 | tf_op jit(solution)/shard_map/dot_general | solution.py:321
  (4 shorter events, 0.0 us)
Async XLA Ops:
  0.6 12.7 %copy-start = (f32[128,16,256]{2,1,0:T(8,128)S(1)}, f32[128,16,256]{2,1,0:T(8,128)}, u32[]{:S(2)}) copy-start(f32[128,16,256]{2,1,0:T(8,128)} %param.6) | copy-start | bytes 6291460
  5.9 27.8 %all-to-all-start = ((bf16[16,65,384]{2,1,0:T(8,128)(2,1)}), bf16[16,65,384]{2,1,0:T(8,128)(2,1)}, u32[]{:S(2)}, u32[]{:S(2)}) async-start(bf16[16,65,384]{2,1,0:T(8,128)(2,1)} %fusion.16), calls=%async_computation | async-start | bytes 1769472 | tf_op jit(solution)/shard_map/all_to_all | solution.py:292
  14.2 5.4 %collective-permute-start = (f32[16,17,128]{2,1,0:T(8,128)S(1)}, f32[16,17,128]{2,1,0:T(8,128)S(1)}, u32[]{:S(2)}, u32[]{:S(2)}) collective-permute-start(f32[16,17,128]{2,1,0:T(8,128)S(1)} %bitcast.48), channel_id=1, source_target_pairs={{1,2},{2,1},{5,6},{6,5},{9,10},{10,9},{13,14},{14,13},{17,18},{18,... | collective-permute-start | bytes 417800 | tf_op jit(solution)/shard_map/ppermute | solution.py:58
  19.6 0.7 copy-start.1
  22.2 7.3 %copy-start.2 = (s32[2,8,8]{2,1,0:T(8,128)S(1)}, s32[2,8,8]{2,1,0:T(8,128)}, u32[]{:S(2)}) copy-start(s32[2,8,8]{2,1,0:T(8,128)} %param.8) | copy-start | bytes 1540
  23.4 23.6 %collective-permute-start.1 = (f32[9,162,128]{2,1,0:T(8,128)}, f32[9,162,128]{2,1,0:T(8,128)}, u32[]{:S(2)}, u32[]{:S(2)}) collective-permute-start(f32[9,162,128]{2,1,0:T(8,128)} %get-tuple-element.25), channel_id=1, source_target_pairs={{0,4},{1,5},{2,6},{3,7},{4,8},{5,9},{6,10},{7,11},{8,12},{9,13},{1... | collective-permute-start | bytes 2239496 | tf_op jit(solution)/shard_map/ppermute | solution.py:58
  28.1 19.3 %collective-permute-start.2 = (f32[9,162,128]{2,1,0:T(8,128)}, f32[9,162,128]{2,1,0:T(8,128)}, u32[]{:S(2)}, u32[]{:S(2)}) collective-permute-start(f32[9,162,128]{2,1,0:T(8,128)} %get-tuple-element.24), channel_id=1, source_target_pairs={{4,0},{5,1},{6,2},{7,3},{8,4},{9,5},{10,6},{11,7},{12,8},{13,9},{1... | collective-permute-start | bytes 2239496 | tf_op jit(solution)/shard_map/ppermute | solution.py:58
  65.6 27.2 %collective-permute-start.3 = (bf16[16,1,128]{2,1,0:T(2,128)(2,1)S(1)}, bf16[16,1,128]{2,1,0:T(2,128)(2,1)S(1)}, u32[]{:S(2)}, u32[]{:S(2)}) collective-permute-start(bf16[16,1,128]{2,1,0:T(2,128)(2,1)S(1)} %get-tuple-element.30), channel_id=1, source_target_pairs={{0,1},{1,2},{2,3},{4,5},{5,6},{6,7},{8,9},{9,10},{10,11},{12,13},{... | collective-permute-start | bytes 12296 | tf_op jit(solution)/shard_map/ppermute | solution.py:58
  70.8 22.0 %collective-permute-start.4 = (bf16[16,1,128]{2,1,0:T(2,128)(2,1)S(1)}, bf16[16,1,128]{2,1,0:T(2,128)(2,1)S(1)}, u32[]{:S(2)}, u32[]{:S(2)}) collective-permute-start(bf16[16,1,128]{2,1,0:T(2,128)(2,1)S(1)} %get-tuple-element.31), channel_id=1, source_target_pairs={{1,0},{2,1},{3,2},{5,4},{6,5},{7,6},{9,8},{10,9},{11,10},{13,12},{... | collective-permute-start | bytes 12296 | tf_op jit(solution)/shard_map/ppermute | solution.py:58
  80.0 19.1 %all-to-all-start.1 = ((bf16[16,64,128]{2,1,0:T(8,128)(2,1)}), bf16[16,64,128]{2,1,0:T(8,128)(2,1)S(1)}, u32[]{:S(2)}, u32[]{:S(2)}) async-start(bf16[16,64,128]{2,1,0:T(8,128)(2,1)} %bitcast.43), calls=%async_computation.1 | async-start | bytes 524288 | tf_op jit(solution)/shard_map/all_to_all | solution.py:318
  87.7 6.0 %collective-permute-start.5 = (bf16[1,128,128]{2,1,0:T(8,128)(2,1)S(1)}, bf16[1,128,128]{2,1,0:T(8,128)(2,1)S(1)}, u32[]{:S(2)}, u32[]{:S(2)}) collective-permute-start(bf16[1,128,128]{2,1,0:T(8,128)(2,1)S(1)} %get-tuple-element.28), channel_id=1, source_target_pairs={{0,4},{1,5},{2,6},{3,7},{4,8},{5,9},{6,10},{7,11},{8,12},{9,13},{1... | collective-permute-start | bytes 98312 | tf_op jit(solution)/shard_map/ppermute | solution.py:58
  91.5 5.9 %collective-permute-start.6 = (bf16[1,128,128]{2,1,0:T(8,128)(2,1)S(1)}, bf16[1,128,128]{2,1,0:T(8,128)(2,1)S(1)}, u32[]{:S(2)}, u32[]{:S(2)}) collective-permute-start(bf16[1,128,128]{2,1,0:T(8,128)(2,1)S(1)} %get-tuple-element.29), channel_id=1, source_target_pairs={{4,0},{5,1},{6,2},{7,3},{8,4},{9,5},{10,6},{11,7},{12,8},{13,9},{1... | collective-permute-start | bytes 98312 | tf_op jit(solution)/shard_map/ppermute | solution.py:58

commit v17 on v16

--- a/solution.py
+++ b/solution.py
@@ -183,30 +183,26 @@
     lax.fori_loop(0, leaf_count, one_leaf, 0)
 
 
-def induced_kernel(bord_hbm, row_leaf_ref, cpl_t_ref, volt_ref, own_ref, acc_ref, sems):
+def induced_kernel(bord_hbm, row_leaf_ref, cpl_t_ref, volt_ref, own_ref, stack_ref, sems):
     leaf_rows = own_ref.shape[0]
     leaf_cols = own_ref.shape[1] - 2
-    cells = own_ref.shape[3]
     copies = [
         pltpu.make_async_copy(bord_hbm.at[r + 1], own_ref.at[r], sems.at[r]) for r in range(leaf_rows)
     ]
     for copy in copies:
         copy.start()
-    acc_ref[...] = jnp.zeros_like(acc_ref)
-
-    def one_leaf(row, col):
-        coupling_t = cpl_t_ref[...]
-        leaf = row * leaf_cols + col
-        coupling_t = jnp.where(row_leaf_ref[...] == leaf, coupling_t, jnp.zeros_like(coupling_t))
-        own = own_ref[row, col + 1].reshape(2 * cells, -1)
-        acc_ref[...] += lax.dot_general(
-            own, coupling_t, (((0,), (0,)), ((), ())), preferred_element_type=jnp.float32
-        )
-
-    for r in range(leaf_rows):
-        copies[r].wait()
-        lax.fori_loop(0, leaf_cols, lambda col, carry: (one_leaf(r, col), carry)[1], 0)
-    volt_ref[...] = acc_ref[...].T.astype(volt_ref.dtype)
+    coupling_t = cpl_t_ref[...]
+    slot_leaf = row_leaf_ref[...]
+    for leaf in range(leaf_rows * leaf_cols):
+        stack_ref[leaf] = jnp.where(slot_leaf == leaf, coupling_t, jnp.zeros_like(coupling_t))
+    for copy in copies:
+        copy.wait()
+    own = own_ref[:, 1 : leaf_cols + 1].reshape(-1, own_ref.shape[-1])
+    stacked = stack_ref[...].reshape(own.shape[0], -1)
+    volt = lax.dot_general(
+        own, stacked, (((0,), (0,)), ((), ())), preferred_element_type=jnp.float32
+    )
+    volt_ref[...] = volt.T.astype(volt_ref.dtype)
 
 
 def leaf_fields(codes, scales, bordered, kernels, filament, row_leaf, coupling_t):
@@ -242,7 +238,7 @@
         out_shape=jax.ShapeDtypeStruct((slot_count, port_count), jnp.bfloat16),
         scratch_shapes=[
             pltpu.VMEM((leaf_rows,) + bordered.shape[1:], bordered.dtype),
-            pltpu.VMEM((port_count, slot_count), jnp.float32),
+            pltpu.VMEM((leaf_count,) + coupling_t.shape, coupling_t.dtype),
             pltpu.SemaphoreType.DMA((leaf_rows,)),
         ],
     )(bordered, row_leaf, coupling_t)

time: 101 us -> 98.8 us (0.978)
  Pallas kernels: 26.3 us -> 23.6 us
    pallas_call x1, Pallas kernels: 7.09 us -> 4.42 us  [leaf_fields(): pl.pallas_call(induced_kernel, in_specs=[hbm, vmem, vmem], out_specs=vmem...]
  transfers between devices with their start and end apart: 9 -> 9, of which waited for: 4 -> 4; matrix products, arithmetic and copies ran while one was open for 18% -> 19% of each run, Pallas kernels for 14% -> 12%
where the time goes in v17:
time: 98.8 us; the launch traced here: 97.8 us
  starting transfers between devices  33.2 us (34%)
  Pallas kernels  23.6 us (24%)
  local copies, waits for them, and re-layouts  19.7 us (20%)
  waiting for transfers between devices  8.45 us (9%)
  other arithmetic  8.33 us (8%)
  matrix products  3.5 us (4%)
    ppermute x7, starting transfers between devices, send(): return lax.ppermute(value, AXES, pairs_by(fn))  18.2 us
    pallas_call x1, Pallas kernels, leaf_fields(): pl.pallas_call(leaf_kernel, in_specs=[smem, smem, hbm, hbm, hbm], out_spe...  12.2 us
    unnamed x11, local copies, waits for them, and re-layouts  8.34 us
    all_to_all x1, starting transfers between devices, body(): lax.all_to_all(induced.reshape(owners, capacity, port_count), AXES, split...  7.67 us
    all_to_all x1, starting transfers between devices, body(): got = lax.all_to_all(payload, AXES, split_axis=0, concat_axis=0, tiled=True)  7.4 us
    pallas_call x1, Pallas kernels, filament_field(): pl.pallas_call(filament_kernel, in_specs=[vmem, vmem, vmem], out_specs=vm...  7.02 us
    ppermute x7, waiting for transfers between devices, send(): return lax.ppermute(value, AXES, pairs_by(fn))  4.8 us
    pallas_call x1, Pallas kernels, leaf_fields(): pl.pallas_call(induced_kernel, in_specs=[hbm, vmem, vmem], out_specs=vmem...  4.42 us
  transfers between devices with their start and end apart: 9, of which 4 were waited for; matrix products, arithmetic and copies ran while one was open for 19% of the time, Pallas kernels for 12%

profile of v17, /device:TPU:0, one launch (start us, length us, event | category | flops | bytes accessed | tf_op | source)
XLA Modules:
  0.0 97.8 jit_solution(300555230774685576)
XLA Ops:
  0.6 0.0 copy-start
  0.6 0.9 fusion.25
  1.5 0.2 convert_reduce_fusion
  1.8 0.5 fusion.3
  2.2 0.1 reshape.77
  2.3 1.0 %copy.46 = bf16[64,8,2,128]{3,1,2,0:T(8,128)(2,1)S(1)} copy(bf16[64,8,2,128]{3,2,1,0:T(2,128)(2,1)} %bitcast.45) | data formatting | bytes 524288
  3.3 1.6 %fusion.6 = bf16[1024,384]{1,0:T(8,128)(2,1)S(1)} fusion(s32[512]{0:T(512)S(1)} %multiply_add_fusion, bf16[512,128]{1,0:T(8,128)(2,1)} %param.10, bf16[512,256]{1,0:T(8,128)(2,1)S(1)} %bitcast.47), kind=kOutput, calls=%fused_computation.15 | convolution fusion | flops 404357120 | bytes 1181696 | tf_op jit(solution)/shard_map/dot_general | solution.py:279
  4.9 1.0 %fusion.16 = bf16[16,65,384]{2,1,0:T(8,128)(2,1)} fusion(bf16[16,1,64]{2,1,0:T(2,128)(2,1)S(1)} %reshape.77, bf16[16,64,384]{2,1,0:T(8,128)(2,1)S(1)} %bitcast.44), kind=kLoop, calls=%fused_computation.29 | loop fusion | flops 2396160 | bytes 1587200 | tf_op jit(solution)/shard_map/concatenate | solution.py:287
  5.9 7.4 %all-to-all-start = ((bf16[16,65,384]{2,1,0:T(8,128)(2,1)}), bf16[16,65,384]{2,1,0:T(8,128)(2,1)}, u32[]{:S(2)}, u32[]{:S(2)}) async-start(bf16[16,65,384]{2,1,0:T(8,128)(2,1)} %fusion.16), calls=%async_computation | async-start | bytes 1769472 | tf_op jit(solution)/shard_map/all_to_all | solution.py:288
  13.3 0.0 copy-done
  13.4 0.3 constant_dynamic-slice_fusion.1
  13.7 0.4 copy.40
  14.2 0.7 collective-permute-start
  14.8 2.0 %constant_dynamic-slice_fusion = f32[128,16,145]{2,1,0:T(8,128)} fusion(f32[128,16,256]{2,1,0:T(8,128)S(1)} %copy-done, s32[]{:T(128)S(6)} %select_n.49), kind=kLoop, calls=%fused_computation.78 | loop fusion | bytes 2375684 | tf_op jit(solution)/shard_map/dynamic-slice.1
  16.8 2.8 %copy.41 = f32[128,16,145]{0,2,1:T(8,128)} copy(f32[128,16,145]{2,1,0:T(8,128)} %constant_dynamic-slice_fusion) | data formatting | bytes 2375680
  19.6 0.0 collective-permute-done
  19.6 0.0 copy-start.1
  19.6 0.7 copy-done.1
  20.2 1.9 %fusion.8 = f32[16,162,128]{2,1,0:T(8,128)S(1)} fusion(s32[]{:T(128)S(6)} %select_n.50, f32[16,17,128]{2,1,0:T(8,128)} %copy-done.1, f32[16,145,128]{2,1,0:T(8,128)} %bitcast.38), kind=kLoop, calls=%fused_computation.17 | loop fusion | flops 663552 | bytes 2654212 | tf_op jit(solution)/shard_map/concatenate | solution.py:79
  22.2 0.0 copy-start.2
  22.2 1.3 %fusion.34 = (f32[9,162,128]{2,1,0:T(8,128)}, f32[9,162,128]{2,1,0:T(8,128)}) fusion(f32[16,162,128]{2,1,0:T(8,128)S(1)} %fusion.8), kind=kLoop, calls=%fused_computation.84 | loop fusion | bytes 2985984 | tf_op jit(solution)/shard_map/slice | solution.py:82
  23.4 4.7 %collective-permute-start.1 = (f32[9,162,128]{2,1,0:T(8,128)}, f32[9,162,128]{2,1,0:T(8,128)}, u32[]{:S(2)}, u32[]{:S(2)}) collective-permute-start(f32[9,162,128]{2,1,0:T(8,128)} %get-tuple-element.25), channel_id=1, source_target_pairs={{0,4},{1,5},{2,6},{3,7},{4,8},{5,9},{6,10},{7,11},{8,12},{9,13},{1... | collective-permute-start | bytes 2239496 | tf_op jit(solution)/shard_map/ppermute | solution.py:58
  28.1 1.3 %collective-permute-start.2 = (f32[9,162,128]{2,1,0:T(8,128)}, f32[9,162,128]{2,1,0:T(8,128)}, u32[]{:S(2)}, u32[]{:S(2)}) collective-permute-start(f32[9,162,128]{2,1,0:T(8,128)} %get-tuple-element.24), channel_id=1, source_target_pairs={{4,0},{5,1},{6,2},{7,3},{8,4},{9,5},{10,6},{11,7},{12,8},{13,9},{1... | collective-permute-start | bytes 2239496 | tf_op jit(solution)/shard_map/ppermute | solution.py:58
  29.4 0.0 copy-done.2
  29.4 0.6 convert_bitcast_fusion.scale_ref
  30.0 3.7 %all-to-all-done = bf16[16,65,384]{2,1,0:T(8,128)(2,1)} async-done(((bf16[16,65,384]{2,1,0:T(8,128)(2,1)}), bf16[16,65,384]{2,1,0:T(8,128)(2,1)}, u32[]{:S(2)}, u32[]{:S(2)}) %all-to-all-start) | async-done | bytes 798752 | tf_op jit(solution)/shard_map/all_to_all | solution.py:288
  33.7 1.2 %slice.93 = bf16[16,64,384]{2,1,0:T(8,128)(2,1)S(1)} slice(bf16[16,65,384]{2,1,0:T(8,128)(2,1)} %all-to-all-done), slice={[0:16], [0:64], [0:384]} | slice | bytes 1572864 | tf_op jit(solution)/shard_map/slice | solution.py:289
  34.9 0.8 slice.94
  35.7 0.7 slice.95.cur_ref
  36.5 2.0 %copy.42 = bf16[1024,256]{0,1:T(8,128)(2,1)} copy(bf16[1024,256]{1,0:T(8,128)(2,1)} %slice.94) | data formatting | bytes 1048576
  38.5 0.8 fusion.22
  39.3 0.7 reshape.74.row_leaf_ref
  40.0 7.0 %shard_map.77.fil_hbm = f32[16,256,128]{2,1,0:T(8,128)} custom-call(s32[1,1024]{1,0:T(1,128)} %reshape.74.row_leaf_ref, bf16[256,1024]{1,0:T(8,128)(2,1)} %bitcast.39, bf16[1024,128]{1,0:T(8,128)(2,1)} %slice.95.cur_ref), custom_call_target="tpu_custom_call" | custom-call | tf_op jit(solution)/shard_map/pallas_call | solution.py:119
  47.0 0.0 collective-permute-done.1
  47.0 0.4 collective-permute-done.2
  47.4 1.6 %pad_maximum_fusion = f32[34,162,128]{2,1,0:T(8,128)S(1)} fusion(f32[9,162,128]{2,1,0:T(8,128)} %collective-permute-done.2, f32[16,162,128]{2,1,0:T(8,128)S(1)} %fusion.8, f32[9,162,128]{2,1,0:T(8,128)} %collective-permute-done.1), kind=kLoop, calls=%fused_computation | loop fusion | flops 1410048 | bytes 5640192 | tf_op jit(solution)/shard_map/concatenate | solution.py:84
  48.9 0.7 fusion.1
  49.6 0.2 maximum_bitcast_fusion
  49.9 2.3 %copy.34 = bf16[4,10,2,8,16,128]{5,4,3,2,1,0:T(8,128)(2,1)} copy(bf16[4,10,2,8,16,128]{5,4,1,3,0,2:T(8,128)(2,1)S(1)} %maximum_bitcast_fusion) | data formatting | bytes 5242880 | tf_op jit(solution)/shard_map/transpose | solution.py:24
  52.1 12.2 %shard_map.78 = bf16[2,16,128,128]{3,2,1,0:T(8,128)(2,1)} custom-call(s32[16,8]{1,0:T(8,128)} %bitcast.49, s32[16,8]{1,0:T(8,128)} %convert_bitcast_fusion.scale_ref, bf16[4,10,2,128,128]{4,3,2,1,0:T(8,128)(2,1)} %bitcast.33, bf16[16,8,2,128,128]{4,3,2,1,0:T(8,128)(2,1)} %bitcast.35, f32[16,256,128]{2,1,0:T(8,128)} %shard_map.77.fil_hbm), custom_call_target="tpu_custom_call" | custom-call | tf_op jit(solution)/shard_map/pallas_call | solution.py:217
  64.3 1.3 %slice_bitcast_fusion.1 = (bf16[16,128,128]{2,1,0:T(8,128)(2,1)S(1)}, bf16[16,128,128]{2,1,0:T(8,128)(2,1)S(1)}) fusion(bf16[2,16,128,128]{3,2,1,0:T(8,128)(2,1)} %shard_map.78), kind=kLoop, calls=%fused_computation.33 | loop fusion | bytes 2097152 | tf_op jit(solution)/shard_map/squeeze | solution.py:88
  65.6 5.2 %collective-permute-start.3 = (bf16[16,1,128]{2,1,0:T(2,128)(2,1)S(1)}, bf16[16,1,128]{2,1,0:T(2,128)(2,1)S(1)}, u32[]{:S(2)}, u32[]{:S(2)}) collective-permute-start(bf16[16,1,128]{2,1,0:T(2,128)(2,1)S(1)} %get-tuple-element.30), channel_id=1, source_target_pairs={{0,1},{1,2},{2,3},{4,5},{5,6},{6,7},{8,9},{9,10},{10,11},{12,13},{... | collective-permute-start | bytes 12296 | tf_op jit(solution)/shard_map/ppermute | solution.py:58
  70.8 1.3 %collective-permute-start.4 = (bf16[16,1,128]{2,1,0:T(2,128)(2,1)S(1)}, bf16[16,1,128]{2,1,0:T(2,128)(2,1)S(1)}, u32[]{:S(2)}, u32[]{:S(2)}) collective-permute-start(bf16[16,1,128]{2,1,0:T(2,128)(2,1)S(1)} %get-tuple-element.31), channel_id=1, source_target_pairs={{1,0},{2,1},{3,2},{5,4},{6,5},{7,6},{9,8},{10,9},{11,10},{13,12},{... | collective-permute-start | bytes 12296 | tf_op jit(solution)/shard_map/ppermute | solution.py:58
  72.1 0.8 slice_bitcast_fusion.3
  72.9 4.4 %shard_map.79 = bf16[1024,128]{1,0:T(8,128)(2,1)} custom-call(bf16[4,10,2,128,128]{4,3,2,1,0:T(8,128)(2,1)} %bitcast.34, s32[1,1024]{1,0:T(1,128)} %reshape.74.row_leaf_ref, bf16[256,1024]{1,0:T(8,128)(2,1)} %bitcast.40), custom_call_target="tpu_custom_call" | custom-call | tf_op jit(solution)/shard_map/pallas_call | solution.py:234
  77.3 7.7 %all-to-all-start.1 = ((bf16[16,64,128]{2,1,0:T(8,128)(2,1)}), bf16[16,64,128]{2,1,0:T(8,128)(2,1)S(1)}, u32[]{:S(2)}, u32[]{:S(2)}) async-start(bf16[16,64,128]{2,1,0:T(8,128)(2,1)} %bitcast.43), calls=%async_computation.1 | async-start | bytes 524288 | tf_op jit(solution)/shard_map/all_to_all | solution.py:314
  85.0 3.8 %collective-permute-start.5 = (bf16[1,128,128]{2,1,0:T(8,128)(2,1)S(1)}, bf16[1,128,128]{2,1,0:T(8,128)(2,1)S(1)}, u32[]{:S(2)}, u32[]{:S(2)}) collective-permute-start(bf16[1,128,128]{2,1,0:T(8,128)(2,1)S(1)} %get-tuple-element.28), channel_id=1, source_target_pairs={{0,4},{1,5},{2,6},{3,7},{4,8},{5,9},{6,10},{7,11},{8,12},{9,13},{1... | collective-permute-start | bytes 98312 | tf_op jit(solution)/shard_map/ppermute | solution.py:58
  88.8 1.3 %collective-permute-start.6 = (bf16[1,128,128]{2,1,0:T(8,128)(2,1)S(1)}, bf16[1,128,128]{2,1,0:T(8,128)(2,1)S(1)}, u32[]{:S(2)}, u32[]{:S(2)}) collective-permute-start(bf16[1,128,128]{2,1,0:T(8,128)(2,1)S(1)} %get-tuple-element.29), channel_id=1, source_target_pairs={{4,0},{5,1},{6,2},{7,3},{8,4},{9,5},{10,6},{11,7},{12,8},{13,9},{1... | collective-permute-start | bytes 98312 | tf_op jit(solution)/shard_map/ppermute | solution.py:58
  90.1 0.0 collective-permute-done.3
  90.1 0.0 collective-permute-done.4
  90.1 0.1 maximum_convert_fusion.1
  90.3 0.7 collective-permute-done.5
  91.0 3.7 %collective-permute-done.6 = bf16[1,128,128]{2,1,0:T(8,128)(2,1)S(1)} collective-permute-done((bf16[1,128,128]{2,1,0:T(8,128)(2,1)S(1)}, bf16[1,128,128]{2,1,0:T(8,128)(2,1)S(1)}, u32[]{:S(2)}, u32[]{:S(2)}) %collective-permute-start.6) | collective-permute-done | bytes 32800 | tf_op jit(solution)/shard_map/ppermute | solution.py:58
  94.7 0.1 maximum_convert_fusion
  94.8 0.2 fusion.11
  95.0 1.4 %copy.37 = f32[128,16,128]{2,1,0:T(8,128)} copy(f32[128,16,128]{0,2,1:T(8,128)S(1)} %fusion.11) | data formatting | bytes 2097152
  96.4 0.0 all-to-all-done.1
  96.4 1.4 %fusion.9 = bf16[512,128]{1,0:T(8,128)(2,1)} fusion(bf16[1024,128]{1,0:T(8,128)(2,1)S(1)} %bitcast.46, s32[512]{0:T(512)S(1)} %multiply_add_fusion), kind=kOutput, calls=%fused_computation.18 | convolution fusion | flops 134807552 | bytes 395264 | tf_op jit(solution)/shard_map/dot_general | solution.py:317
  (4 shorter events, 0.0 us)
Async XLA Ops:
  0.6 12.7 %copy-start = (f32[128,16,256]{2,1,0:T(8,128)S(1)}, f32[128,16,256]{2,1,0:T(8,128)}, u32[]{:S(2)}) copy-start(f32[128,16,256]{2,1,0:T(8,128)} %param.6) | copy-start | bytes 6291460
  5.9 27.8 %all-to-all-start = ((bf16[16,65,384]{2,1,0:T(8,128)(2,1)}), bf16[16,65,384]{2,1,0:T(8,128)(2,1)}, u32[]{:S(2)}, u32[]{:S(2)}) async-start(bf16[16,65,384]{2,1,0:T(8,128)(2,1)} %fusion.16), calls=%async_computation | async-start | bytes 1769472 | tf_op jit(solution)/shard_map/all_to_all | solution.py:288
  14.2 5.4 %collective-permute-start = (f32[16,17,128]{2,1,0:T(8,128)S(1)}, f32[16,17,128]{2,1,0:T(8,128)S(1)}, u32[]{:S(2)}, u32[]{:S(2)}) collective-permute-start(f32[16,17,128]{2,1,0:T(8,128)S(1)} %bitcast.48), channel_id=1, source_target_pairs={{1,2},{2,1},{5,6},{6,5},{9,10},{10,9},{13,14},{14,13},{17,18},{18,... | collective-permute-start | bytes 417800 | tf_op jit(solution)/shard_map/ppermute | solution.py:58
  19.6 0.7 copy-start.1
  22.2 7.3 %copy-start.2 = (s32[2,8,8]{2,1,0:T(8,128)S(1)}, s32[2,8,8]{2,1,0:T(8,128)}, u32[]{:S(2)}) copy-start(s32[2,8,8]{2,1,0:T(8,128)} %param.8) | copy-start | bytes 1540
  23.4 23.6 %collective-permute-start.1 = (f32[9,162,128]{2,1,0:T(8,128)}, f32[9,162,128]{2,1,0:T(8,128)}, u32[]{:S(2)}, u32[]{:S(2)}) collective-permute-start(f32[9,162,128]{2,1,0:T(8,128)} %get-tuple-element.25), channel_id=1, source_target_pairs={{0,4},{1,5},{2,6},{3,7},{4,8},{5,9},{6,10},{7,11},{8,12},{9,13},{1... | collective-permute-start | bytes 2239496 | tf_op jit(solution)/shard_map/ppermute | solution.py:58
  28.1 19.3 %collective-permute-start.2 = (f32[9,162,128]{2,1,0:T(8,128)}, f32[9,162,128]{2,1,0:T(8,128)}, u32[]{:S(2)}, u32[]{:S(2)}) collective-permute-start(f32[9,162,128]{2,1,0:T(8,128)} %get-tuple-element.24), channel_id=1, source_target_pairs={{4,0},{5,1},{6,2},{7,3},{8,4},{9,5},{10,6},{11,7},{12,8},{13,9},{1... | collective-permute-start | bytes 2239496 | tf_op jit(solution)/shard_map/ppermute | solution.py:58
  65.6 24.5 %collective-permute-start.3 = (bf16[16,1,128]{2,1,0:T(2,128)(2,1)S(1)}, bf16[16,1,128]{2,1,0:T(2,128)(2,1)S(1)}, u32[]{:S(2)}, u32[]{:S(2)}) collective-permute-start(bf16[16,1,128]{2,1,0:T(2,128)(2,1)S(1)} %get-tuple-element.30), channel_id=1, source_target_pairs={{0,1},{1,2},{2,3},{4,5},{5,6},{6,7},{8,9},{9,10},{10,11},{12,13},{... | collective-permute-start | bytes 12296 | tf_op jit(solution)/shard_map/ppermute | solution.py:58
  70.8 19.3 %collective-permute-start.4 = (bf16[16,1,128]{2,1,0:T(2,128)(2,1)S(1)}, bf16[16,1,128]{2,1,0:T(2,128)(2,1)S(1)}, u32[]{:S(2)}, u32[]{:S(2)}) collective-permute-start(bf16[16,1,128]{2,1,0:T(2,128)(2,1)S(1)} %get-tuple-element.31), channel_id=1, source_target_pairs={{1,0},{2,1},{3,2},{5,4},{6,5},{7,6},{9,8},{10,9},{11,10},{13,12},{... | collective-permute-start | bytes 12296 | tf_op jit(solution)/shard_map/ppermute | solution.py:58
  77.3 19.0 %all-to-all-start.1 = ((bf16[16,64,128]{2,1,0:T(8,128)(2,1)}), bf16[16,64,128]{2,1,0:T(8,128)(2,1)S(1)}, u32[]{:S(2)}, u32[]{:S(2)}) async-start(bf16[16,64,128]{2,1,0:T(8,128)(2,1)} %bitcast.43), calls=%async_computation.1 | async-start | bytes 524288 | tf_op jit(solution)/shard_map/all_to_all | solution.py:314
  85.0 6.0 %collective-permute-start.5 = (bf16[1,128,128]{2,1,0:T(8,128)(2,1)S(1)}, bf16[1,128,128]{2,1,0:T(8,128)(2,1)S(1)}, u32[]{:S(2)}, u32[]{:S(2)}) collective-permute-start(bf16[1,128,128]{2,1,0:T(8,128)(2,1)S(1)} %get-tuple-element.28), channel_id=1, source_target_pairs={{0,4},{1,5},{2,6},{3,7},{4,8},{5,9},{6,10},{7,11},{8,12},{9,13},{1... | collective-permute-start | bytes 98312 | tf_op jit(solution)/shard_map/ppermute | solution.py:58
  88.8 5.9 %collective-permute-start.6 = (bf16[1,128,128]{2,1,0:T(8,128)(2,1)S(1)}, bf16[1,128,128]{2,1,0:T(8,128)(2,1)S(1)}, u32[]{:S(2)}, u32[]{:S(2)}) collective-permute-start(bf16[1,128,128]{2,1,0:T(8,128)(2,1)S(1)} %get-tuple-element.29), channel_id=1, source_target_pairs={{4,0},{5,1},{6,2},{7,3},{8,4},{9,5},{10,6},{11,7},{12,8},{13,9},{1... | collective-permute-start | bytes 98312 | tf_op jit(solution)/shard_map/ppermute | solution.py:58

commit v18 on v17

--- a/solution.py
+++ b/solution.py
@@ -104,14 +104,15 @@
     return x_pad[:, :-2] - x_pad[:, 2:] + (y_pad[2:] - y_pad[:-2])
 
 
-def filament_kernel(row_leaf_ref, cpl_t_ref, cur_ref, fil_ref):
-    def one_leaf(leaf, carry):
-        coupling_t = cpl_t_ref[...]
-        coupling_t = jnp.where(row_leaf_ref[...] == leaf, coupling_t, jnp.zeros_like(coupling_t))
-        fil_ref[leaf] = jnp.dot(coupling_t, cur_ref[...], preferred_element_type=jnp.float32)
-        return carry
-
-    lax.fori_loop(0, fil_ref.shape[0], one_leaf, 0)
+def filament_kernel(row_leaf_ref, cpl_t_ref, cur_ref, fil_ref, stack_ref):
+    coupling_t = cpl_t_ref[...]
+    slot_leaf = row_leaf_ref[...]
+    for leaf in range(fil_ref.shape[0]):
+        stack_ref[leaf] = jnp.where(slot_leaf == leaf, coupling_t, jnp.zeros_like(coupling_t))
+    stacked = stack_ref[...].reshape(-1, coupling_t.shape[1])
+    fil_ref[...] = jnp.dot(stacked, cur_ref[...], preferred_element_type=jnp.float32).reshape(
+        fil_ref.shape
+    )
 
 
 def filament_field(row_leaf, coupling_t, current, leaf_count):
@@ -123,6 +124,7 @@
         out_shape=jax.ShapeDtypeStruct(
             (leaf_count, coupling_t.shape[0], current.shape[1]), jnp.float32
         ),
+        scratch_shapes=[pltpu.VMEM((leaf_count,) + coupling_t.shape, coupling_t.dtype)],
     )(row_leaf, coupling_t, current)
 
 

time: 98.8 us -> 98.8 us (level)
  waiting for transfers between devices: 8.45 us -> 10.7 us
  Pallas kernels: 23.6 us -> 21.4 us
    ppermute x7, waiting for transfers between devices: 4.8 us -> 7.04 us  [send(): return lax.ppermute(value, AXES, pairs_by(fn))]
    pallas_call x1, Pallas kernels: 7.02 us -> 4.79 us  [filament_field(): pl.pallas_call(filament_kernel, in_specs=[vmem, vmem, vmem], out_specs=vm...]
  transfers between devices with their start and end apart: 9 -> 9, of which waited for: 4 -> 4; matrix products, arithmetic and copies ran while one was open for 19% -> 19% of each run, Pallas kernels for 12% -> 9%
where the time goes in v18:
time: 98.8 us; the launch traced here: 97.8 us
  starting transfers between devices  33.2 us (34%)
  Pallas kernels  21.4 us (22%)
  local copies, waits for them, and re-layouts  19.7 us (20%)
  waiting for transfers between devices  10.7 us (11%)
  other arithmetic  8.33 us (8%)
  matrix products  3.5 us (4%)
    ppermute x7, starting transfers between devices, send(): return lax.ppermute(value, AXES, pairs_by(fn))  18.2 us
    pallas_call x1, Pallas kernels, leaf_fields(): pl.pallas_call(leaf_kernel, in_specs=[smem, smem, hbm, hbm, hbm], out_spe...  12.2 us
    unnamed x11, local copies, waits for them, and re-layouts  8.34 us
    all_to_all x1, starting transfers between devices, body(): lax.all_to_all(induced.reshape(owners, capacity, port_count), AXES, split...  7.67 us
    all_to_all x1, starting transfers between devices, body(): got = lax.all_to_all(payload, AXES, split_axis=0, concat_axis=0, tiled=True)  7.4 us
    ppermute x7, waiting for transfers between devices, send(): return lax.ppermute(value, AXES, pairs_by(fn))  7.04 us
    pallas_call x1, Pallas kernels, filament_field(): pl.pallas_call(filament_kernel, in_specs=[vmem, vmem, vmem], out_specs=vm...  4.79 us
    pallas_call x1, Pallas kernels, leaf_fields(): pl.pallas_call(induced_kernel, in_specs=[hbm, vmem, vmem], out_specs=vmem...  4.42 us
  transfers between devices with their start and end apart: 9, of which 4 were waited for; matrix products, arithmetic and copies ran while one was open for 19% of the time, Pallas kernels for 9%

profile of v18, /device:TPU:0, one launch (start us, length us, event | category | flops | bytes accessed | tf_op | source)
XLA Modules:
  0.0 97.8 jit_solution(10482316504919442714)
XLA Ops:
  0.6 0.0 copy-start
  0.6 0.9 fusion.25
  1.5 0.2 convert_reduce_fusion
  1.8 0.5 fusion.3
  2.2 0.1 reshape.77
  2.3 1.0 %copy.46 = bf16[64,8,2,128]{3,1,2,0:T(8,128)(2,1)S(1)} copy(bf16[64,8,2,128]{3,2,1,0:T(2,128)(2,1)} %bitcast.45) | data formatting | bytes 524288
  3.3 1.6 %fusion.6 = bf16[1024,384]{1,0:T(8,128)(2,1)S(1)} fusion(s32[512]{0:T(512)S(1)} %multiply_add_fusion, bf16[512,128]{1,0:T(8,128)(2,1)} %param.10, bf16[512,256]{1,0:T(8,128)(2,1)S(1)} %bitcast.47), kind=kOutput, calls=%fused_computation.15 | convolution fusion | flops 404357120 | bytes 1181696 | tf_op jit(solution)/shard_map/dot_general | solution.py:281
  4.9 1.0 %fusion.16 = bf16[16,65,384]{2,1,0:T(8,128)(2,1)} fusion(bf16[16,1,64]{2,1,0:T(2,128)(2,1)S(1)} %reshape.77, bf16[16,64,384]{2,1,0:T(8,128)(2,1)S(1)} %bitcast.44), kind=kLoop, calls=%fused_computation.29 | loop fusion | flops 2396160 | bytes 1587200 | tf_op jit(solution)/shard_map/concatenate | solution.py:289
  5.9 7.4 %all-to-all-start = ((bf16[16,65,384]{2,1,0:T(8,128)(2,1)}), bf16[16,65,384]{2,1,0:T(8,128)(2,1)}, u32[]{:S(2)}, u32[]{:S(2)}) async-start(bf16[16,65,384]{2,1,0:T(8,128)(2,1)} %fusion.16), calls=%async_computation | async-start | bytes 1769472 | tf_op jit(solution)/shard_map/all_to_all | solution.py:290
  13.3 0.0 copy-done
  13.4 0.3 constant_dynamic-slice_fusion.1
  13.7 0.4 copy.40
  14.2 0.7 collective-permute-start
  14.8 2.0 %constant_dynamic-slice_fusion = f32[128,16,145]{2,1,0:T(8,128)} fusion(f32[128,16,256]{2,1,0:T(8,128)S(1)} %copy-done, s32[]{:T(128)S(6)} %select_n.49), kind=kLoop, calls=%fused_computation.78 | loop fusion | bytes 2375684 | tf_op jit(solution)/shard_map/dynamic-slice.1
  16.8 2.8 %copy.41 = f32[128,16,145]{0,2,1:T(8,128)} copy(f32[128,16,145]{2,1,0:T(8,128)} %constant_dynamic-slice_fusion) | data formatting | bytes 2375680
  19.6 0.0 collective-permute-done
  19.6 0.0 copy-start.1
  19.6 0.7 copy-done.1
  20.2 1.9 %fusion.8 = f32[16,162,128]{2,1,0:T(8,128)S(1)} fusion(s32[]{:T(128)S(6)} %select_n.50, f32[16,17,128]{2,1,0:T(8,128)} %copy-done.1, f32[16,145,128]{2,1,0:T(8,128)} %bitcast.38), kind=kLoop, calls=%fused_computation.17 | loop fusion | flops 663552 | bytes 2654212 | tf_op jit(solution)/shard_map/concatenate | solution.py:79
  22.2 0.0 copy-start.2
  22.2 1.3 %fusion.34 = (f32[9,162,128]{2,1,0:T(8,128)}, f32[9,162,128]{2,1,0:T(8,128)}) fusion(f32[16,162,128]{2,1,0:T(8,128)S(1)} %fusion.8), kind=kLoop, calls=%fused_computation.84 | loop fusion | bytes 2985984 | tf_op jit(solution)/shard_map/slice | solution.py:82
  23.4 4.7 %collective-permute-start.1 = (f32[9,162,128]{2,1,0:T(8,128)}, f32[9,162,128]{2,1,0:T(8,128)}, u32[]{:S(2)}, u32[]{:S(2)}) collective-permute-start(f32[9,162,128]{2,1,0:T(8,128)} %get-tuple-element.25), channel_id=1, source_target_pairs={{0,4},{1,5},{2,6},{3,7},{4,8},{5,9},{6,10},{7,11},{8,12},{9,13},{1... | collective-permute-start | bytes 2239496 | tf_op jit(solution)/shard_map/ppermute | solution.py:58
  28.1 1.3 %collective-permute-start.2 = (f32[9,162,128]{2,1,0:T(8,128)}, f32[9,162,128]{2,1,0:T(8,128)}, u32[]{:S(2)}, u32[]{:S(2)}) collective-permute-start(f32[9,162,128]{2,1,0:T(8,128)} %get-tuple-element.24), channel_id=1, source_target_pairs={{4,0},{5,1},{6,2},{7,3},{8,4},{9,5},{10,6},{11,7},{12,8},{13,9},{1... | collective-permute-start | bytes 2239496 | tf_op jit(solution)/shard_map/ppermute | solution.py:58
  29.4 0.0 copy-done.2
  29.4 0.6 convert_bitcast_fusion.scale_ref
  30.0 3.7 %all-to-all-done = bf16[16,65,384]{2,1,0:T(8,128)(2,1)} async-done(((bf16[16,65,384]{2,1,0:T(8,128)(2,1)}), bf16[16,65,384]{2,1,0:T(8,128)(2,1)}, u32[]{:S(2)}, u32[]{:S(2)}) %all-to-all-start) | async-done | bytes 798752 | tf_op jit(solution)/shard_map/all_to_all | solution.py:290
  33.7 1.2 %slice.93 = bf16[16,64,384]{2,1,0:T(8,128)(2,1)S(1)} slice(bf16[16,65,384]{2,1,0:T(8,128)(2,1)} %all-to-all-done), slice={[0:16], [0:64], [0:384]} | slice | bytes 1572864 | tf_op jit(solution)/shard_map/slice | solution.py:291
  34.9 0.8 slice.94
  35.7 0.7 slice.95.cur_ref
  36.5 2.0 %copy.42 = bf16[1024,256]{0,1:T(8,128)(2,1)} copy(bf16[1024,256]{1,0:T(8,128)(2,1)} %slice.94) | data formatting | bytes 1048576
  38.5 0.8 fusion.22
  39.3 0.7 reshape.74.row_leaf_ref
  40.0 4.8 %shard_map.77.fil_hbm = f32[16,256,128]{2,1,0:T(8,128)} custom-call(s32[1,1024]{1,0:T(1,128)} %reshape.74.row_leaf_ref, bf16[256,1024]{1,0:T(8,128)(2,1)} %bitcast.39, bf16[1024,128]{1,0:T(8,128)(2,1)} %slice.95.cur_ref), custom_call_target="tpu_custom_call" | custom-call | tf_op jit(solution)/shard_map/pallas_call | solution.py:120
  44.8 0.0 collective-permute-done.1
  44.8 2.6 %collective-permute-done.2 = f32[9,162,128]{2,1,0:T(8,128)} collective-permute-done((f32[9,162,128]{2,1,0:T(8,128)}, f32[9,162,128]{2,1,0:T(8,128)}, u32[]{:S(2)}, u32[]{:S(2)}) %collective-permute-start.2) | collective-permute-done | bytes 746528 | tf_op jit(solution)/shard_map/ppermute | solution.py:58
  47.4 1.6 %pad_maximum_fusion = f32[34,162,128]{2,1,0:T(8,128)S(1)} fusion(f32[9,162,128]{2,1,0:T(8,128)} %collective-permute-done.2, f32[16,162,128]{2,1,0:T(8,128)S(1)} %fusion.8, f32[9,162,128]{2,1,0:T(8,128)} %collective-permute-done.1), kind=kLoop, calls=%fused_computation | loop fusion | flops 1410048 | bytes 5640192 | tf_op jit(solution)/shard_map/concatenate | solution.py:84
  48.9 0.7 fusion.1
  49.6 0.2 maximum_bitcast_fusion
  49.9 2.3 %copy.34 = bf16[4,10,2,8,16,128]{5,4,3,2,1,0:T(8,128)(2,1)} copy(bf16[4,10,2,8,16,128]{5,4,1,3,0,2:T(8,128)(2,1)S(1)} %maximum_bitcast_fusion) | data formatting | bytes 5242880 | tf_op jit(solution)/shard_map/transpose | solution.py:24
  52.1 12.2 %shard_map.78 = bf16[2,16,128,128]{3,2,1,0:T(8,128)(2,1)} custom-call(s32[16,8]{1,0:T(8,128)} %bitcast.49, s32[16,8]{1,0:T(8,128)} %convert_bitcast_fusion.scale_ref, bf16[4,10,2,128,128]{4,3,2,1,0:T(8,128)(2,1)} %bitcast.33, bf16[16,8,2,128,128]{4,3,2,1,0:T(8,128)(2,1)} %bitcast.35, f32[16,256,128]{2,1,0:T(8,128)} %shard_map.77.fil_hbm), custom_call_target="tpu_custom_call" | custom-call | tf_op jit(solution)/shard_map/pallas_call | solution.py:219
  64.3 1.3 %slice_bitcast_fusion.1 = (bf16[16,128,128]{2,1,0:T(8,128)(2,1)S(1)}, bf16[16,128,128]{2,1,0:T(8,128)(2,1)S(1)}) fusion(bf16[2,16,128,128]{3,2,1,0:T(8,128)(2,1)} %shard_map.78), kind=kLoop, calls=%fused_computation.33 | loop fusion | bytes 2097152 | tf_op jit(solution)/shard_map/squeeze | solution.py:88
  65.6 5.2 %collective-permute-start.3 = (bf16[16,1,128]{2,1,0:T(2,128)(2,1)S(1)}, bf16[16,1,128]{2,1,0:T(2,128)(2,1)S(1)}, u32[]{:S(2)}, u32[]{:S(2)}) collective-permute-start(bf16[16,1,128]{2,1,0:T(2,128)(2,1)S(1)} %get-tuple-element.30), channel_id=1, source_target_pairs={{0,1},{1,2},{2,3},{4,5},{5,6},{6,7},{8,9},{9,10},{10,11},{12,13},{... | collective-permute-start | bytes 12296 | tf_op jit(solution)/shard_map/ppermute | solution.py:58
  70.8 1.3 %collective-permute-start.4 = (bf16[16,1,128]{2,1,0:T(2,128)(2,1)S(1)}, bf16[16,1,128]{2,1,0:T(2,128)(2,1)S(1)}, u32[]{:S(2)}, u32[]{:S(2)}) collective-permute-start(bf16[16,1,128]{2,1,0:T(2,128)(2,1)S(1)} %get-tuple-element.31), channel_id=1, source_target_pairs={{1,0},{2,1},{3,2},{5,4},{6,5},{7,6},{9,8},{10,9},{11,10},{13,12},{... | collective-permute-start | bytes 12296 | tf_op jit(solution)/shard_map/ppermute | solution.py:58
  72.1 0.8 slice_bitcast_fusion.3
  72.9 4.4 %shard_map.79 = bf16[1024,128]{1,0:T(8,128)(2,1)} custom-call(bf16[4,10,2,128,128]{4,3,2,1,0:T(8,128)(2,1)} %bitcast.34, s32[1,1024]{1,0:T(1,128)} %reshape.74.row_leaf_ref, bf16[256,1024]{1,0:T(8,128)(2,1)} %bitcast.40), custom_call_target="tpu_custom_call" | custom-call | tf_op jit(solution)/shard_map/pallas_call | solution.py:236
  77.3 7.7 %all-to-all-start.1 = ((bf16[16,64,128]{2,1,0:T(8,128)(2,1)}), bf16[16,64,128]{2,1,0:T(8,128)(2,1)S(1)}, u32[]{:S(2)}, u32[]{:S(2)}) async-start(bf16[16,64,128]{2,1,0:T(8,128)(2,1)} %bitcast.43), calls=%async_computation.1 | async-start | bytes 524288 | tf_op jit(solution)/shard_map/all_to_all | solution.py:316
  85.0 3.8 %collective-permute-start.5 = (bf16[1,128,128]{2,1,0:T(8,128)(2,1)S(1)}, bf16[1,128,128]{2,1,0:T(8,128)(2,1)S(1)}, u32[]{:S(2)}, u32[]{:S(2)}) collective-permute-start(bf16[1,128,128]{2,1,0:T(8,128)(2,1)S(1)} %get-tuple-element.28), channel_id=1, source_target_pairs={{0,4},{1,5},{2,6},{3,7},{4,8},{5,9},{6,10},{7,11},{8,12},{9,13},{1... | collective-permute-start | bytes 98312 | tf_op jit(solution)/shard_map/ppermute | solution.py:58
  88.8 1.3 %collective-permute-start.6 = (bf16[1,128,128]{2,1,0:T(8,128)(2,1)S(1)}, bf16[1,128,128]{2,1,0:T(8,128)(2,1)S(1)}, u32[]{:S(2)}, u32[]{:S(2)}) collective-permute-start(bf16[1,128,128]{2,1,0:T(8,128)(2,1)S(1)} %get-tuple-element.29), channel_id=1, source_target_pairs={{4,0},{5,1},{6,2},{7,3},{8,4},{9,5},{10,6},{11,7},{12,8},{13,9},{1... | collective-permute-start | bytes 98312 | tf_op jit(solution)/shard_map/ppermute | solution.py:58
  90.1 0.0 collective-permute-done.3
  90.1 0.0 collective-permute-done.4
  90.1 0.1 maximum_convert_fusion.1
  90.3 0.7 collective-permute-done.5
  91.0 3.7 %collective-permute-done.6 = bf16[1,128,128]{2,1,0:T(8,128)(2,1)S(1)} collective-permute-done((bf16[1,128,128]{2,1,0:T(8,128)(2,1)S(1)}, bf16[1,128,128]{2,1,0:T(8,128)(2,1)S(1)}, u32[]{:S(2)}, u32[]{:S(2)}) %collective-permute-start.6) | collective-permute-done | bytes 32800 | tf_op jit(solution)/shard_map/ppermute | solution.py:58
  94.7 0.1 maximum_convert_fusion
  94.8 0.2 fusion.11
  95.0 1.4 %copy.37 = f32[128,16,128]{2,1,0:T(8,128)} copy(f32[128,16,128]{0,2,1:T(8,128)S(1)} %fusion.11) | data formatting | bytes 2097152
  96.4 0.0 all-to-all-done.1
  96.4 1.4 %fusion.9 = bf16[512,128]{1,0:T(8,128)(2,1)} fusion(bf16[1024,128]{1,0:T(8,128)(2,1)S(1)} %bitcast.46, s32[512]{0:T(512)S(1)} %multiply_add_fusion), kind=kOutput, calls=%fused_computation.18 | convolution fusion | flops 134807552 | bytes 395264 | tf_op jit(solution)/shard_map/dot_general | solution.py:319
  (4 shorter events, 0.0 us)
Async XLA Ops:
  0.6 12.7 %copy-start = (f32[128,16,256]{2,1,0:T(8,128)S(1)}, f32[128,16,256]{2,1,0:T(8,128)}, u32[]{:S(2)}) copy-start(f32[128,16,256]{2,1,0:T(8,128)} %param.6) | copy-start | bytes 6291460
  5.9 27.8 %all-to-all-start = ((bf16[16,65,384]{2,1,0:T(8,128)(2,1)}), bf16[16,65,384]{2,1,0:T(8,128)(2,1)}, u32[]{:S(2)}, u32[]{:S(2)}) async-start(bf16[16,65,384]{2,1,0:T(8,128)(2,1)} %fusion.16), calls=%async_computation | async-start | bytes 1769472 | tf_op jit(solution)/shard_map/all_to_all | solution.py:290
  14.2 5.4 %collective-permute-start = (f32[16,17,128]{2,1,0:T(8,128)S(1)}, f32[16,17,128]{2,1,0:T(8,128)S(1)}, u32[]{:S(2)}, u32[]{:S(2)}) collective-permute-start(f32[16,17,128]{2,1,0:T(8,128)S(1)} %bitcast.48), channel_id=1, source_target_pairs={{1,2},{2,1},{5,6},{6,5},{9,10},{10,9},{13,14},{14,13},{17,18},{18,... | collective-permute-start | bytes 417800 | tf_op jit(solution)/shard_map/ppermute | solution.py:58
  19.6 0.7 copy-start.1
  22.2 7.3 %copy-start.2 = (s32[2,8,8]{2,1,0:T(8,128)S(1)}, s32[2,8,8]{2,1,0:T(8,128)}, u32[]{:S(2)}) copy-start(s32[2,8,8]{2,1,0:T(8,128)} %param.8) | copy-start | bytes 1540
  23.4 21.3 %collective-permute-start.1 = (f32[9,162,128]{2,1,0:T(8,128)}, f32[9,162,128]{2,1,0:T(8,128)}, u32[]{:S(2)}, u32[]{:S(2)}) collective-permute-start(f32[9,162,128]{2,1,0:T(8,128)} %get-tuple-element.25), channel_id=1, source_target_pairs={{0,4},{1,5},{2,6},{3,7},{4,8},{5,9},{6,10},{7,11},{8,12},{9,13},{1... | collective-permute-start | bytes 2239496 | tf_op jit(solution)/shard_map/ppermute | solution.py:58
  28.1 19.3 %collective-permute-start.2 = (f32[9,162,128]{2,1,0:T(8,128)}, f32[9,162,128]{2,1,0:T(8,128)}, u32[]{:S(2)}, u32[]{:S(2)}) collective-permute-start(f32[9,162,128]{2,1,0:T(8,128)} %get-tuple-element.24), channel_id=1, source_target_pairs={{4,0},{5,1},{6,2},{7,3},{8,4},{9,5},{10,6},{11,7},{12,8},{13,9},{1... | collective-permute-start | bytes 2239496 | tf_op jit(solution)/shard_map/ppermute | solution.py:58
  65.6 24.5 %collective-permute-start.3 = (bf16[16,1,128]{2,1,0:T(2,128)(2,1)S(1)}, bf16[16,1,128]{2,1,0:T(2,128)(2,1)S(1)}, u32[]{:S(2)}, u32[]{:S(2)}) collective-permute-start(bf16[16,1,128]{2,1,0:T(2,128)(2,1)S(1)} %get-tuple-element.30), channel_id=1, source_target_pairs={{0,1},{1,2},{2,3},{4,5},{5,6},{6,7},{8,9},{9,10},{10,11},{12,13},{... | collective-permute-start | bytes 12296 | tf_op jit(solution)/shard_map/ppermute | solution.py:58
  70.8 19.3 %collective-permute-start.4 = (bf16[16,1,128]{2,1,0:T(2,128)(2,1)S(1)}, bf16[16,1,128]{2,1,0:T(2,128)(2,1)S(1)}, u32[]{:S(2)}, u32[]{:S(2)}) collective-permute-start(bf16[16,1,128]{2,1,0:T(2,128)(2,1)S(1)} %get-tuple-element.31), channel_id=1, source_target_pairs={{1,0},{2,1},{3,2},{5,4},{6,5},{7,6},{9,8},{10,9},{11,10},{13,12},{... | collective-permute-start | bytes 12296 | tf_op jit(solution)/shard_map/ppermute | solution.py:58
  77.3 19.0 %all-to-all-start.1 = ((bf16[16,64,128]{2,1,0:T(8,128)(2,1)}), bf16[16,64,128]{2,1,0:T(8,128)(2,1)S(1)}, u32[]{:S(2)}, u32[]{:S(2)}) async-start(bf16[16,64,128]{2,1,0:T(8,128)(2,1)} %bitcast.43), calls=%async_computation.1 | async-start | bytes 524288 | tf_op jit(solution)/shard_map/all_to_all | solution.py:316
  85.0 6.0 %collective-permute-start.5 = (bf16[1,128,128]{2,1,0:T(8,128)(2,1)S(1)}, bf16[1,128,128]{2,1,0:T(8,128)(2,1)S(1)}, u32[]{:S(2)}, u32[]{:S(2)}) collective-permute-start(bf16[1,128,128]{2,1,0:T(8,128)(2,1)S(1)} %get-tuple-element.28), channel_id=1, source_target_pairs={{0,4},{1,5},{2,6},{3,7},{4,8},{5,9},{6,10},{7,11},{8,12},{9,13},{1... | collective-permute-start | bytes 98312 | tf_op jit(solution)/shard_map/ppermute | solution.py:58
  88.8 5.9 %collective-permute-start.6 = (bf16[1,128,128]{2,1,0:T(8,128)(2,1)S(1)}, bf16[1,128,128]{2,1,0:T(8,128)(2,1)S(1)}, u32[]{:S(2)}, u32[]{:S(2)}) collective-permute-start(bf16[1,128,128]{2,1,0:T(8,128)(2,1)S(1)} %get-tuple-element.29), channel_id=1, source_target_pairs={{4,0},{5,1},{6,2},{7,3},{8,4},{9,5},{10,6},{11,7},{12,8},{13,9},{1... | collective-permute-start | bytes 98312 | tf_op jit(solution)/shard_map/ppermute | solution.py:58

commit v19 on v17

--- a/solution.py
+++ b/solution.py
@@ -180,7 +180,7 @@
             )
         return carry
 
-    lax.fori_loop(0, leaf_count, one_leaf, 0)
+    lax.fori_loop(0, leaf_count, one_leaf, 0, unroll=2)
 
 
 def induced_kernel(bord_hbm, row_leaf_ref, cpl_t_ref, volt_ref, own_ref, stack_ref, sems):

time: 98.8 us -> 98.6 us (level)
  no operation moved by 1% of the time
where the time goes in v19:
time: 98.6 us; the launch traced here: 97.7 us
  starting transfers between devices  33.2 us (34%)
  Pallas kernels  23.5 us (24%)
  local copies, waits for them, and re-layouts  19.7 us (20%)
  waiting for transfers between devices  8.45 us (9%)
  other arithmetic  8.33 us (8%)
  matrix products  3.5 us (4%)
    ppermute x7, starting transfers between devices, send(): return lax.ppermute(value, AXES, pairs_by(fn))  18.2 us
    pallas_call x1, Pallas kernels, leaf_fields(): pl.pallas_call(leaf_kernel, in_specs=[smem, smem, hbm, hbm, hbm], out_spe...  12.1 us
    unnamed x11, local copies, waits for them, and re-layouts  8.34 us
    all_to_all x1, starting transfers between devices, body(): lax.all_to_all(induced.reshape(owners, capacity, port_count), AXES, split...  7.69 us
    all_to_all x1, starting transfers between devices, body(): got = lax.all_to_all(payload, AXES, split_axis=0, concat_axis=0, tiled=True)  7.4 us
    pallas_call x1, Pallas kernels, filament_field(): pl.pallas_call(filament_kernel, in_specs=[vmem, vmem, vmem], out_specs=vm...  7.02 us
    ppermute x7, waiting for transfers between devices, send(): return lax.ppermute(value, AXES, pairs_by(fn))  4.8 us
    pallas_call x1, Pallas kernels, leaf_fields(): pl.pallas_call(induced_kernel, in_specs=[hbm, vmem, vmem], out_specs=vmem...  4.42 us
  transfers between devices with their start and end apart: 9, of which 4 were waited for; matrix products, arithmetic and copies ran while one was open for 19% of the time, Pallas kernels for 12%

profile of v19, /device:TPU:0, one launch (start us, length us, event | category | flops | bytes accessed | tf_op | source)
XLA Modules:
  0.0 97.7 jit_solution(17057301676486103622)
XLA Ops:
  0.6 0.0 copy-start
  0.6 0.9 fusion.25
  1.5 0.2 convert_reduce_fusion
  1.8 0.5 fusion.3
  2.2 0.1 reshape.77
  2.3 1.0 %copy.46 = bf16[64,8,2,128]{3,1,2,0:T(8,128)(2,1)S(1)} copy(bf16[64,8,2,128]{3,2,1,0:T(2,128)(2,1)} %bitcast.45) | data formatting | bytes 524288
  3.3 1.6 %fusion.6 = bf16[1024,384]{1,0:T(8,128)(2,1)S(1)} fusion(s32[512]{0:T(512)S(1)} %multiply_add_fusion, bf16[512,128]{1,0:T(8,128)(2,1)} %param.10, bf16[512,256]{1,0:T(8,128)(2,1)S(1)} %bitcast.47), kind=kOutput, calls=%fused_computation.15 | convolution fusion | flops 404357120 | bytes 1181696 | tf_op jit(solution)/shard_map/dot_general | solution.py:279
  4.9 1.0 %fusion.16 = bf16[16,65,384]{2,1,0:T(8,128)(2,1)} fusion(bf16[16,1,64]{2,1,0:T(2,128)(2,1)S(1)} %reshape.77, bf16[16,64,384]{2,1,0:T(8,128)(2,1)S(1)} %bitcast.44), kind=kLoop, calls=%fused_computation.29 | loop fusion | flops 2396160 | bytes 1587200 | tf_op jit(solution)/shard_map/concatenate | solution.py:287
  5.9 7.4 %all-to-all-start = ((bf16[16,65,384]{2,1,0:T(8,128)(2,1)}), bf16[16,65,384]{2,1,0:T(8,128)(2,1)}, u32[]{:S(2)}, u32[]{:S(2)}) async-start(bf16[16,65,384]{2,1,0:T(8,128)(2,1)} %fusion.16), calls=%async_computation | async-start | bytes 1769472 | tf_op jit(solution)/shard_map/all_to_all | solution.py:288
  13.3 0.0 copy-done
  13.4 0.3 constant_dynamic-slice_fusion.1
  13.7 0.4 copy.40
  14.2 0.7 collective-permute-start
  14.8 2.0 %constant_dynamic-slice_fusion = f32[128,16,145]{2,1,0:T(8,128)} fusion(f32[128,16,256]{2,1,0:T(8,128)S(1)} %copy-done, s32[]{:T(128)S(6)} %select_n.49), kind=kLoop, calls=%fused_computation.78 | loop fusion | bytes 2375684 | tf_op jit(solution)/shard_map/dynamic-slice.1
  16.8 2.8 %copy.41 = f32[128,16,145]{0,2,1:T(8,128)} copy(f32[128,16,145]{2,1,0:T(8,128)} %constant_dynamic-slice_fusion) | data formatting | bytes 2375680
  19.6 0.0 collective-permute-done
  19.6 0.0 copy-start.1
  19.6 0.7 copy-done.1
  20.2 1.9 %fusion.8 = f32[16,162,128]{2,1,0:T(8,128)S(1)} fusion(s32[]{:T(128)S(6)} %select_n.50, f32[16,17,128]{2,1,0:T(8,128)} %copy-done.1, f32[16,145,128]{2,1,0:T(8,128)} %bitcast.38), kind=kLoop, calls=%fused_computation.17 | loop fusion | flops 663552 | bytes 2654212 | tf_op jit(solution)/shard_map/concatenate | solution.py:79
  22.2 0.0 copy-start.2
  22.2 1.3 %fusion.34 = (f32[9,162,128]{2,1,0:T(8,128)}, f32[9,162,128]{2,1,0:T(8,128)}) fusion(f32[16,162,128]{2,1,0:T(8,128)S(1)} %fusion.8), kind=kLoop, calls=%fused_computation.84 | loop fusion | bytes 2985984 | tf_op jit(solution)/shard_map/slice | solution.py:82
  23.4 4.7 %collective-permute-start.1 = (f32[9,162,128]{2,1,0:T(8,128)}, f32[9,162,128]{2,1,0:T(8,128)}, u32[]{:S(2)}, u32[]{:S(2)}) collective-permute-start(f32[9,162,128]{2,1,0:T(8,128)} %get-tuple-element.25), channel_id=1, source_target_pairs={{0,4},{1,5},{2,6},{3,7},{4,8},{5,9},{6,10},{7,11},{8,12},{9,13},{1... | collective-permute-start | bytes 2239496 | tf_op jit(solution)/shard_map/ppermute | solution.py:58
  28.1 1.3 %collective-permute-start.2 = (f32[9,162,128]{2,1,0:T(8,128)}, f32[9,162,128]{2,1,0:T(8,128)}, u32[]{:S(2)}, u32[]{:S(2)}) collective-permute-start(f32[9,162,128]{2,1,0:T(8,128)} %get-tuple-element.24), channel_id=1, source_target_pairs={{4,0},{5,1},{6,2},{7,3},{8,4},{9,5},{10,6},{11,7},{12,8},{13,9},{1... | collective-permute-start | bytes 2239496 | tf_op jit(solution)/shard_map/ppermute | solution.py:58
  29.4 0.0 copy-done.2
  29.4 0.6 convert_bitcast_fusion.scale_ref
  30.0 3.7 %all-to-all-done = bf16[16,65,384]{2,1,0:T(8,128)(2,1)} async-done(((bf16[16,65,384]{2,1,0:T(8,128)(2,1)}), bf16[16,65,384]{2,1,0:T(8,128)(2,1)}, u32[]{:S(2)}, u32[]{:S(2)}) %all-to-all-start) | async-done | bytes 798752 | tf_op jit(solution)/shard_map/all_to_all | solution.py:288
  33.7 1.2 %slice.93 = bf16[16,64,384]{2,1,0:T(8,128)(2,1)S(1)} slice(bf16[16,65,384]{2,1,0:T(8,128)(2,1)} %all-to-all-done), slice={[0:16], [0:64], [0:384]} | slice | bytes 1572864 | tf_op jit(solution)/shard_map/slice | solution.py:289
  34.9 0.8 slice.94
  35.7 0.7 slice.95.cur_ref
  36.5 2.0 %copy.42 = bf16[1024,256]{0,1:T(8,128)(2,1)} copy(bf16[1024,256]{1,0:T(8,128)(2,1)} %slice.94) | data formatting | bytes 1048576
  38.5 0.8 fusion.22
  39.3 0.7 reshape.74.row_leaf_ref
  40.0 7.0 %shard_map.77.fil_hbm = f32[16,256,128]{2,1,0:T(8,128)} custom-call(s32[1,1024]{1,0:T(1,128)} %reshape.74.row_leaf_ref, bf16[256,1024]{1,0:T(8,128)(2,1)} %bitcast.39, bf16[1024,128]{1,0:T(8,128)(2,1)} %slice.95.cur_ref), custom_call_target="tpu_custom_call" | custom-call | tf_op jit(solution)/shard_map/pallas_call | solution.py:119
  47.0 0.0 collective-permute-done.1
  47.0 0.4 collective-permute-done.2
  47.4 1.6 %pad_maximum_fusion = f32[34,162,128]{2,1,0:T(8,128)S(1)} fusion(f32[9,162,128]{2,1,0:T(8,128)} %collective-permute-done.2, f32[16,162,128]{2,1,0:T(8,128)S(1)} %fusion.8, f32[9,162,128]{2,1,0:T(8,128)} %collective-permute-done.1), kind=kLoop, calls=%fused_computation | loop fusion | flops 1410048 | bytes 5640192 | tf_op jit(solution)/shard_map/concatenate | solution.py:84
  48.9 0.7 fusion.1
  49.6 0.2 maximum_bitcast_fusion
  49.9 2.3 %copy.34 = bf16[4,10,2,8,16,128]{5,4,3,2,1,0:T(8,128)(2,1)} copy(bf16[4,10,2,8,16,128]{5,4,1,3,0,2:T(8,128)(2,1)S(1)} %maximum_bitcast_fusion) | data formatting | bytes 5242880 | tf_op jit(solution)/shard_map/transpose | solution.py:24
  52.1 12.1 %shard_map.78 = bf16[2,16,128,128]{3,2,1,0:T(8,128)(2,1)} custom-call(s32[16,8]{1,0:T(8,128)} %bitcast.49, s32[16,8]{1,0:T(8,128)} %convert_bitcast_fusion.scale_ref, bf16[4,10,2,128,128]{4,3,2,1,0:T(8,128)(2,1)} %bitcast.33, bf16[16,8,2,128,128]{4,3,2,1,0:T(8,128)(2,1)} %bitcast.35, f32[16,256,128]{2,1,0:T(8,128)} %shard_map.77.fil_hbm), custom_call_target="tpu_custom_call" | custom-call | tf_op jit(solution)/shard_map/pallas_call | solution.py:217
  64.2 1.3 %slice_bitcast_fusion.1 = (bf16[16,128,128]{2,1,0:T(8,128)(2,1)S(1)}, bf16[16,128,128]{2,1,0:T(8,128)(2,1)S(1)}) fusion(bf16[2,16,128,128]{3,2,1,0:T(8,128)(2,1)} %shard_map.78), kind=kLoop, calls=%fused_computation.33 | loop fusion | bytes 2097152 | tf_op jit(solution)/shard_map/squeeze | solution.py:88
  65.5 5.1 %collective-permute-start.3 = (bf16[16,1,128]{2,1,0:T(2,128)(2,1)S(1)}, bf16[16,1,128]{2,1,0:T(2,128)(2,1)S(1)}, u32[]{:S(2)}, u32[]{:S(2)}) collective-permute-start(bf16[16,1,128]{2,1,0:T(2,128)(2,1)S(1)} %get-tuple-element.30), channel_id=1, source_target_pairs={{0,1},{1,2},{2,3},{4,5},{5,6},{6,7},{8,9},{9,10},{10,11},{12,13},{... | collective-permute-start | bytes 12296 | tf_op jit(solution)/shard_map/ppermute | solution.py:58
  70.6 1.3 %collective-permute-start.4 = (bf16[16,1,128]{2,1,0:T(2,128)(2,1)S(1)}, bf16[16,1,128]{2,1,0:T(2,128)(2,1)S(1)}, u32[]{:S(2)}, u32[]{:S(2)}) collective-permute-start(bf16[16,1,128]{2,1,0:T(2,128)(2,1)S(1)} %get-tuple-element.31), channel_id=1, source_target_pairs={{1,0},{2,1},{3,2},{5,4},{6,5},{7,6},{9,8},{10,9},{11,10},{13,12},{... | collective-permute-start | bytes 12296 | tf_op jit(solution)/shard_map/ppermute | solution.py:58
  71.9 0.8 slice_bitcast_fusion.3
  72.7 4.4 %shard_map.79 = bf16[1024,128]{1,0:T(8,128)(2,1)} custom-call(bf16[4,10,2,128,128]{4,3,2,1,0:T(8,128)(2,1)} %bitcast.34, s32[1,1024]{1,0:T(1,128)} %reshape.74.row_leaf_ref, bf16[256,1024]{1,0:T(8,128)(2,1)} %bitcast.40), custom_call_target="tpu_custom_call" | custom-call | tf_op jit(solution)/shard_map/pallas_call | solution.py:234
  77.2 7.7 %all-to-all-start.1 = ((bf16[16,64,128]{2,1,0:T(8,128)(2,1)}), bf16[16,64,128]{2,1,0:T(8,128)(2,1)S(1)}, u32[]{:S(2)}, u32[]{:S(2)}) async-start(bf16[16,64,128]{2,1,0:T(8,128)(2,1)} %bitcast.43), calls=%async_computation.1 | async-start | bytes 524288 | tf_op jit(solution)/shard_map/all_to_all | solution.py:314
  84.9 3.8 %collective-permute-start.5 = (bf16[1,128,128]{2,1,0:T(8,128)(2,1)S(1)}, bf16[1,128,128]{2,1,0:T(8,128)(2,1)S(1)}, u32[]{:S(2)}, u32[]{:S(2)}) collective-permute-start(bf16[1,128,128]{2,1,0:T(8,128)(2,1)S(1)} %get-tuple-element.28), channel_id=1, source_target_pairs={{0,4},{1,5},{2,6},{3,7},{4,8},{5,9},{6,10},{7,11},{8,12},{9,13},{1... | collective-permute-start | bytes 98312 | tf_op jit(solution)/shard_map/ppermute | solution.py:58
  88.7 1.3 %collective-permute-start.6 = (bf16[1,128,128]{2,1,0:T(8,128)(2,1)S(1)}, bf16[1,128,128]{2,1,0:T(8,128)(2,1)S(1)}, u32[]{:S(2)}, u32[]{:S(2)}) collective-permute-start(bf16[1,128,128]{2,1,0:T(8,128)(2,1)S(1)} %get-tuple-element.29), channel_id=1, source_target_pairs={{4,0},{5,1},{6,2},{7,3},{8,4},{9,5},{10,6},{11,7},{12,8},{13,9},{1... | collective-permute-start | bytes 98312 | tf_op jit(solution)/shard_map/ppermute | solution.py:58
  90.0 0.0 collective-permute-done.3
  90.0 0.0 collective-permute-done.4
  90.0 0.1 maximum_convert_fusion.1
  90.1 0.7 collective-permute-done.5
  90.8 3.7 %collective-permute-done.6 = bf16[1,128,128]{2,1,0:T(8,128)(2,1)S(1)} collective-permute-done((bf16[1,128,128]{2,1,0:T(8,128)(2,1)S(1)}, bf16[1,128,128]{2,1,0:T(8,128)(2,1)S(1)}, u32[]{:S(2)}, u32[]{:S(2)}) %collective-permute-start.6) | collective-permute-done | bytes 32800 | tf_op jit(solution)/shard_map/ppermute | solution.py:58
  94.6 0.1 maximum_convert_fusion
  94.7 0.2 fusion.11
  94.8 1.4 %copy.37 = f32[128,16,128]{2,1,0:T(8,128)} copy(f32[128,16,128]{0,2,1:T(8,128)S(1)} %fusion.11) | data formatting | bytes 2097152
  96.2 0.0 all-to-all-done.1
  96.2 1.4 %fusion.9 = bf16[512,128]{1,0:T(8,128)(2,1)} fusion(bf16[1024,128]{1,0:T(8,128)(2,1)S(1)} %bitcast.46, s32[512]{0:T(512)S(1)} %multiply_add_fusion), kind=kOutput, calls=%fused_computation.18 | convolution fusion | flops 134807552 | bytes 395264 | tf_op jit(solution)/shard_map/dot_general | solution.py:317
  (4 shorter events, 0.0 us)
Async XLA Ops:
  0.6 12.7 %copy-start = (f32[128,16,256]{2,1,0:T(8,128)S(1)}, f32[128,16,256]{2,1,0:T(8,128)}, u32[]{:S(2)}) copy-start(f32[128,16,256]{2,1,0:T(8,128)} %param.6) | copy-start | bytes 6291460
  5.9 27.8 %all-to-all-start = ((bf16[16,65,384]{2,1,0:T(8,128)(2,1)}), bf16[16,65,384]{2,1,0:T(8,128)(2,1)}, u32[]{:S(2)}, u32[]{:S(2)}) async-start(bf16[16,65,384]{2,1,0:T(8,128)(2,1)} %fusion.16), calls=%async_computation | async-start | bytes 1769472 | tf_op jit(solution)/shard_map/all_to_all | solution.py:288
  14.2 5.4 %collective-permute-start = (f32[16,17,128]{2,1,0:T(8,128)S(1)}, f32[16,17,128]{2,1,0:T(8,128)S(1)}, u32[]{:S(2)}, u32[]{:S(2)}) collective-permute-start(f32[16,17,128]{2,1,0:T(8,128)S(1)} %bitcast.48), channel_id=1, source_target_pairs={{1,2},{2,1},{5,6},{6,5},{9,10},{10,9},{13,14},{14,13},{17,18},{18,... | collective-permute-start | bytes 417800 | tf_op jit(solution)/shard_map/ppermute | solution.py:58
  19.6 0.7 copy-start.1
  22.2 7.3 %copy-start.2 = (s32[2,8,8]{2,1,0:T(8,128)S(1)}, s32[2,8,8]{2,1,0:T(8,128)}, u32[]{:S(2)}) copy-start(s32[2,8,8]{2,1,0:T(8,128)} %param.8) | copy-start | bytes 1540
  23.4 23.6 %collective-permute-start.1 = (f32[9,162,128]{2,1,0:T(8,128)}, f32[9,162,128]{2,1,0:T(8,128)}, u32[]{:S(2)}, u32[]{:S(2)}) collective-permute-start(f32[9,162,128]{2,1,0:T(8,128)} %get-tuple-element.25), channel_id=1, source_target_pairs={{0,4},{1,5},{2,6},{3,7},{4,8},{5,9},{6,10},{7,11},{8,12},{9,13},{1... | collective-permute-start | bytes 2239496 | tf_op jit(solution)/shard_map/ppermute | solution.py:58
  28.1 19.3 %collective-permute-start.2 = (f32[9,162,128]{2,1,0:T(8,128)}, f32[9,162,128]{2,1,0:T(8,128)}, u32[]{:S(2)}, u32[]{:S(2)}) collective-permute-start(f32[9,162,128]{2,1,0:T(8,128)} %get-tuple-element.24), channel_id=1, source_target_pairs={{4,0},{5,1},{6,2},{7,3},{8,4},{9,5},{10,6},{11,7},{12,8},{13,9},{1... | collective-permute-start | bytes 2239496 | tf_op jit(solution)/shard_map/ppermute | solution.py:58
  65.5 24.5 %collective-permute-start.3 = (bf16[16,1,128]{2,1,0:T(2,128)(2,1)S(1)}, bf16[16,1,128]{2,1,0:T(2,128)(2,1)S(1)}, u32[]{:S(2)}, u32[]{:S(2)}) collective-permute-start(bf16[16,1,128]{2,1,0:T(2,128)(2,1)S(1)} %get-tuple-element.30), channel_id=1, source_target_pairs={{0,1},{1,2},{2,3},{4,5},{5,6},{6,7},{8,9},{9,10},{10,11},{12,13},{... | collective-permute-start | bytes 12296 | tf_op jit(solution)/shard_map/ppermute | solution.py:58
  70.6 19.4 %collective-permute-start.4 = (bf16[16,1,128]{2,1,0:T(2,128)(2,1)S(1)}, bf16[16,1,128]{2,1,0:T(2,128)(2,1)S(1)}, u32[]{:S(2)}, u32[]{:S(2)}) collective-permute-start(bf16[16,1,128]{2,1,0:T(2,128)(2,1)S(1)} %get-tuple-element.31), channel_id=1, source_target_pairs={{1,0},{2,1},{3,2},{5,4},{6,5},{7,6},{9,8},{10,9},{11,10},{13,12},{... | collective-permute-start | bytes 12296 | tf_op jit(solution)/shard_map/ppermute | solution.py:58
  77.2 19.1 %all-to-all-start.1 = ((bf16[16,64,128]{2,1,0:T(8,128)(2,1)}), bf16[16,64,128]{2,1,0:T(8,128)(2,1)S(1)}, u32[]{:S(2)}, u32[]{:S(2)}) async-start(bf16[16,64,128]{2,1,0:T(8,128)(2,1)} %bitcast.43), calls=%async_computation.1 | async-start | bytes 524288 | tf_op jit(solution)/shard_map/all_to_all | solution.py:314
  84.9 6.0 %collective-permute-start.5 = (bf16[1,128,128]{2,1,0:T(8,128)(2,1)S(1)}, bf16[1,128,128]{2,1,0:T(8,128)(2,1)S(1)}, u32[]{:S(2)}, u32[]{:S(2)}) collective-permute-start(bf16[1,128,128]{2,1,0:T(8,128)(2,1)S(1)} %get-tuple-element.28), channel_id=1, source_target_pairs={{0,4},{1,5},{2,6},{3,7},{4,8},{5,9},{6,10},{7,11},{8,12},{9,13},{1... | collective-permute-start | bytes 98312 | tf_op jit(solution)/shard_map/ppermute | solution.py:58
  88.7 5.9 %collective-permute-start.6 = (bf16[1,128,128]{2,1,0:T(8,128)(2,1)S(1)}, bf16[1,128,128]{2,1,0:T(8,128)(2,1)S(1)}, u32[]{:S(2)}, u32[]{:S(2)}) collective-permute-start(bf16[1,128,128]{2,1,0:T(8,128)(2,1)S(1)} %get-tuple-element.29), channel_id=1, source_target_pairs={{4,0},{5,1},{6,2},{7,3},{8,4},{9,5},{10,6},{11,7},{12,8},{13,9},{1... | collective-permute-start | bytes 98312 | tf_op jit(solution)/shard_map/ppermute | solution.py:58

commit v20 on v19

--- a/solution.py
+++ b/solution.py
@@ -84,21 +84,20 @@
     return jnp.concatenate([v_top, wide, v_bot], 0), ready
 
 
-def field_halo(grid_field):
+def field_halo(grid_field, edges):
     x_field = grid_field[0]
     y_field = grid_field[1]
-    rows = y_field.shape[0]
-    cols = x_field.shape[1]
+    x_first, x_last, y_first, y_last = edges
 
     def step(x, y, z, dc):
         nz = lax.axis_size("gz")
         c = y * nz + z + dc
         return (x, c // nz, c % nz) if c >= 0 else None
 
-    x_left = send(x_field[:, cols - 1 :], lambda x, y, z: step(x, y, z, 1))
-    x_right = send(x_field[:, :1], lambda x, y, z: step(x, y, z, -1))
-    y_top = send(y_field[rows - 1 :], lambda x, y, z: (x + 1, y, z))
-    y_bot = send(y_field[:1], lambda x, y, z: (x - 1, y, z))
+    x_left = send(x_last, lambda x, y, z: step(x, y, z, 1))
+    x_right = send(x_first, lambda x, y, z: step(x, y, z, -1))
+    y_top = send(y_last, lambda x, y, z: (x + 1, y, z))
+    y_bot = send(y_first, lambda x, y, z: (x - 1, y, z))
     x_pad = jnp.concatenate([x_left, x_field, x_right], 1).astype(jnp.float32)
     y_pad = jnp.concatenate([y_top, y_field, y_bot], 0).astype(jnp.float32)
     return x_pad[:, :-2] - x_pad[:, 2:] + (y_pad[2:] - y_pad[:-2])
@@ -128,7 +127,8 @@
 
 def leaf_kernel(
     codes_ref, scale_ref, bord_hbm, ind_hbm, fil_hbm,
-    field_ref, bord_ref, ind_ref, fil_ref, sems, fil_sems, ind_sems,
+    field_ref, x_first_ref, x_last_ref, y_first_ref, y_last_ref,
+    bord_ref, ind_ref, fil_ref, sems, fil_sems, ind_sems,
 ):
     leaf_count = ind_ref.shape[0]
     leaf_cols = bord_ref.shape[1] - 2
@@ -181,6 +181,11 @@
         return carry
 
     lax.fori_loop(0, leaf_count, one_leaf, 0, unroll=2)
+    rows, cols = field_ref.shape[1], field_ref.shape[2]
+    x_first_ref[...] = field_ref[0, :, 0:1]
+    x_last_ref[...] = field_ref[0, :, cols - 1 : cols]
+    y_first_ref[...] = field_ref[1, 0:1]
+    y_last_ref[...] = field_ref[1, rows - 1 : rows]
 
 
 def induced_kernel(bord_hbm, row_leaf_ref, cpl_t_ref, volt_ref, own_ref, stack_ref, sems):
@@ -214,13 +219,18 @@
     smem = pl.BlockSpec(memory_space=pltpu.SMEM)
     hbm = pl.BlockSpec(memory_space=pl.ANY)
     vmem = pl.BlockSpec(memory_space=pltpu.VMEM)
-    field = pl.pallas_call(
+    rows, cols = leaf_rows * LEAF_R, leaf_cols * LEAF_C
+    field, *edges = pl.pallas_call(
         leaf_kernel,
         in_specs=[smem, smem, hbm, hbm, hbm],
-        out_specs=vmem,
-        out_shape=jax.ShapeDtypeStruct(
-            (components, leaf_rows * LEAF_R, leaf_cols * LEAF_C, port_count), jnp.bfloat16
-        ),
+        out_specs=[vmem] * 5,
+        out_shape=[
+            jax.ShapeDtypeStruct((components, rows, cols, port_count), jnp.bfloat16),
+            jax.ShapeDtypeStruct((rows, 1, port_count), jnp.bfloat16),
+            jax.ShapeDtypeStruct((rows, 1, port_count), jnp.bfloat16),
+            jax.ShapeDtypeStruct((1, cols, port_count), jnp.bfloat16),
+            jax.ShapeDtypeStruct((1, cols, port_count), jnp.bfloat16),
+        ],
         scratch_shapes=[
             pltpu.VMEM(bordered.shape, bordered.dtype),
             pltpu.VMEM(kernels.shape, kernels.dtype),
@@ -230,7 +240,7 @@
             pltpu.SemaphoreType.DMA((leaf_count,)),
         ],
     )(codes, scales, bordered, kernels, filament)
-    field, bordered = lax.optimization_barrier((field, bordered))
+    field, edges, bordered = lax.optimization_barrier((field, edges, bordered))
     volt = pl.pallas_call(
         induced_kernel,
         in_specs=[hbm, vmem, vmem],
@@ -242,7 +252,7 @@
             pltpu.SemaphoreType.DMA((leaf_rows,)),
         ],
     )(bordered, row_leaf, coupling_t)
-    return field, volt
+    return (field, edges), volt
 
 
 def body(stream, inductance, near_lists, filament_leaf, filament_current, filament_coupling):
@@ -318,7 +328,7 @@
         placement, returned, (((0,), (0,)), ((), ())), preferred_element_type=jnp.float32
     ).astype(jnp.bfloat16)
 
-    loop_voltage = field_halo(total_field).transpose(2, 0, 1)
+    loop_voltage = field_halo(*total_field).transpose(2, 0, 1)
     return (loop_voltage, filament_voltage)
 
 

time: 98.6 us -> 95.3 us (0.967)
  starting transfers between devices: 33.2 us -> 31.1 us
  local copies, waits for them, and re-layouts: 19.7 us -> 17.8 us
    ppermute x7, starting transfers between devices: 18.2 us -> 15.1 us  [send(): return lax.ppermute(value, AXES, pairs_by(fn))]
    squeeze x1, local copies, waits for them, and re-layouts: 1.27 us -> 0.1 us  [field_halo(): x_field = grid_field[0]]
    unnamed x11 -> x21, local copies, waits for them, and re-layouts: 8.34 us -> 8.36 us
  transfers between devices with their start and end apart: 9 -> 9, of which waited for: 4 -> 4; matrix products, arithmetic and copies ran while one was open for 19% -> 19% of each run, Pallas kernels for 12% -> 8%
where the time goes in v20:
time: 95.3 us; the launch traced here: 93.6 us
  starting transfers between devices  31.1 us (33%)
  Pallas kernels  23.6 us (25%)
  local copies, waits for them, and re-layouts  17.8 us (19%)
  waiting for transfers between devices  8.37 us (9%)
  other arithmetic  8.32 us (9%)
  matrix products  3.5 us (4%)
  between operations  0.96 us (1%)
    ppermute x7, starting transfers between devices, send(): return lax.ppermute(value, AXES, pairs_by(fn))  15.1 us
    pallas_call x1, Pallas kernels, leaf_fields(): pl.pallas_call(leaf_kernel, in_specs=[smem, smem, hbm, hbm, hbm], out_spe...  12.1 us
    all_to_all x1, starting transfers between devices, body(): lax.all_to_all(induced.reshape(owners, capacity, port_count), AXES, split...  8.57 us
    unnamed x21, local copies, waits for them, and re-layouts  8.36 us
    all_to_all x1, starting transfers between devices, body(): got = lax.all_to_all(payload, AXES, split_axis=0, concat_axis=0, tiled=True)  7.4 us
    pallas_call x1, Pallas kernels, filament_field(): pl.pallas_call(filament_kernel, in_specs=[vmem, vmem, vmem], out_specs=vm...  7.02 us
    ppermute x7, waiting for transfers between devices, send(): return lax.ppermute(value, AXES, pairs_by(fn))  4.72 us
    pallas_call x1, Pallas kernels, leaf_fields(): pl.pallas_call(induced_kernel, in_specs=[hbm, vmem, vmem], out_specs=vmem...  4.52 us
  transfers between devices with their start and end apart: 9, of which 4 were waited for; matrix products, arithmetic and copies ran while one was open for 19% of the time, Pallas kernels for 8%

profile of v20, /device:TPU:0, one launch (start us, length us, event | category | flops | bytes accessed | tf_op | source)
XLA Modules:
  0.0 93.6 jit_solution(18174526348314054479)
XLA Ops:
  0.6 0.0 copy-start
  0.6 0.9 fusion.25
  1.5 0.2 convert_reduce_fusion
  1.8 0.5 fusion.3
  2.2 0.1 reshape.75
  2.3 1.0 %copy.46 = bf16[64,8,2,128]{3,1,2,0:T(8,128)(2,1)S(1)} copy(bf16[64,8,2,128]{3,2,1,0:T(2,128)(2,1)} %bitcast.41) | data formatting | bytes 524288
  3.3 1.6 %fusion.6 = bf16[1024,384]{1,0:T(8,128)(2,1)S(1)} fusion(s32[512]{0:T(512)S(1)} %multiply_add_fusion, bf16[512,128]{1,0:T(8,128)(2,1)} %param.10, bf16[512,256]{1,0:T(8,128)(2,1)S(1)} %bitcast.43), kind=kOutput, calls=%fused_computation.15 | convolution fusion | flops 404357120 | bytes 1181696 | tf_op jit(solution)/shard_map/dot_general | solution.py:289
  4.9 1.0 %fusion.16 = bf16[16,65,384]{2,1,0:T(8,128)(2,1)} fusion(bf16[16,1,64]{2,1,0:T(2,128)(2,1)S(1)} %reshape.75, bf16[16,64,384]{2,1,0:T(8,128)(2,1)S(1)} %bitcast.40), kind=kLoop, calls=%fused_computation.29 | loop fusion | flops 2396160 | bytes 1587200 | tf_op jit(solution)/shard_map/concatenate | solution.py:297
  5.9 7.4 %all-to-all-start = ((bf16[16,65,384]{2,1,0:T(8,128)(2,1)}), bf16[16,65,384]{2,1,0:T(8,128)(2,1)}, u32[]{:S(2)}, u32[]{:S(2)}) async-start(bf16[16,65,384]{2,1,0:T(8,128)(2,1)} %fusion.16), calls=%async_computation | async-start | bytes 1769472 | tf_op jit(solution)/shard_map/all_to_all | solution.py:298
  13.3 0.0 copy-done
  13.4 0.3 constant_dynamic-slice_fusion.1
  13.7 0.4 copy.40
  14.2 0.7 collective-permute-start
  14.8 2.0 %constant_dynamic-slice_fusion = f32[128,16,145]{2,1,0:T(8,128)} fusion(f32[128,16,256]{2,1,0:T(8,128)S(1)} %copy-done, s32[]{:T(128)S(6)} %select_n.49), kind=kLoop, calls=%fused_computation.76 | loop fusion | bytes 2375684 | tf_op jit(solution)/shard_map/dynamic-slice.1
  16.8 2.8 %copy.41 = f32[128,16,145]{0,2,1:T(8,128)} copy(f32[128,16,145]{2,1,0:T(8,128)} %constant_dynamic-slice_fusion) | data formatting | bytes 2375680
  19.5 0.0 collective-permute-done
  19.6 0.7 copy-done.2
  20.2 1.9 %fusion.8 = f32[16,162,128]{2,1,0:T(8,128)S(1)} fusion(s32[]{:T(128)S(6)} %select_n.50, f32[16,17,128]{2,1,0:T(8,128)} %copy-done.2, f32[16,145,128]{2,1,0:T(8,128)} %bitcast.34), kind=kLoop, calls=%fused_computation.17 | loop fusion | flops 663552 | bytes 2654212 | tf_op jit(solution)/shard_map/concatenate | solution.py:79
  22.2 0.0 copy-start.3
  22.2 1.3 %fusion.34 = (f32[9,162,128]{2,1,0:T(8,128)}, f32[9,162,128]{2,1,0:T(8,128)}) fusion(f32[16,162,128]{2,1,0:T(8,128)S(1)} %fusion.8), kind=kLoop, calls=%fused_computation.82 | loop fusion | bytes 2985984 | tf_op jit(solution)/shard_map/slice | solution.py:82
  23.4 4.7 %collective-permute-start.1 = (f32[9,162,128]{2,1,0:T(8,128)}, f32[9,162,128]{2,1,0:T(8,128)}, u32[]{:S(2)}, u32[]{:S(2)}) collective-permute-start(f32[9,162,128]{2,1,0:T(8,128)} %get-tuple-element.43), channel_id=1, source_target_pairs={{0,4},{1,5},{2,6},{3,7},{4,8},{5,9},{6,10},{7,11},{8,12},{9,13},{1... | collective-permute-start | bytes 2239496 | tf_op jit(solution)/shard_map/ppermute | solution.py:58
  28.1 1.3 %collective-permute-start.2 = (f32[9,162,128]{2,1,0:T(8,128)}, f32[9,162,128]{2,1,0:T(8,128)}, u32[]{:S(2)}, u32[]{:S(2)}) collective-permute-start(f32[9,162,128]{2,1,0:T(8,128)} %get-tuple-element.42), channel_id=1, source_target_pairs={{4,0},{5,1},{6,2},{7,3},{8,4},{9,5},{10,6},{11,7},{12,8},{13,9},{1... | collective-permute-start | bytes 2239496 | tf_op jit(solution)/shard_map/ppermute | solution.py:58
  29.4 0.0 copy-done.3
  29.4 0.6 convert_bitcast_fusion.scale_ref
  30.0 3.6 %all-to-all-done = bf16[16,65,384]{2,1,0:T(8,128)(2,1)} async-done(((bf16[16,65,384]{2,1,0:T(8,128)(2,1)}), bf16[16,65,384]{2,1,0:T(8,128)(2,1)}, u32[]{:S(2)}, u32[]{:S(2)}) %all-to-all-start) | async-done | bytes 798752 | tf_op jit(solution)/shard_map/all_to_all | solution.py:298
  33.7 1.2 %slice.67 = bf16[16,64,384]{2,1,0:T(8,128)(2,1)S(1)} slice(bf16[16,65,384]{2,1,0:T(8,128)(2,1)} %all-to-all-done), slice={[0:16], [0:64], [0:384]} | slice | bytes 1572864 | tf_op jit(solution)/shard_map/slice | solution.py:299
  34.9 0.8 slice.68
  35.7 0.7 slice.69.cur_ref
  36.5 2.0 %copy.42 = bf16[1024,256]{0,1:T(8,128)(2,1)} copy(bf16[1024,256]{1,0:T(8,128)(2,1)} %slice.68) | data formatting | bytes 1048576
  38.5 0.8 fusion.22
  39.3 0.7 reshape.72.row_leaf_ref
  40.0 7.0 %shard_map.77.fil_hbm = f32[16,256,128]{2,1,0:T(8,128)} custom-call(s32[1,1024]{1,0:T(1,128)} %reshape.72.row_leaf_ref, bf16[256,1024]{1,0:T(8,128)(2,1)} %bitcast.35, bf16[1024,128]{1,0:T(8,128)(2,1)} %slice.69.cur_ref), custom_call_target="tpu_custom_call" | custom-call | tf_op jit(solution)/shard_map/pallas_call | solution.py:118
  47.0 0.0 collective-permute-done.1
  47.0 0.4 collective-permute-done.2
  47.4 1.6 %pad_maximum_fusion = f32[34,162,128]{2,1,0:T(8,128)S(1)} fusion(f32[9,162,128]{2,1,0:T(8,128)} %collective-permute-done.2, f32[16,162,128]{2,1,0:T(8,128)S(1)} %fusion.8, f32[9,162,128]{2,1,0:T(8,128)} %collective-permute-done.1), kind=kLoop, calls=%fused_computation | loop fusion | flops 1410048 | bytes 5640192 | tf_op jit(solution)/shard_map/concatenate | solution.py:84
  48.9 0.7 fusion.1
  49.6 0.2 maximum_bitcast_fusion
  49.9 2.3 %copy.34 = bf16[4,10,2,8,16,128]{5,4,3,2,1,0:T(8,128)(2,1)} copy(bf16[4,10,2,8,16,128]{5,4,1,3,0,2:T(8,128)(2,1)S(1)} %maximum_bitcast_fusion) | data formatting | bytes 5242880 | tf_op jit(solution)/shard_map/transpose | solution.py:24
  52.1 12.1 %shard_map.78 = (bf16[2,16,128,128]{3,2,1,0:T(8,128)(2,1)}, bf16[16,1,128]{2,1,0:T(2,128)(2,1)}, bf16[16,1,128]{2,1,0:T(2,128)(2,1)}, bf16[1,128,128]{2,1,0:T(8,128)(2,1)}, bf16[1,128,128]{2,1,0:T(8,128)(2,1)}) custom-call(s32[16,8]{1,0:T(8,128)} %bitcast.45, s32[16,8]{1,0:T(8,128)} %convert_bitcast_fusion.scale_ref, bf16[4,10,2,128,128]{4,3,2,1,0:T(8,128)(2,1)} %bitcast.29, ...), custom_call_target="tpu_custom_call" | custom-call | tf_op jit(solution)/shard_map/pallas_call | solution.py:223
  64.2 0.0 copy-start.7
  64.2 0.0 copy-start.6
  64.2 0.0 copy-start.1
  64.2 4.5 %shard_map.79 = bf16[1024,128]{1,0:T(8,128)(2,1)} custom-call(bf16[4,10,2,128,128]{4,3,2,1,0:T(8,128)(2,1)} %bitcast.30, s32[1,1024]{1,0:T(1,128)} %reshape.72.row_leaf_ref, bf16[256,1024]{1,0:T(8,128)(2,1)} %bitcast.36), custom_call_target="tpu_custom_call" | custom-call | tf_op jit(solution)/shard_map/pallas_call | solution.py:244
  68.8 0.0 copy-start.5
  68.8 0.0 copy-start.4
  68.8 8.6 %all-to-all-start.1 = ((bf16[16,64,128]{2,1,0:T(8,128)(2,1)}), bf16[16,64,128]{2,1,0:T(8,128)(2,1)S(1)}, u32[]{:S(2)}, u32[]{:S(2)}) async-start(bf16[16,64,128]{2,1,0:T(8,128)(2,1)} %bitcast.39), calls=%async_computation.1 | async-start | bytes 524288 | tf_op jit(solution)/shard_map/all_to_all | solution.py:324
  77.4 0.0 copy-done.7
  77.4 2.3 %collective-permute-start.3 = (bf16[16,1,128]{2,1,0:T(2,128)(2,1)S(1)}, bf16[16,1,128]{2,1,0:T(2,128)(2,1)S(1)}, u32[]{:S(2)}, u32[]{:S(2)}) collective-permute-start(bf16[16,1,128]{2,1,0:T(2,128)(2,1)S(1)} %copy-done.7), channel_id=1, source_target_pairs={{0,1},{1,2},{2,3},{4,5},{5,6},{6,7},{8,9},{9,10},{10,11},{12,13},{... | collective-permute-start | bytes 12296 | tf_op jit(solution)/shard_map/ppermute | solution.py:58
  79.7 0.0 copy-done.6
  79.7 1.3 %collective-permute-start.4 = (bf16[16,1,128]{2,1,0:T(2,128)(2,1)S(1)}, bf16[16,1,128]{2,1,0:T(2,128)(2,1)S(1)}, u32[]{:S(2)}, u32[]{:S(2)}) collective-permute-start(bf16[16,1,128]{2,1,0:T(2,128)(2,1)S(1)} %copy-done.6), channel_id=1, source_target_pairs={{1,0},{2,1},{3,2},{5,4},{6,5},{7,6},{9,8},{10,9},{11,10},{13,12},{... | collective-permute-start | bytes 12296 | tf_op jit(solution)/shard_map/ppermute | solution.py:58
  81.0 0.0 copy-done.1
  81.0 0.1 slice_bitcast_fusion.1
  81.1 3.6 %collective-permute-start.5 = (bf16[1,128,128]{2,1,0:T(8,128)(2,1)S(1)}, bf16[1,128,128]{2,1,0:T(8,128)(2,1)S(1)}, u32[]{:S(2)}, u32[]{:S(2)}) collective-permute-start(bf16[1,128,128]{2,1,0:T(8,128)(2,1)S(1)} %copy-done.5), channel_id=1, source_target_pairs={{0,4},{1,5},{2,6},{3,7},{4,8},{5,9},{6,10},{7,11},{8,12},{9,13},{1... | collective-permute-start | bytes 98312 | tf_op jit(solution)/shard_map/ppermute | solution.py:58
  84.7 1.3 %collective-permute-start.6 = (bf16[1,128,128]{2,1,0:T(8,128)(2,1)S(1)}, bf16[1,128,128]{2,1,0:T(8,128)(2,1)S(1)}, u32[]{:S(2)}, u32[]{:S(2)}) collective-permute-start(bf16[1,128,128]{2,1,0:T(8,128)(2,1)S(1)} %copy-done.4), channel_id=1, source_target_pairs={{4,0},{5,1},{6,2},{7,3},{8,4},{9,5},{10,6},{11,7},{12,8},{13,9},{1... | collective-permute-start | bytes 98312 | tf_op jit(solution)/shard_map/ppermute | solution.py:58
  86.0 0.0 collective-permute-done.3
  86.0 0.0 collective-permute-done.4
  86.0 0.1 maximum_convert_fusion.1
  86.2 0.1 collective-permute-done.5
  86.3 4.2 %collective-permute-done.6 = bf16[1,128,128]{2,1,0:T(8,128)(2,1)S(1)} collective-permute-done((bf16[1,128,128]{2,1,0:T(8,128)(2,1)S(1)}, bf16[1,128,128]{2,1,0:T(8,128)(2,1)S(1)}, u32[]{:S(2)}, u32[]{:S(2)}) %collective-permute-start.6) | collective-permute-done | bytes 32800 | tf_op jit(solution)/shard_map/ppermute | solution.py:58
  90.5 0.1 maximum_convert_fusion
  90.6 0.2 fusion.11
  90.8 1.4 %copy.37 = f32[128,16,128]{2,1,0:T(8,128)} copy(f32[128,16,128]{0,2,1:T(8,128)S(1)} %fusion.11) | data formatting | bytes 2097152
  92.2 0.0 all-to-all-done.1
  92.2 1.4 %fusion.9 = bf16[512,128]{1,0:T(8,128)(2,1)} fusion(bf16[1024,128]{1,0:T(8,128)(2,1)S(1)} %bitcast.42, s32[512]{0:T(512)S(1)} %multiply_add_fusion), kind=kOutput, calls=%fused_computation.18 | convolution fusion | flops 134807552 | bytes 395264 | tf_op jit(solution)/shard_map/dot_general | solution.py:327
  (6 shorter events, 0.0 us)
Async XLA Ops:
  0.6 12.7 %copy-start = (f32[128,16,256]{2,1,0:T(8,128)S(1)}, f32[128,16,256]{2,1,0:T(8,128)}, u32[]{:S(2)}) copy-start(f32[128,16,256]{2,1,0:T(8,128)} %param.6) | copy-start | bytes 6291460
  5.9 27.8 %all-to-all-start = ((bf16[16,65,384]{2,1,0:T(8,128)(2,1)}), bf16[16,65,384]{2,1,0:T(8,128)(2,1)}, u32[]{:S(2)}, u32[]{:S(2)}) async-start(bf16[16,65,384]{2,1,0:T(8,128)(2,1)} %fusion.16), calls=%async_computation | async-start | bytes 1769472 | tf_op jit(solution)/shard_map/all_to_all | solution.py:298
  14.2 5.4 %collective-permute-start = (f32[16,17,128]{2,1,0:T(8,128)S(1)}, f32[16,17,128]{2,1,0:T(8,128)S(1)}, u32[]{:S(2)}, u32[]{:S(2)}) collective-permute-start(f32[16,17,128]{2,1,0:T(8,128)S(1)} %bitcast.44), channel_id=1, source_target_pairs={{1,2},{2,1},{5,6},{6,5},{9,10},{10,9},{13,14},{14,13},{17,18},{18,... | collective-permute-start | bytes 417800 | tf_op jit(solution)/shard_map/ppermute | solution.py:58
  19.5 0.7 copy-start.2
  22.2 7.3 %copy-start.3 = (s32[2,8,8]{2,1,0:T(8,128)S(1)}, s32[2,8,8]{2,1,0:T(8,128)}, u32[]{:S(2)}) copy-start(s32[2,8,8]{2,1,0:T(8,128)} %param.8) | copy-start | bytes 1540
  23.4 23.6 %collective-permute-start.1 = (f32[9,162,128]{2,1,0:T(8,128)}, f32[9,162,128]{2,1,0:T(8,128)}, u32[]{:S(2)}, u32[]{:S(2)}) collective-permute-start(f32[9,162,128]{2,1,0:T(8,128)} %get-tuple-element.43), channel_id=1, source_target_pairs={{0,4},{1,5},{2,6},{3,7},{4,8},{5,9},{6,10},{7,11},{8,12},{9,13},{1... | collective-permute-start | bytes 2239496 | tf_op jit(solution)/shard_map/ppermute | solution.py:58
  28.1 19.3 %collective-permute-start.2 = (f32[9,162,128]{2,1,0:T(8,128)}, f32[9,162,128]{2,1,0:T(8,128)}, u32[]{:S(2)}, u32[]{:S(2)}) collective-permute-start(f32[9,162,128]{2,1,0:T(8,128)} %get-tuple-element.42), channel_id=1, source_target_pairs={{4,0},{5,1},{6,2},{7,3},{8,4},{9,5},{10,6},{11,7},{12,8},{13,9},{1... | collective-permute-start | bytes 2239496 | tf_op jit(solution)/shard_map/ppermute | solution.py:58
  64.2 13.2 %copy-start.7 = (bf16[16,1,128]{2,1,0:T(2,128)(2,1)S(1)}, bf16[16,1,128]{2,1,0:T(2,128)(2,1)}, u32[]{:S(2)}) copy-start(bf16[16,1,128]{2,1,0:T(2,128)(2,1)} %get-tuple-element.26) | copy-start | bytes 12292
  64.2 15.5 %copy-start.6 = (bf16[16,1,128]{2,1,0:T(2,128)(2,1)S(1)}, bf16[16,1,128]{2,1,0:T(2,128)(2,1)}, u32[]{:S(2)}) copy-start(bf16[16,1,128]{2,1,0:T(2,128)(2,1)} %get-tuple-element.28) | copy-start | bytes 12292
  64.2 16.8 %copy-start.1 = (bf16[2,16,128,128]{3,2,1,0:T(8,128)(2,1)S(1)}, bf16[2,16,128,128]{3,2,1,0:T(8,128)(2,1)}, u32[]{:S(2)}) copy-start(bf16[2,16,128,128]{3,2,1,0:T(8,128)(2,1)} %get-tuple-element.27) | copy-start | bytes 3145732
  68.8 12.4 %copy-start.5 = (bf16[1,128,128]{2,1,0:T(8,128)(2,1)S(1)}, bf16[1,128,128]{2,1,0:T(8,128)(2,1)}, u32[]{:S(2)}) copy-start(bf16[1,128,128]{2,1,0:T(8,128)(2,1)} %get-tuple-element.29) | copy-start | bytes 98308
  68.8 15.9 %copy-start.4 = (bf16[1,128,128]{2,1,0:T(8,128)(2,1)S(1)}, bf16[1,128,128]{2,1,0:T(8,128)(2,1)}, u32[]{:S(2)}) copy-start(bf16[1,128,128]{2,1,0:T(8,128)(2,1)} %get-tuple-element.30) | copy-start | bytes 98308
  68.8 23.4 %all-to-all-start.1 = ((bf16[16,64,128]{2,1,0:T(8,128)(2,1)}), bf16[16,64,128]{2,1,0:T(8,128)(2,1)S(1)}, u32[]{:S(2)}, u32[]{:S(2)}) async-start(bf16[16,64,128]{2,1,0:T(8,128)(2,1)} %bitcast.39), calls=%async_computation.1 | async-start | bytes 524288 | tf_op jit(solution)/shard_map/all_to_all | solution.py:324
  77.4 8.7 %collective-permute-start.3 = (bf16[16,1,128]{2,1,0:T(2,128)(2,1)S(1)}, bf16[16,1,128]{2,1,0:T(2,128)(2,1)S(1)}, u32[]{:S(2)}, u32[]{:S(2)}) collective-permute-start(bf16[16,1,128]{2,1,0:T(2,128)(2,1)S(1)} %copy-done.7), channel_id=1, source_target_pairs={{0,1},{1,2},{2,3},{4,5},{5,6},{6,7},{8,9},{9,10},{10,11},{12,13},{... | collective-permute-start | bytes 12296 | tf_op jit(solution)/shard_map/ppermute | solution.py:58
  79.7 6.3 %collective-permute-start.4 = (bf16[16,1,128]{2,1,0:T(2,128)(2,1)S(1)}, bf16[16,1,128]{2,1,0:T(2,128)(2,1)S(1)}, u32[]{:S(2)}, u32[]{:S(2)}) collective-permute-start(bf16[16,1,128]{2,1,0:T(2,128)(2,1)S(1)} %copy-done.6), channel_id=1, source_target_pairs={{1,0},{2,1},{3,2},{5,4},{6,5},{7,6},{9,8},{10,9},{11,10},{13,12},{... | collective-permute-start | bytes 12296 | tf_op jit(solution)/shard_map/ppermute | solution.py:58
  81.1 5.2 %collective-permute-start.5 = (bf16[1,128,128]{2,1,0:T(8,128)(2,1)S(1)}, bf16[1,128,128]{2,1,0:T(8,128)(2,1)S(1)}, u32[]{:S(2)}, u32[]{:S(2)}) collective-permute-start(bf16[1,128,128]{2,1,0:T(8,128)(2,1)S(1)} %copy-done.5), channel_id=1, source_target_pairs={{0,4},{1,5},{2,6},{3,7},{4,8},{5,9},{6,10},{7,11},{8,12},{9,13},{1... | collective-permute-start | bytes 98312 | tf_op jit(solution)/shard_map/ppermute | solution.py:58
  84.7 5.8 %collective-permute-start.6 = (bf16[1,128,128]{2,1,0:T(8,128)(2,1)S(1)}, bf16[1,128,128]{2,1,0:T(8,128)(2,1)S(1)}, u32[]{:S(2)}, u32[]{:S(2)}) collective-permute-start(bf16[1,128,128]{2,1,0:T(8,128)(2,1)S(1)} %copy-done.4), channel_id=1, source_target_pairs={{4,0},{5,1},{6,2},{7,3},{8,4},{9,5},{10,6},{11,7},{12,8},{13,9},{1... | collective-permute-start | bytes 98312 | tf_op jit(solution)/shard_map/ppermute | solution.py:58

commit v21 on v20

--- a/solution.py
+++ b/solution.py
@@ -180,7 +180,7 @@
             )
         return carry
 
-    lax.fori_loop(0, leaf_count, one_leaf, 0, unroll=2)
+    lax.fori_loop(0, leaf_count, one_leaf, 0, unroll=4)
     rows, cols = field_ref.shape[1], field_ref.shape[2]
     x_first_ref[...] = field_ref[0, :, 0:1]
     x_last_ref[...] = field_ref[0, :, cols - 1 : cols]

time: 95.3 us -> 95.3 us (level)
  no operation moved by 1% of the time
where the time goes in v21:
time: 95.3 us; the launch traced here: 93.6 us
  starting transfers between devices  31 us (33%)
  Pallas kernels  23.6 us (25%)
  local copies, waits for them, and re-layouts  17.8 us (19%)
  waiting for transfers between devices  8.37 us (9%)
  other arithmetic  8.32 us (9%)
  matrix products  3.5 us (4%)
  between operations  0.96 us (1%)
    ppermute x7, starting transfers between devices, send(): return lax.ppermute(value, AXES, pairs_by(fn))  15.1 us
    pallas_call x1, Pallas kernels, leaf_fields(): pl.pallas_call(leaf_kernel, in_specs=[smem, smem, hbm, hbm, hbm], out_spe...  12 us
    all_to_all x1, starting transfers between devices, body(): lax.all_to_all(induced.reshape(owners, capacity, port_count), AXES, split...  8.56 us
    unnamed x21, local copies, waits for them, and re-layouts  8.36 us
    all_to_all x1, starting transfers between devices, body(): got = lax.all_to_all(payload, AXES, split_axis=0, concat_axis=0, tiled=True)  7.4 us
    pallas_call x1, Pallas kernels, filament_field(): pl.pallas_call(filament_kernel, in_specs=[vmem, vmem, vmem], out_specs=vm...  7.02 us
    ppermute x7, waiting for transfers between devices, send(): return lax.ppermute(value, AXES, pairs_by(fn))  4.72 us
    pallas_call x1, Pallas kernels, leaf_fields(): pl.pallas_call(induced_kernel, in_specs=[hbm, vmem, vmem], out_specs=vmem...  4.53 us
  transfers between devices with their start and end apart: 9, of which 4 were waited for; matrix products, arithmetic and copies ran while one was open for 19% of the time, Pallas kernels for 8%

profile of v21, /device:TPU:0, one launch (start us, length us, event | category | flops | bytes accessed | tf_op | source)
XLA Modules:
  0.0 93.6 jit_solution(13795007091973863439)
XLA Ops:
  0.6 0.0 copy-start
  0.6 0.9 fusion.25
  1.5 0.2 convert_reduce_fusion
  1.8 0.5 fusion.3
  2.2 0.1 reshape.75
  2.3 1.0 %copy.46 = bf16[64,8,2,128]{3,1,2,0:T(8,128)(2,1)S(1)} copy(bf16[64,8,2,128]{3,2,1,0:T(2,128)(2,1)} %bitcast.41) | data formatting | bytes 524288
  3.3 1.6 %fusion.6 = bf16[1024,384]{1,0:T(8,128)(2,1)S(1)} fusion(s32[512]{0:T(512)S(1)} %multiply_add_fusion, bf16[512,128]{1,0:T(8,128)(2,1)} %param.10, bf16[512,256]{1,0:T(8,128)(2,1)S(1)} %bitcast.43), kind=kOutput, calls=%fused_computation.15 | convolution fusion | flops 404357120 | bytes 1181696 | tf_op jit(solution)/shard_map/dot_general | solution.py:289
  4.9 1.0 %fusion.16 = bf16[16,65,384]{2,1,0:T(8,128)(2,1)} fusion(bf16[16,1,64]{2,1,0:T(2,128)(2,1)S(1)} %reshape.75, bf16[16,64,384]{2,1,0:T(8,128)(2,1)S(1)} %bitcast.40), kind=kLoop, calls=%fused_computation.29 | loop fusion | flops 2396160 | bytes 1587200 | tf_op jit(solution)/shard_map/concatenate | solution.py:297
  5.9 7.4 %all-to-all-start = ((bf16[16,65,384]{2,1,0:T(8,128)(2,1)}), bf16[16,65,384]{2,1,0:T(8,128)(2,1)}, u32[]{:S(2)}, u32[]{:S(2)}) async-start(bf16[16,65,384]{2,1,0:T(8,128)(2,1)} %fusion.16), calls=%async_computation | async-start | bytes 1769472 | tf_op jit(solution)/shard_map/all_to_all | solution.py:298
  13.3 0.0 copy-done
  13.4 0.3 constant_dynamic-slice_fusion.1
  13.7 0.4 copy.40
  14.2 0.7 collective-permute-start
  14.8 2.0 %constant_dynamic-slice_fusion = f32[128,16,145]{2,1,0:T(8,128)} fusion(f32[128,16,256]{2,1,0:T(8,128)S(1)} %copy-done, s32[]{:T(128)S(6)} %select_n.49), kind=kLoop, calls=%fused_computation.76 | loop fusion | bytes 2375684 | tf_op jit(solution)/shard_map/dynamic-slice.1
  16.8 2.8 %copy.41 = f32[128,16,145]{0,2,1:T(8,128)} copy(f32[128,16,145]{2,1,0:T(8,128)} %constant_dynamic-slice_fusion) | data formatting | bytes 2375680
  19.5 0.0 collective-permute-done
  19.6 0.7 copy-done.2
  20.2 1.9 %fusion.8 = f32[16,162,128]{2,1,0:T(8,128)S(1)} fusion(s32[]{:T(128)S(6)} %select_n.50, f32[16,17,128]{2,1,0:T(8,128)} %copy-done.2, f32[16,145,128]{2,1,0:T(8,128)} %bitcast.34), kind=kLoop, calls=%fused_computation.17 | loop fusion | flops 663552 | bytes 2654212 | tf_op jit(solution)/shard_map/concatenate | solution.py:79
  22.2 0.0 copy-start.3
  22.2 1.3 %fusion.34 = (f32[9,162,128]{2,1,0:T(8,128)}, f32[9,162,128]{2,1,0:T(8,128)}) fusion(f32[16,162,128]{2,1,0:T(8,128)S(1)} %fusion.8), kind=kLoop, calls=%fused_computation.82 | loop fusion | bytes 2985984 | tf_op jit(solution)/shard_map/slice | solution.py:82
  23.4 4.7 %collective-permute-start.1 = (f32[9,162,128]{2,1,0:T(8,128)}, f32[9,162,128]{2,1,0:T(8,128)}, u32[]{:S(2)}, u32[]{:S(2)}) collective-permute-start(f32[9,162,128]{2,1,0:T(8,128)} %get-tuple-element.43), channel_id=1, source_target_pairs={{0,4},{1,5},{2,6},{3,7},{4,8},{5,9},{6,10},{7,11},{8,12},{9,13},{1... | collective-permute-start | bytes 2239496 | tf_op jit(solution)/shard_map/ppermute | solution.py:58
  28.1 1.3 %collective-permute-start.2 = (f32[9,162,128]{2,1,0:T(8,128)}, f32[9,162,128]{2,1,0:T(8,128)}, u32[]{:S(2)}, u32[]{:S(2)}) collective-permute-start(f32[9,162,128]{2,1,0:T(8,128)} %get-tuple-element.42), channel_id=1, source_target_pairs={{4,0},{5,1},{6,2},{7,3},{8,4},{9,5},{10,6},{11,7},{12,8},{13,9},{1... | collective-permute-start | bytes 2239496 | tf_op jit(solution)/shard_map/ppermute | solution.py:58
  29.4 0.0 copy-done.3
  29.4 0.6 convert_bitcast_fusion.scale_ref
  30.0 3.6 %all-to-all-done = bf16[16,65,384]{2,1,0:T(8,128)(2,1)} async-done(((bf16[16,65,384]{2,1,0:T(8,128)(2,1)}), bf16[16,65,384]{2,1,0:T(8,128)(2,1)}, u32[]{:S(2)}, u32[]{:S(2)}) %all-to-all-start) | async-done | bytes 798752 | tf_op jit(solution)/shard_map/all_to_all | solution.py:298
  33.7 1.2 %slice.67 = bf16[16,64,384]{2,1,0:T(8,128)(2,1)S(1)} slice(bf16[16,65,384]{2,1,0:T(8,128)(2,1)} %all-to-all-done), slice={[0:16], [0:64], [0:384]} | slice | bytes 1572864 | tf_op jit(solution)/shard_map/slice | solution.py:299
  34.9 0.8 slice.68
  35.7 0.7 slice.69.cur_ref
  36.5 2.0 %copy.42 = bf16[1024,256]{0,1:T(8,128)(2,1)} copy(bf16[1024,256]{1,0:T(8,128)(2,1)} %slice.68) | data formatting | bytes 1048576
  38.5 0.8 fusion.22
  39.3 0.7 reshape.72.row_leaf_ref
  40.0 7.0 %shard_map.77.fil_hbm = f32[16,256,128]{2,1,0:T(8,128)} custom-call(s32[1,1024]{1,0:T(1,128)} %reshape.72.row_leaf_ref, bf16[256,1024]{1,0:T(8,128)(2,1)} %bitcast.35, bf16[1024,128]{1,0:T(8,128)(2,1)} %slice.69.cur_ref), custom_call_target="tpu_custom_call" | custom-call | tf_op jit(solution)/shard_map/pallas_call | solution.py:118
  47.0 0.0 collective-permute-done.1
  47.0 0.4 collective-permute-done.2
  47.4 1.6 %pad_maximum_fusion = f32[34,162,128]{2,1,0:T(8,128)S(1)} fusion(f32[9,162,128]{2,1,0:T(8,128)} %collective-permute-done.2, f32[16,162,128]{2,1,0:T(8,128)S(1)} %fusion.8, f32[9,162,128]{2,1,0:T(8,128)} %collective-permute-done.1), kind=kLoop, calls=%fused_computation | loop fusion | flops 1410048 | bytes 5640192 | tf_op jit(solution)/shard_map/concatenate | solution.py:84
  48.9 0.7 fusion.1
  49.6 0.2 maximum_bitcast_fusion
  49.9 2.3 %copy.34 = bf16[4,10,2,8,16,128]{5,4,3,2,1,0:T(8,128)(2,1)} copy(bf16[4,10,2,8,16,128]{5,4,1,3,0,2:T(8,128)(2,1)S(1)} %maximum_bitcast_fusion) | data formatting | bytes 5242880 | tf_op jit(solution)/shard_map/transpose | solution.py:24
  52.1 12.0 %shard_map.78 = (bf16[2,16,128,128]{3,2,1,0:T(8,128)(2,1)}, bf16[16,1,128]{2,1,0:T(2,128)(2,1)}, bf16[16,1,128]{2,1,0:T(2,128)(2,1)}, bf16[1,128,128]{2,1,0:T(8,128)(2,1)}, bf16[1,128,128]{2,1,0:T(8,128)(2,1)}) custom-call(s32[16,8]{1,0:T(8,128)} %bitcast.45, s32[16,8]{1,0:T(8,128)} %convert_bitcast_fusion.scale_ref, bf16[4,10,2,128,128]{4,3,2,1,0:T(8,128)(2,1)} %bitcast.29, ...), custom_call_target="tpu_custom_call" | custom-call | tf_op jit(solution)/shard_map/pallas_call | solution.py:223
  64.2 0.0 copy-start.7
  64.2 0.0 copy-start.6
  64.2 0.0 copy-start.1
  64.2 4.5 %shard_map.79 = bf16[1024,128]{1,0:T(8,128)(2,1)} custom-call(bf16[4,10,2,128,128]{4,3,2,1,0:T(8,128)(2,1)} %bitcast.30, s32[1,1024]{1,0:T(1,128)} %reshape.72.row_leaf_ref, bf16[256,1024]{1,0:T(8,128)(2,1)} %bitcast.36), custom_call_target="tpu_custom_call" | custom-call | tf_op jit(solution)/shard_map/pallas_call | solution.py:244
  68.7 0.0 copy-start.5
  68.7 0.0 copy-start.4
  68.8 8.6 %all-to-all-start.1 = ((bf16[16,64,128]{2,1,0:T(8,128)(2,1)}), bf16[16,64,128]{2,1,0:T(8,128)(2,1)S(1)}, u32[]{:S(2)}, u32[]{:S(2)}) async-start(bf16[16,64,128]{2,1,0:T(8,128)(2,1)} %bitcast.39), calls=%async_computation.1 | async-start | bytes 524288 | tf_op jit(solution)/shard_map/all_to_all | solution.py:324
  77.3 0.0 copy-done.7
  77.3 2.3 %collective-permute-start.3 = (bf16[16,1,128]{2,1,0:T(2,128)(2,1)S(1)}, bf16[16,1,128]{2,1,0:T(2,128)(2,1)S(1)}, u32[]{:S(2)}, u32[]{:S(2)}) collective-permute-start(bf16[16,1,128]{2,1,0:T(2,128)(2,1)S(1)} %copy-done.7), channel_id=1, source_target_pairs={{0,1},{1,2},{2,3},{4,5},{5,6},{6,7},{8,9},{9,10},{10,11},{12,13},{... | collective-permute-start | bytes 12296 | tf_op jit(solution)/shard_map/ppermute | solution.py:58
  79.6 0.0 copy-done.6
  79.7 1.3 %collective-permute-start.4 = (bf16[16,1,128]{2,1,0:T(2,128)(2,1)S(1)}, bf16[16,1,128]{2,1,0:T(2,128)(2,1)S(1)}, u32[]{:S(2)}, u32[]{:S(2)}) collective-permute-start(bf16[16,1,128]{2,1,0:T(2,128)(2,1)S(1)} %copy-done.6), channel_id=1, source_target_pairs={{1,0},{2,1},{3,2},{5,4},{6,5},{7,6},{9,8},{10,9},{11,10},{13,12},{... | collective-permute-start | bytes 12296 | tf_op jit(solution)/shard_map/ppermute | solution.py:58
  81.0 0.0 copy-done.1
  81.0 0.1 slice_bitcast_fusion.1
  81.1 3.6 %collective-permute-start.5 = (bf16[1,128,128]{2,1,0:T(8,128)(2,1)S(1)}, bf16[1,128,128]{2,1,0:T(8,128)(2,1)S(1)}, u32[]{:S(2)}, u32[]{:S(2)}) collective-permute-start(bf16[1,128,128]{2,1,0:T(8,128)(2,1)S(1)} %copy-done.5), channel_id=1, source_target_pairs={{0,4},{1,5},{2,6},{3,7},{4,8},{5,9},{6,10},{7,11},{8,12},{9,13},{1... | collective-permute-start | bytes 98312 | tf_op jit(solution)/shard_map/ppermute | solution.py:58
  84.7 1.3 %collective-permute-start.6 = (bf16[1,128,128]{2,1,0:T(8,128)(2,1)S(1)}, bf16[1,128,128]{2,1,0:T(8,128)(2,1)S(1)}, u32[]{:S(2)}, u32[]{:S(2)}) collective-permute-start(bf16[1,128,128]{2,1,0:T(8,128)(2,1)S(1)} %copy-done.4), channel_id=1, source_target_pairs={{4,0},{5,1},{6,2},{7,3},{8,4},{9,5},{10,6},{11,7},{12,8},{13,9},{1... | collective-permute-start | bytes 98312 | tf_op jit(solution)/shard_map/ppermute | solution.py:58
  86.0 0.0 collective-permute-done.3
  86.0 0.0 collective-permute-done.4
  86.0 0.1 maximum_convert_fusion.1
  86.1 0.1 collective-permute-done.5
  86.2 4.2 %collective-permute-done.6 = bf16[1,128,128]{2,1,0:T(8,128)(2,1)S(1)} collective-permute-done((bf16[1,128,128]{2,1,0:T(8,128)(2,1)S(1)}, bf16[1,128,128]{2,1,0:T(8,128)(2,1)S(1)}, u32[]{:S(2)}, u32[]{:S(2)}) %collective-permute-start.6) | collective-permute-done | bytes 32800 | tf_op jit(solution)/shard_map/ppermute | solution.py:58
  90.5 0.1 maximum_convert_fusion
  90.6 0.2 fusion.11
  90.8 1.4 %copy.37 = f32[128,16,128]{2,1,0:T(8,128)} copy(f32[128,16,128]{0,2,1:T(8,128)S(1)} %fusion.11) | data formatting | bytes 2097152
  92.1 0.0 all-to-all-done.1
  92.1 1.4 %fusion.9 = bf16[512,128]{1,0:T(8,128)(2,1)} fusion(bf16[1024,128]{1,0:T(8,128)(2,1)S(1)} %bitcast.42, s32[512]{0:T(512)S(1)} %multiply_add_fusion), kind=kOutput, calls=%fused_computation.18 | convolution fusion | flops 134807552 | bytes 395264 | tf_op jit(solution)/shard_map/dot_general | solution.py:327
  (6 shorter events, 0.0 us)
Async XLA Ops:
  0.6 12.7 %copy-start = (f32[128,16,256]{2,1,0:T(8,128)S(1)}, f32[128,16,256]{2,1,0:T(8,128)}, u32[]{:S(2)}) copy-start(f32[128,16,256]{2,1,0:T(8,128)} %param.6) | copy-start | bytes 6291460
  5.9 27.8 %all-to-all-start = ((bf16[16,65,384]{2,1,0:T(8,128)(2,1)}), bf16[16,65,384]{2,1,0:T(8,128)(2,1)}, u32[]{:S(2)}, u32[]{:S(2)}) async-start(bf16[16,65,384]{2,1,0:T(8,128)(2,1)} %fusion.16), calls=%async_computation | async-start | bytes 1769472 | tf_op jit(solution)/shard_map/all_to_all | solution.py:298
  14.2 5.4 %collective-permute-start = (f32[16,17,128]{2,1,0:T(8,128)S(1)}, f32[16,17,128]{2,1,0:T(8,128)S(1)}, u32[]{:S(2)}, u32[]{:S(2)}) collective-permute-start(f32[16,17,128]{2,1,0:T(8,128)S(1)} %bitcast.44), channel_id=1, source_target_pairs={{1,2},{2,1},{5,6},{6,5},{9,10},{10,9},{13,14},{14,13},{17,18},{18,... | collective-permute-start | bytes 417800 | tf_op jit(solution)/shard_map/ppermute | solution.py:58
  19.5 0.7 copy-start.2
  22.2 7.3 %copy-start.3 = (s32[2,8,8]{2,1,0:T(8,128)S(1)}, s32[2,8,8]{2,1,0:T(8,128)}, u32[]{:S(2)}) copy-start(s32[2,8,8]{2,1,0:T(8,128)} %param.8) | copy-start | bytes 1540
  23.4 23.6 %collective-permute-start.1 = (f32[9,162,128]{2,1,0:T(8,128)}, f32[9,162,128]{2,1,0:T(8,128)}, u32[]{:S(2)}, u32[]{:S(2)}) collective-permute-start(f32[9,162,128]{2,1,0:T(8,128)} %get-tuple-element.43), channel_id=1, source_target_pairs={{0,4},{1,5},{2,6},{3,7},{4,8},{5,9},{6,10},{7,11},{8,12},{9,13},{1... | collective-permute-start | bytes 2239496 | tf_op jit(solution)/shard_map/ppermute | solution.py:58
  28.1 19.3 %collective-permute-start.2 = (f32[9,162,128]{2,1,0:T(8,128)}, f32[9,162,128]{2,1,0:T(8,128)}, u32[]{:S(2)}, u32[]{:S(2)}) collective-permute-start(f32[9,162,128]{2,1,0:T(8,128)} %get-tuple-element.42), channel_id=1, source_target_pairs={{4,0},{5,1},{6,2},{7,3},{8,4},{9,5},{10,6},{11,7},{12,8},{13,9},{1... | collective-permute-start | bytes 2239496 | tf_op jit(solution)/shard_map/ppermute | solution.py:58
  64.2 13.2 %copy-start.7 = (bf16[16,1,128]{2,1,0:T(2,128)(2,1)S(1)}, bf16[16,1,128]{2,1,0:T(2,128)(2,1)}, u32[]{:S(2)}) copy-start(bf16[16,1,128]{2,1,0:T(2,128)(2,1)} %get-tuple-element.26) | copy-start | bytes 12292
  64.2 15.5 %copy-start.6 = (bf16[16,1,128]{2,1,0:T(2,128)(2,1)S(1)}, bf16[16,1,128]{2,1,0:T(2,128)(2,1)}, u32[]{:S(2)}) copy-start(bf16[16,1,128]{2,1,0:T(2,128)(2,1)} %get-tuple-element.28) | copy-start | bytes 12292
  64.2 16.8 %copy-start.1 = (bf16[2,16,128,128]{3,2,1,0:T(8,128)(2,1)S(1)}, bf16[2,16,128,128]{3,2,1,0:T(8,128)(2,1)}, u32[]{:S(2)}) copy-start(bf16[2,16,128,128]{3,2,1,0:T(8,128)(2,1)} %get-tuple-element.27) | copy-start | bytes 3145732
  68.7 12.3 %copy-start.5 = (bf16[1,128,128]{2,1,0:T(8,128)(2,1)S(1)}, bf16[1,128,128]{2,1,0:T(8,128)(2,1)}, u32[]{:S(2)}) copy-start(bf16[1,128,128]{2,1,0:T(8,128)(2,1)} %get-tuple-element.29) | copy-start | bytes 98308
  68.7 15.9 %copy-start.4 = (bf16[1,128,128]{2,1,0:T(8,128)(2,1)S(1)}, bf16[1,128,128]{2,1,0:T(8,128)(2,1)}, u32[]{:S(2)}) copy-start(bf16[1,128,128]{2,1,0:T(8,128)(2,1)} %get-tuple-element.30) | copy-start | bytes 98308
  68.8 23.4 %all-to-all-start.1 = ((bf16[16,64,128]{2,1,0:T(8,128)(2,1)}), bf16[16,64,128]{2,1,0:T(8,128)(2,1)S(1)}, u32[]{:S(2)}, u32[]{:S(2)}) async-start(bf16[16,64,128]{2,1,0:T(8,128)(2,1)} %bitcast.39), calls=%async_computation.1 | async-start | bytes 524288 | tf_op jit(solution)/shard_map/all_to_all | solution.py:324
  77.3 8.7 %collective-permute-start.3 = (bf16[16,1,128]{2,1,0:T(2,128)(2,1)S(1)}, bf16[16,1,128]{2,1,0:T(2,128)(2,1)S(1)}, u32[]{:S(2)}, u32[]{:S(2)}) collective-permute-start(bf16[16,1,128]{2,1,0:T(2,128)(2,1)S(1)} %copy-done.7), channel_id=1, source_target_pairs={{0,1},{1,2},{2,3},{4,5},{5,6},{6,7},{8,9},{9,10},{10,11},{12,13},{... | collective-permute-start | bytes 12296 | tf_op jit(solution)/shard_map/ppermute | solution.py:58
  79.7 6.3 %collective-permute-start.4 = (bf16[16,1,128]{2,1,0:T(2,128)(2,1)S(1)}, bf16[16,1,128]{2,1,0:T(2,128)(2,1)S(1)}, u32[]{:S(2)}, u32[]{:S(2)}) collective-permute-start(bf16[16,1,128]{2,1,0:T(2,128)(2,1)S(1)} %copy-done.6), channel_id=1, source_target_pairs={{1,0},{2,1},{3,2},{5,4},{6,5},{7,6},{9,8},{10,9},{11,10},{13,12},{... | collective-permute-start | bytes 12296 | tf_op jit(solution)/shard_map/ppermute | solution.py:58
  81.1 5.2 %collective-permute-start.5 = (bf16[1,128,128]{2,1,0:T(8,128)(2,1)S(1)}, bf16[1,128,128]{2,1,0:T(8,128)(2,1)S(1)}, u32[]{:S(2)}, u32[]{:S(2)}) collective-permute-start(bf16[1,128,128]{2,1,0:T(8,128)(2,1)S(1)} %copy-done.5), channel_id=1, source_target_pairs={{0,4},{1,5},{2,6},{3,7},{4,8},{5,9},{6,10},{7,11},{8,12},{9,13},{1... | collective-permute-start | bytes 98312 | tf_op jit(solution)/shard_map/ppermute | solution.py:58
  84.7 5.8 %collective-permute-start.6 = (bf16[1,128,128]{2,1,0:T(8,128)(2,1)S(1)}, bf16[1,128,128]{2,1,0:T(8,128)(2,1)S(1)}, u32[]{:S(2)}, u32[]{:S(2)}) collective-permute-start(bf16[1,128,128]{2,1,0:T(8,128)(2,1)S(1)} %copy-done.4), channel_id=1, source_target_pairs={{4,0},{5,1},{6,2},{7,3},{8,4},{9,5},{10,6},{11,7},{12,8},{13,9},{1... | collective-permute-start | bytes 98312 | tf_op jit(solution)/shard_map/ppermute | solution.py:58

commit v22 on v20

--- a/solution.py
+++ b/solution.py
@@ -103,14 +103,15 @@
     return x_pad[:, :-2] - x_pad[:, 2:] + (y_pad[2:] - y_pad[:-2])
 
 
-def filament_kernel(row_leaf_ref, cpl_t_ref, cur_ref, fil_ref):
-    def one_leaf(leaf, carry):
-        coupling_t = cpl_t_ref[...]
-        coupling_t = jnp.where(row_leaf_ref[...] == leaf, coupling_t, jnp.zeros_like(coupling_t))
-        fil_ref[leaf] = jnp.dot(coupling_t, cur_ref[...], preferred_element_type=jnp.float32)
-        return carry
-
-    lax.fori_loop(0, fil_ref.shape[0], one_leaf, 0)
+def filament_kernel(row_leaf_ref, cpl_t_ref, cur_ref, fil_ref, stack_ref):
+    coupling_t = cpl_t_ref[...]
+    slot_leaf = row_leaf_ref[...]
+    for leaf in range(fil_ref.shape[0]):
+        stack_ref[leaf] = jnp.where(slot_leaf == leaf, coupling_t, jnp.zeros_like(coupling_t))
+    stacked = stack_ref[...].reshape(-1, coupling_t.shape[1])
+    fil_ref[...] = jnp.dot(stacked, cur_ref[...], preferred_element_type=jnp.float32).reshape(
+        fil_ref.shape
+    )
 
 
 def filament_field(row_leaf, coupling_t, current, leaf_count):
@@ -122,6 +123,7 @@
         out_shape=jax.ShapeDtypeStruct(
             (leaf_count, coupling_t.shape[0], current.shape[1]), jnp.float32
         ),
+        scratch_shapes=[pltpu.VMEM((leaf_count,) + coupling_t.shape, coupling_t.dtype)],
     )(row_leaf, coupling_t, current)
 
 

time: 95.3 us -> 95.3 us (level)
  waiting for transfers between devices: 8.37 us -> 10.6 us
  Pallas kernels: 23.6 us -> 21.4 us
    ppermute x7, waiting for transfers between devices: 4.72 us -> 6.97 us  [send(): return lax.ppermute(value, AXES, pairs_by(fn))]
    pallas_call x1, Pallas kernels: 7.02 us -> 4.78 us  [filament_field(): pl.pallas_call(filament_kernel, in_specs=[vmem, vmem, vmem], out_specs=vm...]
  transfers between devices with their start and end apart: 9 -> 9, of which waited for: 4 -> 4; matrix products, arithmetic and copies ran while one was open for 19% -> 19% of each run, Pallas kernels for 8% -> 5%
where the time goes in v22:
time: 95.3 us; the launch traced here: 93.6 us
  starting transfers between devices  31.1 us (33%)
  Pallas kernels  21.4 us (22%)
  local copies, waits for them, and re-layouts  17.8 us (19%)
  waiting for transfers between devices  10.6 us (11%)
  other arithmetic  8.32 us (9%)
  matrix products  3.5 us (4%)
  between operations  0.96 us (1%)
    ppermute x7, starting transfers between devices, send(): return lax.ppermute(value, AXES, pairs_by(fn))  15.1 us
    pallas_call x1, Pallas kernels, leaf_fields(): pl.pallas_call(leaf_kernel, in_specs=[smem, smem, hbm, hbm, hbm], out_spe...  12.1 us
    all_to_all x1, starting transfers between devices, body(): lax.all_to_all(induced.reshape(owners, capacity, port_count), AXES, split...  8.57 us
    unnamed x21, local copies, waits for them, and re-layouts  8.36 us
    all_to_all x1, starting transfers between devices, body(): got = lax.all_to_all(payload, AXES, split_axis=0, concat_axis=0, tiled=True)  7.4 us
    ppermute x7, waiting for transfers between devices, send(): return lax.ppermute(value, AXES, pairs_by(fn))  6.97 us
    pallas_call x1, Pallas kernels, filament_field(): pl.pallas_call(filament_kernel, in_specs=[vmem, vmem, vmem], out_specs=vm...  4.78 us
    pallas_call x1, Pallas kernels, leaf_fields(): pl.pallas_call(induced_kernel, in_specs=[hbm, vmem, vmem], out_specs=vmem...  4.52 us
  transfers between devices with their start and end apart: 9, of which 4 were waited for; matrix products, arithmetic and copies ran while one was open for 19% of the time, Pallas kernels for 5%

profile of v22, /device:TPU:0, one launch (start us, length us, event | category | flops | bytes accessed | tf_op | source)
XLA Modules:
  0.0 93.6 jit_solution(15963383274333429162)
XLA Ops:
  0.6 0.0 copy-start
  0.6 0.9 fusion.25
  1.5 0.2 convert_reduce_fusion
  1.8 0.5 fusion.3
  2.2 0.1 reshape.75
  2.3 1.0 %copy.46 = bf16[64,8,2,128]{3,1,2,0:T(8,128)(2,1)S(1)} copy(bf16[64,8,2,128]{3,2,1,0:T(2,128)(2,1)} %bitcast.41) | data formatting | bytes 524288
  3.3 1.6 %fusion.6 = bf16[1024,384]{1,0:T(8,128)(2,1)S(1)} fusion(s32[512]{0:T(512)S(1)} %multiply_add_fusion, bf16[512,128]{1,0:T(8,128)(2,1)} %param.10, bf16[512,256]{1,0:T(8,128)(2,1)S(1)} %bitcast.43), kind=kOutput, calls=%fused_computation.15 | convolution fusion | flops 404357120 | bytes 1181696 | tf_op jit(solution)/shard_map/dot_general | solution.py:291
  4.9 1.0 %fusion.16 = bf16[16,65,384]{2,1,0:T(8,128)(2,1)} fusion(bf16[16,1,64]{2,1,0:T(2,128)(2,1)S(1)} %reshape.75, bf16[16,64,384]{2,1,0:T(8,128)(2,1)S(1)} %bitcast.40), kind=kLoop, calls=%fused_computation.29 | loop fusion | flops 2396160 | bytes 1587200 | tf_op jit(solution)/shard_map/concatenate | solution.py:299
  5.9 7.4 %all-to-all-start = ((bf16[16,65,384]{2,1,0:T(8,128)(2,1)}), bf16[16,65,384]{2,1,0:T(8,128)(2,1)}, u32[]{:S(2)}, u32[]{:S(2)}) async-start(bf16[16,65,384]{2,1,0:T(8,128)(2,1)} %fusion.16), calls=%async_computation | async-start | bytes 1769472 | tf_op jit(solution)/shard_map/all_to_all | solution.py:300
  13.3 0.0 copy-done
  13.4 0.3 constant_dynamic-slice_fusion.1
  13.7 0.4 copy.40
  14.2 0.7 collective-permute-start
  14.8 2.0 %constant_dynamic-slice_fusion = f32[128,16,145]{2,1,0:T(8,128)} fusion(f32[128,16,256]{2,1,0:T(8,128)S(1)} %copy-done, s32[]{:T(128)S(6)} %select_n.49), kind=kLoop, calls=%fused_computation.76 | loop fusion | bytes 2375684 | tf_op jit(solution)/shard_map/dynamic-slice.1
  16.8 2.8 %copy.41 = f32[128,16,145]{0,2,1:T(8,128)} copy(f32[128,16,145]{2,1,0:T(8,128)} %constant_dynamic-slice_fusion) | data formatting | bytes 2375680
  19.5 0.0 collective-permute-done
  19.6 0.7 copy-done.2
  20.2 1.9 %fusion.8 = f32[16,162,128]{2,1,0:T(8,128)S(1)} fusion(s32[]{:T(128)S(6)} %select_n.50, f32[16,17,128]{2,1,0:T(8,128)} %copy-done.2, f32[16,145,128]{2,1,0:T(8,128)} %bitcast.34), kind=kLoop, calls=%fused_computation.17 | loop fusion | flops 663552 | bytes 2654212 | tf_op jit(solution)/shard_map/concatenate | solution.py:79
  22.2 0.0 copy-start.3
  22.2 1.3 %fusion.34 = (f32[9,162,128]{2,1,0:T(8,128)}, f32[9,162,128]{2,1,0:T(8,128)}) fusion(f32[16,162,128]{2,1,0:T(8,128)S(1)} %fusion.8), kind=kLoop, calls=%fused_computation.82 | loop fusion | bytes 2985984 | tf_op jit(solution)/shard_map/slice | solution.py:82
  23.4 4.7 %collective-permute-start.1 = (f32[9,162,128]{2,1,0:T(8,128)}, f32[9,162,128]{2,1,0:T(8,128)}, u32[]{:S(2)}, u32[]{:S(2)}) collective-permute-start(f32[9,162,128]{2,1,0:T(8,128)} %get-tuple-element.43), channel_id=1, source_target_pairs={{0,4},{1,5},{2,6},{3,7},{4,8},{5,9},{6,10},{7,11},{8,12},{9,13},{1... | collective-permute-start | bytes 2239496 | tf_op jit(solution)/shard_map/ppermute | solution.py:58
  28.1 1.3 %collective-permute-start.2 = (f32[9,162,128]{2,1,0:T(8,128)}, f32[9,162,128]{2,1,0:T(8,128)}, u32[]{:S(2)}, u32[]{:S(2)}) collective-permute-start(f32[9,162,128]{2,1,0:T(8,128)} %get-tuple-element.42), channel_id=1, source_target_pairs={{4,0},{5,1},{6,2},{7,3},{8,4},{9,5},{10,6},{11,7},{12,8},{13,9},{1... | collective-permute-start | bytes 2239496 | tf_op jit(solution)/shard_map/ppermute | solution.py:58
  29.4 0.0 copy-done.3
  29.4 0.6 convert_bitcast_fusion.scale_ref
  30.0 3.6 %all-to-all-done = bf16[16,65,384]{2,1,0:T(8,128)(2,1)} async-done(((bf16[16,65,384]{2,1,0:T(8,128)(2,1)}), bf16[16,65,384]{2,1,0:T(8,128)(2,1)}, u32[]{:S(2)}, u32[]{:S(2)}) %all-to-all-start) | async-done | bytes 798752 | tf_op jit(solution)/shard_map/all_to_all | solution.py:300
  33.7 1.2 %slice.67 = bf16[16,64,384]{2,1,0:T(8,128)(2,1)S(1)} slice(bf16[16,65,384]{2,1,0:T(8,128)(2,1)} %all-to-all-done), slice={[0:16], [0:64], [0:384]} | slice | bytes 1572864 | tf_op jit(solution)/shard_map/slice | solution.py:301
  34.9 0.8 slice.68
  35.7 0.7 slice.69.cur_ref
  36.5 2.0 %copy.42 = bf16[1024,256]{0,1:T(8,128)(2,1)} copy(bf16[1024,256]{1,0:T(8,128)(2,1)} %slice.68) | data formatting | bytes 1048576
  38.5 0.8 fusion.22
  39.3 0.7 reshape.72.row_leaf_ref
  40.0 4.8 %shard_map.77.fil_hbm = f32[16,256,128]{2,1,0:T(8,128)} custom-call(s32[1,1024]{1,0:T(1,128)} %reshape.72.row_leaf_ref, bf16[256,1024]{1,0:T(8,128)(2,1)} %bitcast.35, bf16[1024,128]{1,0:T(8,128)(2,1)} %slice.69.cur_ref), custom_call_target="tpu_custom_call" | custom-call | tf_op jit(solution)/shard_map/pallas_call | solution.py:119
  44.8 0.0 collective-permute-done.1
  44.8 2.6 %collective-permute-done.2 = f32[9,162,128]{2,1,0:T(8,128)} collective-permute-done((f32[9,162,128]{2,1,0:T(8,128)}, f32[9,162,128]{2,1,0:T(8,128)}, u32[]{:S(2)}, u32[]{:S(2)}) %collective-permute-start.2) | collective-permute-done | bytes 746528 | tf_op jit(solution)/shard_map/ppermute | solution.py:58
  47.4 1.6 %pad_maximum_fusion = f32[34,162,128]{2,1,0:T(8,128)S(1)} fusion(f32[9,162,128]{2,1,0:T(8,128)} %collective-permute-done.2, f32[16,162,128]{2,1,0:T(8,128)S(1)} %fusion.8, f32[9,162,128]{2,1,0:T(8,128)} %collective-permute-done.1), kind=kLoop, calls=%fused_computation | loop fusion | flops 1410048 | bytes 5640192 | tf_op jit(solution)/shard_map/concatenate | solution.py:84
  48.9 0.7 fusion.1
  49.6 0.2 maximum_bitcast_fusion
  49.9 2.3 %copy.34 = bf16[4,10,2,8,16,128]{5,4,3,2,1,0:T(8,128)(2,1)} copy(bf16[4,10,2,8,16,128]{5,4,1,3,0,2:T(8,128)(2,1)S(1)} %maximum_bitcast_fusion) | data formatting | bytes 5242880 | tf_op jit(solution)/shard_map/transpose | solution.py:24
  52.1 12.1 %shard_map.78 = (bf16[2,16,128,128]{3,2,1,0:T(8,128)(2,1)}, bf16[16,1,128]{2,1,0:T(2,128)(2,1)}, bf16[16,1,128]{2,1,0:T(2,128)(2,1)}, bf16[1,128,128]{2,1,0:T(8,128)(2,1)}, bf16[1,128,128]{2,1,0:T(8,128)(2,1)}) custom-call(s32[16,8]{1,0:T(8,128)} %bitcast.45, s32[16,8]{1,0:T(8,128)} %convert_bitcast_fusion.scale_ref, bf16[4,10,2,128,128]{4,3,2,1,0:T(8,128)(2,1)} %bitcast.29, ...), custom_call_target="tpu_custom_call" | custom-call | tf_op jit(solution)/shard_map/pallas_call | solution.py:225
  64.2 0.0 copy-start.7
  64.2 0.0 copy-start.6
  64.2 0.0 copy-start.1
  64.2 4.5 %shard_map.79 = bf16[1024,128]{1,0:T(8,128)(2,1)} custom-call(bf16[4,10,2,128,128]{4,3,2,1,0:T(8,128)(2,1)} %bitcast.30, s32[1,1024]{1,0:T(1,128)} %reshape.72.row_leaf_ref, bf16[256,1024]{1,0:T(8,128)(2,1)} %bitcast.36), custom_call_target="tpu_custom_call" | custom-call | tf_op jit(solution)/shard_map/pallas_call | solution.py:246
  68.8 0.0 copy-start.5
  68.8 0.0 copy-start.4
  68.8 8.6 %all-to-all-start.1 = ((bf16[16,64,128]{2,1,0:T(8,128)(2,1)}), bf16[16,64,128]{2,1,0:T(8,128)(2,1)S(1)}, u32[]{:S(2)}, u32[]{:S(2)}) async-start(bf16[16,64,128]{2,1,0:T(8,128)(2,1)} %bitcast.39), calls=%async_computation.1 | async-start | bytes 524288 | tf_op jit(solution)/shard_map/all_to_all | solution.py:326
  77.4 0.0 copy-done.7
  77.4 2.3 %collective-permute-start.3 = (bf16[16,1,128]{2,1,0:T(2,128)(2,1)S(1)}, bf16[16,1,128]{2,1,0:T(2,128)(2,1)S(1)}, u32[]{:S(2)}, u32[]{:S(2)}) collective-permute-start(bf16[16,1,128]{2,1,0:T(2,128)(2,1)S(1)} %copy-done.7), channel_id=1, source_target_pairs={{0,1},{1,2},{2,3},{4,5},{5,6},{6,7},{8,9},{9,10},{10,11},{12,13},{... | collective-permute-start | bytes 12296 | tf_op jit(solution)/shard_map/ppermute | solution.py:58
  79.7 0.0 copy-done.6
  79.7 1.3 %collective-permute-start.4 = (bf16[16,1,128]{2,1,0:T(2,128)(2,1)S(1)}, bf16[16,1,128]{2,1,0:T(2,128)(2,1)S(1)}, u32[]{:S(2)}, u32[]{:S(2)}) collective-permute-start(bf16[16,1,128]{2,1,0:T(2,128)(2,1)S(1)} %copy-done.6), channel_id=1, source_target_pairs={{1,0},{2,1},{3,2},{5,4},{6,5},{7,6},{9,8},{10,9},{11,10},{13,12},{... | collective-permute-start | bytes 12296 | tf_op jit(solution)/shard_map/ppermute | solution.py:58
  81.0 0.0 copy-done.1
  81.0 0.1 slice_bitcast_fusion.1
  81.1 3.6 %collective-permute-start.5 = (bf16[1,128,128]{2,1,0:T(8,128)(2,1)S(1)}, bf16[1,128,128]{2,1,0:T(8,128)(2,1)S(1)}, u32[]{:S(2)}, u32[]{:S(2)}) collective-permute-start(bf16[1,128,128]{2,1,0:T(8,128)(2,1)S(1)} %copy-done.5), channel_id=1, source_target_pairs={{0,4},{1,5},{2,6},{3,7},{4,8},{5,9},{6,10},{7,11},{8,12},{9,13},{1... | collective-permute-start | bytes 98312 | tf_op jit(solution)/shard_map/ppermute | solution.py:58
  84.7 1.3 %collective-permute-start.6 = (bf16[1,128,128]{2,1,0:T(8,128)(2,1)S(1)}, bf16[1,128,128]{2,1,0:T(8,128)(2,1)S(1)}, u32[]{:S(2)}, u32[]{:S(2)}) collective-permute-start(bf16[1,128,128]{2,1,0:T(8,128)(2,1)S(1)} %copy-done.4), channel_id=1, source_target_pairs={{4,0},{5,1},{6,2},{7,3},{8,4},{9,5},{10,6},{11,7},{12,8},{13,9},{1... | collective-permute-start | bytes 98312 | tf_op jit(solution)/shard_map/ppermute | solution.py:58
  86.0 0.0 collective-permute-done.3
  86.0 0.0 collective-permute-done.4
  86.0 0.1 maximum_convert_fusion.1
  86.2 0.1 collective-permute-done.5
  86.3 4.2 %collective-permute-done.6 = bf16[1,128,128]{2,1,0:T(8,128)(2,1)S(1)} collective-permute-done((bf16[1,128,128]{2,1,0:T(8,128)(2,1)S(1)}, bf16[1,128,128]{2,1,0:T(8,128)(2,1)S(1)}, u32[]{:S(2)}, u32[]{:S(2)}) %collective-permute-start.6) | collective-permute-done | bytes 32800 | tf_op jit(solution)/shard_map/ppermute | solution.py:58
  90.5 0.1 maximum_convert_fusion
  90.6 0.2 fusion.11
  90.8 1.4 %copy.37 = f32[128,16,128]{2,1,0:T(8,128)} copy(f32[128,16,128]{0,2,1:T(8,128)S(1)} %fusion.11) | data formatting | bytes 2097152
  92.2 0.0 all-to-all-done.1
  92.2 1.4 %fusion.9 = bf16[512,128]{1,0:T(8,128)(2,1)} fusion(bf16[1024,128]{1,0:T(8,128)(2,1)S(1)} %bitcast.42, s32[512]{0:T(512)S(1)} %multiply_add_fusion), kind=kOutput, calls=%fused_computation.18 | convolution fusion | flops 134807552 | bytes 395264 | tf_op jit(solution)/shard_map/dot_general | solution.py:329
  (6 shorter events, 0.0 us)
Async XLA Ops:
  0.6 12.7 %copy-start = (f32[128,16,256]{2,1,0:T(8,128)S(1)}, f32[128,16,256]{2,1,0:T(8,128)}, u32[]{:S(2)}) copy-start(f32[128,16,256]{2,1,0:T(8,128)} %param.6) | copy-start | bytes 6291460
  5.9 27.8 %all-to-all-start = ((bf16[16,65,384]{2,1,0:T(8,128)(2,1)}), bf16[16,65,384]{2,1,0:T(8,128)(2,1)}, u32[]{:S(2)}, u32[]{:S(2)}) async-start(bf16[16,65,384]{2,1,0:T(8,128)(2,1)} %fusion.16), calls=%async_computation | async-start | bytes 1769472 | tf_op jit(solution)/shard_map/all_to_all | solution.py:300
  14.2 5.4 %collective-permute-start = (f32[16,17,128]{2,1,0:T(8,128)S(1)}, f32[16,17,128]{2,1,0:T(8,128)S(1)}, u32[]{:S(2)}, u32[]{:S(2)}) collective-permute-start(f32[16,17,128]{2,1,0:T(8,128)S(1)} %bitcast.44), channel_id=1, source_target_pairs={{1,2},{2,1},{5,6},{6,5},{9,10},{10,9},{13,14},{14,13},{17,18},{18,... | collective-permute-start | bytes 417800 | tf_op jit(solution)/shard_map/ppermute | solution.py:58
  19.5 0.7 copy-start.2
  22.2 7.3 %copy-start.3 = (s32[2,8,8]{2,1,0:T(8,128)S(1)}, s32[2,8,8]{2,1,0:T(8,128)}, u32[]{:S(2)}) copy-start(s32[2,8,8]{2,1,0:T(8,128)} %param.8) | copy-start | bytes 1540
  23.4 21.3 %collective-permute-start.1 = (f32[9,162,128]{2,1,0:T(8,128)}, f32[9,162,128]{2,1,0:T(8,128)}, u32[]{:S(2)}, u32[]{:S(2)}) collective-permute-start(f32[9,162,128]{2,1,0:T(8,128)} %get-tuple-element.43), channel_id=1, source_target_pairs={{0,4},{1,5},{2,6},{3,7},{4,8},{5,9},{6,10},{7,11},{8,12},{9,13},{1... | collective-permute-start | bytes 2239496 | tf_op jit(solution)/shard_map/ppermute | solution.py:58
  28.1 19.3 %collective-permute-start.2 = (f32[9,162,128]{2,1,0:T(8,128)}, f32[9,162,128]{2,1,0:T(8,128)}, u32[]{:S(2)}, u32[]{:S(2)}) collective-permute-start(f32[9,162,128]{2,1,0:T(8,128)} %get-tuple-element.42), channel_id=1, source_target_pairs={{4,0},{5,1},{6,2},{7,3},{8,4},{9,5},{10,6},{11,7},{12,8},{13,9},{1... | collective-permute-start | bytes 2239496 | tf_op jit(solution)/shard_map/ppermute | solution.py:58
  64.2 13.2 %copy-start.7 = (bf16[16,1,128]{2,1,0:T(2,128)(2,1)S(1)}, bf16[16,1,128]{2,1,0:T(2,128)(2,1)}, u32[]{:S(2)}) copy-start(bf16[16,1,128]{2,1,0:T(2,128)(2,1)} %get-tuple-element.26) | copy-start | bytes 12292
  64.2 15.5 %copy-start.6 = (bf16[16,1,128]{2,1,0:T(2,128)(2,1)S(1)}, bf16[16,1,128]{2,1,0:T(2,128)(2,1)}, u32[]{:S(2)}) copy-start(bf16[16,1,128]{2,1,0:T(2,128)(2,1)} %get-tuple-element.28) | copy-start | bytes 12292
  64.2 16.8 %copy-start.1 = (bf16[2,16,128,128]{3,2,1,0:T(8,128)(2,1)S(1)}, bf16[2,16,128,128]{3,2,1,0:T(8,128)(2,1)}, u32[]{:S(2)}) copy-start(bf16[2,16,128,128]{3,2,1,0:T(8,128)(2,1)} %get-tuple-element.27) | copy-start | bytes 3145732
  68.8 12.4 %copy-start.5 = (bf16[1,128,128]{2,1,0:T(8,128)(2,1)S(1)}, bf16[1,128,128]{2,1,0:T(8,128)(2,1)}, u32[]{:S(2)}) copy-start(bf16[1,128,128]{2,1,0:T(8,128)(2,1)} %get-tuple-element.29) | copy-start | bytes 98308
  68.8 15.9 %copy-start.4 = (bf16[1,128,128]{2,1,0:T(8,128)(2,1)S(1)}, bf16[1,128,128]{2,1,0:T(8,128)(2,1)}, u32[]{:S(2)}) copy-start(bf16[1,128,128]{2,1,0:T(8,128)(2,1)} %get-tuple-element.30) | copy-start | bytes 98308
  68.8 23.4 %all-to-all-start.1 = ((bf16[16,64,128]{2,1,0:T(8,128)(2,1)}), bf16[16,64,128]{2,1,0:T(8,128)(2,1)S(1)}, u32[]{:S(2)}, u32[]{:S(2)}) async-start(bf16[16,64,128]{2,1,0:T(8,128)(2,1)} %bitcast.39), calls=%async_computation.1 | async-start | bytes 524288 | tf_op jit(solution)/shard_map/all_to_all | solution.py:326
  77.4 8.7 %collective-permute-start.3 = (bf16[16,1,128]{2,1,0:T(2,128)(2,1)S(1)}, bf16[16,1,128]{2,1,0:T(2,128)(2,1)S(1)}, u32[]{:S(2)}, u32[]{:S(2)}) collective-permute-start(bf16[16,1,128]{2,1,0:T(2,128)(2,1)S(1)} %copy-done.7), channel_id=1, source_target_pairs={{0,1},{1,2},{2,3},{4,5},{5,6},{6,7},{8,9},{9,10},{10,11},{12,13},{... | collective-permute-start | bytes 12296 | tf_op jit(solution)/shard_map/ppermute | solution.py:58
  79.7 6.3 %collective-permute-start.4 = (bf16[16,1,128]{2,1,0:T(2,128)(2,1)S(1)}, bf16[16,1,128]{2,1,0:T(2,128)(2,1)S(1)}, u32[]{:S(2)}, u32[]{:S(2)}) collective-permute-start(bf16[16,1,128]{2,1,0:T(2,128)(2,1)S(1)} %copy-done.6), channel_id=1, source_target_pairs={{1,0},{2,1},{3,2},{5,4},{6,5},{7,6},{9,8},{10,9},{11,10},{13,12},{... | collective-permute-start | bytes 12296 | tf_op jit(solution)/shard_map/ppermute | solution.py:58
  81.1 5.2 %collective-permute-start.5 = (bf16[1,128,128]{2,1,0:T(8,128)(2,1)S(1)}, bf16[1,128,128]{2,1,0:T(8,128)(2,1)S(1)}, u32[]{:S(2)}, u32[]{:S(2)}) collective-permute-start(bf16[1,128,128]{2,1,0:T(8,128)(2,1)S(1)} %copy-done.5), channel_id=1, source_target_pairs={{0,4},{1,5},{2,6},{3,7},{4,8},{5,9},{6,10},{7,11},{8,12},{9,13},{1... | collective-permute-start | bytes 98312 | tf_op jit(solution)/shard_map/ppermute | solution.py:58
  84.7 5.8 %collective-permute-start.6 = (bf16[1,128,128]{2,1,0:T(8,128)(2,1)S(1)}, bf16[1,128,128]{2,1,0:T(8,128)(2,1)S(1)}, u32[]{:S(2)}, u32[]{:S(2)}) collective-permute-start(bf16[1,128,128]{2,1,0:T(8,128)(2,1)S(1)} %copy-done.4), channel_id=1, source_target_pairs={{4,0},{5,1},{6,2},{7,3},{8,4},{9,5},{10,6},{11,7},{12,8},{13,9},{1... | collective-permute-start | bytes 98312 | tf_op jit(solution)/shard_map/ppermute | solution.py:58

commit v23 on v20

--- a/solution.py
+++ b/solution.py
@@ -240,7 +240,7 @@
             pltpu.SemaphoreType.DMA((leaf_count,)),
         ],
     )(codes, scales, bordered, kernels, filament)
-    field, edges, bordered = lax.optimization_barrier((field, edges, bordered))
+
     volt = pl.pallas_call(
         induced_kernel,
         in_specs=[hbm, vmem, vmem],

time: 95.3 us -> 96.4 us (1.012)
  local copies, waits for them, and re-layouts: 17.8 us -> 18.9 us
    squeeze x1, local copies, waits for them, and re-layouts: 0.1 us -> 1.27 us  [field_halo(): x_field = grid_field[0]]
    unnamed x21 -> x15, local copies, waits for them, and re-layouts: 8.36 us -> 8.35 us
  transfers between devices with their start and end apart: 9 -> 9, of which waited for: 4 -> 4; matrix products, arithmetic and copies ran while one was open for 19% -> 20% of each run, Pallas kernels for 8% -> 20%
where the time goes in v23:
time: 96.4 us; the launch traced here: 94.7 us
  starting transfers between devices  31 us (32%)
  Pallas kernels  23.6 us (24%)
  local copies, waits for them, and re-layouts  18.9 us (20%)
  waiting for transfers between devices  8.37 us (9%)
  other arithmetic  8.33 us (9%)
  matrix products  3.5 us (4%)
    ppermute x7, starting transfers between devices, send(): return lax.ppermute(value, AXES, pairs_by(fn))  15.1 us
    pallas_call x1, Pallas kernels, leaf_fields(): pl.pallas_call(leaf_kernel, in_specs=[smem, smem, hbm, hbm, hbm], out_spe...  12.1 us
    all_to_all x1, starting transfers between devices, body(): lax.all_to_all(induced.reshape(owners, capacity, port_count), AXES, split...  8.55 us
    unnamed x15, local copies, waits for them, and re-layouts  8.35 us
    all_to_all x1, starting transfers between devices, body(): got = lax.all_to_all(payload, AXES, split_axis=0, concat_axis=0, tiled=True)  7.4 us
    pallas_call x1, Pallas kernels, filament_field(): pl.pallas_call(filament_kernel, in_specs=[vmem, vmem, vmem], out_specs=vm...  7.05 us
    ppermute x7, waiting for transfers between devices, send(): return lax.ppermute(value, AXES, pairs_by(fn))  4.69 us
    pallas_call x1, Pallas kernels, leaf_fields(): pl.pallas_call(induced_kernel, in_specs=[hbm, vmem, vmem], out_specs=vmem...  4.45 us
  transfers between devices with their start and end apart: 9, of which 4 were waited for; matrix products, arithmetic and copies ran while one was open for 20% of the time, Pallas kernels for 20%

profile of v23, /device:TPU:0, one launch (start us, length us, event | category | flops | bytes accessed | tf_op | source)
XLA Modules:
  0.0 94.7 jit_solution(16621615391376303145)
XLA Ops:
  0.6 0.0 copy-start
  0.6 0.9 fusion.25
  1.5 0.2 convert_reduce_fusion
  1.8 0.5 fusion.3
  2.2 0.1 reshape.75
  2.3 1.0 %copy.46 = bf16[64,8,2,128]{3,1,2,0:T(8,128)(2,1)S(1)} copy(bf16[64,8,2,128]{3,2,1,0:T(2,128)(2,1)} %bitcast.41) | data formatting | bytes 524288
  3.3 1.6 %fusion.6 = bf16[1024,384]{1,0:T(8,128)(2,1)S(1)} fusion(s32[512]{0:T(512)S(1)} %multiply_add_fusion, bf16[512,128]{1,0:T(8,128)(2,1)} %param.10, bf16[512,256]{1,0:T(8,128)(2,1)S(1)} %bitcast.43), kind=kOutput, calls=%fused_computation.15 | convolution fusion | flops 404357120 | bytes 1181696 | tf_op jit(solution)/shard_map/dot_general | solution.py:289
  4.9 1.0 %fusion.16 = bf16[16,65,384]{2,1,0:T(8,128)(2,1)} fusion(bf16[16,1,64]{2,1,0:T(2,128)(2,1)S(1)} %reshape.75, bf16[16,64,384]{2,1,0:T(8,128)(2,1)S(1)} %bitcast.40), kind=kLoop, calls=%fused_computation.29 | loop fusion | flops 2396160 | bytes 1587200 | tf_op jit(solution)/shard_map/concatenate | solution.py:297
  5.9 7.4 %all-to-all-start = ((bf16[16,65,384]{2,1,0:T(8,128)(2,1)}), bf16[16,65,384]{2,1,0:T(8,128)(2,1)}, u32[]{:S(2)}, u32[]{:S(2)}) async-start(bf16[16,65,384]{2,1,0:T(8,128)(2,1)} %fusion.16), calls=%async_computation | async-start | bytes 1769472 | tf_op jit(solution)/shard_map/all_to_all | solution.py:298
  13.3 0.0 copy-done
  13.4 0.3 constant_dynamic-slice_fusion.1
  13.7 0.4 copy.40
  14.2 0.7 collective-permute-start
  14.8 1.9 %constant_dynamic-slice_fusion = f32[128,16,145]{2,1,0:T(8,128)} fusion(f32[128,16,256]{2,1,0:T(8,128)S(1)} %copy-done, s32[]{:T(128)S(6)} %select_n.49), kind=kLoop, calls=%fused_computation.76 | loop fusion | bytes 2375684 | tf_op jit(solution)/shard_map/dynamic-slice.1
  16.8 2.8 %copy.41 = f32[128,16,145]{0,2,1:T(8,128)} copy(f32[128,16,145]{2,1,0:T(8,128)} %constant_dynamic-slice_fusion) | data formatting | bytes 2375680
  19.5 0.0 collective-permute-done
  19.5 0.0 copy-start.1
  19.6 0.7 copy-done.1
  20.2 1.9 %fusion.8 = f32[16,162,128]{2,1,0:T(8,128)S(1)} fusion(s32[]{:T(128)S(6)} %select_n.50, f32[16,17,128]{2,1,0:T(8,128)} %copy-done.1, f32[16,145,128]{2,1,0:T(8,128)} %bitcast.34), kind=kLoop, calls=%fused_computation.17 | loop fusion | flops 663552 | bytes 2654212 | tf_op jit(solution)/shard_map/concatenate | solution.py:79
  22.1 0.0 copy-start.2
  22.2 1.3 %fusion.34 = (f32[9,162,128]{2,1,0:T(8,128)}, f32[9,162,128]{2,1,0:T(8,128)}) fusion(f32[16,162,128]{2,1,0:T(8,128)S(1)} %fusion.8), kind=kLoop, calls=%fused_computation.82 | loop fusion | bytes 2985984 | tf_op jit(solution)/shard_map/slice | solution.py:82
  23.4 4.7 %collective-permute-start.1 = (f32[9,162,128]{2,1,0:T(8,128)}, f32[9,162,128]{2,1,0:T(8,128)}, u32[]{:S(2)}, u32[]{:S(2)}) collective-permute-start(f32[9,162,128]{2,1,0:T(8,128)} %get-tuple-element.31), channel_id=1, source_target_pairs={{0,4},{1,5},{2,6},{3,7},{4,8},{5,9},{6,10},{7,11},{8,12},{9,13},{1... | collective-permute-start | bytes 2239496 | tf_op jit(solution)/shard_map/ppermute | solution.py:58
  28.1 1.3 %collective-permute-start.2 = (f32[9,162,128]{2,1,0:T(8,128)}, f32[9,162,128]{2,1,0:T(8,128)}, u32[]{:S(2)}, u32[]{:S(2)}) collective-permute-start(f32[9,162,128]{2,1,0:T(8,128)} %get-tuple-element.30), channel_id=1, source_target_pairs={{4,0},{5,1},{6,2},{7,3},{8,4},{9,5},{10,6},{11,7},{12,8},{13,9},{1... | collective-permute-start | bytes 2239496 | tf_op jit(solution)/shard_map/ppermute | solution.py:58
  29.4 0.0 copy-done.2
  29.4 0.6 convert_bitcast_fusion.scale_ref
  30.0 3.7 %all-to-all-done = bf16[16,65,384]{2,1,0:T(8,128)(2,1)} async-done(((bf16[16,65,384]{2,1,0:T(8,128)(2,1)}), bf16[16,65,384]{2,1,0:T(8,128)(2,1)}, u32[]{:S(2)}, u32[]{:S(2)}) %all-to-all-start) | async-done | bytes 798752 | tf_op jit(solution)/shard_map/all_to_all | solution.py:298
  33.7 1.2 %slice.67 = bf16[16,64,384]{2,1,0:T(8,128)(2,1)S(1)} slice(bf16[16,65,384]{2,1,0:T(8,128)(2,1)} %all-to-all-done), slice={[0:16], [0:64], [0:384]} | slice | bytes 1572864 | tf_op jit(solution)/shard_map/slice | solution.py:299
  34.9 0.8 slice.68
  35.7 0.7 slice.69.cur_ref
  36.5 2.1 %copy.42 = bf16[1024,256]{0,1:T(8,128)(2,1)} copy(bf16[1024,256]{1,0:T(8,128)(2,1)} %slice.68) | data formatting | bytes 1048576
  38.5 0.8 fusion.22
  39.3 0.7 reshape.72.row_leaf_ref
  40.0 7.0 %shard_map.77.fil_hbm = f32[16,256,128]{2,1,0:T(8,128)} custom-call(s32[1,1024]{1,0:T(1,128)} %reshape.72.row_leaf_ref, bf16[256,1024]{1,0:T(8,128)(2,1)} %bitcast.35, bf16[1024,128]{1,0:T(8,128)(2,1)} %slice.69.cur_ref), custom_call_target="tpu_custom_call" | custom-call | tf_op jit(solution)/shard_map/pallas_call | solution.py:118
  47.0 0.0 collective-permute-done.1
  47.0 0.3 collective-permute-done.2
  47.4 1.6 %pad_maximum_fusion = f32[34,162,128]{2,1,0:T(8,128)S(1)} fusion(f32[9,162,128]{2,1,0:T(8,128)} %collective-permute-done.2, f32[16,162,128]{2,1,0:T(8,128)S(1)} %fusion.8, f32[9,162,128]{2,1,0:T(8,128)} %collective-permute-done.1), kind=kLoop, calls=%fused_computation | loop fusion | flops 1410048 | bytes 5640192 | tf_op jit(solution)/shard_map/concatenate | solution.py:84
  48.9 0.7 fusion.1
  49.6 0.2 maximum_bitcast_fusion
  49.9 2.2 %copy.34 = bf16[4,10,2,8,16,128]{5,4,3,2,1,0:T(8,128)(2,1)} copy(bf16[4,10,2,8,16,128]{5,4,1,3,0,2:T(8,128)(2,1)S(1)} %maximum_bitcast_fusion) | data formatting | bytes 5242880 | tf_op jit(solution)/shard_map/transpose | solution.py:24
  52.1 4.5 %shard_map.79 = bf16[1024,128]{1,0:T(8,128)(2,1)} custom-call(bf16[4,10,2,128,128]{4,3,2,1,0:T(8,128)(2,1)} %bitcast.29, s32[1,1024]{1,0:T(1,128)} %reshape.72.row_leaf_ref, bf16[256,1024]{1,0:T(8,128)(2,1)} %bitcast.36), custom_call_target="tpu_custom_call" | custom-call | tf_op jit(solution)/shard_map/pallas_call | solution.py:244
  56.6 8.6 %all-to-all-start.1 = ((bf16[16,64,128]{2,1,0:T(8,128)(2,1)}), bf16[16,64,128]{2,1,0:T(8,128)(2,1)S(1)}, u32[]{:S(2)}, u32[]{:S(2)}) async-start(bf16[16,64,128]{2,1,0:T(8,128)(2,1)} %bitcast.39), calls=%async_computation.1 | async-start | bytes 524288 | tf_op jit(solution)/shard_map/all_to_all | solution.py:324
  65.1 12.1 %shard_map.78 = (bf16[2,16,128,128]{3,2,1,0:T(8,128)(2,1)}, bf16[16,1,128]{2,1,0:T(2,128)(2,1)}, bf16[16,1,128]{2,1,0:T(2,128)(2,1)}, bf16[1,128,128]{2,1,0:T(8,128)(2,1)}, bf16[1,128,128]{2,1,0:T(8,128)(2,1)}) custom-call(s32[16,8]{1,0:T(8,128)} %bitcast.45, s32[16,8]{1,0:T(8,128)} %convert_bitcast_fusion.scale_ref, bf16[4,10,2,128,128]{4,3,2,1,0:T(8,128)(2,1)} %bitcast.30, ...), custom_call_target="tpu_custom_call" | custom-call | tf_op jit(solution)/shard_map/pallas_call | solution.py:223
  77.2 0.0 copy-start.4
  77.2 0.0 copy-start.3
  77.2 2.3 %collective-permute-start.3 = (bf16[16,1,128]{2,1,0:T(2,128)(2,1)}, bf16[16,1,128]{2,1,0:T(2,128)(2,1)S(1)}, u32[]{:S(2)}, u32[]{:S(2)}) collective-permute-start(bf16[16,1,128]{2,1,0:T(2,128)(2,1)} %get-tuple-element.15), channel_id=1, source_target_pairs={{0,1},{1,2},{2,3},{4,5},{5,6},{6,7},{8,9},{9,10},{10,11},{12,13},{... | collective-permute-start | bytes 12296 | tf_op jit(solution)/shard_map/ppermute | solution.py:58
  79.6 1.3 %collective-permute-start.4 = (bf16[16,1,128]{2,1,0:T(2,128)(2,1)}, bf16[16,1,128]{2,1,0:T(2,128)(2,1)S(1)}, u32[]{:S(2)}, u32[]{:S(2)}) collective-permute-start(bf16[16,1,128]{2,1,0:T(2,128)(2,1)} %get-tuple-element.17), channel_id=1, source_target_pairs={{1,0},{2,1},{3,2},{5,4},{6,5},{7,6},{9,8},{10,9},{11,10},{13,12},{... | collective-permute-start | bytes 12296 | tf_op jit(solution)/shard_map/ppermute | solution.py:58
  80.9 1.3 %slice_bitcast_fusion.1 = (bf16[16,128,128]{2,1,0:T(8,128)(2,1)S(1)}, bf16[16,128,128]{2,1,0:T(8,128)(2,1)S(1)}) fusion(bf16[2,16,128,128]{3,2,1,0:T(8,128)(2,1)} %get-tuple-element.16), kind=kLoop, calls=%fused_computation.33 | loop fusion | bytes 2097152 | tf_op jit(solution)/shard_map/squeeze | solution.py:88
  82.2 0.0 copy-done.4
  82.2 3.6 %collective-permute-start.5 = (bf16[1,128,128]{2,1,0:T(8,128)(2,1)S(1)}, bf16[1,128,128]{2,1,0:T(8,128)(2,1)S(1)}, u32[]{:S(2)}, u32[]{:S(2)}) collective-permute-start(bf16[1,128,128]{2,1,0:T(8,128)(2,1)S(1)} %copy-done.4), channel_id=1, source_target_pairs={{0,4},{1,5},{2,6},{3,7},{4,8},{5,9},{6,10},{7,11},{8,12},{9,13},{1... | collective-permute-start | bytes 98312 | tf_op jit(solution)/shard_map/ppermute | solution.py:58
  85.7 0.0 copy-done.3
  85.8 1.3 %collective-permute-start.6 = (bf16[1,128,128]{2,1,0:T(8,128)(2,1)S(1)}, bf16[1,128,128]{2,1,0:T(8,128)(2,1)S(1)}, u32[]{:S(2)}, u32[]{:S(2)}) collective-permute-start(bf16[1,128,128]{2,1,0:T(8,128)(2,1)S(1)} %copy-done.3), channel_id=1, source_target_pairs={{4,0},{5,1},{6,2},{7,3},{8,4},{9,5},{10,6},{11,7},{12,8},{13,9},{1... | collective-permute-start | bytes 98312 | tf_op jit(solution)/shard_map/ppermute | solution.py:58
  87.1 0.0 collective-permute-done.3
  87.1 0.0 collective-permute-done.4
  87.1 0.1 maximum_convert_fusion.1
  87.2 0.1 collective-permute-done.5
  87.3 4.2 %collective-permute-done.6 = bf16[1,128,128]{2,1,0:T(8,128)(2,1)S(1)} collective-permute-done((bf16[1,128,128]{2,1,0:T(8,128)(2,1)S(1)}, bf16[1,128,128]{2,1,0:T(8,128)(2,1)S(1)}, u32[]{:S(2)}, u32[]{:S(2)}) %collective-permute-start.6) | collective-permute-done | bytes 32800 | tf_op jit(solution)/shard_map/ppermute | solution.py:58
  91.6 0.1 maximum_convert_fusion
  91.7 0.2 fusion.11
  91.8 1.4 %copy.37 = f32[128,16,128]{2,1,0:T(8,128)} copy(f32[128,16,128]{0,2,1:T(8,128)S(1)} %fusion.11) | data formatting | bytes 2097152
  93.2 0.0 all-to-all-done.1
  93.2 1.4 %fusion.9 = bf16[512,128]{1,0:T(8,128)(2,1)} fusion(bf16[1024,128]{1,0:T(8,128)(2,1)S(1)} %bitcast.42, s32[512]{0:T(512)S(1)} %multiply_add_fusion), kind=kOutput, calls=%fused_computation.18 | convolution fusion | flops 134807552 | bytes 395264 | tf_op jit(solution)/shard_map/dot_general | solution.py:327
  (3 shorter events, 0.0 us)
Async XLA Ops:
  0.6 12.7 %copy-start = (f32[128,16,256]{2,1,0:T(8,128)S(1)}, f32[128,16,256]{2,1,0:T(8,128)}, u32[]{:S(2)}) copy-start(f32[128,16,256]{2,1,0:T(8,128)} %param.6) | copy-start | bytes 6291460
  5.9 27.8 %all-to-all-start = ((bf16[16,65,384]{2,1,0:T(8,128)(2,1)}), bf16[16,65,384]{2,1,0:T(8,128)(2,1)}, u32[]{:S(2)}, u32[]{:S(2)}) async-start(bf16[16,65,384]{2,1,0:T(8,128)(2,1)} %fusion.16), calls=%async_computation | async-start | bytes 1769472 | tf_op jit(solution)/shard_map/all_to_all | solution.py:298
  14.2 5.4 %collective-permute-start = (f32[16,17,128]{2,1,0:T(8,128)S(1)}, f32[16,17,128]{2,1,0:T(8,128)S(1)}, u32[]{:S(2)}, u32[]{:S(2)}) collective-permute-start(f32[16,17,128]{2,1,0:T(8,128)S(1)} %bitcast.44), channel_id=1, source_target_pairs={{1,2},{2,1},{5,6},{6,5},{9,10},{10,9},{13,14},{14,13},{17,18},{18,... | collective-permute-start | bytes 417800 | tf_op jit(solution)/shard_map/ppermute | solution.py:58
  19.5 0.7 copy-start.1
  22.1 7.3 %copy-start.2 = (s32[2,8,8]{2,1,0:T(8,128)S(1)}, s32[2,8,8]{2,1,0:T(8,128)}, u32[]{:S(2)}) copy-start(s32[2,8,8]{2,1,0:T(8,128)} %param.8) | copy-start | bytes 1540
  23.4 23.6 %collective-permute-start.1 = (f32[9,162,128]{2,1,0:T(8,128)}, f32[9,162,128]{2,1,0:T(8,128)}, u32[]{:S(2)}, u32[]{:S(2)}) collective-permute-start(f32[9,162,128]{2,1,0:T(8,128)} %get-tuple-element.31), channel_id=1, source_target_pairs={{0,4},{1,5},{2,6},{3,7},{4,8},{5,9},{6,10},{7,11},{8,12},{9,13},{1... | collective-permute-start | bytes 2239496 | tf_op jit(solution)/shard_map/ppermute | solution.py:58
  28.1 19.3 %collective-permute-start.2 = (f32[9,162,128]{2,1,0:T(8,128)}, f32[9,162,128]{2,1,0:T(8,128)}, u32[]{:S(2)}, u32[]{:S(2)}) collective-permute-start(f32[9,162,128]{2,1,0:T(8,128)} %get-tuple-element.30), channel_id=1, source_target_pairs={{4,0},{5,1},{6,2},{7,3},{8,4},{9,5},{10,6},{11,7},{12,8},{13,9},{1... | collective-permute-start | bytes 2239496 | tf_op jit(solution)/shard_map/ppermute | solution.py:58
  56.6 36.7 %all-to-all-start.1 = ((bf16[16,64,128]{2,1,0:T(8,128)(2,1)}), bf16[16,64,128]{2,1,0:T(8,128)(2,1)S(1)}, u32[]{:S(2)}, u32[]{:S(2)}) async-start(bf16[16,64,128]{2,1,0:T(8,128)(2,1)} %bitcast.39), calls=%async_computation.1 | async-start | bytes 524288 | tf_op jit(solution)/shard_map/all_to_all | solution.py:324
  77.2 4.9 %copy-start.4 = (bf16[1,128,128]{2,1,0:T(8,128)(2,1)S(1)}, bf16[1,128,128]{2,1,0:T(8,128)(2,1)}, u32[]{:S(2)}) copy-start(bf16[1,128,128]{2,1,0:T(8,128)(2,1)} %get-tuple-element.18) | copy-start | bytes 98308
  77.2 8.5 %copy-start.3 = (bf16[1,128,128]{2,1,0:T(8,128)(2,1)S(1)}, bf16[1,128,128]{2,1,0:T(8,128)(2,1)}, u32[]{:S(2)}) copy-start(bf16[1,128,128]{2,1,0:T(8,128)(2,1)} %get-tuple-element.19) | copy-start | bytes 98308
  77.2 9.8 %collective-permute-start.3 = (bf16[16,1,128]{2,1,0:T(2,128)(2,1)}, bf16[16,1,128]{2,1,0:T(2,128)(2,1)S(1)}, u32[]{:S(2)}, u32[]{:S(2)}) collective-permute-start(bf16[16,1,128]{2,1,0:T(2,128)(2,1)} %get-tuple-element.15), channel_id=1, source_target_pairs={{0,1},{1,2},{2,3},{4,5},{5,6},{6,7},{8,9},{9,10},{10,11},{12,13},{... | collective-permute-start | bytes 12296 | tf_op jit(solution)/shard_map/ppermute | solution.py:58
  79.6 7.5 %collective-permute-start.4 = (bf16[16,1,128]{2,1,0:T(2,128)(2,1)}, bf16[16,1,128]{2,1,0:T(2,128)(2,1)S(1)}, u32[]{:S(2)}, u32[]{:S(2)}) collective-permute-start(bf16[16,1,128]{2,1,0:T(2,128)(2,1)} %get-tuple-element.17), channel_id=1, source_target_pairs={{1,0},{2,1},{3,2},{5,4},{6,5},{7,6},{9,8},{10,9},{11,10},{13,12},{... | collective-permute-start | bytes 12296 | tf_op jit(solution)/shard_map/ppermute | solution.py:58
  82.2 5.1 %collective-permute-start.5 = (bf16[1,128,128]{2,1,0:T(8,128)(2,1)S(1)}, bf16[1,128,128]{2,1,0:T(8,128)(2,1)S(1)}, u32[]{:S(2)}, u32[]{:S(2)}) collective-permute-start(bf16[1,128,128]{2,1,0:T(8,128)(2,1)S(1)} %copy-done.4), channel_id=1, source_target_pairs={{0,4},{1,5},{2,6},{3,7},{4,8},{5,9},{6,10},{7,11},{8,12},{9,13},{1... | collective-permute-start | bytes 98312 | tf_op jit(solution)/shard_map/ppermute | solution.py:58
  85.8 5.8 %collective-permute-start.6 = (bf16[1,128,128]{2,1,0:T(8,128)(2,1)S(1)}, bf16[1,128,128]{2,1,0:T(8,128)(2,1)S(1)}, u32[]{:S(2)}, u32[]{:S(2)}) collective-permute-start(bf16[1,128,128]{2,1,0:T(8,128)(2,1)S(1)} %copy-done.3), channel_id=1, source_target_pairs={{4,0},{5,1},{6,2},{7,3},{8,4},{9,5},{10,6},{11,7},{12,8},{13,9},{1... | collective-permute-start | bytes 98312 | tf_op jit(solution)/shard_map/ppermute | solution.py:58
